TPU v7x, 128 devices: a whole 4x4x4 slice. The times are simulated.
128 devices in a mesh: req: 8 (over y, core), voc: 16 (over x, z).
Axes of the slice: x: 4, y: 4, z: 4, core: 2. Of those that a mesh axis runs over, the one named last changes fastest.
Arguments:
- hidden: bfloat16 [16384, 1536], P(('req', 'voc')), may hold values from -64 to 64
- norm_gain: float32 [1536], replicated, may hold values from 0.1 to 1.9
- head: bfloat16 [1536, 49152], P(None, 'voc'), may hold values from -8 to 8
- targets: int32 [16384], P(('req', 'voc')), may hold values from 0 to 49151
- bounds: int32 [128, 2], P(('req', 'voc')), may hold values from 0 to 128, as said below
Outputs:
- logprob: float32 [16384], P(('req', 'voc'))
- entropy: float32 [16384], P(('req', 'voc'))
- target_logit: float32 [16384], P(('req', 'voc'))
- mean_entropy: float32 [1], replicated
Inputs may be any that keep to these rules, and one draw needn't show every extreme that they name: bounds[d] = (lo, hi): slots lo to hi - 1 of device d hold live response rows; 1 <= hi - lo <= 96, lo <= 32; some device has hi - lo = 96 and hi = 128, some has lo = 0.
All inputs are finite; a program needn't handle non-finite values.
Results may differ from a plain program's by a relative error of at most 0.00075.
The roundings to bfloat16 on the way count: a program that leaves them out, or rounds other values in their place, can miss the bound.
Values may be sent and summed in bfloat16 or wider, within the bound.
No kernel may reach another device: no remote copies, remote signals or barrier semaphores. Data moves between devices by JAX's collectives and lax.ppermute only.
A program may use at most 64 MiB of HBM per device.

v0:
```python
import jax
import jax.numpy as jnp
from jax import lax
from jax.sharding import PartitionSpec as P


def joined(part, axis, combine):
    gathered = jax.tree.map(lambda a: lax.all_gather(a, axis), part)

    def take(source):
        return jax.tree.map(lambda a: lax.dynamic_index_in_dim(a, source, 0, False), gathered)

    return lax.fori_loop(
        1, lax.axis_size(axis), lambda source, state: combine(state, take(source)), take(0)
    )


def pick_block(count):
    size = min(count, 512)
    while count % size:
        size -= 1
    return size


def combine_stats(first, second):
    top = jnp.maximum(first[0], second[0])
    weight_a = jnp.exp(first[0] - top)
    weight_b = jnp.exp(second[0] - top)
    return (
        top,
        first[1] * weight_a + second[1] * weight_b,
        first[2] * weight_a + second[2] * weight_b,
        first[3] + second[3],
    )


def shard_stats(gathered, local_ids, head):
    count = gathered.shape[0]
    width = gathered.shape[1]
    block = pick_block(count)
    columns = jnp.arange(head.shape[1], dtype=jnp.int32)

    def one_block(pair):
        rows_in, ids = pair
        logits = jnp.dot(rows_in, head, preferred_element_type=jnp.float32)
        top = jnp.max(logits, axis=-1)
        expo = jnp.exp(logits - top[:, None])
        total = jnp.sum(expo, axis=-1)
        weighted = jnp.sum(expo * logits, axis=-1)
        picked = jnp.sum(jnp.where(columns[None, :] == ids[:, None], logits, 0.0), axis=-1)
        return (top, total, weighted, picked)

    outputs = lax.map(
        one_block,
        (gathered.reshape(count // block, block, width), local_ids.reshape(count // block, block)),
    )
    return tuple((a.reshape(count) for a in outputs))


def shards(hidden, norm_gain, head, targets, bounds):
    slots = hidden.shape[0]
    shard_width = head.shape[1]
    position = lax.axis_index("voc")
    values = hidden.astype(jnp.float32)
    meansq = jnp.mean(values * values, axis=-1, keepdims=True)
    normed = (values * lax.rsqrt(meansq + 1e-05) * norm_gain).astype(jnp.bfloat16)
    start = bounds[0, 0]
    finish = bounds[0, 1]
    gathered, gathered_ids = (
        lax.all_gather(normed, "voc", axis=0, tiled=True),
        lax.all_gather(targets, "voc", axis=0, tiled=True),
    )
    local_ids = gathered_ids - position * shard_width
    stats = shard_stats(gathered, local_ids, head)
    merged = joined(stats, "voc", combine_stats)
    top, total, weighted, picked = [
        lax.dynamic_slice_in_dim(a, position * slots, slots, 0) for a in merged
    ]
    lse = top + jnp.log(total)
    row_entropy = lse - weighted / total
    row_logprob = picked - lse
    slot_index = jnp.arange(slots, dtype=jnp.int32)
    live = (slot_index >= start) & (slot_index < finish)
    zero = jnp.zeros((slots,), jnp.float32)
    entropy = jnp.where(live, row_entropy, zero)
    logprob = jnp.where(live, row_logprob, zero)
    target_logit = jnp.where(live, picked, zero)
    ent_sum, live_count = lax.psum(
        (jnp.sum(entropy), jnp.sum(live.astype(jnp.float32))), ("req", "voc")
    )
    mean_entropy = (ent_sum / live_count).reshape(1)
    return (logprob, entropy, target_logit, mean_entropy)


def solution(mesh):
    placed = (
        P(("req", "voc"), None),
        P(),
        P(None, "voc"),
        P(("req", "voc")),
        P(("req", "voc"), None),
    )
    return jax.shard_map(
        shards,
        mesh=mesh,
        in_specs=placed,
        out_specs=(P(("req", "voc")), P(("req", "voc")), P(("req", "voc")), P()),
        check_vma=False,
    )
```

profile of v0, /device:TPU:0, one launch (start us, length us, event | category | flops | bytes accessed | tf_op | source)
XLA Modules:
  0.0 285.9 jit_solution(3310339040187960190)
XLA Ops:
  7.2 0.0 all-gather.7.cloned.1.call-start
  7.2 1.2 fusion.7
  8.4 1.9 fusion.9
  10.3 0.0 all-gather.7.cloned.1.call-update
  10.4 22.1 %all-gather = s32[16,1,128]{2,1,0:T(1,128)S(1)} all-gather(s32[1,1,128]{2,1,0:T(1,128)} %bitcast.76), channel_id=1, replica_groups=mesh['req'=8,'voc'=16] {'voc'}, dimensions={0}, use_global_device_ids=true | all-gather | bytes 8704 | tf_op jit(solution)/shard_map/all_gather | solution.py:71
  32.5 1.3 fusion.12
  33.8 2.0 convert_reduce_fusion
  35.8 38.6 %all-gather.7.cloned.1.call-done = bf16[2048,1536]{1,0:T(8,128)(2,1)} async-done(((bf16[128,1536]{1,0:T(8,128)(2,1)}), bf16[2048,1536]{1,0:T(8,128)(2,1)}) %all-gather.7.cloned.1.call-update) | async-done | bytes 6291472 | tf_op jit(solution)/shard_map/all_gather | solution.py:70
  74.4 44.3 %while.39 = (s32[]{:T(128)}, f32[4,512]{1,0:T(4,128)S(1)}, f32[4,512]{1,0:T(4,128)S(1)}, f32[4,512]{1,0:T(4,128)S(1)}, f32[4,512]{1,0:T(4,128)S(1)}, /*index=5*/...) while((s32[]{:T(128)}, f32[4,512]{1,0:T(4,128)S(1)}, ...), condition=%wide.region_6.7_spmd.clone, body=%wide.region_1.6_spmd.clone.sunk | while | flops 4844419072 | bytes 23626360 | solution.py:53
  74.4 8.2 %fusion.17 = (f32[512]{0:T(512)S(1)}, f32[512,3072]{1,0:T(8,128)S(1)}) fusion(bf16[1536,3072]{1,0:T(8,128)(2,1)} %get-tuple-element.510, bf16[4,512,1536]{2,1,0:T(8,128)(2,1)} %get-tuple-element.509, s32[]{:T(128)} %get-tuple-element.494), kind=kOutput, calls=%fused_computation.37.clone.1 | convolution fusion | flops 4833410560 | bytes 17304064 | tf_op jit(solution)/shard_map/while/body/eval_jaxpr/dot_general | solution.py:45
  82.6 2.6 multiply_reduce_fusion.2
  85.3 0.1 dynamic_update_slice.24
  85.3 0.1 dynamic_update_slice.22
  85.4 0.1 dynamic_update_slice.21
  85.5 8.2 %fusion.17 = (f32[512]{0:T(512)S(1)}, f32[512,3072]{1,0:T(8,128)S(1)}) fusion(bf16[1536,3072]{1,0:T(8,128)(2,1)} %get-tuple-element.510, bf16[4,512,1536]{2,1,0:T(8,128)(2,1)} %get-tuple-element.509, s32[]{:T(128)} %get-tuple-element.494), kind=kOutput, calls=%fused_computation.37.clone.1 | convolution fusion | flops 4833410560 | bytes 17304064 | tf_op jit(solution)/shard_map/while/body/eval_jaxpr/dot_general | solution.py:45
  93.7 2.6 multiply_reduce_fusion.2
  96.4 0.1 dynamic_update_slice.24
  96.4 0.1 dynamic_update_slice.22
  96.5 0.1 dynamic_update_slice.21
  96.6 8.2 %fusion.17 = (f32[512]{0:T(512)S(1)}, f32[512,3072]{1,0:T(8,128)S(1)}) fusion(bf16[1536,3072]{1,0:T(8,128)(2,1)} %get-tuple-element.510, bf16[4,512,1536]{2,1,0:T(8,128)(2,1)} %get-tuple-element.509, s32[]{:T(128)} %get-tuple-element.494), kind=kOutput, calls=%fused_computation.37.clone.1 | convolution fusion | flops 4833410560 | bytes 17304064 | tf_op jit(solution)/shard_map/while/body/eval_jaxpr/dot_general | solution.py:45
  104.8 2.6 multiply_reduce_fusion.2
  107.5 0.1 dynamic_update_slice.24
  107.5 0.1 dynamic_update_slice.22
  107.6 0.1 dynamic_update_slice.21
  107.7 8.2 %fusion.17 = (f32[512]{0:T(512)S(1)}, f32[512,3072]{1,0:T(8,128)S(1)}) fusion(bf16[1536,3072]{1,0:T(8,128)(2,1)} %get-tuple-element.510, bf16[4,512,1536]{2,1,0:T(8,128)(2,1)} %get-tuple-element.509, s32[]{:T(128)} %get-tuple-element.494), kind=kOutput, calls=%fused_computation.37.clone.1 | convolution fusion | flops 4833410560 | bytes 17304064 | tf_op jit(solution)/shard_map/while/body/eval_jaxpr/dot_general | solution.py:45
  115.9 2.6 multiply_reduce_fusion.2
  118.6 0.1 dynamic_update_slice.24
  118.6 0.1 dynamic_update_slice.22
  118.7 0.1 dynamic_update_slice.21
  118.8 23.4 %all-gather.3 = f32[16,1,2048]{2,1,0:T(1,128)S(1)} all-gather(f32[1,1,2048]{2,1,0:T(1,128)S(1)} %reshape.39), channel_id=1, replica_groups=mesh['req'=8,'voc'=16] {'voc'}, dimensions={0}, use_global_device_ids=true | all-gather | bytes 139264 | tf_op jit(solution)/shard_map/all_gather | solution.py:8
  142.2 21.5 %all-gather.4 = f32[16,1,2048]{2,1,0:T(1,128)S(1)} all-gather(f32[1,1,2048]{2,1,0:T(1,128)S(1)} %reshape.41), channel_id=1, replica_groups=mesh['req'=8,'voc'=16] {'voc'}, dimensions={0}, use_global_device_ids=true | all-gather | bytes 139264 | tf_op jit(solution)/shard_map/all_gather | solution.py:8
  163.8 23.0 %all-gather.1 = f32[16,1,2048]{2,1,0:T(1,128)S(1)} all-gather(f32[1,1,2048]{2,1,0:T(1,128)S(1)} %reshape.35), channel_id=1, replica_groups=mesh['req'=8,'voc'=16] {'voc'}, dimensions={0}, use_global_device_ids=true | all-gather | bytes 139264 | tf_op jit(solution)/shard_map/all_gather | solution.py:8
  186.9 21.5 %all-gather.2 = f32[16,1,2048]{2,1,0:T(1,128)S(1)} all-gather(f32[1,1,2048]{2,1,0:T(1,128)S(1)} %reshape.37), channel_id=1, replica_groups=mesh['req'=8,'voc'=16] {'voc'}, dimensions={0}, use_global_device_ids=true | all-gather | bytes 139264 | tf_op jit(solution)/shard_map/all_gather | solution.py:8
  208.5 2.1 while.38
  210.6 1.2 fusion.10
  211.8 64.7 %all-reduce = (f32[]{:T(128)}, f32[]{:T(128)}) all-reduce(f32[]{:T(128)} %get-tuple-element.346, f32[]{:T(128)} %get-tuple-element.344), channel_id=1, replica_groups=mesh['req'=8,'voc'=16] {'req','voc'}, use_global_device_ids=true, to_apply=%region_10.11 | all-reduce | flops 2 | bytes 16 | tf_op jit(solution)/shard_map/psum | solution.py:88
  (117 shorter events, 1.7 us)
Async XLA Ops:
  7.2 67.2 %all-gather.7.cloned.1.call-start = ((), (), s32[]{:S(2)}) async-start(), calls=%async_computation | async-start | bytes 6684672 | tf_op jit(solution)/shard_map/all_gather | solution.py:70
Sparse Core Ops, SparseCore 0:
  10.5 63.8 all-gather.6
where the time goes:
time: 287 us; the launch traced here: 286 us
  blocking collectives  176 us (61%)
  waiting for transfers between devices  38.6 us (13%)
  matrix products  32.9 us (11%)
  other arithmetic  17.2 us (6%)
  between operations  16.7 us (6%)
  local copies, waits for them, and re-layouts  3.1 us (1%)
    all_gather x4, blocking collectives, joined(): gathered = jax.tree.map(lambda a: lax.all_gather(a, axis), part)  89.4 us
    psum x1, blocking collectives, shards(): lax.psum((jnp.sum(entropy), jnp.sum(live.astype(jnp.float32))), ('req', '...  64.7 us
    all_gather x1, waiting for transfers between devices, shards(): lax.all_gather(normed, 'voc', axis=0, tiled=True)  38.6 us
    dot_general x4, matrix products, one_block(): logits = jnp.dot(rows_in, head, preferred_element_type=jnp.float32)  32.9 us
    all_gather x1, blocking collectives, shards(): lax.all_gather(targets, 'voc', axis=0, tiled=True)  22.1 us
    reduce_sum x4, other arithmetic, one_block(): weighted = jnp.sum(expo * logits, axis=-1)  10.4 us
  transfers between devices with their start and end apart: 1, of which 1 were waited for; matrix products, arithmetic and copies ran while one was open for 1% of the time, Pallas kernels for 0%

commit v1 on v0

v1 whole, which is shorter than its diff:
```python
import jax
import jax.numpy as jnp
from jax import lax
from jax.sharding import PartitionSpec as P

LIVE = 96


def pick_block(count):
    size = min(count, 512)
    while count % size:
        size -= 1
    return size


def combine_stats(first, second):
    top = jnp.maximum(first[0], second[0])
    weight_a = jnp.exp(first[0] - top)
    weight_b = jnp.exp(second[0] - top)
    return jnp.stack(
        [
            top,
            first[1] * weight_a + second[1] * weight_b,
            first[2] * weight_a + second[2] * weight_b,
            first[3] + second[3],
        ]
    )


def butterfly(value, axis, combine):
    size = lax.axis_size(axis)
    index = lax.axis_index(axis)
    step = 1
    while step < size:
        other = lax.ppermute(value, axis, [(i, i ^ step) for i in range(size)])
        upper = (index & step) != 0
        first = jnp.where(upper, other, value)
        second = jnp.where(upper, value, other)
        value = combine(first, second)
        step *= 2
    return value


def shard_stats(gathered, local_ids, head):
    count = gathered.shape[0]
    width = gathered.shape[1]
    block = pick_block(count)
    columns = jnp.arange(head.shape[1], dtype=jnp.int32)

    def one_block(pair):
        rows_in, ids = pair
        logits = jnp.dot(rows_in, head, preferred_element_type=jnp.float32)
        top = jnp.max(logits, axis=-1)
        expo = jnp.exp(logits - top[:, None])
        total = jnp.sum(expo, axis=-1)
        weighted = jnp.sum(expo * logits, axis=-1)
        picked = jnp.sum(jnp.where(columns[None, :] == ids[:, None], logits, 0.0), axis=-1)
        return jnp.stack([top, total, weighted, picked])

    outputs = lax.map(
        one_block,
        (gathered.reshape(count // block, block, width), local_ids.reshape(count // block, block)),
    )
    return jnp.transpose(outputs, (1, 0, 2)).reshape(4, count)


def shards(hidden, norm_gain, head, targets, bounds):
    slots = hidden.shape[0]
    shard_width = head.shape[1]
    groups = lax.axis_size("voc")
    position = lax.axis_index("voc")
    start = bounds[0, 0]
    finish = bounds[0, 1]
    live_count = finish - start
    rows = lax.dynamic_slice_in_dim(hidden, start, LIVE, 0)
    values = rows.astype(jnp.float32)
    meansq = jnp.mean(values * values, axis=-1, keepdims=True)
    normed = (values * lax.rsqrt(meansq + 1e-05) * norm_gain).astype(jnp.bfloat16)
    ids = lax.dynamic_slice_in_dim(targets, start, LIVE, 0)
    meta = jnp.concatenate([ids, jnp.full((8,), live_count, jnp.int32)])
    gathered = lax.all_gather(normed, "voc", axis=0, tiled=True)
    gathered_meta = lax.all_gather(meta, "voc", axis=0)
    gathered_ids = gathered_meta[:, :LIVE].reshape(groups * LIVE)
    counts = gathered_meta[:, LIVE]
    local_ids = gathered_ids - position * shard_width
    stats = shard_stats(gathered, local_ids, head)
    merged = butterfly(stats, "voc", combine_stats)
    top, total, weighted, picked = merged[0], merged[1], merged[2], merged[3]
    lse = top + jnp.log(total)
    row_entropy = lse - weighted / total
    row_logprob = picked - lse
    slot = jnp.arange(LIVE, dtype=jnp.int32)
    group_live = slot[None, :] < counts[:, None]
    group_entropy = jnp.where(group_live, row_entropy.reshape(groups, LIVE), 0.0)
    totals = jnp.stack([jnp.sum(group_entropy), jnp.sum(counts).astype(jnp.float32)])
    totals = butterfly(totals, "req", lambda a, b: a + b)
    mean_entropy = (totals[0] / totals[1]).reshape(1)
    own = lambda a: lax.dynamic_slice_in_dim(a, position * LIVE, LIVE, 0)
    live = slot < live_count
    zero = jnp.zeros((LIVE,), jnp.float32)
    place = lambda a: lax.dynamic_update_slice_in_dim(jnp.zeros((slots,), jnp.float32), a, start, 0)
    entropy = place(jnp.where(live, own(row_entropy), zero))
    logprob = place(jnp.where(live, own(row_logprob), zero))
    target_logit = place(jnp.where(live, own(picked), zero))
    return (logprob, entropy, target_logit, mean_entropy)


def solution(mesh):
    placed = (
        P(("req", "voc"), None),
        P(),
        P(None, "voc"),
        P(("req", "voc")),
        P(("req", "voc"), None),
    )
    return jax.shard_map(
        shards,
        mesh=mesh,
        in_specs=placed,
        out_specs=(P(("req", "voc")), P(("req", "voc")), P(("req", "voc")), P()),
        check_vma=False,
    )
```

time: 287 us -> 144 us (0.50)
  blocking collectives: 176 us -> 17.5 us
  starting transfers between devices: 0.04 us -> 13.7 us
  waiting for transfers between devices: 38.6 us -> 47.5 us
  matrix products: 32.9 us -> 24.7 us
  between operations: 16.7 us -> 21.3 us
    all_gather x5 -> x0, blocking collectives: 112 us -> none  [the longest x4 89.4 us: joined(): gathered = jax.tree.map(lambda a: lax.all_gather(a, axis), part)]
    psum x1 -> x0, blocking collectives: 64.7 us -> none  [shards(): lax.psum((jnp.sum(entropy), jnp.sum(live.astype(jnp.float32))), ('req', '...]
    unnamed x0 -> x1, blocking collectives: none -> 17.5 us
    ppermute x0 -> x7, starting transfers between devices: none -> 13.7 us  [butterfly(): other = lax.ppermute(value, axis, [(i, i ^ step) for i in range(size)])]
    ppermute x0 -> x7, waiting for transfers between devices: none -> 12.7 us  [butterfly(): other = lax.ppermute(value, axis, [(i, i ^ step) for i in range(size)])]
    dot_general x4 -> x3, matrix products: 32.9 us -> 24.7 us  [one_block(): logits = jnp.dot(rows_in, head, preferred_element_type=jnp.float32)]
    reduce_sum x6 -> x4, other arithmetic: 13.6 us -> 8.74 us  [the longest x3 7.98 us: one_block(): total = jnp.sum(expo, axis=-1)]
    all_gather x1, waiting for transfers between devices: 38.6 us -> 34.8 us  [shards(): gathered = lax.all_gather(normed, 'voc', axis=0, tiled=True)]
  transfers between devices with their start and end apart: 1 -> 8, of which waited for: 1 -> 8; matrix products, arithmetic and copies ran while one was open for 1% -> 3% of each run, Pallas kernels for 0% -> 0%
where the time goes in v1:
time: 144 us
  waiting for transfers between devices  47.5 us (33%)
  matrix products  24.7 us (17%)
  between operations  21.3 us (15%)
  blocking collectives  17.5 us (12%)
  other arithmetic  15 us (10%)
  starting transfers between devices  13.7 us (10%)
  local copies, waits for them, and re-layouts  4.31 us (3%)
    all_gather x1, waiting for transfers between devices, shards(): gathered = lax.all_gather(normed, 'voc', axis=0, tiled=True)  34.8 us
    dot_general x3, matrix products, one_block(): logits = jnp.dot(rows_in, head, preferred_element_type=jnp.float32)  24.7 us
    unnamed x1, blocking collectives  17.5 us
    ppermute x7, starting transfers between devices, butterfly(): other = lax.ppermute(value, axis, [(i, i ^ step) for i in range(size)])  13.7 us
    ppermute x7, waiting for transfers between devices, butterfly(): other = lax.ppermute(value, axis, [(i, i ^ step) for i in range(size)])  12.7 us
    reduce_sum x3, other arithmetic, one_block(): total = jnp.sum(expo, axis=-1)  7.98 us
  transfers between devices with their start and end apart: 8, of which 8 were waited for; matrix products, arithmetic and copies ran while one was open for 3% of the time, Pallas kernels for 0%

profile of v1, /device:TPU:0, one launch (start us, length us, event | category | flops | bytes accessed | tf_op | source)
XLA Modules:
  0.0 144.1 jit_solution(2353106291241718862)
XLA Ops:
  7.2 0.0 all-gather.3.cloned.1.call-start
  7.2 1.3 fusion.28
  10.5 1.2 fusion.8
  11.7 1.8 %fusion.10 = bf16[96,1536]{1,0:T(8,128)(2,1)} fusion(f32[1536]{0:T(1024)} %param.8, f32[96]{0:T(128)S(1)} %add_rsqrt_fusion, bf16[128,1536]{1,0:T(8,128)(2,1)} %param.7, s32[]{:T(128)S(6)} %select_n.109), kind=kLoop, calls=%fused_computation.17 | loop fusion | flops 589824 | bytes 596356 | tf_op jit(solution)/shard_map/convert_element_type | solution.py:78
  13.5 0.0 all-gather.3.cloned.1.call-update
  13.5 0.7 dynamic_slice.26
  15.6 1.2 dynamic-slice.1
  17.5 0.1 pad_dynamic-update-slice_fusion
  17.6 17.5 %all-reduce.1 = s32[1664]{0:T(1024)S(1)} all-reduce(s32[1664]{0:T(1024)S(1)} %pad_dynamic-update-slice_fusion), channel_id=2, replica_groups=mesh['req'=8,'voc'=16] {'voc'}, use_global_device_ids=true, to_apply=%add.1 | all-reduce | flops 1664 | bytes 13312
  35.1 0.1 reshape.68
  35.2 0.1 sub.78
  35.3 34.8 %all-gather.3.cloned.1.call-done = bf16[1536,1536]{1,0:T(8,128)(2,1)} async-done(((bf16[96,1536]{1,0:T(8,128)(2,1)}), bf16[1536,1536]{1,0:T(8,128)(2,1)}) %all-gather.3.cloned.1.call-update) | async-done | bytes 4718608 | tf_op jit(solution)/shard_map/all_gather | solution.py:81
  70.0 32.9 %while.11 = (s32[]{:T(128)}, f32[3,4,512]{2,1,0:T(4,128)S(1)}, bf16[3,512,1536]{2,1,0:T(8,128)(2,1)}, bf16[1536,3072]{1,0:T(8,128)(2,1)}, s32[3,512]{1,0:T(4,128)S(1)}, /*index=5*/s32[]{:T(128)}) while((s32[]{:T(128)}, f32[3,4,512]{2,1,0:T(4,128)S(1)}, bf16[3,512,1536]{2,1,0:T(8,128)(2,1)}, bf16[1536,3072]{1,0:T(8,128)(2,1)}, ...), condition=%wide.region_6.7_spmd.clone, body=%wide.region_1.6_spmd.clone.sunk | while | flops 4844425216 | bytes 23625816 | solution.py:60
  70.0 8.2 %fusion.35 = (f32[512]{0:T(512)S(1)}, f32[512,3072]{1,0:T(8,128)S(1)}) fusion(bf16[1536,3072]{1,0:T(8,128)(2,1)} %get-tuple-element.161, bf16[3,512,1536]{2,1,0:T(8,128)(2,1)} %get-tuple-element.160, s32[]{:T(128)S(6)} %copy.14), kind=kOutput, calls=%fused_computation.101.clone.1 | convolution fusion | flops 4833410560 | bytes 17303556 | tf_op jit(solution)/shard_map/while/body/eval_jaxpr/dot_general | solution.py:52
  78.3 2.7 %fusion.36 = (f32[512]{0:T(512)S(1)}, f32[512]{0:T(512)S(1)}, f32[512]{0:T(512)S(1)}) fusion(f32[512,3072]{1,0:T(8,128)S(1)} %get-tuple-element.141, f32[512]{0:T(512)S(1)} %get-tuple-element.142, s32[512]{0:T(512)S(1)} %bitcast.48), kind=kLoop, calls=%fused_computation.5.clone.1 | loop fusion | flops 11008512 | bytes 6301696 | tf_op jit(solution)/shard_map/while/body/eval_jaxpr/reduce_sum | solution.py:55
  81.0 8.2 %fusion.35 = (f32[512]{0:T(512)S(1)}, f32[512,3072]{1,0:T(8,128)S(1)}) fusion(bf16[1536,3072]{1,0:T(8,128)(2,1)} %get-tuple-element.161, bf16[3,512,1536]{2,1,0:T(8,128)(2,1)} %get-tuple-element.160, s32[]{:T(128)S(6)} %copy.14), kind=kOutput, calls=%fused_computation.101.clone.1 | convolution fusion | flops 4833410560 | bytes 17303556 | tf_op jit(solution)/shard_map/while/body/eval_jaxpr/dot_general | solution.py:52
  89.3 2.7 %fusion.36 = (f32[512]{0:T(512)S(1)}, f32[512]{0:T(512)S(1)}, f32[512]{0:T(512)S(1)}) fusion(f32[512,3072]{1,0:T(8,128)S(1)} %get-tuple-element.141, f32[512]{0:T(512)S(1)} %get-tuple-element.142, s32[512]{0:T(512)S(1)} %bitcast.48), kind=kLoop, calls=%fused_computation.5.clone.1 | loop fusion | flops 11008512 | bytes 6301696 | tf_op jit(solution)/shard_map/while/body/eval_jaxpr/reduce_sum | solution.py:55
  92.0 8.2 %fusion.35 = (f32[512]{0:T(512)S(1)}, f32[512,3072]{1,0:T(8,128)S(1)}) fusion(bf16[1536,3072]{1,0:T(8,128)(2,1)} %get-tuple-element.161, bf16[3,512,1536]{2,1,0:T(8,128)(2,1)} %get-tuple-element.160, s32[]{:T(128)S(6)} %copy.14), kind=kOutput, calls=%fused_computation.101.clone.1 | convolution fusion | flops 4833410560 | bytes 17303556 | tf_op jit(solution)/shard_map/while/body/eval_jaxpr/dot_general | solution.py:52
  100.2 2.7 %fusion.36 = (f32[512]{0:T(512)S(1)}, f32[512]{0:T(512)S(1)}, f32[512]{0:T(512)S(1)}) fusion(f32[512,3072]{1,0:T(8,128)S(1)} %get-tuple-element.141, f32[512]{0:T(512)S(1)} %get-tuple-element.142, s32[512]{0:T(512)S(1)} %bitcast.48), kind=kLoop, calls=%fused_computation.5.clone.1 | loop fusion | flops 11008512 | bytes 6301696 | tf_op jit(solution)/shard_map/while/body/eval_jaxpr/reduce_sum | solution.py:55
  102.9 1.4 collective-permute-start
  104.3 2.5 %collective-permute-done = f32[4,1536]{1,0:T(4,128)S(1)} collective-permute-done((f32[4,1536]{1,0:T(4,128)S(1)}, f32[4,1536]{1,0:T(4,128)S(1)}, u32[]{:S(2)}, u32[]{:S(2)}) %collective-permute-start) | collective-permute-done | bytes 24608 | tf_op jit(solution)/shard_map/ppermute | solution.py:35
  107.0 3.0 %collective-permute-start.1 = (f32[4,1536]{1,0:T(4,128)S(1)}, f32[4,1536]{1,0:T(4,128)S(1)}, u32[]{:S(2)}, u32[]{:S(2)}) collective-permute-start(f32[4,1536]{1,0:T(4,128)S(1)} %pad_maximum_fusion), channel_id=1, source_target_pairs={{0,2},{1,3},{2,0},{3,1},{4,6},{5,7},{6,4},{7,5},{8,10},{9,11},{10,... | collective-permute-start | bytes 73736 | tf_op jit(solution)/shard_map/ppermute | solution.py:35
  109.9 2.4 %collective-permute-done.1 = f32[4,1536]{1,0:T(4,128)S(1)} collective-permute-done((f32[4,1536]{1,0:T(4,128)S(1)}, f32[4,1536]{1,0:T(4,128)S(1)}, u32[]{:S(2)}, u32[]{:S(2)}) %collective-permute-start.1) | collective-permute-done | bytes 24608 | tf_op jit(solution)/shard_map/ppermute | solution.py:35
  112.5 1.5 %collective-permute-start.2 = (f32[4,1536]{1,0:T(4,128)S(1)}, f32[4,1536]{1,0:T(4,128)S(1)}, u32[]{:S(2)}, u32[]{:S(2)}) collective-permute-start(f32[4,1536]{1,0:T(4,128)S(1)} %pad_maximum_fusion.1), channel_id=1, source_target_pairs={{0,4},{1,5},{2,6},{3,7},{4,0},{5,1},{6,2},{7,3},{8,12},{9,13},{10,... | collective-permute-start | bytes 73736 | tf_op jit(solution)/shard_map/ppermute | solution.py:35
  114.1 0.7 slice_reduce_fusion.1
  114.8 1.7 %collective-permute-done.2 = f32[4,1536]{1,0:T(4,128)S(1)} collective-permute-done((f32[4,1536]{1,0:T(4,128)S(1)}, f32[4,1536]{1,0:T(4,128)S(1)}, u32[]{:S(2)}, u32[]{:S(2)}) %collective-permute-start.2) | collective-permute-done | bytes 24608 | tf_op jit(solution)/shard_map/ppermute | solution.py:35
  116.6 3.2 %collective-permute-start.3 = (f32[4,1536]{1,0:T(4,128)S(1)}, f32[4,1536]{1,0:T(4,128)S(1)}, u32[]{:S(2)}, u32[]{:S(2)}) collective-permute-start(f32[4,1536]{1,0:T(4,128)S(1)} %pad_maximum_fusion.2), channel_id=1, source_target_pairs={{0,8},{1,9},{2,10},{3,11},{4,12},{5,13},{6,14},{7,15},{8,0},{9,1},... | collective-permute-start | bytes 73736 | tf_op jit(solution)/shard_map/ppermute | solution.py:35
  119.8 0.1 iota_compare_fusion.1
  119.9 0.1 lt.54
  120.7 1.3 collective-permute-done.3
  122.0 0.8 select_reduce_fusion.1
  122.8 0.7 pad_maximum_fusion.3
  123.5 0.0 collective-permute-start.4
  123.6 0.2 fusion.24
  123.7 0.0 copy-start.1
  123.8 0.2 fusion.23
  123.9 0.0 copy-start.2
  123.9 0.2 select_dynamic-update-slice_fusion
  124.1 0.0 copy-start
  124.1 0.6 collective-permute-done.4
  124.7 0.7 fusion.20
  125.4 1.5 %collective-permute-start.5 = (f32[2]{0:T(128)S(1)}, f32[2]{0:T(128)S(1)}, u32[]{:S(2)}, u32[]{:S(2)}) collective-permute-start(f32[2]{0:T(128)S(1)} %fusion.20), channel_id=1, source_target_pairs={{0,32},{16,48},{32,0},{48,16},{64,96},{80,112},{96,64},{112,80},{1... | collective-permute-start | bytes 32 | tf_op jit(solution)/shard_map/ppermute | solution.py:35
  126.9 2.1 %collective-permute-done.5 = f32[2]{0:T(128)S(1)} collective-permute-done((f32[2]{0:T(128)S(1)}, f32[2]{0:T(128)S(1)}, u32[]{:S(2)}, u32[]{:S(2)}) %collective-permute-start.5) | collective-permute-done | bytes 40 | tf_op jit(solution)/shard_map/ppermute | solution.py:35
  129.0 3.0 %collective-permute-start.6 = (f32[2]{0:T(128)S(1)}, f32[2]{0:T(128)S(1)}, u32[]{:S(2)}, u32[]{:S(2)}) collective-permute-start(f32[2]{0:T(128)S(1)} %fusion.19), channel_id=1, source_target_pairs={{0,64},{16,80},{32,96},{48,112},{64,0},{80,16},{96,32},{112,48},{1... | collective-permute-start | bytes 32 | tf_op jit(solution)/shard_map/ppermute | solution.py:35
  132.0 2.1 %collective-permute-done.6 = f32[2]{0:T(128)S(1)} collective-permute-done((f32[2]{0:T(128)S(1)}, f32[2]{0:T(128)S(1)}, u32[]{:S(2)}, u32[]{:S(2)}) %collective-permute-start.6) | collective-permute-done | bytes 40 | tf_op jit(solution)/shard_map/ppermute | solution.py:35
  134.1 0.6 fusion.27
  136.1 0.0 copy-done.1
  136.1 0.0 copy-done.2
  136.1 0.0 copy-done
  (29 shorter events, 0.6 us)
Async XLA Ops:
  7.2 62.9 %all-gather.3.cloned.1.call-start = ((), (), s32[]{:S(2)}) async-start(), calls=%async_computation | async-start | bytes 5013504 | tf_op jit(solution)/shard_map/all_gather | solution.py:81
  102.9 3.9 %collective-permute-start = (f32[4,1536]{1,0:T(4,128)S(1)}, f32[4,1536]{1,0:T(4,128)S(1)}, u32[]{:S(2)}, u32[]{:S(2)}) collective-permute-start(f32[4,1536]{1,0:T(4,128)S(1)} %bitcast.49), channel_id=1, source_target_pairs={{0,1},{1,0},{2,3},{3,2},{4,5},{5,4},{6,7},{7,6},{8,9},{9,8},{10,11... | collective-permute-start | bytes 73736 | tf_op jit(solution)/shard_map/ppermute | solution.py:35
  107.0 5.4 %collective-permute-start.1 = (f32[4,1536]{1,0:T(4,128)S(1)}, f32[4,1536]{1,0:T(4,128)S(1)}, u32[]{:S(2)}, u32[]{:S(2)}) collective-permute-start(f32[4,1536]{1,0:T(4,128)S(1)} %pad_maximum_fusion), channel_id=1, source_target_pairs={{0,2},{1,3},{2,0},{3,1},{4,6},{5,7},{6,4},{7,5},{8,10},{9,11},{10,... | collective-permute-start | bytes 73736 | tf_op jit(solution)/shard_map/ppermute | solution.py:35
  112.5 3.9 %collective-permute-start.2 = (f32[4,1536]{1,0:T(4,128)S(1)}, f32[4,1536]{1,0:T(4,128)S(1)}, u32[]{:S(2)}, u32[]{:S(2)}) collective-permute-start(f32[4,1536]{1,0:T(4,128)S(1)} %pad_maximum_fusion.1), channel_id=1, source_target_pairs={{0,4},{1,5},{2,6},{3,7},{4,0},{5,1},{6,2},{7,3},{8,12},{9,13},{10,... | collective-permute-start | bytes 73736 | tf_op jit(solution)/shard_map/ppermute | solution.py:35
  116.6 5.4 %collective-permute-start.3 = (f32[4,1536]{1,0:T(4,128)S(1)}, f32[4,1536]{1,0:T(4,128)S(1)}, u32[]{:S(2)}, u32[]{:S(2)}) collective-permute-start(f32[4,1536]{1,0:T(4,128)S(1)} %pad_maximum_fusion.2), channel_id=1, source_target_pairs={{0,8},{1,9},{2,10},{3,11},{4,12},{5,13},{6,14},{7,15},{8,0},{9,1},... | collective-permute-start | bytes 73736 | tf_op jit(solution)/shard_map/ppermute | solution.py:35
  123.5 1.2 collective-permute-start.4
  123.7 12.3 %copy-start.1 = (f32[128]{0:T(128)}, f32[128]{0:T(128)S(1)}, u32[]{:S(2)}) copy-start(f32[128]{0:T(128)S(1)} %fusion.24) | copy-start | bytes 1540
  123.9 12.1 %copy-start.2 = (f32[128]{0:T(128)}, f32[128]{0:T(128)S(1)}, u32[]{:S(2)}) copy-start(f32[128]{0:T(128)S(1)} %fusion.23) | copy-start | bytes 1540
  124.1 12.0 %copy-start = (f32[128]{0:T(128)}, f32[128]{0:T(128)S(1)}, u32[]{:S(2)}) copy-start(f32[128]{0:T(128)S(1)} %select_dynamic-update-slice_fusion) | copy-start | bytes 1540
  125.4 3.6 %collective-permute-start.5 = (f32[2]{0:T(128)S(1)}, f32[2]{0:T(128)S(1)}, u32[]{:S(2)}, u32[]{:S(2)}) collective-permute-start(f32[2]{0:T(128)S(1)} %fusion.20), channel_id=1, source_target_pairs={{0,32},{16,48},{32,0},{48,16},{64,96},{80,112},{96,64},{112,80},{1... | collective-permute-start | bytes 32 | tf_op jit(solution)/shard_map/ppermute | solution.py:35
  129.0 5.1 %collective-permute-start.6 = (f32[2]{0:T(128)S(1)}, f32[2]{0:T(128)S(1)}, u32[]{:S(2)}, u32[]{:S(2)}) collective-permute-start(f32[2]{0:T(128)S(1)} %fusion.19), channel_id=1, source_target_pairs={{0,64},{16,80},{32,96},{48,112},{64,0},{80,16},{96,32},{112,48},{1... | collective-permute-start | bytes 32 | tf_op jit(solution)/shard_map/ppermute | solution.py:35
Sparse Core Ops, SparseCore 0:
  13.6 56.3 all-gather.2

commit v2 on v1

--- a/solution.py
+++ b/solution.py
@@ -4,6 +4,7 @@
 from jax.sharding import PartitionSpec as P
 
 LIVE = 96
+CHUNK = 32
 
 
 def pick_block(count):
@@ -39,6 +40,27 @@
         value = combine(first, second)
         step *= 2
     return value
+
+
+def members(value, axis, sub, stride):
+    size = lax.axis_size(axis)
+    digit = (lax.axis_index(axis) // stride) % sub
+    received = [value]
+    for shift in range(1, sub):
+        pairs = []
+        for i in range(size):
+            d = (i // stride) % sub
+            pairs.append((i, i + ((d + shift) % sub - d) * stride))
+        received.append(lax.ppermute(value, axis, pairs))
+    order = (digit - jnp.arange(sub, dtype=jnp.int32)) % sub
+    return jnp.take(jnp.stack(received), order, axis=0)
+
+
+def tree(items, combine):
+    items = list(items)
+    while len(items) > 1:
+        items = [combine(items[i], items[i + 1]) for i in range(0, len(items), 2)]
+    return items[0]
 
 
 def shard_stats(gathered, local_ids, head):
@@ -78,13 +100,21 @@
     normed = (values * lax.rsqrt(meansq + 1e-05) * norm_gain).astype(jnp.bfloat16)
     ids = lax.dynamic_slice_in_dim(targets, start, LIVE, 0)
     meta = jnp.concatenate([ids, jnp.full((8,), live_count, jnp.int32)])
-    gathered = lax.all_gather(normed, "voc", axis=0, tiled=True)
     gathered_meta = lax.all_gather(meta, "voc", axis=0)
-    gathered_ids = gathered_meta[:, :LIVE].reshape(groups * LIVE)
+    gathered_ids = gathered_meta[:, :LIVE]
     counts = gathered_meta[:, LIVE]
     local_ids = gathered_ids - position * shard_width
-    stats = shard_stats(gathered, local_ids, head)
-    merged = butterfly(stats, "voc", combine_stats)
+    parts = []
+    for first in range(0, LIVE, CHUNK):
+        gathered = lax.all_gather(normed[first:first + CHUNK], "voc", axis=0, tiled=True)
+        part = shard_stats(gathered, local_ids[:, first:first + CHUNK].reshape(-1), head)
+        parts.append(part.reshape(4, groups, CHUNK))
+    stats = jnp.stack(parts, axis=2).reshape(4, groups * LIVE)
+    inner = 4 if groups % 4 == 0 else 1
+    merged = stats
+    if inner > 1:
+        merged = tree(members(merged, "voc", inner, 1), combine_stats)
+    merged = tree(members(merged, "voc", groups // inner, inner), combine_stats)
     top, total, weighted, picked = merged[0], merged[1], merged[2], merged[3]
     lse = top + jnp.log(total)
     row_entropy = lse - weighted / total
@@ -93,7 +123,7 @@
     group_live = slot[None, :] < counts[:, None]
     group_entropy = jnp.where(group_live, row_entropy.reshape(groups, LIVE), 0.0)
     totals = jnp.stack([jnp.sum(group_entropy), jnp.sum(counts).astype(jnp.float32)])
-    totals = butterfly(totals, "req", lambda a, b: a + b)
+    totals = tree(members(totals, "req", lax.axis_size("req"), 1), lambda a, b: a + b)
     mean_entropy = (totals[0] / totals[1]).reshape(1)
     own = lambda a: lax.dynamic_slice_in_dim(a, position * LIVE, LIVE, 0)
     live = slot < live_count

time: 144 us -> 206 us (1.43)
  waiting for transfers between devices: 47.5 us -> 90.7 us
  other arithmetic: 15 us -> 20.6 us
  matrix products: 24.7 us -> 29.5 us
  local copies, waits for them, and re-layouts: 4.31 us -> 8.44 us
  starting transfers between devices: 13.7 us -> 17.7 us
    all_gather x1 -> x3, waiting for transfers between devices: 34.8 us -> 83 us  [shards(): lax.all_gather(normed[first:first + CHUNK], 'voc', axis=0, tiled=True)]
    ppermute x7 -> x13, waiting for transfers between devices: 12.7 us -> 6.3 us  [members(): received.append(lax.ppermute(value, axis, pairs))]
    reduce_sum x3, other arithmetic: 7.98 us -> 14 us  [one_block(): total = jnp.sum(expo, axis=-1)]
    dot_general x3, matrix products: 24.7 us -> 29.5 us  [one_block(): logits = jnp.dot(rows_in, head, preferred_element_type=jnp.float32)]
    ppermute x7 -> x13, starting transfers between devices: 13.7 us -> 17.6 us  [members(): received.append(lax.ppermute(value, axis, pairs))]
  transfers between devices with their start and end apart: 8 -> 16, of which waited for: 8 -> 10; matrix products, arithmetic and copies ran while one was open for 3% -> 17% of each run, Pallas kernels for 0% -> 0%
where the time goes in v2:
time: 206 us; the launch traced here: 205 us
  waiting for transfers between devices  90.7 us (44%)
  matrix products  29.5 us (14%)
  between operations  21.1 us (10%)
  other arithmetic  20.6 us (10%)
  starting transfers between devices  17.7 us (9%)
  blocking collectives  17.5 us (8%)
  local copies, waits for them, and re-layouts  8.44 us (4%)
    all_gather x3, waiting for transfers between devices, shards(): lax.all_gather(normed[first:first + CHUNK], 'voc', axis=0, tiled=True)  83 us
    dot_general x3, matrix products, one_block(): logits = jnp.dot(rows_in, head, preferred_element_type=jnp.float32)  29.5 us
    ppermute x13, starting transfers between devices, members(): received.append(lax.ppermute(value, axis, pairs))  17.6 us
    unnamed x1, blocking collectives  17.5 us
    reduce_sum x3, other arithmetic, one_block(): total = jnp.sum(expo, axis=-1)  14 us
    ppermute x13, waiting for transfers between devices, members(): received.append(lax.ppermute(value, axis, pairs))  6.3 us
  transfers between devices with their start and end apart: 16, of which 10 were waited for; matrix products, arithmetic and copies ran while one was open for 17% of the time, Pallas kernels for 0%

profile of v2, /device:TPU:0, one launch (start us, length us, event | category | flops | bytes accessed | tf_op | source)
XLA Modules:
  0.0 205.5 jit_solution(10489201134984408602)
XLA Ops:
  7.2 1.3 fusion.51
  10.5 1.2 fusion.3
  11.7 1.1 fusion.5
  12.8 0.7 fusion.48
  13.6 0.7 all-gather.7.cloned.1.call-update
  14.3 0.7 all-gather.9.cloned.1.call-update
  15.1 0.7 dynamic_slice.32
  17.1 1.2 dynamic-slice.4
  19.0 0.1 pad_dynamic-update-slice_fusion
  19.1 17.5 %all-reduce.1 = s32[1664]{0:T(1024)S(1)} all-reduce(s32[1664]{0:T(1024)S(1)} %pad_dynamic-update-slice_fusion), channel_id=2, replica_groups=mesh['req'=8,'voc'=16] {'voc'}, use_global_device_ids=true, to_apply=%add.1 | all-reduce | flops 1664 | bytes 13312
  36.7 0.7 slice_reduce_fusion.1
  37.9 22.1 %all-gather.5.cloned.1.call-done = bf16[512,1536]{1,0:T(8,128)(2,1)} async-done(((bf16[32,1536]{1,0:T(8,128)(2,1)}), bf16[512,1536]{1,0:T(8,128)(2,1)}) %all-gather.5.cloned.1.call-update) | async-done | bytes 1572880 | tf_op jit(solution)/shard_map/all_gather | solution.py:109
  60.0 9.8 %fusion.54 = (f32[512]{0:T(512)S(1)}, f32[512,3072]{1,0:T(8,128)}) fusion(bf16[512,1536]{1,0:T(8,128)(2,1)} %all-gather.5.cloned.1.call-done, bf16[1536,3072]{1,0:T(8,128)(2,1)} %param.9), kind=kOutput, calls=%fused_computation.162 | convolution fusion | flops 4833410560 | bytes 17303552 | tf_op jit(solution)/shard_map/while/body/eval_jaxpr/dot_general | solution.py:74
  69.9 0.1 stack.133
  69.9 4.7 %fusion.2 = (f32[512]{0:T(512)S(1)}, f32[512]{0:T(512)S(1)}, f32[512]{0:T(512)S(1)}) fusion(f32[512,3072]{1,0:T(8,128)} %get-tuple-element.117, f32[512]{0:T(512)S(1)} %get-tuple-element.116, s32[512]{0:T(512)S(1)} %eq.76), kind=kLoop, calls=%fused_computation.17 | loop fusion | flops 11008512 | bytes 6301696 | tf_op jit(solution)/shard_map/while/body/eval_jaxpr/reduce_sum | solution.py:77
  74.6 0.1 stack.134
  74.7 0.1 stack.135
  74.9 30.4 %all-gather.7.cloned.1.call-done = bf16[512,1536]{1,0:T(8,128)(2,1)} async-done(((bf16[32,1536]{1,0:T(8,128)(2,1)}), bf16[512,1536]{1,0:T(8,128)(2,1)}) %all-gather.7.cloned.1.call-update) | async-done | bytes 1572880 | tf_op jit(solution)/shard_map/all_gather | solution.py:109
  105.3 9.8 %fusion.53 = (f32[512]{0:T(512)S(1)}, f32[512,3072]{1,0:T(8,128)}) fusion(bf16[512,1536]{1,0:T(8,128)(2,1)} %all-gather.7.cloned.1.call-done, bf16[1536,3072]{1,0:T(8,128)(2,1)} %param.9), kind=kOutput, calls=%fused_computation.161 | convolution fusion | flops 4833410560 | bytes 17303552 | tf_op jit(solution)/shard_map/while/body/eval_jaxpr/dot_general | solution.py:74
  115.2 0.1 stack.138
  115.2 4.7 %fusion.1 = (f32[512]{0:T(512)S(1)}, f32[512]{0:T(512)S(1)}, f32[512]{0:T(512)S(1)}) fusion(f32[512,3072]{1,0:T(8,128)} %get-tuple-element.115, f32[512]{0:T(512)S(1)} %get-tuple-element.114, s32[512]{0:T(512)S(1)} %eq.80), kind=kLoop, calls=%fused_computation.12 | loop fusion | flops 11008512 | bytes 6301696 | tf_op jit(solution)/shard_map/while/body/eval_jaxpr/reduce_sum | solution.py:77
  119.9 0.1 stack.139
  120.0 0.1 stack.140
  120.1 0.1 stack.141
  120.2 30.4 %all-gather.9.cloned.1.call-done = bf16[512,1536]{1,0:T(8,128)(2,1)} async-done(((bf16[32,1536]{1,0:T(8,128)(2,1)}), bf16[512,1536]{1,0:T(8,128)(2,1)}) %all-gather.9.cloned.1.call-update) | async-done | bytes 1572880 | tf_op jit(solution)/shard_map/all_gather | solution.py:109
  150.6 9.8 %fusion.52 = (f32[512]{0:T(512)S(1)}, f32[512,3072]{1,0:T(8,128)}) fusion(bf16[512,1536]{1,0:T(8,128)(2,1)} %all-gather.9.cloned.1.call-done, bf16[1536,3072]{1,0:T(8,128)(2,1)} %param.9), kind=kOutput, calls=%fused_computation.160 | convolution fusion | flops 4833410560 | bytes 17303552 | tf_op jit(solution)/shard_map/while/body/eval_jaxpr/dot_general | solution.py:74
  160.4 0.1 stack.143
  160.5 4.6 %fusion = (f32[512]{0:T(512)S(1)}, f32[512]{0:T(512)S(1)}, f32[512]{0:T(512)S(1)}) fusion(f32[512,3072]{1,0:T(8,128)} %get-tuple-element.113, f32[512]{0:T(512)S(1)} %get-tuple-element.112, s32[512]{0:T(512)S(1)} %eq.84), kind=kLoop, calls=%fused_computation.7 | loop fusion | flops 11008512 | bytes 6301696 | tf_op jit(solution)/shard_map/while/body/eval_jaxpr/reduce_sum | solution.py:77
  165.2 0.1 stack.144
  165.4 0.1 maximum_maximum_fusion
  165.6 0.1 reshape.534
  165.7 1.2 collective-permute-start
  166.9 2.7 %collective-permute-start.1 = (f32[4,1536]{1,0:T(4,128)S(1)}, f32[4,1536]{1,0:T(4,128)S(1)}, u32[]{:S(2)}, u32[]{:S(2)}) collective-permute-start(f32[4,1536]{1,0:T(4,128)S(1)} %reshape.534), channel_id=1, source_target_pairs={{0,2},{1,3},{2,0},{3,1},{4,6},{5,7},{6,4},{7,5},{8,10},{9,11},{10,... | collective-permute-start | bytes 73736 | tf_op jit(solution)/shard_map/ppermute | solution.py:54
  169.6 0.8 collective-permute-start.2
  170.4 0.1 stack_reshape.3
  170.5 0.3 collective-permute-done
  170.8 1.5 collective-permute-done.1
  172.3 1.2 collective-permute-done.2
  173.5 0.6 gather_fusion.1
  174.1 0.1 broadcast_select_fusion.1
  174.4 0.3 collective-permute-start.3
  174.7 2.1 %collective-permute-start.4 = (f32[4,1536]{1,0:T(4,128)S(1)}, f32[4,1536]{1,0:T(4,128)S(1)}, u32[]{:S(2)}, u32[]{:S(2)}) collective-permute-start(f32[4,1536]{1,0:T(4,128)S(1)} %get-tuple-element.104), channel_id=1, source_target_pairs={{0,8},{1,9},{2,10},{3,11},{4,12},{5,13},{6,14},{7,15},{8,0},{9,1},... | collective-permute-start | bytes 73736 | tf_op jit(solution)/shard_map/ppermute | solution.py:54
  176.8 1.8 collective-permute-start.5
  178.6 0.1 lt.111
  179.3 0.2 collective-permute-done.3
  179.5 0.6 collective-permute-done.4
  180.1 0.6 collective-permute-done.5
  180.6 0.6 gather_fusion.2
  181.3 0.1 broadcast_select_fusion
  181.4 0.8 select_reduce_fusion.3
  182.2 0.7 pad_maximum_fusion.3
  182.9 1.5 collective-permute-start.7
  184.4 2.1 %collective-permute-start.8 = (f32[2]{0:T(128)S(1)}, f32[2]{0:T(128)S(1)}, u32[]{:S(2)}, u32[]{:S(2)}) collective-permute-start(f32[2]{0:T(128)S(1)} %pad_maximum_fusion.3), channel_id=1, source_target_pairs={{0,48},{16,64},{32,80},{48,96},{64,112},{80,0},{96,16},{112,32},{1... | collective-permute-start | bytes 32 | tf_op jit(solution)/shard_map/ppermute | solution.py:54
  186.5 2.0 collective-permute-start.9
  188.5 1.6 collective-permute-start.10
  190.1 0.7 fusion.61
  190.8 0.1 slice_reduce_fusion.4
  190.9 0.2 fusion.41
  191.2 0.2 fusion.40
  191.3 0.2 select_dynamic-update-slice_fusion
  191.5 1.5 collective-permute-start.11
  193.1 2.1 %collective-permute-done.11 = f32[2]{0:T(128)S(1)} collective-permute-done((f32[2]{0:T(128)S(1)}, f32[2]{0:T(128)S(1)}, u32[]{:S(2)}, u32[]{:S(2)}) %collective-permute-start.11) | collective-permute-done | bytes 40 | tf_op jit(solution)/shard_map/ppermute | solution.py:54
  195.2 0.6 gather_fusion
  195.8 0.6 fusion.50
  (52 shorter events, 1.4 us)
Async XLA Ops:
  7.2 52.9 %all-gather.5.cloned.1.call-start = ((), (), s32[]{:S(2)}) async-start(), calls=%async_computation | async-start | bytes 1671168 | tf_op jit(solution)/shard_map/all_gather | solution.py:109
  13.5 91.8 %all-gather.7.cloned.1.call-start = ((), (), s32[]{:S(2)}) async-start(), calls=%async_computation.1 | async-start | bytes 1671168 | tf_op jit(solution)/shard_map/all_gather | solution.py:109
  14.3 136.3 %all-gather.9.cloned.1.call-start = ((), (), s32[]{:S(2)}) async-start(), calls=%async_computation.2 | async-start | bytes 1671168 | tf_op jit(solution)/shard_map/all_gather | solution.py:109
  165.7 5.1 %collective-permute-start = (f32[4,1536]{1,0:T(4,128)S(1)}, f32[4,1536]{1,0:T(4,128)S(1)}, u32[]{:S(2)}, u32[]{:S(2)}) collective-permute-start(f32[4,1536]{1,0:T(4,128)S(1)} %reshape.534), channel_id=1, source_target_pairs={{0,1},{1,2},{2,3},{3,0},{4,5},{5,6},{6,7},{7,4},{8,9},{9,10},{10,1... | collective-permute-start | bytes 73736 | tf_op jit(solution)/shard_map/ppermute | solution.py:54
  166.9 5.3 %collective-permute-start.1 = (f32[4,1536]{1,0:T(4,128)S(1)}, f32[4,1536]{1,0:T(4,128)S(1)}, u32[]{:S(2)}, u32[]{:S(2)}) collective-permute-start(f32[4,1536]{1,0:T(4,128)S(1)} %reshape.534), channel_id=1, source_target_pairs={{0,2},{1,3},{2,0},{3,1},{4,6},{5,7},{6,4},{7,5},{8,10},{9,11},{10,... | collective-permute-start | bytes 73736 | tf_op jit(solution)/shard_map/ppermute | solution.py:54
  169.6 3.8 %collective-permute-start.2 = (f32[4,1536]{1,0:T(4,128)S(1)}, f32[4,1536]{1,0:T(4,128)S(1)}, u32[]{:S(2)}, u32[]{:S(2)}) collective-permute-start(f32[4,1536]{1,0:T(4,128)S(1)} %reshape.534), channel_id=1, source_target_pairs={{0,3},{1,0},{2,1},{3,2},{4,7},{5,4},{6,5},{7,6},{8,11},{9,8},{10,9... | collective-permute-start | bytes 73736 | tf_op jit(solution)/shard_map/ppermute | solution.py:54
  174.4 5.1 %collective-permute-start.3 = (f32[4,1536]{1,0:T(4,128)S(1)}, f32[4,1536]{1,0:T(4,128)S(1)}, u32[]{:S(2)}, u32[]{:S(2)}) collective-permute-start(f32[4,1536]{1,0:T(4,128)S(1)} %get-tuple-element.104), channel_id=1, source_target_pairs={{0,4},{1,5},{2,6},{3,7},{4,8},{5,9},{6,10},{7,11},{8,12},{9,13},{1... | collective-permute-start | bytes 73736 | tf_op jit(solution)/shard_map/ppermute | solution.py:54
  174.7 5.3 %collective-permute-start.4 = (f32[4,1536]{1,0:T(4,128)S(1)}, f32[4,1536]{1,0:T(4,128)S(1)}, u32[]{:S(2)}, u32[]{:S(2)}) collective-permute-start(f32[4,1536]{1,0:T(4,128)S(1)} %get-tuple-element.104), channel_id=1, source_target_pairs={{0,8},{1,9},{2,10},{3,11},{4,12},{5,13},{6,14},{7,15},{8,0},{9,1},... | collective-permute-start | bytes 73736 | tf_op jit(solution)/shard_map/ppermute | solution.py:54
  176.8 3.8 %collective-permute-start.5 = (f32[4,1536]{1,0:T(4,128)S(1)}, f32[4,1536]{1,0:T(4,128)S(1)}, u32[]{:S(2)}, u32[]{:S(2)}) collective-permute-start(f32[4,1536]{1,0:T(4,128)S(1)} %get-tuple-element.104), channel_id=1, source_target_pairs={{0,12},{1,13},{2,14},{3,15},{4,0},{5,1},{6,2},{7,3},{8,4},{9,5},{1... | collective-permute-start | bytes 73736 | tf_op jit(solution)/shard_map/ppermute | solution.py:54
  182.9 8.6 %collective-permute-start.6 = (f32[2]{0:T(128)S(1)}, f32[2]{0:T(128)S(1)}, u32[]{:S(2)}, u32[]{:S(2)}) collective-permute-start(f32[2]{0:T(128)S(1)} %pad_maximum_fusion.3), channel_id=1, source_target_pairs={{0,16},{16,32},{32,48},{48,64},{64,80},{80,96},{96,112},{112,0},{1... | collective-permute-start | bytes 32 | tf_op jit(solution)/shard_map/ppermute | solution.py:54
  182.9 10.1 %collective-permute-start.7 = (f32[2]{0:T(128)S(1)}, f32[2]{0:T(128)S(1)}, u32[]{:S(2)}, u32[]{:S(2)}) collective-permute-start(f32[2]{0:T(128)S(1)} %pad_maximum_fusion.3), channel_id=1, source_target_pairs={{0,32},{16,48},{32,64},{48,80},{64,96},{80,112},{96,0},{112,16},{1... | collective-permute-start | bytes 32 | tf_op jit(solution)/shard_map/ppermute | solution.py:54
  184.4 8.6 %collective-permute-start.8 = (f32[2]{0:T(128)S(1)}, f32[2]{0:T(128)S(1)}, u32[]{:S(2)}, u32[]{:S(2)}) collective-permute-start(f32[2]{0:T(128)S(1)} %pad_maximum_fusion.3), channel_id=1, source_target_pairs={{0,48},{16,64},{32,80},{48,96},{64,112},{80,0},{96,16},{112,32},{1... | collective-permute-start | bytes 32 | tf_op jit(solution)/shard_map/ppermute | solution.py:54
  186.5 6.5 %collective-permute-start.9 = (f32[2]{0:T(128)S(1)}, f32[2]{0:T(128)S(1)}, u32[]{:S(2)}, u32[]{:S(2)}) collective-permute-start(f32[2]{0:T(128)S(1)} %pad_maximum_fusion.3), channel_id=1, source_target_pairs={{0,64},{16,80},{32,96},{48,112},{64,0},{80,16},{96,32},{112,48},{1... | collective-permute-start | bytes 32 | tf_op jit(solution)/shard_map/ppermute | solution.py:54
  188.5 4.5 %collective-permute-start.10 = (f32[2]{0:T(128)S(1)}, f32[2]{0:T(128)S(1)}, u32[]{:S(2)}, u32[]{:S(2)}) collective-permute-start(f32[2]{0:T(128)S(1)} %pad_maximum_fusion.3), channel_id=1, source_target_pairs={{0,80},{16,96},{32,112},{48,0},{64,16},{80,32},{96,48},{112,64},{1... | collective-permute-start | bytes 32 | tf_op jit(solution)/shard_map/ppermute | solution.py:54
  191.1 6.7 %copy-start.1 = (f32[128]{0:T(128)}, f32[128]{0:T(128)S(1)}, u32[]{:S(2)}) copy-start(f32[128]{0:T(128)S(1)} %fusion.41) | copy-start | bytes 1540
  191.3 6.5 %copy-start.2 = (f32[128]{0:T(128)}, f32[128]{0:T(128)S(1)}, u32[]{:S(2)}) copy-start(f32[128]{0:T(128)S(1)} %fusion.40) | copy-start | bytes 1540
  191.5 6.3 %copy-start = (f32[128]{0:T(128)}, f32[128]{0:T(128)S(1)}, u32[]{:S(2)}) copy-start(f32[128]{0:T(128)S(1)} %select_dynamic-update-slice_fusion) | copy-start | bytes 1540
  191.5 3.6 %collective-permute-start.11 = (f32[2]{0:T(128)S(1)}, f32[2]{0:T(128)S(1)}, u32[]{:S(2)}, u32[]{:S(2)}) collective-permute-start(f32[2]{0:T(128)S(1)} %pad_maximum_fusion.3), channel_id=1, source_target_pairs={{0,96},{16,112},{32,0},{48,16},{64,32},{80,48},{96,64},{112,80},{1... | collective-permute-start | bytes 32 | tf_op jit(solution)/shard_map/ppermute | solution.py:54
  193.0 2.1 %collective-permute-start.12 = (f32[2]{0:T(128)S(1)}, f32[2]{0:T(128)S(1)}, u32[]{:S(2)}, u32[]{:S(2)}) collective-permute-start(f32[2]{0:T(128)S(1)} %pad_maximum_fusion.3), channel_id=1, source_target_pairs={{0,112},{16,0},{32,16},{48,32},{64,48},{80,64},{96,80},{112,96},{1... | collective-permute-start | bytes 32 | tf_op jit(solution)/shard_map/ppermute | solution.py:54
Sparse Core Ops, SparseCore 0:
  13.7 46.3 all-gather.4
  62.2 43.0 all-gather.6
  107.5 43.0 all-gather.8

commit v3 on v2

v3 whole, which is shorter than its diff:
```python
import jax
import jax.numpy as jnp
from jax import lax
from jax.sharding import PartitionSpec as P

LIVE = 96
HALF = LIVE // 2
EXTRA = 128
SIDE = 4
AXES = ("req", "voc")


def combine_stats(first, second):
    top = jnp.maximum(first[0], second[0])
    weight_a = jnp.exp(first[0] - top)
    weight_b = jnp.exp(second[0] - top)
    return jnp.stack(
        [
            top,
            first[1] * weight_a + second[1] * weight_b,
            first[2] * weight_a + second[2] * weight_b,
            first[3] + second[3],
        ]
    )


def butterfly(value, axis, combine):
    size = lax.axis_size(axis)
    index = lax.axis_index(axis)
    step = 1
    while step < size:
        other = lax.ppermute(value, axis, [(i, i ^ step) for i in range(size)])
        upper = (index & step) != 0
        first = jnp.where(upper, other, value)
        second = jnp.where(upper, value, other)
        value = combine(first, second)
        step *= 2
    return value


def members(value, axis, sub, stride):
    size = lax.axis_size(axis)
    digit = (lax.axis_index(axis) // stride) % sub
    received = [value]
    for shift in range(1, sub):
        pairs = []
        for i in range(size):
            d = (i // stride) % sub
            pairs.append((i, i + ((d + shift) % sub - d) * stride))
        received.append(lax.ppermute(value, axis, pairs))
    order = (digit - jnp.arange(sub, dtype=jnp.int32)) % sub
    return jnp.take(jnp.stack(received), order, axis=0)


def tree(items, combine):
    items = list(items)
    while len(items) > 1:
        items = [combine(items[i], items[i + 1]) for i in range(0, len(items), 2)]
    return items[0]


def digits(voc, core):
    z, x = voc % SIDE, voc // SIDE
    return (z, x) if core == 0 else (x, z)


def compose(first, second, core):
    return first * SIDE + second if core else second * SIDE + first


def shift(value, phase, step, reqs, vocs):
    pairs = []
    for req in range(reqs):
        core = req % 2
        for voc in range(vocs):
            ring = list(digits(voc, core))
            ring[phase] = (ring[phase] + step) % SIDE
            pairs.append((req * vocs + voc, req * vocs + compose(ring[0], ring[1], core)))
    return lax.ppermute(value, AXES, pairs)


def block_stats(block, head, position):
    width = head.shape[0]
    shard_width = head.shape[1]
    rows_in = block[:, :width]
    meta = block[:, width:width + 2].astype(jnp.int32)
    ids = meta[:, 0] * 256 + meta[:, 1] - position * shard_width
    columns = jnp.arange(shard_width, dtype=jnp.int32)
    logits = jnp.dot(rows_in, head, preferred_element_type=jnp.float32)
    top = jnp.max(logits, axis=-1)
    expo = jnp.exp(logits - top[:, None])
    total = jnp.sum(expo, axis=-1)
    weighted = jnp.sum(expo * logits, axis=-1)
    picked = jnp.sum(jnp.where(columns[None, :] == ids[:, None], logits, 0.0), axis=-1)
    return jnp.stack([top, total, weighted, picked])


def shards(hidden, norm_gain, head, targets, bounds):
    slots = hidden.shape[0]
    width = hidden.shape[1]
    reqs = lax.axis_size("req")
    vocs = lax.axis_size("voc")
    position = lax.axis_index("voc")
    core = lax.axis_index("req") % 2
    start = bounds[0, 0]
    finish = bounds[0, 1]
    live_count = finish - start
    rows = lax.dynamic_slice_in_dim(hidden, start, LIVE, 0)
    values = rows.astype(jnp.float32)
    meansq = jnp.mean(values * values, axis=-1, keepdims=True)
    normed = (values * lax.rsqrt(meansq + 1e-05) * norm_gain).astype(jnp.bfloat16)
    ids = lax.dynamic_slice_in_dim(targets, start, LIVE, 0)
    meta = jnp.zeros((LIVE, EXTRA), jnp.int32)
    meta = meta.at[:, 0].set(ids // 256).at[:, 1].set(ids % 256).at[:, 2].set(live_count)
    own = jnp.concatenate([normed, meta.astype(jnp.bfloat16)], axis=1)

    stats = lambda block: block_stats(block, head, position)
    left = shift(own, 0, 1, reqs, vocs)
    right = shift(own, 0, -1, reqs, vocs)
    part_own = stats(own)
    far_a = shift(left[:HALF], 0, 1, reqs, vocs)
    far_b = shift(right[HALF:], 0, -1, reqs, vocs)
    part_near = stats(jnp.concatenate([left, right]))
    far = jnp.concatenate([far_a, far_b])
    line = jnp.stack([own, left, right, far])
    line_left = shift(line, 1, 1, reqs, vocs)
    line_right = shift(line, 1, -1, reqs, vocs)
    part_far = stats(far)
    line_far_a = shift(line_left[:, :HALF], 1, 1, reqs, vocs)
    line_far_b = shift(line_right[:, HALF:], 1, -1, reqs, vocs)
    part_lines = stats(jnp.concatenate([line_left, line_right]).reshape(-1, own.shape[1]))
    line_far = jnp.concatenate([line_far_a, line_far_b], axis=1)
    part_line_far = stats(line_far.reshape(-1, own.shape[1]))
    processed = jnp.concatenate([part_own, part_near, part_far, part_lines, part_line_far], axis=1)
    processed = processed.reshape(4, vocs, LIVE)
    blocks = jnp.concatenate(
        [own[None], left[None], right[None], far[None], line_left, line_right, line_far]
    )
    processed_counts = blocks[:, 0, width + 2].astype(jnp.int32)

    source = jnp.arange(vocs, dtype=jnp.int32)
    slot_of = jnp.array([0, 2, 3, 1], jnp.int32)
    my_a = jnp.where(core == 0, position % SIDE, position // SIDE)
    my_b = jnp.where(core == 0, position // SIDE, position % SIDE)
    src_a = jnp.where(core == 0, source % SIDE, source // SIDE)
    src_b = jnp.where(core == 0, source // SIDE, source % SIDE)
    where_is = slot_of[(src_b - my_b) % SIDE] * SIDE + slot_of[(src_a - my_a) % SIDE]
    canonical = jnp.take(processed, where_is, axis=1).reshape(4, vocs * LIVE)
    counts = jnp.take(processed_counts, where_is, axis=0)

    merged = tree(members(canonical, "voc", SIDE, 1), combine_stats)
    merged = tree(members(merged, "voc", vocs // SIDE, SIDE), combine_stats)
    top, total, weighted, picked = merged[0], merged[1], merged[2], merged[3]
    lse = top + jnp.log(total)
    row_entropy = lse - weighted / total
    row_logprob = picked - lse
    slot = jnp.arange(LIVE, dtype=jnp.int32)
    group_live = slot[None, :] < counts[:, None]
    group_entropy = jnp.where(group_live, row_entropy.reshape(vocs, LIVE), 0.0)
    totals = jnp.stack([jnp.sum(group_entropy), jnp.sum(counts).astype(jnp.float32)])
    totals = butterfly(totals, "req", lambda a, b: a + b)
    mean_entropy = (totals[0] / totals[1]).reshape(1)
    mine = lambda a: lax.dynamic_slice_in_dim(a, position * LIVE, LIVE, 0)
    live = slot < live_count
    zero = jnp.zeros((LIVE,), jnp.float32)
    place = lambda a: lax.dynamic_update_slice_in_dim(jnp.zeros((slots,), jnp.float32), a, start, 0)
    entropy = place(jnp.where(live, mine(row_entropy), zero))
    logprob = place(jnp.where(live, mine(row_logprob), zero))
    target_logit = place(jnp.where(live, mine(picked), zero))
    return (logprob, entropy, target_logit, mean_entropy)


def solution(mesh):
    placed = (
        P(AXES, None),
        P(),
        P(None, "voc"),
        P(AXES),
        P(AXES, None),
    )
    return jax.shard_map(
        shards,
        mesh=mesh,
        in_specs=placed,
        out_specs=(P(AXES), P(AXES), P(AXES), P()),
        check_vma=False,
    )
```

time: 206 us -> 132 us (0.64)
  waiting for transfers between devices: 90.7 us -> 25 us
  blocking collectives: 17.5 us -> 0 us
  between operations: 21.1 us -> 7.69 us
  starting transfers between devices: 17.7 us -> 26.5 us
  local copies, waits for them, and re-layouts: 8.44 us -> 17.1 us
  other arithmetic: 20.6 us -> 24.6 us
    all_gather x3 -> x0, waiting for transfers between devices: 83 us -> none  [shards(): lax.all_gather(normed[first:first + CHUNK], 'voc', axis=0, tiled=True)]
    ppermute x0 -> x11, starting transfers between devices: none -> 17.9 us  [the longest x8 13.1 us: shift(): return lax.ppermute(value, AXES, pairs)]
    unnamed x1 -> x0, blocking collectives: 17.5 us -> none
    ppermute x0 -> x11, waiting for transfers between devices: none -> 17.3 us  [the longest x8 12.9 us: shift(): return lax.ppermute(value, AXES, pairs)]
    ppermute x13 -> x6, starting transfers between devices: 17.6 us -> 8.65 us  [members(): received.append(lax.ppermute(value, axis, pairs))]
    another operation x1 -> x12, other arithmetic: 0.11 us -> 7.36 us  [shards(): stats = jnp.stack(parts, axis=2).reshape(4, groups * LIVE)]
    unnamed x9 -> x40, local copies, waits for them, and re-layouts: 1.38 us -> 6.2 us
    reduce_sum x3 -> x6, other arithmetic: 14 us -> 11 us  [the longest x5 10.4 us: block_stats(): total = jnp.sum(expo, axis=-1)]
  transfers between devices with their start and end apart: 16 -> 17, of which waited for: 10 -> 12; matrix products, arithmetic and copies ran while one was open for 17% -> 24% of each run, Pallas kernels for 0% -> 0%
where the time goes in v3:
time: 132 us; the launch traced here: 131 us
  matrix products  30.3 us (23%)
  starting transfers between devices  26.5 us (20%)
  waiting for transfers between devices  25 us (19%)
  other arithmetic  24.6 us (19%)
  local copies, waits for them, and re-layouts  17.1 us (13%)
  between operations  7.69 us (6%)
    dot_general x5, matrix products, block_stats(): logits = jnp.dot(rows_in, head, preferred_element_type=jnp.float32)  30.3 us
    ppermute x8, starting transfers between devices, shift(): return lax.ppermute(value, AXES, pairs)  13.1 us
    ppermute x8, waiting for transfers between devices, shift(): return lax.ppermute(value, AXES, pairs)  12.9 us
    reduce_sum x5, other arithmetic, block_stats(): total = jnp.sum(expo, axis=-1)  10.4 us
    ppermute x6, starting transfers between devices, members(): received.append(lax.ppermute(value, axis, pairs))  8.65 us
    ppermute x6, waiting for transfers between devices, members(): received.append(lax.ppermute(value, axis, pairs))  7.64 us
    unnamed x40, local copies, waits for them, and re-layouts  6.2 us
    ppermute x3, starting transfers between devices, butterfly(): other = lax.ppermute(value, axis, [(i, i ^ step) for i in range(size)])  4.81 us
  transfers between devices with their start and end apart: 17, of which 12 were waited for; matrix products, arithmetic and copies ran while one was open for 24% of the time, Pallas kernels for 0%

profile of v3, /device:TPU:0, one launch (start us, length us, event | category | flops | bytes accessed | tf_op | source)
XLA Modules:
  0.0 131.3 jit_solution(4055197069986259369)
XLA Ops:
  0.7 0.6 compare_reduce_fusion.1
  1.3 0.6 compare_reduce_fusion.2
  1.9 0.7 compare_reduce_fusion
  2.7 1.3 %fusion.86 = (s32[1,1]{1,0:T(1,128)}, s32[1,1]{1,0:T(1,128)}) fusion(s32[1,2]{1,0:T(1,128)} %param.18), kind=kLoop, calls=%fused_computation.266 | loop fusion | bytes 16 | tf_op jit(solution)/shard_map/slice | solution.py:106
  5.9 2.0 %fusion.74 = (s32[96,1]{0,1:T(1,128)S(1)}, s32[96,1]{0,1:T(1,128)S(1)}) fusion(pred[]{:T(512)} %compare_reduce_fusion.1, s32[128]{0:T(128)} %param.17, s32[]{:T(128)S(6)} %select_n.303, pred[]{:T(512)} %compare_reduce_fusion.2), kind=kLoop, calls=%fused_computation.255 | loop fusion | flops 2016 | bytes 1158 | tf_op jit(solution)/shard_map/reshape.432
  9.3 0.7 broadcast_select_fusion.10
  10.6 1.0 fusion.14
  11.6 0.9 fusion.79
  12.5 2.0 %collective-permute-start = (bf16[96,1664]{0,1:T(8,128)(2,1)}, bf16[96,1664]{0,1:T(8,128)(2,1)S(1)}, u32[]{:S(2)}, u32[]{:S(2)}) collective-permute-start(bf16[96,1664]{0,1:T(8,128)(2,1)} %get-tuple-element.88), channel_id=1, source_target_pairs={{0,1},{1,2},{2,3},{3,0},{4,5},{5,6},{6,7},{7,4},{8,9},{9,10},{10,1... | collective-permute-start | bytes 958472 | tf_op jit(solution)/shard_map/ppermute | solution.py:79
  14.5 2.1 %collective-permute-start.1 = (bf16[96,1664]{0,1:T(8,128)(2,1)}, bf16[96,1664]{0,1:T(8,128)(2,1)S(1)}, u32[]{:S(2)}, u32[]{:S(2)}) collective-permute-start(bf16[96,1664]{0,1:T(8,128)(2,1)} %get-tuple-element.88), channel_id=1, source_target_pairs={{0,3},{1,0},{2,1},{3,2},{4,7},{5,4},{6,5},{7,6},{8,11},{9,8},{10,9... | collective-permute-start | bytes 958472 | tf_op jit(solution)/shard_map/ppermute | solution.py:79
  16.6 0.9 copy.26
  17.7 0.7 gather_fusion.1
  18.3 0.7 gather_fusion
  19.0 5.5 %fusion.87 = (f32[96]{0:T(128)S(1)}, f32[96,3072]{1,0:T(8,128)S(1)}) fusion(bf16[96,1536]{0,1:T(8,128)(2,1)S(1)} %fusion.14, bf16[1536,3072]{1,0:T(8,128)(2,1)} %param.16), kind=kOutput, calls=%fused_computation.267 | convolution fusion | flops 906264448 | bytes 10912128 | tf_op jit(solution)/shard_map/dot_general | solution.py:89
  24.6 0.5 fusion.8
  25.1 1.7 %constant_dynamic-update-slice_fusion.7 = bf16[16,96,1664]{2,1,0:T(8,128)(2,1)} fusion(bf16[1,96,1664]{2,1,0:T(8,128)(2,1)} %copy.26), kind=kLoop, calls=%fused_computation.79 | loop fusion | bytes 638976
  27.5 2.1 %collective-permute-start.3 = (bf16[48,1664]{0,1:T(8,128)(2,1)S(1)}, bf16[48,1664]{0,1:T(8,128)(2,1)S(1)}, u32[]{:S(2)}, u32[]{:S(2)}) collective-permute-start(bf16[48,1664]{0,1:T(8,128)(2,1)S(1)} %slice.378), channel_id=1, source_target_pairs={{0,3},{1,0},{2,1},{3,2},{4,7},{5,4},{6,5},{7,6},{8,11},{9,8},{10,9... | collective-permute-start | bytes 479240 | tf_op jit(solution)/shard_map/ppermute | solution.py:79
  29.6 0.7 constant_dynamic-update-slice_fusion.6
  30.4 5.9 %fusion.88 = (f32[192]{0:T(256)S(1)}, f32[192,3072]{1,0:T(8,128)S(1)}) fusion(bf16[1536,3072]{1,0:T(8,128)(2,1)} %param.16, bf16[96,1664]{0,1:T(8,128)(2,1)S(1)} %collective-permute-done, bf16[96,1664]{0,1:T(8,128)(2,1)S(1)} %collective-permute-done.1), kind=kOutput, calls=%fused_computation.268 | convolution fusion | flops 1813708544 | bytes 12436224 | tf_op jit(solution)/shard_map/dot_general | solution.py:89
  36.3 1.0 fusion.4
  37.3 0.8 constant_dynamic-update-slice_fusion.5
  38.1 0.8 collective-permute-done.2
  38.9 0.8 copy-done.5
  39.9 0.8 copy-done.2
  40.7 0.9 copy.29
  41.6 1.5 %pad_maximum_fusion.1 = bf16[4,96,1664]{1,2,0:T(8,128)(2,1)S(1)} fusion(bf16[1,96,1664]{1,2,0:T(8,128)(2,1)} %copy-done.2, bf16[1,96,1664]{1,2,0:T(8,128)(2,1)S(1)} %bitcast.206, bf16[1,96,1664]{1,2,0:T(8,128)(2,1)S(1)} %bitcast.209, bf16[1,96,1664]{1,2,0:T(8,128)(2,1)S(1)} %get-tuple-element.87), kind=kLoop, calls=%fused_computation.24 | loop fusion | flops 1916928 | bytes 2555904 | tf_op jit(solution)/shard_map/stack | solution.py:125
  43.1 1.6 %copy.21 = bf16[4,96,1664]{2,1,0:T(8,128)(2,1)} copy(bf16[4,96,1664]{1,2,0:T(8,128)(2,1)S(1)} %pad_maximum_fusion.1) | data formatting | bytes 2555904 | tf_op jit(solution)/shard_map/stack | solution.py:125
  44.7 1.5 %collective-permute-start.4 = (bf16[4,96,1664]{2,1,0:T(8,128)(2,1)}, bf16[4,96,1664]{2,1,0:T(8,128)(2,1)S(1)}, u32[]{:S(2)}, u32[]{:S(2)}) collective-permute-start(bf16[4,96,1664]{2,1,0:T(8,128)(2,1)} %copy.21), channel_id=1, source_target_pairs={{0,4},{1,5},{2,6},{3,7},{4,8},{5,9},{6,10},{7,11},{8,12},{9,13},{1... | collective-permute-start | bytes 3833864 | tf_op jit(solution)/shard_map/ppermute | solution.py:79
  46.2 1.7 %collective-permute-start.5 = (bf16[4,96,1664]{2,1,0:T(8,128)(2,1)}, bf16[4,96,1664]{2,1,0:T(8,128)(2,1)S(1)}, u32[]{:S(2)}, u32[]{:S(2)}) collective-permute-start(bf16[4,96,1664]{2,1,0:T(8,128)(2,1)} %copy.21), channel_id=1, source_target_pairs={{0,12},{1,13},{2,14},{3,15},{4,0},{5,1},{6,2},{7,3},{8,4},{9,5},{1... | collective-permute-start | bytes 3833864 | tf_op jit(solution)/shard_map/ppermute | solution.py:79
  48.0 5.7 %fusion.89 = (f32[96]{0:T(128)S(1)}, f32[96,3072]{1,0:T(8,128)S(1)}) fusion(bf16[1536,3072]{1,0:T(8,128)(2,1)} %param.16, bf16[48,1664]{0,1:T(8,128)(2,1)S(1)} %copy-done.4, bf16[48,1664]{0,1:T(8,128)(2,1)S(1)} %copy-done.6), kind=kOutput, calls=%fused_computation.269 | convolution fusion | flops 906854272 | bytes 10936704 | tf_op jit(solution)/shard_map/dot_general | solution.py:89
  53.7 0.5 fusion.7
  54.3 0.8 constant_dynamic-update-slice_fusion.4
  55.0 8.3 %collective-permute-done.4 = bf16[4,96,1664]{2,1,0:T(8,128)(2,1)S(1)} collective-permute-done((bf16[4,96,1664]{2,1,0:T(8,128)(2,1)}, bf16[4,96,1664]{2,1,0:T(8,128)(2,1)S(1)}, u32[]{:S(2)}, u32[]{:S(2)}) %collective-permute-start.4) | collective-permute-done | bytes 1277984 | tf_op jit(solution)/shard_map/ppermute | solution.py:79
  63.9 7.6 %fusion.90 = (f32[768]{0:T(1024)S(1)}, f32[768,3072]{1,0:T(8,128)S(1)}) fusion(bf16[1536,3072]{1,0:T(8,128)(2,1)S(1)} %bitcast.204, bf16[768,1664]{1,0:T(8,128)(2,1)S(1)} %bitcast.210), kind=kOutput, calls=%fused_computation.270 | convolution fusion | flops 7250115584 | bytes 21236736 | tf_op jit(solution)/shard_map/dot_general | solution.py:89
  71.6 1.6 %collective-permute-start.6 = (bf16[4,48,1664]{2,1,0:T(8,128)(2,1)S(1)}, bf16[4,48,1664]{2,1,0:T(8,128)(2,1)S(1)}, u32[]{:S(2)}, u32[]{:S(2)}) collective-permute-start(bf16[4,48,1664]{2,1,0:T(8,128)(2,1)S(1)} %slice.387), channel_id=1, source_target_pairs={{0,4},{1,5},{2,6},{3,7},{4,8},{5,9},{6,10},{7,11},{8,12},{9,13},{1... | collective-permute-start | bytes 1916936 | tf_op jit(solution)/shard_map/ppermute | solution.py:79
  73.2 2.0 %collective-permute-start.7 = (bf16[4,48,1664]{2,1,0:T(8,128)(2,1)S(1)}, bf16[4,48,1664]{2,1,0:T(8,128)(2,1)S(1)}, u32[]{:S(2)}, u32[]{:S(2)}) collective-permute-start(bf16[4,48,1664]{2,1,0:T(8,128)(2,1)S(1)} %slice.388), channel_id=1, source_target_pairs={{0,12},{1,13},{2,14},{3,15},{4,0},{5,1},{6,2},{7,3},{8,4},{9,5},{1... | collective-permute-start | bytes 1916936 | tf_op jit(solution)/shard_map/ppermute | solution.py:79
  75.6 4.4 %fusion = (f32[768]{0:T(1024)S(1)}, f32[768]{0:T(1024)S(1)}, f32[768]{0:T(1024)S(1)}) fusion(f32[768,3072]{1,0:T(8,128)S(1)} %get-tuple-element.106, f32[768]{0:T(1024)S(1)} %get-tuple-element.105, s32[768]{0:T(1024)S(1)} %fusion.16), kind=kLoop, calls=%fused_computation.10 | loop fusion | flops 16512768 | bytes 9452544 | tf_op jit(solution)/shard_map/reduce_sum | solution.py:92
  80.4 2.9 %collective-permute-done.6 = bf16[4,48,1664]{2,1,0:T(8,128)(2,1)S(1)} collective-permute-done((bf16[4,48,1664]{2,1,0:T(8,128)(2,1)S(1)}, bf16[4,48,1664]{2,1,0:T(8,128)(2,1)S(1)}, u32[]{:S(2)}, u32[]{:S(2)}) %collective-permute-start.6) | collective-permute-done | bytes 639008 | tf_op jit(solution)/shard_map/ppermute | solution.py:79
  83.3 0.6 collective-permute-done.7
  84.0 5.7 %fusion.91 = (f32[384]{0:T(512)S(1)}, f32[384,3072]{1,0:T(8,128)}) fusion(bf16[1536,3072]{1,0:T(8,128)(2,1)S(1)} %bitcast.204, bf16[384,1664]{1,0:T(8,128)(2,1)S(1)} %bitcast.212), kind=kOutput, calls=%fused_computation.271 | convolution fusion | flops 3625057792 | bytes 15336960 | tf_op jit(solution)/shard_map/dot_general | solution.py:89
  89.9 0.4 fusion.25
  90.3 0.7 gather_fusion.3
  91.0 0.6 fusion.80
  91.9 4.0 %fusion.1 = (f32[384]{0:T(512)S(1)}, f32[384]{0:T(512)S(1)}, f32[384]{0:T(512)S(1)}) fusion(f32[384,3072]{1,0:T(8,128)} %get-tuple-element.108, f32[384]{0:T(512)S(1)} %get-tuple-element.107, s32[384]{0:T(512)S(1)} %fusion.24), kind=kLoop, calls=%fused_computation.15 | loop fusion | flops 8256384 | bytes 4726272 | tf_op jit(solution)/shard_map/reduce_sum | solution.py:92
  96.1 0.6 gather_fusion.2
  97.0 3.3 %collective-permute-start.10 = (f32[4,1536]{1,0:T(4,128)S(1)}, f32[4,1536]{1,0:T(4,128)S(1)}, u32[]{:S(2)}, u32[]{:S(2)}) collective-permute-start(f32[4,1536]{1,0:T(4,128)S(1)} %broadcast_select_fusion.2), channel_id=1, source_target_pairs={{0,3},{1,0},{2,1},{3,2},{4,7},{5,4},{6,5},{7,6},{8,11},{9,8},{10,9... | collective-permute-start | bytes 73736 | tf_op jit(solution)/shard_map/ppermute | solution.py:50
  100.3 0.9 collective-permute-start.8
  101.3 0.5 collective-permute-done.10
  101.8 3.8 %collective-permute-done.9 = f32[4,1536]{1,0:T(4,128)S(1)} collective-permute-done((f32[4,1536]{1,0:T(4,128)S(1)}, f32[4,1536]{1,0:T(4,128)S(1)}, u32[]{:S(2)}, u32[]{:S(2)}) %collective-permute-start.9) | collective-permute-done | bytes 24608 | tf_op jit(solution)/shard_map/ppermute | solution.py:50
  105.6 0.6 gather_fusion.4
  106.5 3.0 %collective-permute-start.13 = (f32[4,1536]{1,0:T(4,128)S(1)}, f32[4,1536]{1,0:T(4,128)S(1)}, u32[]{:S(2)}, u32[]{:S(2)}) collective-permute-start(f32[4,1536]{1,0:T(4,128)S(1)} %get-tuple-element.92), channel_id=1, source_target_pairs={{0,12},{1,13},{2,14},{3,15},{4,0},{5,1},{6,2},{7,3},{8,4},{9,5},{1... | collective-permute-start | bytes 73736 | tf_op jit(solution)/shard_map/ppermute | solution.py:50
  109.6 0.3 collective-permute-start.12
  109.9 1.1 collective-permute-start.11
  111.8 3.1 %collective-permute-done.12 = f32[4,1536]{1,0:T(4,128)S(1)} collective-permute-done((f32[4,1536]{1,0:T(4,128)S(1)}, f32[4,1536]{1,0:T(4,128)S(1)}, u32[]{:S(2)}, u32[]{:S(2)}) %collective-permute-start.12) | collective-permute-done | bytes 24608 | tf_op jit(solution)/shard_map/ppermute | solution.py:50
  115.2 0.6 gather_fusion.5
  116.0 0.8 select_reduce_fusion.5
  116.8 0.7 pad_maximum_fusion.13
  118.2 0.6 collective-permute-done.14
  118.7 0.7 fusion.60
  119.4 1.6 %collective-permute-start.15 = (f32[2]{0:T(128)S(1)}, f32[2]{0:T(128)S(1)}, u32[]{:S(2)}, u32[]{:S(2)}) collective-permute-start(f32[2]{0:T(128)S(1)} %fusion.60), channel_id=1, source_target_pairs={{0,32},{16,48},{32,0},{48,16},{64,96},{80,112},{96,64},{112,80},{1... | collective-permute-start | bytes 32 | tf_op jit(solution)/shard_map/ppermute | solution.py:32
  121.0 2.0 %collective-permute-done.15 = f32[2]{0:T(128)S(1)} collective-permute-done((f32[2]{0:T(128)S(1)}, f32[2]{0:T(128)S(1)}, u32[]{:S(2)}, u32[]{:S(2)}) %collective-permute-start.15) | collective-permute-done | bytes 40 | tf_op jit(solution)/shard_map/ppermute | solution.py:32
  123.0 3.2 %collective-permute-start.16 = (f32[2]{0:T(128)S(1)}, f32[2]{0:T(128)S(1)}, u32[]{:S(2)}, u32[]{:S(2)}) collective-permute-start(f32[2]{0:T(128)S(1)} %fusion.59), channel_id=1, source_target_pairs={{0,64},{16,80},{32,96},{48,112},{64,0},{80,16},{96,32},{112,48},{1... | collective-permute-start | bytes 32 | tf_op jit(solution)/shard_map/ppermute | solution.py:32
  126.2 1.9 %collective-permute-done.16 = f32[2]{0:T(128)S(1)} collective-permute-done((f32[2]{0:T(128)S(1)}, f32[2]{0:T(128)S(1)}, u32[]{:S(2)}, u32[]{:S(2)}) %collective-permute-start.16) | collective-permute-done | bytes 40 | tf_op jit(solution)/shard_map/ppermute | solution.py:32
  128.1 0.6 fusion.85
  (125 shorter events, 5.9 us)
Async XLA Ops:
  0.6 9.4 %copy-start = (bf16[128,1536]{1,0:T(8,128)(2,1)S(1)}, bf16[128,1536]{1,0:T(8,128)(2,1)}, u32[]{:S(2)}) copy-start(bf16[128,1536]{1,0:T(8,128)(2,1)} %param.14) | copy-start | bytes 1179652
  0.6 17.0 %copy-start.1 = (s32[4]{0:T(128)S(1)}, s32[4]{0:T(128)}, u32[]{:S(2)}) copy-start(s32[4]{0:T(128)} %constant.286.clone) | copy-start | bytes 52
  12.5 14.3 %collective-permute-start = (bf16[96,1664]{0,1:T(8,128)(2,1)}, bf16[96,1664]{0,1:T(8,128)(2,1)S(1)}, u32[]{:S(2)}, u32[]{:S(2)}) collective-permute-start(bf16[96,1664]{0,1:T(8,128)(2,1)} %get-tuple-element.88), channel_id=1, source_target_pairs={{0,1},{1,2},{2,3},{3,0},{4,5},{5,6},{6,7},{7,4},{8,9},{9,10},{10,1... | collective-permute-start | bytes 958472 | tf_op jit(solution)/shard_map/ppermute | solution.py:79
  14.5 12.5 %collective-permute-start.1 = (bf16[96,1664]{0,1:T(8,128)(2,1)}, bf16[96,1664]{0,1:T(8,128)(2,1)S(1)}, u32[]{:S(2)}, u32[]{:S(2)}) collective-permute-start(bf16[96,1664]{0,1:T(8,128)(2,1)} %get-tuple-element.88), channel_id=1, source_target_pairs={{0,3},{1,0},{2,1},{3,2},{4,7},{5,4},{6,5},{7,6},{8,11},{9,8},{10,9... | collective-permute-start | bytes 958472 | tf_op jit(solution)/shard_map/ppermute | solution.py:79
  27.5 10.6 %collective-permute-start.3 = (bf16[48,1664]{0,1:T(8,128)(2,1)S(1)}, bf16[48,1664]{0,1:T(8,128)(2,1)S(1)}, u32[]{:S(2)}, u32[]{:S(2)}) collective-permute-start(bf16[48,1664]{0,1:T(8,128)(2,1)S(1)} %slice.378), channel_id=1, source_target_pairs={{0,3},{1,0},{2,1},{3,2},{4,7},{5,4},{6,5},{7,6},{8,11},{9,8},{10,9... | collective-permute-start | bytes 479240 | tf_op jit(solution)/shard_map/ppermute | solution.py:79
  29.6 9.3 %collective-permute-start.2 = (bf16[48,1664]{0,1:T(8,128)(2,1)S(1)}, bf16[48,1664]{0,1:T(8,128)(2,1)S(1)}, u32[]{:S(2)}, u32[]{:S(2)}) collective-permute-start(bf16[48,1664]{0,1:T(8,128)(2,1)S(1)} %bitcast.208), channel_id=1, source_target_pairs={{0,1},{1,2},{2,3},{3,0},{4,5},{5,6},{6,7},{7,4},{8,9},{9,10},{10,1... | collective-permute-start | bytes 479240 | tf_op jit(solution)/shard_map/ppermute | solution.py:79
  38.1 0.8 copy-start.3
  38.9 0.8 copy-start.5
  39.9 0.8 copy-start.2
  43.1 4.8 %copy-start.4 = (bf16[48,1664]{0,1:T(8,128)(2,1)S(1)}, bf16[48,1664]{0,1:T(8,128)(2,1)}, u32[]{:S(2)}) copy-start(bf16[48,1664]{0,1:T(8,128)(2,1)} %copy-done.3) | copy-start | bytes 479236
  43.1 4.8 %copy-start.6 = (bf16[48,1664]{0,1:T(8,128)(2,1)S(1)}, bf16[48,1664]{0,1:T(8,128)(2,1)}, u32[]{:S(2)}) copy-start(bf16[48,1664]{0,1:T(8,128)(2,1)} %copy-done.5) | copy-start | bytes 479236
  44.7 18.7 %collective-permute-start.4 = (bf16[4,96,1664]{2,1,0:T(8,128)(2,1)}, bf16[4,96,1664]{2,1,0:T(8,128)(2,1)S(1)}, u32[]{:S(2)}, u32[]{:S(2)}) collective-permute-start(bf16[4,96,1664]{2,1,0:T(8,128)(2,1)} %copy.21), channel_id=1, source_target_pairs={{0,4},{1,5},{2,6},{3,7},{4,8},{5,9},{6,10},{7,11},{8,12},{9,13},{1... | collective-permute-start | bytes 3833864 | tf_op jit(solution)/shard_map/ppermute | solution.py:79
  46.2 17.5 %collective-permute-start.5 = (bf16[4,96,1664]{2,1,0:T(8,128)(2,1)}, bf16[4,96,1664]{2,1,0:T(8,128)(2,1)S(1)}, u32[]{:S(2)}, u32[]{:S(2)}) collective-permute-start(bf16[4,96,1664]{2,1,0:T(8,128)(2,1)} %copy.21), channel_id=1, source_target_pairs={{0,12},{1,13},{2,14},{3,15},{4,0},{5,1},{6,2},{7,3},{8,4},{9,5},{1... | collective-permute-start | bytes 3833864 | tf_op jit(solution)/shard_map/ppermute | solution.py:79
  47.9 16.0 %slice-start = ((s8[9437184]{0:T(1024)(128)(4,1)}), s8[4194304]{0:T(1024)(128)(4,1)S(1)}, s32[]{:S(2)}) async-start(s8[9437184]{0:T(1024)(128)(4,1)} %bitcast.203), calls=%async_computation | async-start | bytes 8388608
  48.0 6.3 %copy-start.7 = (bf16[1,96,1664]{2,1,0:T(8,128)(2,1)S(1)}, bf16[1,96,1664]{2,1,0:T(8,128)(2,1)}, u32[]{:S(2)}) copy-start(bf16[1,96,1664]{2,1,0:T(8,128)(2,1)} %copy.29) | copy-start | bytes 958468
  48.0 15.9 %slice-start.1 = ((s8[9437184]{0:T(1024)(128)(4,1)}), s8[4194304]{0:T(1024)(128)(4,1)S(1)}, s32[]{:S(2)}) async-start(s8[9437184]{0:T(1024)(128)(4,1)} %bitcast.203), calls=%async_computation.1 | async-start | bytes 8388608
  48.0 15.9 %slice-start.2 = ((s8[9437184]{0:T(1024)(128)(4,1)}), s8[1048576]{0:T(1024)(128)(4,1)S(1)}, s32[]{:S(2)}) async-start(s8[9437184]{0:T(1024)(128)(4,1)} %bitcast.203), calls=%async_computation.2 | async-start | bytes 2097152
  71.6 11.7 %collective-permute-start.6 = (bf16[4,48,1664]{2,1,0:T(8,128)(2,1)S(1)}, bf16[4,48,1664]{2,1,0:T(8,128)(2,1)S(1)}, u32[]{:S(2)}, u32[]{:S(2)}) collective-permute-start(bf16[4,48,1664]{2,1,0:T(8,128)(2,1)S(1)} %slice.387), channel_id=1, source_target_pairs={{0,4},{1,5},{2,6},{3,7},{4,8},{5,9},{6,10},{7,11},{8,12},{9,13},{1... | collective-permute-start | bytes 1916936 | tf_op jit(solution)/shard_map/ppermute | solution.py:79
  73.2 10.7 %collective-permute-start.7 = (bf16[4,48,1664]{2,1,0:T(8,128)(2,1)S(1)}, bf16[4,48,1664]{2,1,0:T(8,128)(2,1)S(1)}, u32[]{:S(2)}, u32[]{:S(2)}) collective-permute-start(bf16[4,48,1664]{2,1,0:T(8,128)(2,1)S(1)} %slice.388), channel_id=1, source_target_pairs={{0,12},{1,13},{2,14},{3,15},{4,0},{5,1},{6,2},{7,3},{8,4},{9,5},{1... | collective-permute-start | bytes 1916936 | tf_op jit(solution)/shard_map/ppermute | solution.py:79
  75.2 4.7 %slice-start.3 = ((s8[5111808]{0:T(1024)(128)(4,1)}), s8[4194304]{0:T(1024)(128)(4,1)S(1)}, s32[]{:S(2)}) async-start(s8[5111808]{0:T(1024)(128)(4,1)} %bitcast.221), calls=%async_computation.3 | async-start | bytes 8388608
  75.6 4.4 %slice-start.4 = ((s8[5111808]{0:T(1024)(128)(4,1)}), s8[917504]{0:T(1024)(128)(4,1)S(1)}, s32[]{:S(2)}) async-start(s8[5111808]{0:T(1024)(128)(4,1)} %bitcast.221), calls=%async_computation.4 | async-start | bytes 1835008
  97.0 4.8 %collective-permute-start.10 = (f32[4,1536]{1,0:T(4,128)S(1)}, f32[4,1536]{1,0:T(4,128)S(1)}, u32[]{:S(2)}, u32[]{:S(2)}) collective-permute-start(f32[4,1536]{1,0:T(4,128)S(1)} %broadcast_select_fusion.2), channel_id=1, source_target_pairs={{0,3},{1,0},{2,1},{3,2},{4,7},{5,4},{6,5},{7,6},{8,11},{9,8},{10,9... | collective-permute-start | bytes 73736 | tf_op jit(solution)/shard_map/ppermute | solution.py:50
  100.3 5.3 %collective-permute-start.9 = (f32[4,1536]{1,0:T(4,128)S(1)}, f32[4,1536]{1,0:T(4,128)S(1)}, u32[]{:S(2)}, u32[]{:S(2)}) collective-permute-start(f32[4,1536]{1,0:T(4,128)S(1)} %broadcast_select_fusion.2), channel_id=1, source_target_pairs={{0,2},{1,3},{2,0},{3,1},{4,6},{5,7},{6,4},{7,5},{8,10},{9,11},{10,... | collective-permute-start | bytes 73736 | tf_op jit(solution)/shard_map/ppermute | solution.py:50
  100.3 5.3 %collective-permute-start.8 = (f32[4,1536]{1,0:T(4,128)S(1)}, f32[4,1536]{1,0:T(4,128)S(1)}, u32[]{:S(2)}, u32[]{:S(2)}) collective-permute-start(f32[4,1536]{1,0:T(4,128)S(1)} %broadcast_select_fusion.2), channel_id=1, source_target_pairs={{0,1},{1,2},{2,3},{3,0},{4,5},{5,6},{6,7},{7,4},{8,9},{9,10},{10,1... | collective-permute-start | bytes 73736 | tf_op jit(solution)/shard_map/ppermute | solution.py:50
  106.5 5.3 %collective-permute-start.13 = (f32[4,1536]{1,0:T(4,128)S(1)}, f32[4,1536]{1,0:T(4,128)S(1)}, u32[]{:S(2)}, u32[]{:S(2)}) collective-permute-start(f32[4,1536]{1,0:T(4,128)S(1)} %get-tuple-element.92), channel_id=1, source_target_pairs={{0,12},{1,13},{2,14},{3,15},{4,0},{5,1},{6,2},{7,3},{8,4},{9,5},{1... | collective-permute-start | bytes 73736 | tf_op jit(solution)/shard_map/ppermute | solution.py:50
  109.6 5.4 %collective-permute-start.12 = (f32[4,1536]{1,0:T(4,128)S(1)}, f32[4,1536]{1,0:T(4,128)S(1)}, u32[]{:S(2)}, u32[]{:S(2)}) collective-permute-start(f32[4,1536]{1,0:T(4,128)S(1)} %get-tuple-element.92), channel_id=1, source_target_pairs={{0,8},{1,9},{2,10},{3,11},{4,12},{5,13},{6,14},{7,15},{8,0},{9,1},... | collective-permute-start | bytes 73736 | tf_op jit(solution)/shard_map/ppermute | solution.py:50
  109.9 5.3 %collective-permute-start.11 = (f32[4,1536]{1,0:T(4,128)S(1)}, f32[4,1536]{1,0:T(4,128)S(1)}, u32[]{:S(2)}, u32[]{:S(2)}) collective-permute-start(f32[4,1536]{1,0:T(4,128)S(1)} %get-tuple-element.92), channel_id=1, source_target_pairs={{0,4},{1,5},{2,6},{3,7},{4,8},{5,9},{6,10},{7,11},{8,12},{9,13},{1... | collective-permute-start | bytes 73736 | tf_op jit(solution)/shard_map/ppermute | solution.py:50
  117.5 1.2 collective-permute-start.14
  117.8 12.3 %copy-start.9 = (f32[128]{0:T(128)}, f32[128]{0:T(128)S(1)}, u32[]{:S(2)}) copy-start(f32[128]{0:T(128)S(1)} %fusion.73) | copy-start | bytes 1540
  118.0 12.1 %copy-start.10 = (f32[128]{0:T(128)}, f32[128]{0:T(128)S(1)}, u32[]{:S(2)}) copy-start(f32[128]{0:T(128)S(1)} %fusion.72) | copy-start | bytes 1540
  118.2 12.0 %copy-start.8 = (f32[128]{0:T(128)}, f32[128]{0:T(128)S(1)}, u32[]{:S(2)}) copy-start(f32[128]{0:T(128)S(1)} %select_dynamic-update-slice_fusion) | copy-start | bytes 1540
  119.4 3.6 %collective-permute-start.15 = (f32[2]{0:T(128)S(1)}, f32[2]{0:T(128)S(1)}, u32[]{:S(2)}, u32[]{:S(2)}) collective-permute-start(f32[2]{0:T(128)S(1)} %fusion.60), channel_id=1, source_target_pairs={{0,32},{16,48},{32,0},{48,16},{64,96},{80,112},{96,64},{112,80},{1... | collective-permute-start | bytes 32 | tf_op jit(solution)/shard_map/ppermute | solution.py:32
  123.0 5.1 %collective-permute-start.16 = (f32[2]{0:T(128)S(1)}, f32[2]{0:T(128)S(1)}, u32[]{:S(2)}, u32[]{:S(2)}) collective-permute-start(f32[2]{0:T(128)S(1)} %fusion.59), channel_id=1, source_target_pairs={{0,64},{16,80},{32,96},{48,112},{64,0},{80,16},{96,32},{112,48},{1... | collective-permute-start | bytes 32 | tf_op jit(solution)/shard_map/ppermute | solution.py:32

commit v4 on v3

--- a/solution.py
+++ b/solution.py
@@ -117,25 +117,21 @@
     stats = lambda block: block_stats(block, head, position)
     left = shift(own, 0, 1, reqs, vocs)
     right = shift(own, 0, -1, reqs, vocs)
-    part_own = stats(own)
     far_a = shift(left[:HALF], 0, 1, reqs, vocs)
     far_b = shift(right[HALF:], 0, -1, reqs, vocs)
-    part_near = stats(jnp.concatenate([left, right]))
     far = jnp.concatenate([far_a, far_b])
     line = jnp.stack([own, left, right, far])
     line_left = shift(line, 1, 1, reqs, vocs)
     line_right = shift(line, 1, -1, reqs, vocs)
-    part_far = stats(far)
+    part_line = stats(line.reshape(-1, own.shape[1]))
     line_far_a = shift(line_left[:, :HALF], 1, 1, reqs, vocs)
     line_far_b = shift(line_right[:, HALF:], 1, -1, reqs, vocs)
     part_lines = stats(jnp.concatenate([line_left, line_right]).reshape(-1, own.shape[1]))
     line_far = jnp.concatenate([line_far_a, line_far_b], axis=1)
     part_line_far = stats(line_far.reshape(-1, own.shape[1]))
-    processed = jnp.concatenate([part_own, part_near, part_far, part_lines, part_line_far], axis=1)
+    processed = jnp.concatenate([part_line, part_lines, part_line_far], axis=1)
     processed = processed.reshape(4, vocs, LIVE)
-    blocks = jnp.concatenate(
-        [own[None], left[None], right[None], far[None], line_left, line_right, line_far]
-    )
+    blocks = jnp.concatenate([line, line_left, line_right, line_far])
     processed_counts = blocks[:, 0, width + 2].astype(jnp.int32)
 
     source = jnp.arange(vocs, dtype=jnp.int32)
@@ -148,8 +144,7 @@
     canonical = jnp.take(processed, where_is, axis=1).reshape(4, vocs * LIVE)
     counts = jnp.take(processed_counts, where_is, axis=0)
 
-    merged = tree(members(canonical, "voc", SIDE, 1), combine_stats)
-    merged = tree(members(merged, "voc", vocs // SIDE, SIDE), combine_stats)
+    merged = butterfly(canonical, "voc", combine_stats)
     top, total, weighted, picked = merged[0], merged[1], merged[2], merged[3]
     lse = top + jnp.log(total)
     row_entropy = lse - weighted / total

time: 132 us -> 134 us (1.015)
  other arithmetic: 24.6 us -> 31.8 us
  waiting for transfers between devices: 25 us -> 29.8 us
  matrix products: 30.3 us -> 25.7 us
  starting transfers between devices: 26.5 us -> 22 us
    ppermute x3 -> x7, waiting for transfers between devices: 4.43 us -> 19.4 us  [butterfly(): other = lax.ppermute(value, axis, [(i, i ^ step) for i in range(size)])]
    ppermute x6 -> x0, starting transfers between devices: 8.65 us -> none  [members(): received.append(lax.ppermute(value, axis, pairs))]
    ppermute x6 -> x0, waiting for transfers between devices: 7.64 us -> none  [members(): received.append(lax.ppermute(value, axis, pairs))]
    reduce_sum x5 -> x3, other arithmetic: 10.4 us -> 15.2 us  [block_stats(): total = jnp.sum(expo, axis=-1)]
    dot_general x5 -> x3, matrix products: 30.3 us -> 25.7 us  [block_stats(): logits = jnp.dot(rows_in, head, preferred_element_type=jnp.float32)]
    another operation x8 -> x5, local copies, waits for them, and re-layouts: 3.92 us -> 0.22 us  [the longest x5 3.91 us: shards(): line = jnp.stack([own, left, right, far])]
    ppermute x3 -> x7, starting transfers between devices: 4.81 us -> 7.64 us  [butterfly(): other = lax.ppermute(value, axis, [(i, i ^ step) for i in range(size)])]
    ppermute x8, waiting for transfers between devices: 12.9 us -> 10.4 us  [shift(): return lax.ppermute(value, AXES, pairs)]
  transfers between devices with their start and end apart: 17 -> 15, of which waited for: 12 -> 12; matrix products, arithmetic and copies ran while one was open for 24% -> 21% of each run, Pallas kernels for 0% -> 0%
where the time goes in v4:
time: 134 us
  other arithmetic  31.8 us (24%)
  waiting for transfers between devices  29.8 us (22%)
  matrix products  25.7 us (19%)
  starting transfers between devices  22 us (16%)
  local copies, waits for them, and re-layouts  16.9 us (13%)
  between operations  7.56 us (6%)
    dot_general x3, matrix products, block_stats(): logits = jnp.dot(rows_in, head, preferred_element_type=jnp.float32)  25.7 us
    ppermute x7, waiting for transfers between devices, butterfly(): other = lax.ppermute(value, axis, [(i, i ^ step) for i in range(size)])  19.4 us
    reduce_sum x3, other arithmetic, block_stats(): total = jnp.sum(expo, axis=-1)  15.2 us
    ppermute x8, starting transfers between devices, shift(): return lax.ppermute(value, AXES, pairs)  14.3 us
    ppermute x8, waiting for transfers between devices, shift(): return lax.ppermute(value, AXES, pairs)  10.4 us
    ppermute x7, starting transfers between devices, butterfly(): other = lax.ppermute(value, axis, [(i, i ^ step) for i in range(size)])  7.64 us
    unnamed x26, local copies, waits for them, and re-layouts  5.06 us
    another operation x5, other arithmetic  4.79 us
  transfers between devices with their start and end apart: 15, of which 12 were waited for; matrix products, arithmetic and copies ran while one was open for 21% of the time, Pallas kernels for 0%

profile of v4, /device:TPU:0, one launch (start us, length us, event | category | flops | bytes accessed | tf_op | source)
XLA Modules:
  0.0 133.8 jit_solution(3895474760560162996)
XLA Ops:
  0.6 0.6 compare_reduce_fusion.1
  1.3 0.6 compare_reduce_fusion.2
  1.9 0.7 compare_reduce_fusion
  2.6 1.3 fusion.46
  5.9 2.0 %fusion.41 = (s32[96,1]{0,1:T(1,128)S(1)}, s32[96,1]{0,1:T(1,128)S(1)}) fusion(pred[]{:T(512)} %compare_reduce_fusion.1, s32[128]{0:T(128)} %param.15, s32[]{:T(128)S(6)} %select_n.307, pred[]{:T(512)} %compare_reduce_fusion.2), kind=kLoop, calls=%fused_computation.179 | loop fusion | flops 2016 | bytes 1158 | tf_op jit(solution)/shard_map/reshape.233
  9.4 0.3 scatter.11
  9.8 0.8 slice_select_fusion
  10.5 0.3 scatter.14
  10.9 1.2 fusion.9
  12.0 1.1 fusion.11
  13.2 2.1 %collective-permute-start = (bf16[96,1664]{1,0:T(8,128)(2,1)S(1)}, bf16[96,1664]{1,0:T(8,128)(2,1)S(1)}, u32[]{:S(2)}, u32[]{:S(2)}) collective-permute-start(bf16[96,1664]{1,0:T(8,128)(2,1)S(1)} %get-tuple-element.72), channel_id=1, source_target_pairs={{0,1},{1,2},{2,3},{3,0},{4,5},{5,6},{6,7},{7,4},{8,9},{9,10},{10,1... | collective-permute-start | bytes 958472 | tf_op jit(solution)/shard_map/ppermute | solution.py:79
  15.3 2.2 %collective-permute-start.1 = (bf16[96,1664]{1,0:T(8,128)(2,1)S(1)}, bf16[96,1664]{1,0:T(8,128)(2,1)S(1)}, u32[]{:S(2)}, u32[]{:S(2)}) collective-permute-start(bf16[96,1664]{1,0:T(8,128)(2,1)S(1)} %get-tuple-element.72), channel_id=1, source_target_pairs={{0,3},{1,0},{2,1},{3,2},{4,7},{5,4},{6,5},{7,6},{8,11},{9,8},{10,9... | collective-permute-start | bytes 958472 | tf_op jit(solution)/shard_map/ppermute | solution.py:79
  17.6 1.3 gather_fusion.1
  18.9 1.3 gather_fusion
  20.2 0.8 constant_dynamic-update-slice_fusion.7
  21.0 1.3 collective-permute-done.1
  22.3 3.5 %collective-permute-start.3 = (bf16[48,1664]{1,0:T(8,128)(2,1)S(1)}, bf16[48,1664]{1,0:T(8,128)(2,1)S(1)}, u32[]{:S(2)}, u32[]{:S(2)}) collective-permute-start(bf16[48,1664]{1,0:T(8,128)(2,1)S(1)} %slice.277), channel_id=1, source_target_pairs={{0,3},{1,0},{2,1},{3,2},{4,7},{5,4},{6,5},{7,6},{8,11},{9,8},{10,9... | collective-permute-start | bytes 479240 | tf_op jit(solution)/shard_map/ppermute | solution.py:79
  25.9 0.8 constant_dynamic-update-slice_fusion.6
  26.7 0.7 constant_dynamic-update-slice_fusion.5
  27.4 1.2 collective-permute-done.3
  28.6 3.8 %collective-permute-done.2 = bf16[48,1664]{1,0:T(8,128)(2,1)S(1)} collective-permute-done((bf16[48,1664]{1,0:T(8,128)(2,1)S(1)}, bf16[48,1664]{1,0:T(8,128)(2,1)S(1)}, u32[]{:S(2)}, u32[]{:S(2)}) %collective-permute-start.2) | collective-permute-done | bytes 159776 | tf_op jit(solution)/shard_map/ppermute | solution.py:79
  32.4 1.2 pad_maximum_fusion.1
  33.7 1.5 %collective-permute-start.4 = (bf16[4,96,1664]{2,1,0:T(8,128)(2,1)}, bf16[4,96,1664]{2,1,0:T(8,128)(2,1)S(1)}, u32[]{:S(2)}, u32[]{:S(2)}) collective-permute-start(bf16[4,96,1664]{2,1,0:T(8,128)(2,1)} %pad_maximum_fusion.1), channel_id=1, source_target_pairs={{0,4},{1,5},{2,6},{3,7},{4,8},{5,9},{6,10},{7,11},{8,12},{9,13},{1... | collective-permute-start | bytes 3833864 | tf_op jit(solution)/shard_map/ppermute | solution.py:79
  35.1 1.7 %collective-permute-start.5 = (bf16[4,96,1664]{2,1,0:T(8,128)(2,1)}, bf16[4,96,1664]{2,1,0:T(8,128)(2,1)S(1)}, u32[]{:S(2)}, u32[]{:S(2)}) collective-permute-start(bf16[4,96,1664]{2,1,0:T(8,128)(2,1)} %pad_maximum_fusion.1), channel_id=1, source_target_pairs={{0,12},{1,13},{2,14},{3,15},{4,0},{5,1},{6,2},{7,3},{8,4},{9,5},{1... | collective-permute-start | bytes 3833864 | tf_op jit(solution)/shard_map/ppermute | solution.py:79
  36.9 0.9 slice.279
  38.0 10.1 %fusion.49 = (f32[384]{0:T(512)S(1)}, f32[384,3072]{1,0:T(8,128)}) fusion(bf16[1536,3072]{1,0:T(8,128)(2,1)} %param.14, bf16[384,1664]{1,0:T(8,128)(2,1)} %bitcast.10), kind=kOutput, calls=%fused_computation.188 | convolution fusion | flops 3625057792 | bytes 15336960 | tf_op jit(solution)/shard_map/dot_general | solution.py:89
  48.1 0.8 constant_dynamic-update-slice_fusion.4
  48.9 3.5 %collective-permute-done.4 = bf16[4,96,1664]{2,1,0:T(8,128)(2,1)S(1)} collective-permute-done((bf16[4,96,1664]{2,1,0:T(8,128)(2,1)}, bf16[4,96,1664]{2,1,0:T(8,128)(2,1)S(1)}, u32[]{:S(2)}, u32[]{:S(2)}) %collective-permute-start.4) | collective-permute-done | bytes 1277984 | tf_op jit(solution)/shard_map/ppermute | solution.py:79
  52.3 0.7 collective-permute-done.5
  53.0 0.3 pad_maximum_fusion
  53.3 9.9 %fusion.48 = (f32[768]{0:T(1024)S(1)}, f32[768,3072]{1,0:T(8,128)}) fusion(bf16[1536,3072]{1,0:T(8,128)(2,1)S(1)} %bitcast.46, bf16[768,1664]{1,0:T(8,128)(2,1)S(1)} %bitcast.38), kind=kOutput, calls=%fused_computation.187 | convolution fusion | flops 7250115584 | bytes 21236736 | tf_op jit(solution)/shard_map/dot_general | solution.py:89
  63.2 0.9 slice.286
  64.1 2.0 %collective-permute-start.6 = (bf16[4,48,1664]{2,1,0:T(8,128)(2,1)}, bf16[4,48,1664]{2,1,0:T(8,128)(2,1)S(1)}, u32[]{:S(2)}, u32[]{:S(2)}) collective-permute-start(bf16[4,48,1664]{2,1,0:T(8,128)(2,1)} %slice.286), channel_id=1, source_target_pairs={{0,4},{1,5},{2,6},{3,7},{4,8},{5,9},{6,10},{7,11},{8,12},{9,13},{1... | collective-permute-start | bytes 1916936 | tf_op jit(solution)/shard_map/ppermute | solution.py:79
  66.1 0.9 slice.287
  67.0 1.2 collective-permute-start.7
  68.4 7.2 %fusion = (f32[768]{0:T(1024)S(1)}, f32[768]{0:T(1024)S(1)}, f32[768]{0:T(1024)S(1)}) fusion(f32[768,3072]{1,0:T(8,128)} %get-tuple-element.98, f32[768]{0:T(1024)S(1)} %get-tuple-element.97, s32[768]{0:T(1024)S(1)} %fusion.21), kind=kLoop, calls=%fused_computation.8 | loop fusion | flops 16512768 | bytes 9452544 | tf_op jit(solution)/shard_map/reduce_sum | solution.py:92
  75.7 1.2 constant_dynamic-update-slice_fusion.3
  76.9 1.2 constant_dynamic-update-slice_fusion.2
  78.1 1.2 pad_maximum_fusion.2
  79.3 5.7 %fusion.47 = (f32[384]{0:T(512)S(1)}, f32[384,3072]{1,0:T(8,128)}) fusion(bf16[1536,3072]{1,0:T(8,128)(2,1)S(1)} %bitcast.48, bf16[384,1664]{1,0:T(8,128)(2,1)S(1)} %bitcast.42), kind=kOutput, calls=%fused_computation.186 | convolution fusion | flops 3625057792 | bytes 15336960 | tf_op jit(solution)/shard_map/dot_general | solution.py:89
  84.9 0.9 constant_dynamic-update-slice_fusion.1
  85.8 2.0 %constant_dynamic-update-slice_fusion = bf16[16,96,1664]{2,1,0:T(8,128)(2,1)} fusion(bf16[16,96,1664]{2,1,0:T(8,128)(2,1)} %constant_dynamic-update-slice_fusion.1, bf16[4,48,1664]{2,1,0:T(8,128)(2,1)} %collective-permute-done.7), kind=kLoop, calls=%fused_computation.40 | loop fusion | bytes 1277952 | tf_op jit(solution)/shard_map/concatenate | solution.py:134
  87.8 1.2 fusion.12
  89.0 0.7 gather_fusion.3
  89.7 0.6 fusion.43
  90.5 4.0 %fusion.1 = (f32[384]{0:T(512)S(1)}, f32[384]{0:T(512)S(1)}, f32[384]{0:T(512)S(1)}) fusion(f32[384,3072]{1,0:T(8,128)} %get-tuple-element.96, f32[384]{0:T(512)S(1)} %get-tuple-element.95, s32[384]{0:T(512)S(1)} %get-tuple-element.104), kind=kLoop, calls=%fused_computation.13 | loop fusion | flops 8256384 | bytes 4726272 | tf_op jit(solution)/shard_map/reduce_sum | solution.py:92
  94.5 4.0 %fusion.2 = (f32[384]{0:T(512)S(1)}, f32[384]{0:T(512)S(1)}, f32[384]{0:T(512)S(1)}) fusion(f32[384,3072]{1,0:T(8,128)} %get-tuple-element.100, f32[384]{0:T(512)S(1)} %get-tuple-element.99, s32[384]{0:T(512)S(1)} %get-tuple-element.103), kind=kLoop, calls=%fused_computation.18 | loop fusion | flops 8256384 | bytes 4726272 | tf_op jit(solution)/shard_map/reduce_sum | solution.py:92
  98.7 0.6 gather_fusion.2
  99.6 3.8 %collective-permute-done.8 = f32[4,1536]{1,0:T(4,128)S(1)} collective-permute-done((f32[4,1536]{1,0:T(4,128)S(1)}, f32[4,1536]{1,0:T(4,128)S(1)}, u32[]{:S(2)}, u32[]{:S(2)}) %collective-permute-start.8) | collective-permute-done | bytes 24608 | tf_op jit(solution)/shard_map/ppermute | solution.py:32
  103.7 5.3 %collective-permute-done.9 = f32[4,1536]{1,0:T(4,128)S(1)} collective-permute-done((f32[4,1536]{1,0:T(4,128)S(1)}, f32[4,1536]{1,0:T(4,128)S(1)}, u32[]{:S(2)}, u32[]{:S(2)}) %collective-permute-start.9) | collective-permute-done | bytes 24608 | tf_op jit(solution)/shard_map/ppermute | solution.py:32
  109.2 0.9 collective-permute-start.10
  110.0 3.0 %collective-permute-done.10 = f32[4,1536]{1,0:T(4,128)S(1)} collective-permute-done((f32[4,1536]{1,0:T(4,128)S(1)}, f32[4,1536]{1,0:T(4,128)S(1)}, u32[]{:S(2)}, u32[]{:S(2)}) %collective-permute-start.10) | collective-permute-done | bytes 24608 | tf_op jit(solution)/shard_map/ppermute | solution.py:32
  113.2 1.8 %collective-permute-start.11 = (f32[4,1536]{1,0:T(4,128)S(1)}, f32[4,1536]{1,0:T(4,128)S(1)}, u32[]{:S(2)}, u32[]{:S(2)}) collective-permute-start(f32[4,1536]{1,0:T(4,128)S(1)} %pad_maximum_fusion.6), channel_id=1, source_target_pairs={{0,8},{1,9},{2,10},{3,11},{4,12},{5,13},{6,14},{7,15},{8,0},{9,1},... | collective-permute-start | bytes 73736 | tf_op jit(solution)/shard_map/ppermute | solution.py:32
  115.8 2.8 %collective-permute-done.11 = f32[4,1536]{1,0:T(4,128)S(1)} collective-permute-done((f32[4,1536]{1,0:T(4,128)S(1)}, f32[4,1536]{1,0:T(4,128)S(1)}, u32[]{:S(2)}, u32[]{:S(2)}) %collective-permute-start.11) | collective-permute-done | bytes 24608 | tf_op jit(solution)/shard_map/ppermute | solution.py:32
  118.7 0.8 select_reduce_fusion.3
  119.4 0.7 pad_maximum_fusion.7
  120.4 0.2 fusion.39
  120.7 0.6 collective-permute-done.12
  121.3 0.7 fusion.31
  122.0 1.6 %collective-permute-start.13 = (f32[2]{0:T(128)S(1)}, f32[2]{0:T(128)S(1)}, u32[]{:S(2)}, u32[]{:S(2)}) collective-permute-start(f32[2]{0:T(128)S(1)} %fusion.31), channel_id=1, source_target_pairs={{0,32},{16,48},{32,0},{48,16},{64,96},{80,112},{96,64},{112,80},{1... | collective-permute-start | bytes 32 | tf_op jit(solution)/shard_map/ppermute | solution.py:32
  123.6 2.0 %collective-permute-done.13 = f32[2]{0:T(128)S(1)} collective-permute-done((f32[2]{0:T(128)S(1)}, f32[2]{0:T(128)S(1)}, u32[]{:S(2)}, u32[]{:S(2)}) %collective-permute-start.13) | collective-permute-done | bytes 40 | tf_op jit(solution)/shard_map/ppermute | solution.py:32
  125.6 3.2 %collective-permute-start.14 = (f32[2]{0:T(128)S(1)}, f32[2]{0:T(128)S(1)}, u32[]{:S(2)}, u32[]{:S(2)}) collective-permute-start(f32[2]{0:T(128)S(1)} %fusion.30), channel_id=1, source_target_pairs={{0,64},{16,80},{32,96},{48,112},{64,0},{80,16},{96,32},{112,48},{1... | collective-permute-start | bytes 32 | tf_op jit(solution)/shard_map/ppermute | solution.py:32
  128.8 1.9 %collective-permute-done.14 = f32[2]{0:T(128)S(1)} collective-permute-done((f32[2]{0:T(128)S(1)}, f32[2]{0:T(128)S(1)}, u32[]{:S(2)}, u32[]{:S(2)}) %collective-permute-start.14) | collective-permute-done | bytes 40 | tf_op jit(solution)/shard_map/ppermute | solution.py:32
  130.7 0.6 fusion.45
  (94 shorter events, 2.5 us)
Async XLA Ops:
  13.2 12.6 %collective-permute-start = (bf16[96,1664]{1,0:T(8,128)(2,1)S(1)}, bf16[96,1664]{1,0:T(8,128)(2,1)S(1)}, u32[]{:S(2)}, u32[]{:S(2)}) collective-permute-start(bf16[96,1664]{1,0:T(8,128)(2,1)S(1)} %get-tuple-element.72), channel_id=1, source_target_pairs={{0,1},{1,2},{2,3},{3,0},{4,5},{5,6},{6,7},{7,4},{8,9},{9,10},{10,1... | collective-permute-start | bytes 958472 | tf_op jit(solution)/shard_map/ppermute | solution.py:79
  15.3 7.0 %collective-permute-start.1 = (bf16[96,1664]{1,0:T(8,128)(2,1)S(1)}, bf16[96,1664]{1,0:T(8,128)(2,1)S(1)}, u32[]{:S(2)}, u32[]{:S(2)}) collective-permute-start(bf16[96,1664]{1,0:T(8,128)(2,1)S(1)} %get-tuple-element.72), channel_id=1, source_target_pairs={{0,3},{1,0},{2,1},{3,2},{4,7},{5,4},{6,5},{7,6},{8,11},{9,8},{10,9... | collective-permute-start | bytes 958472 | tf_op jit(solution)/shard_map/ppermute | solution.py:79
  22.3 6.3 %collective-permute-start.3 = (bf16[48,1664]{1,0:T(8,128)(2,1)S(1)}, bf16[48,1664]{1,0:T(8,128)(2,1)S(1)}, u32[]{:S(2)}, u32[]{:S(2)}) collective-permute-start(bf16[48,1664]{1,0:T(8,128)(2,1)S(1)} %slice.277), channel_id=1, source_target_pairs={{0,3},{1,0},{2,1},{3,2},{4,7},{5,4},{6,5},{7,6},{8,11},{9,8},{10,9... | collective-permute-start | bytes 479240 | tf_op jit(solution)/shard_map/ppermute | solution.py:79
  25.8 6.6 %collective-permute-start.2 = (bf16[48,1664]{1,0:T(8,128)(2,1)S(1)}, bf16[48,1664]{1,0:T(8,128)(2,1)S(1)}, u32[]{:S(2)}, u32[]{:S(2)}) collective-permute-start(bf16[48,1664]{1,0:T(8,128)(2,1)S(1)} %slice.276), channel_id=1, source_target_pairs={{0,1},{1,2},{2,3},{3,0},{4,5},{5,6},{6,7},{7,4},{8,9},{9,10},{10,1... | collective-permute-start | bytes 479240 | tf_op jit(solution)/shard_map/ppermute | solution.py:79
  33.7 18.7 %collective-permute-start.4 = (bf16[4,96,1664]{2,1,0:T(8,128)(2,1)}, bf16[4,96,1664]{2,1,0:T(8,128)(2,1)S(1)}, u32[]{:S(2)}, u32[]{:S(2)}) collective-permute-start(bf16[4,96,1664]{2,1,0:T(8,128)(2,1)} %pad_maximum_fusion.1), channel_id=1, source_target_pairs={{0,4},{1,5},{2,6},{3,7},{4,8},{5,9},{6,10},{7,11},{8,12},{9,13},{1... | collective-permute-start | bytes 3833864 | tf_op jit(solution)/shard_map/ppermute | solution.py:79
  35.1 17.8 %collective-permute-start.5 = (bf16[4,96,1664]{2,1,0:T(8,128)(2,1)}, bf16[4,96,1664]{2,1,0:T(8,128)(2,1)S(1)}, u32[]{:S(2)}, u32[]{:S(2)}) collective-permute-start(bf16[4,96,1664]{2,1,0:T(8,128)(2,1)} %pad_maximum_fusion.1), channel_id=1, source_target_pairs={{0,12},{1,13},{2,14},{3,15},{4,0},{5,1},{6,2},{7,3},{8,4},{9,5},{1... | collective-permute-start | bytes 3833864 | tf_op jit(solution)/shard_map/ppermute | solution.py:79
  37.9 15.3 %slice-start = ((s8[9437184]{0:T(1024)(128)(4,1)}), s8[4194304]{0:T(1024)(128)(4,1)S(1)}, s32[]{:S(2)}) async-start(s8[9437184]{0:T(1024)(128)(4,1)} %bitcast.45), calls=%async_computation | async-start | bytes 8388608
  37.9 15.3 %slice-start.1 = ((s8[9437184]{0:T(1024)(128)(4,1)}), s8[4194304]{0:T(1024)(128)(4,1)S(1)}, s32[]{:S(2)}) async-start(s8[9437184]{0:T(1024)(128)(4,1)} %bitcast.45), calls=%async_computation.1 | async-start | bytes 8388608
  38.0 15.3 %slice-start.2 = ((s8[9437184]{0:T(1024)(128)(4,1)}), s8[1048576]{0:T(1024)(128)(4,1)S(1)}, s32[]{:S(2)}) async-start(s8[9437184]{0:T(1024)(128)(4,1)} %bitcast.45), calls=%async_computation.2 | async-start | bytes 2097152
  64.1 13.9 %collective-permute-start.6 = (bf16[4,48,1664]{2,1,0:T(8,128)(2,1)}, bf16[4,48,1664]{2,1,0:T(8,128)(2,1)S(1)}, u32[]{:S(2)}, u32[]{:S(2)}) collective-permute-start(bf16[4,48,1664]{2,1,0:T(8,128)(2,1)} %slice.286), channel_id=1, source_target_pairs={{0,4},{1,5},{2,6},{3,7},{4,8},{5,9},{6,10},{7,11},{8,12},{9,13},{1... | collective-permute-start | bytes 1916936 | tf_op jit(solution)/shard_map/ppermute | solution.py:79
  67.0 11.1 %collective-permute-start.7 = (bf16[4,48,1664]{2,1,0:T(8,128)(2,1)}, bf16[4,48,1664]{2,1,0:T(8,128)(2,1)}, u32[]{:S(2)}, u32[]{:S(2)}) collective-permute-start(bf16[4,48,1664]{2,1,0:T(8,128)(2,1)} %slice.287), channel_id=1, source_target_pairs={{0,12},{1,13},{2,14},{3,15},{4,0},{5,1},{6,2},{7,3},{8,4},{9,5},{1... | collective-permute-start | bytes 1916936 | tf_op jit(solution)/shard_map/ppermute | solution.py:79
  68.4 10.8 %slice-start.3 = ((s8[9437184]{0:T(1024)(128)(4,1)}), s8[4194304]{0:T(1024)(128)(4,1)S(1)}, s32[]{:S(2)}) async-start(s8[9437184]{0:T(1024)(128)(4,1)} %bitcast.47), calls=%async_computation.3 | async-start | bytes 8388608
  68.4 10.8 %slice-start.4 = ((s8[9437184]{0:T(1024)(128)(4,1)}), s8[4194304]{0:T(1024)(128)(4,1)S(1)}, s32[]{:S(2)}) async-start(s8[9437184]{0:T(1024)(128)(4,1)} %bitcast.47), calls=%async_computation.4 | async-start | bytes 8388608
  75.7 3.6 %slice-start.5 = ((s8[9437184]{0:T(1024)(128)(4,1)}), s8[1048576]{0:T(1024)(128)(4,1)S(1)}, s32[]{:S(2)}) async-start(s8[9437184]{0:T(1024)(128)(4,1)} %bitcast.47), calls=%async_computation.5 | async-start | bytes 2097152
  99.5 3.9 %collective-permute-start.8 = (f32[4,1536]{1,0:T(4,128)S(1)}, f32[4,1536]{1,0:T(4,128)S(1)}, u32[]{:S(2)}, u32[]{:S(2)}) collective-permute-start(f32[4,1536]{1,0:T(4,128)S(1)} %broadcast_select_fusion), channel_id=1, source_target_pairs={{0,1},{1,0},{2,3},{3,2},{4,5},{5,4},{6,7},{7,6},{8,9},{9,8},{10,11... | collective-permute-start | bytes 73736 | tf_op jit(solution)/shard_map/ppermute | solution.py:32
  103.6 5.4 %collective-permute-start.9 = (f32[4,1536]{1,0:T(4,128)S(1)}, f32[4,1536]{1,0:T(4,128)S(1)}, u32[]{:S(2)}, u32[]{:S(2)}) collective-permute-start(f32[4,1536]{1,0:T(4,128)S(1)} %pad_maximum_fusion.4), channel_id=1, source_target_pairs={{0,2},{1,3},{2,0},{3,1},{4,6},{5,7},{6,4},{7,5},{8,10},{9,11},{10,... | collective-permute-start | bytes 73736 | tf_op jit(solution)/shard_map/ppermute | solution.py:32
  109.2 3.9 %collective-permute-start.10 = (f32[4,1536]{1,0:T(4,128)S(1)}, f32[4,1536]{1,0:T(4,128)S(1)}, u32[]{:S(2)}, u32[]{:S(2)}) collective-permute-start(f32[4,1536]{1,0:T(4,128)S(1)} %pad_maximum_fusion.5), channel_id=1, source_target_pairs={{0,4},{1,5},{2,6},{3,7},{4,0},{5,1},{6,2},{7,3},{8,12},{9,13},{10,... | collective-permute-start | bytes 73736 | tf_op jit(solution)/shard_map/ppermute | solution.py:32
  113.2 5.4 %collective-permute-start.11 = (f32[4,1536]{1,0:T(4,128)S(1)}, f32[4,1536]{1,0:T(4,128)S(1)}, u32[]{:S(2)}, u32[]{:S(2)}) collective-permute-start(f32[4,1536]{1,0:T(4,128)S(1)} %pad_maximum_fusion.6), channel_id=1, source_target_pairs={{0,8},{1,9},{2,10},{3,11},{4,12},{5,13},{6,14},{7,15},{8,0},{9,1},... | collective-permute-start | bytes 73736 | tf_op jit(solution)/shard_map/ppermute | solution.py:32
  120.1 1.2 collective-permute-start.12
  120.4 12.3 %copy-start.1 = (f32[128]{0:T(128)}, f32[128]{0:T(128)S(1)}, u32[]{:S(2)}) copy-start(f32[128]{0:T(128)S(1)} %fusion.40) | copy-start | bytes 1540
  120.6 12.1 %copy-start.2 = (f32[128]{0:T(128)}, f32[128]{0:T(128)S(1)}, u32[]{:S(2)}) copy-start(f32[128]{0:T(128)S(1)} %fusion.39) | copy-start | bytes 1540
  120.7 12.0 %copy-start = (f32[128]{0:T(128)}, f32[128]{0:T(128)S(1)}, u32[]{:S(2)}) copy-start(f32[128]{0:T(128)S(1)} %select_dynamic-update-slice_fusion) | copy-start | bytes 1540
  122.0 3.6 %collective-permute-start.13 = (f32[2]{0:T(128)S(1)}, f32[2]{0:T(128)S(1)}, u32[]{:S(2)}, u32[]{:S(2)}) collective-permute-start(f32[2]{0:T(128)S(1)} %fusion.31), channel_id=1, source_target_pairs={{0,32},{16,48},{32,0},{48,16},{64,96},{80,112},{96,64},{112,80},{1... | collective-permute-start | bytes 32 | tf_op jit(solution)/shard_map/ppermute | solution.py:32
  125.6 5.1 %collective-permute-start.14 = (f32[2]{0:T(128)S(1)}, f32[2]{0:T(128)S(1)}, u32[]{:S(2)}, u32[]{:S(2)}) collective-permute-start(f32[2]{0:T(128)S(1)} %fusion.30), channel_id=1, source_target_pairs={{0,64},{16,80},{32,96},{48,112},{64,0},{80,16},{96,32},{112,48},{1... | collective-permute-start | bytes 32 | tf_op jit(solution)/shard_map/ppermute | solution.py:32

commit v5 on v4

--- a/solution.py
+++ b/solution.py
@@ -1,6 +1,9 @@
 import jax
 import jax.numpy as jnp
 from jax import lax
+import functools
+from jax.experimental import pallas as pl
+from jax.experimental.pallas import tpu as pltpu
 from jax.sharding import PartitionSpec as P
 
 LIVE = 96
@@ -8,6 +11,7 @@
 EXTRA = 128
 SIDE = 4
 AXES = ("req", "voc")
+TM = 384
 
 
 def combine_stats(first, second):
@@ -79,20 +83,60 @@
     return lax.ppermute(value, AXES, pairs)
 
 
-def block_stats(block, head, position):
-    width = head.shape[0]
-    shard_width = head.shape[1]
-    rows_in = block[:, :width]
+TN = 512
+
+def stats_kernel(ids_ref, rows_ref, head_ref, out_ref, acc_ref, *, width):
+    j = pl.program_id(1)
+    @pl.when(j == 0)
+    def _():
+        acc_ref[0:1, :] = jnp.full((1, acc_ref.shape[1]), -jnp.inf, jnp.float32)
+        acc_ref[1:4, :] = jnp.zeros((3, acc_ref.shape[1]), jnp.float32)
+    rows = rows_ref[:, :width]
+    s = lax.dot_general(head_ref[...], rows, (((1,), (1,)), ((), ())), preferred_element_type=jnp.float32)
+    tn = s.shape[0]
+    top_old = acc_ref[0:1, :]
+    top = jnp.maximum(top_old, jnp.max(s, axis=0, keepdims=True))
+    scale = jnp.exp(top_old - top)
+    e = jnp.exp(s - top)
+    total = acc_ref[1:2, :] * scale + jnp.sum(e, axis=0, keepdims=True)
+    weighted = acc_ref[2:3, :] * scale + jnp.sum(e * s, axis=0, keepdims=True)
+    col = lax.broadcasted_iota(jnp.int32, s.shape, 0) + j * tn
+    picked = acc_ref[3:4, :] + jnp.sum(jnp.where(col == ids_ref[...], s, 0.0), axis=0, keepdims=True)
+    acc_ref[0:1, :] = top
+    acc_ref[1:2, :] = total
+    acc_ref[2:3, :] = weighted
+    acc_ref[3:4, :] = picked
+    @pl.when(j == pl.num_programs(1) - 1)
+    def _():
+        out_ref[...] = acc_ref[...]
+
+def pallas_stats(block, head_t, ids, tm):
+    n, cols = block.shape
+    vocab, width = head_t.shape
+    out = pl.pallas_call(
+        functools.partial(stats_kernel, width=width),
+        out_shape=jax.ShapeDtypeStruct((8, n), jnp.float32),
+        grid=(n // tm, vocab // TN),
+        in_specs=[
+            pl.BlockSpec((1, tm), lambda i, j: (0, i)),
+            pl.BlockSpec((tm, cols), lambda i, j: (i, 0)),
+            pl.BlockSpec((TN, width), lambda i, j: (j, 0)),
+        ],
+        out_specs=pl.BlockSpec((8, tm), lambda i, j: (0, i)),
+        scratch_shapes=[pltpu.VMEM((8, tm), jnp.float32)],
+        compiler_params=pltpu.CompilerParams(dimension_semantics=("arbitrary", "arbitrary")),
+        cost_estimate=pl.CostEstimate(flops=2 * n * width * vocab, transcendentals=n * vocab,
+                                      bytes_accessed=vocab * width * 2 * (n // tm) + n * cols * 2),
+    )(ids.reshape(1, n), block, head_t)
+    return out[:4]
+
+
+def block_stats(block, head_t, position):
+    width = head_t.shape[1]
+    shard_width = head_t.shape[0]
     meta = block[:, width:width + 2].astype(jnp.int32)
     ids = meta[:, 0] * 256 + meta[:, 1] - position * shard_width
-    columns = jnp.arange(shard_width, dtype=jnp.int32)
-    logits = jnp.dot(rows_in, head, preferred_element_type=jnp.float32)
-    top = jnp.max(logits, axis=-1)
-    expo = jnp.exp(logits - top[:, None])
-    total = jnp.sum(expo, axis=-1)
-    weighted = jnp.sum(expo * logits, axis=-1)
-    picked = jnp.sum(jnp.where(columns[None, :] == ids[:, None], logits, 0.0), axis=-1)
-    return jnp.stack([top, total, weighted, picked])
+    return pallas_stats(block, head_t, ids, TM)
 
 
 def shards(hidden, norm_gain, head, targets, bounds):
@@ -114,7 +158,8 @@
     meta = meta.at[:, 0].set(ids // 256).at[:, 1].set(ids % 256).at[:, 2].set(live_count)
     own = jnp.concatenate([normed, meta.astype(jnp.bfloat16)], axis=1)
 
-    stats = lambda block: block_stats(block, head, position)
+    head_t = head.T
+    stats = lambda block: block_stats(block, head_t, position)
     left = shift(own, 0, 1, reqs, vocs)
     right = shift(own, 0, -1, reqs, vocs)
     far_a = shift(left[:HALF], 0, 1, reqs, vocs)
@@ -124,9 +169,11 @@
     line_left = shift(line, 1, 1, reqs, vocs)
     line_right = shift(line, 1, -1, reqs, vocs)
     part_line = stats(line.reshape(-1, own.shape[1]))
+    part_line, line_left, line_right = lax.optimization_barrier((part_line, line_left, line_right))
     line_far_a = shift(line_left[:, :HALF], 1, 1, reqs, vocs)
     line_far_b = shift(line_right[:, HALF:], 1, -1, reqs, vocs)
     part_lines = stats(jnp.concatenate([line_left, line_right]).reshape(-1, own.shape[1]))
+    part_lines, line_far_a, line_far_b = lax.optimization_barrier((part_lines, line_far_a, line_far_b))
     line_far = jnp.concatenate([line_far_a, line_far_b], axis=1)
     part_line_far = stats(line_far.reshape(-1, own.shape[1]))
     processed = jnp.concatenate([part_line, part_lines, part_line_far], axis=1)

time: 134 us -> 142 us (1.060)
  Pallas kernels: 0 us -> 39.6 us
  matrix products: 25.7 us -> 0 us
  other arithmetic: 31.8 us -> 18.3 us
  local copies, waits for them, and re-layouts: 16.9 us -> 30.1 us
  waiting for transfers between devices: 29.8 us -> 21.3 us
  starting transfers between devices: 22 us -> 24.5 us
    pallas_call x0 -> x3, Pallas kernels: none -> 39.6 us  [pallas_stats(): pl.pallas_call(functools.partial(stats_kernel, width=width), out_shape=ja...]
    dot_general x3 -> x0, matrix products: 25.7 us -> none  [block_stats(): logits = jnp.dot(rows_in, head, preferred_element_type=jnp.float32)]
    reduce_sum x3 -> x0, other arithmetic: 15.2 us -> none  [block_stats(): total = jnp.sum(expo, axis=-1)]
    unnamed x26 -> x18, local copies, waits for them, and re-layouts: 5.06 us -> 17.8 us
    ppermute x8, waiting for transfers between devices: 10.4 us -> 4.55 us  [shift(): return lax.ppermute(value, AXES, pairs)]
    ppermute x7, starting transfers between devices: 7.64 us -> 10.3 us  [butterfly(): other = lax.ppermute(value, axis, [(i, i ^ step) for i in range(size)])]
    ppermute x7, waiting for transfers between devices: 19.4 us -> 16.8 us  [butterfly(): other = lax.ppermute(value, axis, [(i, i ^ step) for i in range(size)])]
    sub x0 -> x3, local copies, waits for them, and re-layouts: none -> 1.97 us  [block_stats(): ids = meta[:, 0] * 256 + meta[:, 1] - position * shard_width]
  transfers between devices with their start and end apart: 15 -> 15, of which waited for: 12 -> 10; matrix products, arithmetic and copies ran while one was open for 21% -> 16% of each run, Pallas kernels for 0% -> 21%
where the time goes in v5:
time: 142 us; the launch traced here: 141 us
  Pallas kernels  39.6 us (28%)
  local copies, waits for them, and re-layouts  30.1 us (21%)
  starting transfers between devices  24.5 us (17%)
  waiting for transfers between devices  21.3 us (15%)
  other arithmetic  18.3 us (13%)
  between operations  7.36 us (5%)
    pallas_call x3, Pallas kernels, pallas_stats(): pl.pallas_call(functools.partial(stats_kernel, width=width), out_shape=ja...  39.6 us
    unnamed x18, local copies, waits for them, and re-layouts  17.8 us
    ppermute x7, waiting for transfers between devices, butterfly(): other = lax.ppermute(value, axis, [(i, i ^ step) for i in range(size)])  16.8 us
    ppermute x8, starting transfers between devices, shift(): return lax.ppermute(value, AXES, pairs)  14.1 us
    ppermute x7, starting transfers between devices, butterfly(): other = lax.ppermute(value, axis, [(i, i ^ step) for i in range(size)])  10.3 us
    another operation x5, other arithmetic  4.79 us
    ppermute x8, waiting for transfers between devices, shift(): return lax.ppermute(value, AXES, pairs)  4.55 us
  transfers between devices with their start and end apart: 15, of which 10 were waited for; matrix products, arithmetic and copies ran while one was open for 16% of the time, Pallas kernels for 21%

profile of v5, /device:TPU:0, one launch (start us, length us, event | category | flops | bytes accessed | tf_op | source)
XLA Modules:
  0.0 141.1 jit_solution(2034304822930018800)
XLA Ops:
  0.6 0.6 compare_reduce_fusion.1
  1.3 0.6 compare_reduce_fusion.2
  1.9 0.7 compare_reduce_fusion
  2.6 1.3 fusion.37
  5.9 2.0 %fusion.32 = (s32[96,1]{0,1:T(1,128)S(1)}, s32[96,1]{0,1:T(1,128)S(1)}) fusion(pred[]{:T(512)} %compare_reduce_fusion.1, s32[128]{0:T(128)} %param.15, s32[]{:T(128)S(6)} %select_n.296, pred[]{:T(512)} %compare_reduce_fusion.2), kind=kLoop, calls=%fused_computation.161 | loop fusion | flops 2016 | bytes 1158 | tf_op jit(solution)/shard_map/reshape.260
  9.4 0.3 scatter.11
  9.8 0.8 slice_select_fusion
  10.5 0.3 scatter.14
  10.9 1.2 fusion
  12.0 1.1 fusion.2
  13.2 2.1 %collective-permute-start = (bf16[96,1664]{1,0:T(8,128)(2,1)S(1)}, bf16[96,1664]{1,0:T(8,128)(2,1)S(1)}, u32[]{:S(2)}, u32[]{:S(2)}) collective-permute-start(bf16[96,1664]{1,0:T(8,128)(2,1)S(1)} %get-tuple-element.75), channel_id=1, source_target_pairs={{0,1},{1,2},{2,3},{3,0},{4,5},{5,6},{6,7},{7,4},{8,9},{9,10},{10,1... | collective-permute-start | bytes 958472 | tf_op jit(solution)/shard_map/ppermute | solution.py:83
  15.3 2.2 %collective-permute-start.1 = (bf16[96,1664]{1,0:T(8,128)(2,1)S(1)}, bf16[96,1664]{1,0:T(8,128)(2,1)S(1)}, u32[]{:S(2)}, u32[]{:S(2)}) collective-permute-start(bf16[96,1664]{1,0:T(8,128)(2,1)S(1)} %get-tuple-element.75), channel_id=1, source_target_pairs={{0,3},{1,0},{2,1},{3,2},{4,7},{5,4},{6,5},{7,6},{8,11},{9,8},{10,9... | collective-permute-start | bytes 958472 | tf_op jit(solution)/shard_map/ppermute | solution.py:83
  17.5 12.7 %copy.21 = bf16[1536,3072]{0,1:T(8,128)(2,1)} copy(bf16[1536,3072]{1,0:T(8,128)(2,1)} %param.14) | data formatting | bytes 18874368 | tf_op args[2]
  30.3 0.7 gather_fusion
  31.0 0.7 gather_fusion.1
  31.7 0.8 constant_dynamic-update-slice_fusion.7
  32.5 3.3 %collective-permute-start.3 = (bf16[48,1664]{1,0:T(8,128)(2,1)S(1)}, bf16[48,1664]{1,0:T(8,128)(2,1)S(1)}, u32[]{:S(2)}, u32[]{:S(2)}) collective-permute-start(bf16[48,1664]{1,0:T(8,128)(2,1)S(1)} %slice.277), channel_id=1, source_target_pairs={{0,3},{1,0},{2,1},{3,2},{4,7},{5,4},{6,5},{7,6},{8,11},{9,8},{10,9... | collective-permute-start | bytes 479240 | tf_op jit(solution)/shard_map/ppermute | solution.py:83
  35.8 0.8 constant_dynamic-update-slice_fusion.6
  36.6 2.4 %collective-permute-done.2 = bf16[48,1664]{1,0:T(8,128)(2,1)S(1)} collective-permute-done((bf16[48,1664]{1,0:T(8,128)(2,1)S(1)}, bf16[48,1664]{1,0:T(8,128)(2,1)S(1)}, u32[]{:S(2)}, u32[]{:S(2)}) %collective-permute-start.2) | collective-permute-done | bytes 159776 | tf_op jit(solution)/shard_map/ppermute | solution.py:83
  39.0 1.3 pad_maximum_fusion.1
  40.3 1.5 %collective-permute-start.4 = (bf16[4,96,1664]{2,1,0:T(8,128)(2,1)}, bf16[4,96,1664]{2,1,0:T(8,128)(2,1)S(1)}, u32[]{:S(2)}, u32[]{:S(2)}) collective-permute-start(bf16[4,96,1664]{2,1,0:T(8,128)(2,1)} %pad_maximum_fusion.1), channel_id=1, source_target_pairs={{0,4},{1,5},{2,6},{3,7},{4,8},{5,9},{6,10},{7,11},{8,12},{9,13},{1... | collective-permute-start | bytes 3833864 | tf_op jit(solution)/shard_map/ppermute | solution.py:83
  41.8 1.7 %collective-permute-start.5 = (bf16[4,96,1664]{2,1,0:T(8,128)(2,1)}, bf16[4,96,1664]{2,1,0:T(8,128)(2,1)S(1)}, u32[]{:S(2)}, u32[]{:S(2)}) collective-permute-start(bf16[4,96,1664]{2,1,0:T(8,128)(2,1)} %pad_maximum_fusion.1), channel_id=1, source_target_pairs={{0,12},{1,13},{2,14},{3,15},{4,0},{5,1},{6,2},{7,3},{8,4},{9,5},{1... | collective-permute-start | bytes 3833864 | tf_op jit(solution)/shard_map/ppermute | solution.py:83
  43.5 0.7 constant_dynamic-update-slice_fusion.5
  44.3 0.9 slice_convert_fusion.2
  45.4 0.6 sub.157.ids_ref
  46.0 10.3 %shard_map.93 = f32[8,384]{1,0:T(8,128)} custom-call(s32[1,384]{1,0:T(1,128)} %sub.157.ids_ref, bf16[384,1664]{1,0:T(8,128)(2,1)} %bitcast.10.rows_ref, bf16[3072,1536]{1,0:T(8,128)(2,1)} %bitcast.36), custom_call_target="tpu_custom_call" | custom-call | flops 3623878656 | bytes 10715136 | tf_op jit(solution)/shard_map/pallas_call | solution.py:116
  56.3 0.8 constant_dynamic-update-slice_fusion.4
  57.1 1.9 %collective-permute-done.4 = bf16[4,96,1664]{2,1,0:T(8,128)(2,1)S(1)} collective-permute-done((bf16[4,96,1664]{2,1,0:T(8,128)(2,1)}, bf16[4,96,1664]{2,1,0:T(8,128)(2,1)S(1)}, u32[]{:S(2)}, u32[]{:S(2)}) %collective-permute-start.4) | collective-permute-done | bytes 1277984 | tf_op jit(solution)/shard_map/ppermute | solution.py:83
  59.2 0.9 slice.226
  60.4 1.0 slice.227
  61.7 0.3 copy-done.1
  62.0 0.6 sub.160.ids_ref
  62.6 1.5 %collective-permute-start.6 = (bf16[4,48,1664]{2,1,0:T(8,128)(2,1)}, bf16[4,48,1664]{2,1,0:T(8,128)(2,1)S(1)}, u32[]{:S(2)}, u32[]{:S(2)}) collective-permute-start(bf16[4,48,1664]{2,1,0:T(8,128)(2,1)} %slice.226), channel_id=1, source_target_pairs={{0,4},{1,5},{2,6},{3,7},{4,8},{5,9},{6,10},{7,11},{8,12},{9,13},{1... | collective-permute-start | bytes 1916936 | tf_op jit(solution)/shard_map/ppermute | solution.py:83
  64.1 1.7 %collective-permute-start.7 = (bf16[4,48,1664]{2,1,0:T(8,128)(2,1)}, bf16[4,48,1664]{2,1,0:T(8,128)(2,1)}, u32[]{:S(2)}, u32[]{:S(2)}) collective-permute-start(bf16[4,48,1664]{2,1,0:T(8,128)(2,1)} %slice.227), channel_id=1, source_target_pairs={{0,12},{1,13},{2,14},{3,15},{4,0},{5,1},{6,2},{7,3},{8,4},{9,5},{1... | collective-permute-start | bytes 1916936 | tf_op jit(solution)/shard_map/ppermute | solution.py:83
  65.9 18.9 %shard_map.94 = f32[8,768]{1,0:T(8,128)} custom-call(s32[1,768]{1,0:T(1,128)} %sub.160.ids_ref, bf16[768,1664]{1,0:T(8,128)(2,1)} %bitcast.40, bf16[3072,1536]{1,0:T(8,128)(2,1)} %bitcast.37), custom_call_target="tpu_custom_call" | custom-call | flops 7247757312 | bytes 21430272 | tf_op jit(solution)/shard_map/pallas_call | solution.py:116
  84.7 1.2 constant_dynamic-update-slice_fusion.3
  85.9 1.2 constant_dynamic-update-slice_fusion.2
  87.1 1.2 pad_maximum_fusion.2
  88.5 0.8 sub.162.ids_ref
  89.4 10.3 %shard_map.95 = f32[8,384]{1,0:T(8,128)} custom-call(s32[1,384]{1,0:T(1,128)} %sub.162.ids_ref, bf16[384,1664]{1,0:T(8,128)(2,1)} %bitcast.44, bf16[3072,1536]{1,0:T(8,128)(2,1)} %bitcast.38), custom_call_target="tpu_custom_call" | custom-call | flops 3623878656 | bytes 10715136 | tf_op jit(solution)/shard_map/pallas_call | solution.py:116
  99.7 0.7 slice.289
  100.5 0.6 gather_fusion.2
  101.2 0.9 constant_dynamic-update-slice_fusion.1
  102.1 2.0 %constant_dynamic-update-slice_fusion = bf16[16,96,1664]{2,1,0:T(8,128)(2,1)} fusion(bf16[16,96,1664]{2,1,0:T(8,128)(2,1)} %constant_dynamic-update-slice_fusion.1, bf16[4,48,1664]{2,1,0:T(8,128)(2,1)} %collective-permute-done.7), kind=kLoop, calls=%fused_computation.34 | loop fusion | bytes 1277952 | tf_op jit(solution)/shard_map/concatenate | solution.py:181
  104.1 1.2 fusion.9
  105.3 0.7 gather_fusion.3
  106.0 0.6 fusion.34
  106.8 0.7 collective-permute-start.8
  107.5 3.2 %collective-permute-done.8 = f32[4,1536]{1,0:T(4,128)S(1)} collective-permute-done((f32[4,1536]{1,0:T(4,128)S(1)}, f32[4,1536]{1,0:T(4,128)S(1)}, u32[]{:S(2)}, u32[]{:S(2)}) %collective-permute-start.8) | collective-permute-done | bytes 24608 | tf_op jit(solution)/shard_map/ppermute | solution.py:36
  110.8 2.8 %collective-permute-start.9 = (f32[4,1536]{1,0:T(4,128)S(1)}, f32[4,1536]{1,0:T(4,128)S(1)}, u32[]{:S(2)}, u32[]{:S(2)}) collective-permute-start(f32[4,1536]{1,0:T(4,128)S(1)} %pad_maximum_fusion.5), channel_id=1, source_target_pairs={{0,2},{1,3},{2,0},{3,1},{4,6},{5,7},{6,4},{7,5},{8,10},{9,11},{10,... | collective-permute-start | bytes 73736 | tf_op jit(solution)/shard_map/ppermute | solution.py:36
  113.7 2.6 %collective-permute-done.9 = f32[4,1536]{1,0:T(4,128)S(1)} collective-permute-done((f32[4,1536]{1,0:T(4,128)S(1)}, f32[4,1536]{1,0:T(4,128)S(1)}, u32[]{:S(2)}, u32[]{:S(2)}) %collective-permute-start.9) | collective-permute-done | bytes 24608 | tf_op jit(solution)/shard_map/ppermute | solution.py:36
  116.4 0.4 collective-permute-start.10
  116.8 3.5 %collective-permute-done.10 = f32[4,1536]{1,0:T(4,128)S(1)} collective-permute-done((f32[4,1536]{1,0:T(4,128)S(1)}, f32[4,1536]{1,0:T(4,128)S(1)}, u32[]{:S(2)}, u32[]{:S(2)}) %collective-permute-start.10) | collective-permute-done | bytes 24608 | tf_op jit(solution)/shard_map/ppermute | solution.py:36
  120.5 1.6 %collective-permute-start.11 = (f32[4,1536]{1,0:T(4,128)S(1)}, f32[4,1536]{1,0:T(4,128)S(1)}, u32[]{:S(2)}, u32[]{:S(2)}) collective-permute-start(f32[4,1536]{1,0:T(4,128)S(1)} %pad_maximum_fusion.7), channel_id=1, source_target_pairs={{0,8},{1,9},{2,10},{3,11},{4,12},{5,13},{6,14},{7,15},{8,0},{9,1},... | collective-permute-start | bytes 73736 | tf_op jit(solution)/shard_map/ppermute | solution.py:36
  122.9 3.0 %collective-permute-done.11 = f32[4,1536]{1,0:T(4,128)S(1)} collective-permute-done((f32[4,1536]{1,0:T(4,128)S(1)}, f32[4,1536]{1,0:T(4,128)S(1)}, u32[]{:S(2)}, u32[]{:S(2)}) %collective-permute-start.11) | collective-permute-done | bytes 24608 | tf_op jit(solution)/shard_map/ppermute | solution.py:36
  125.9 0.8 select_reduce_fusion
  126.7 0.7 pad_maximum_fusion.8
  128.0 0.6 collective-permute-done.12
  128.6 0.7 fusion.22
  129.3 1.6 %collective-permute-start.13 = (f32[2]{0:T(128)S(1)}, f32[2]{0:T(128)S(1)}, u32[]{:S(2)}, u32[]{:S(2)}) collective-permute-start(f32[2]{0:T(128)S(1)} %fusion.22), channel_id=1, source_target_pairs={{0,32},{16,48},{32,0},{48,16},{64,96},{80,112},{96,64},{112,80},{1... | collective-permute-start | bytes 32 | tf_op jit(solution)/shard_map/ppermute | solution.py:36
  130.9 2.0 %collective-permute-done.13 = f32[2]{0:T(128)S(1)} collective-permute-done((f32[2]{0:T(128)S(1)}, f32[2]{0:T(128)S(1)}, u32[]{:S(2)}, u32[]{:S(2)}) %collective-permute-start.13) | collective-permute-done | bytes 40 | tf_op jit(solution)/shard_map/ppermute | solution.py:36
  132.9 3.2 %collective-permute-start.14 = (f32[2]{0:T(128)S(1)}, f32[2]{0:T(128)S(1)}, u32[]{:S(2)}, u32[]{:S(2)}) collective-permute-start(f32[2]{0:T(128)S(1)} %fusion.21), channel_id=1, source_target_pairs={{0,64},{16,80},{32,96},{48,112},{64,0},{80,16},{96,32},{112,48},{1... | collective-permute-start | bytes 32 | tf_op jit(solution)/shard_map/ppermute | solution.py:36
  136.1 1.9 %collective-permute-done.14 = f32[2]{0:T(128)S(1)} collective-permute-done((f32[2]{0:T(128)S(1)}, f32[2]{0:T(128)S(1)}, u32[]{:S(2)}, u32[]{:S(2)}) %collective-permute-start.14) | collective-permute-done | bytes 40 | tf_op jit(solution)/shard_map/ppermute | solution.py:36
  138.0 0.6 fusion.36
  (75 shorter events, 3.4 us)
Async XLA Ops:
  13.2 19.2 %collective-permute-start = (bf16[96,1664]{1,0:T(8,128)(2,1)S(1)}, bf16[96,1664]{1,0:T(8,128)(2,1)S(1)}, u32[]{:S(2)}, u32[]{:S(2)}) collective-permute-start(bf16[96,1664]{1,0:T(8,128)(2,1)S(1)} %get-tuple-element.75), channel_id=1, source_target_pairs={{0,1},{1,2},{2,3},{3,0},{4,5},{5,6},{6,7},{7,4},{8,9},{9,10},{10,1... | collective-permute-start | bytes 958472 | tf_op jit(solution)/shard_map/ppermute | solution.py:83
  15.3 17.2 %collective-permute-start.1 = (bf16[96,1664]{1,0:T(8,128)(2,1)S(1)}, bf16[96,1664]{1,0:T(8,128)(2,1)S(1)}, u32[]{:S(2)}, u32[]{:S(2)}) collective-permute-start(bf16[96,1664]{1,0:T(8,128)(2,1)S(1)} %get-tuple-element.75), channel_id=1, source_target_pairs={{0,3},{1,0},{2,1},{3,2},{4,7},{5,4},{6,5},{7,6},{8,11},{9,8},{10,9... | collective-permute-start | bytes 958472 | tf_op jit(solution)/shard_map/ppermute | solution.py:83
  17.5 12.8 %copy-start = (s32[4]{0:T(128)S(1)}, s32[4]{0:T(128)}, u32[]{:S(2)}) copy-start(s32[4]{0:T(128)} %constant.242.clone) | copy-start | bytes 52
  32.4 6.6 %collective-permute-start.2 = (bf16[48,1664]{1,0:T(8,128)(2,1)S(1)}, bf16[48,1664]{1,0:T(8,128)(2,1)S(1)}, u32[]{:S(2)}, u32[]{:S(2)}) collective-permute-start(bf16[48,1664]{1,0:T(8,128)(2,1)S(1)} %slice.276), channel_id=1, source_target_pairs={{0,1},{1,2},{2,3},{3,0},{4,5},{5,6},{6,7},{7,4},{8,9},{9,10},{10,1... | collective-permute-start | bytes 479240 | tf_op jit(solution)/shard_map/ppermute | solution.py:83
  32.5 6.4 %collective-permute-start.3 = (bf16[48,1664]{1,0:T(8,128)(2,1)S(1)}, bf16[48,1664]{1,0:T(8,128)(2,1)S(1)}, u32[]{:S(2)}, u32[]{:S(2)}) collective-permute-start(bf16[48,1664]{1,0:T(8,128)(2,1)S(1)} %slice.277), channel_id=1, source_target_pairs={{0,3},{1,0},{2,1},{3,2},{4,7},{5,4},{6,5},{7,6},{8,11},{9,8},{10,9... | collective-permute-start | bytes 479240 | tf_op jit(solution)/shard_map/ppermute | solution.py:83
  40.3 18.7 %collective-permute-start.4 = (bf16[4,96,1664]{2,1,0:T(8,128)(2,1)}, bf16[4,96,1664]{2,1,0:T(8,128)(2,1)S(1)}, u32[]{:S(2)}, u32[]{:S(2)}) collective-permute-start(bf16[4,96,1664]{2,1,0:T(8,128)(2,1)} %pad_maximum_fusion.1), channel_id=1, source_target_pairs={{0,4},{1,5},{2,6},{3,7},{4,8},{5,9},{6,10},{7,11},{8,12},{9,13},{1... | collective-permute-start | bytes 3833864 | tf_op jit(solution)/shard_map/ppermute | solution.py:83
  41.8 17.5 %collective-permute-start.5 = (bf16[4,96,1664]{2,1,0:T(8,128)(2,1)}, bf16[4,96,1664]{2,1,0:T(8,128)(2,1)S(1)}, u32[]{:S(2)}, u32[]{:S(2)}) collective-permute-start(bf16[4,96,1664]{2,1,0:T(8,128)(2,1)} %pad_maximum_fusion.1), channel_id=1, source_target_pairs={{0,12},{1,13},{2,14},{3,15},{4,0},{5,1},{6,2},{7,3},{8,4},{9,5},{1... | collective-permute-start | bytes 3833864 | tf_op jit(solution)/shard_map/ppermute | solution.py:83
  60.4 1.6 %copy-start.1 = (bf16[8,96,1664]{2,1,0:T(8,128)(2,1)}, bf16[8,96,1664]{2,1,0:T(8,128)(2,1)S(1)}, u32[]{:S(2)}) copy-start(bf16[8,96,1664]{2,1,0:T(8,128)(2,1)S(1)} %pad_maximum_fusion) | copy-start | bytes 7667716
  62.6 24.5 %collective-permute-start.6 = (bf16[4,48,1664]{2,1,0:T(8,128)(2,1)}, bf16[4,48,1664]{2,1,0:T(8,128)(2,1)S(1)}, u32[]{:S(2)}, u32[]{:S(2)}) collective-permute-start(bf16[4,48,1664]{2,1,0:T(8,128)(2,1)} %slice.226), channel_id=1, source_target_pairs={{0,4},{1,5},{2,6},{3,7},{4,8},{5,9},{6,10},{7,11},{8,12},{9,13},{1... | collective-permute-start | bytes 1916936 | tf_op jit(solution)/shard_map/ppermute | solution.py:83
  64.1 23.0 %collective-permute-start.7 = (bf16[4,48,1664]{2,1,0:T(8,128)(2,1)}, bf16[4,48,1664]{2,1,0:T(8,128)(2,1)}, u32[]{:S(2)}, u32[]{:S(2)}) collective-permute-start(bf16[4,48,1664]{2,1,0:T(8,128)(2,1)} %slice.227), channel_id=1, source_target_pairs={{0,12},{1,13},{2,14},{3,15},{4,0},{5,1},{6,2},{7,3},{8,4},{9,5},{1... | collective-permute-start | bytes 1916936 | tf_op jit(solution)/shard_map/ppermute | solution.py:83
  88.3 1.1 copy-start.2
  89.3 11.1 %slice-start = ((f32[8,768]{1,0:T(8,128)}), f32[4,768]{1,0:T(4,128)S(1)}, s32[]{:S(2)}) async-start(f32[8,768]{1,0:T(8,128)} %shard_map.94), calls=%async_computation | async-start | bytes 24576 | tf_op jit(solution)/shard_map/slice | solution.py:131
  89.3 11.1 %slice-start.1 = ((f32[8,384]{1,0:T(8,128)}), f32[4,384]{1,0:T(4,128)S(1)}, s32[]{:S(2)}) async-start(f32[8,384]{1,0:T(8,128)} %shard_map.93), calls=%async_computation.1 | async-start | bytes 12288 | tf_op jit(solution)/shard_map/slice | solution.py:131
  106.8 3.9 %collective-permute-start.8 = (f32[4,1536]{1,0:T(4,128)S(1)}, f32[4,1536]{1,0:T(4,128)S(1)}, u32[]{:S(2)}, u32[]{:S(2)}) collective-permute-start(f32[4,1536]{1,0:T(4,128)S(1)} %broadcast_select_fusion), channel_id=1, source_target_pairs={{0,1},{1,0},{2,3},{3,2},{4,5},{5,4},{6,7},{7,6},{8,9},{9,8},{10,11... | collective-permute-start | bytes 73736 | tf_op jit(solution)/shard_map/ppermute | solution.py:36
  110.8 5.4 %collective-permute-start.9 = (f32[4,1536]{1,0:T(4,128)S(1)}, f32[4,1536]{1,0:T(4,128)S(1)}, u32[]{:S(2)}, u32[]{:S(2)}) collective-permute-start(f32[4,1536]{1,0:T(4,128)S(1)} %pad_maximum_fusion.5), channel_id=1, source_target_pairs={{0,2},{1,3},{2,0},{3,1},{4,6},{5,7},{6,4},{7,5},{8,10},{9,11},{10,... | collective-permute-start | bytes 73736 | tf_op jit(solution)/shard_map/ppermute | solution.py:36
  116.4 3.9 %collective-permute-start.10 = (f32[4,1536]{1,0:T(4,128)S(1)}, f32[4,1536]{1,0:T(4,128)S(1)}, u32[]{:S(2)}, u32[]{:S(2)}) collective-permute-start(f32[4,1536]{1,0:T(4,128)S(1)} %pad_maximum_fusion.6), channel_id=1, source_target_pairs={{0,4},{1,5},{2,6},{3,7},{4,0},{5,1},{6,2},{7,3},{8,12},{9,13},{10,... | collective-permute-start | bytes 73736 | tf_op jit(solution)/shard_map/ppermute | solution.py:36
  120.5 5.4 %collective-permute-start.11 = (f32[4,1536]{1,0:T(4,128)S(1)}, f32[4,1536]{1,0:T(4,128)S(1)}, u32[]{:S(2)}, u32[]{:S(2)}) collective-permute-start(f32[4,1536]{1,0:T(4,128)S(1)} %pad_maximum_fusion.7), channel_id=1, source_target_pairs={{0,8},{1,9},{2,10},{3,11},{4,12},{5,13},{6,14},{7,15},{8,0},{9,1},... | collective-permute-start | bytes 73736 | tf_op jit(solution)/shard_map/ppermute | solution.py:36
  127.4 1.2 collective-permute-start.12
  127.6 12.3 %copy-start.4 = (f32[128]{0:T(128)}, f32[128]{0:T(128)S(1)}, u32[]{:S(2)}) copy-start(f32[128]{0:T(128)S(1)} %fusion.31) | copy-start | bytes 1540
  127.8 12.1 %copy-start.5 = (f32[128]{0:T(128)}, f32[128]{0:T(128)S(1)}, u32[]{:S(2)}) copy-start(f32[128]{0:T(128)S(1)} %fusion.30) | copy-start | bytes 1540
  128.0 12.0 %copy-start.3 = (f32[128]{0:T(128)}, f32[128]{0:T(128)S(1)}, u32[]{:S(2)}) copy-start(f32[128]{0:T(128)S(1)} %select_dynamic-update-slice_fusion) | copy-start | bytes 1540
  129.3 3.6 %collective-permute-start.13 = (f32[2]{0:T(128)S(1)}, f32[2]{0:T(128)S(1)}, u32[]{:S(2)}, u32[]{:S(2)}) collective-permute-start(f32[2]{0:T(128)S(1)} %fusion.22), channel_id=1, source_target_pairs={{0,32},{16,48},{32,0},{48,16},{64,96},{80,112},{96,64},{112,80},{1... | collective-permute-start | bytes 32 | tf_op jit(solution)/shard_map/ppermute | solution.py:36
  132.9 5.1 %collective-permute-start.14 = (f32[2]{0:T(128)S(1)}, f32[2]{0:T(128)S(1)}, u32[]{:S(2)}, u32[]{:S(2)}) collective-permute-start(f32[2]{0:T(128)S(1)} %fusion.21), channel_id=1, source_target_pairs={{0,64},{16,80},{32,96},{48,112},{64,0},{80,16},{96,32},{112,48},{1... | collective-permute-start | bytes 32 | tf_op jit(solution)/shard_map/ppermute | solution.py:36

commit v6 on v5

--- a/solution.py
+++ b/solution.py
@@ -89,54 +89,54 @@
     j = pl.program_id(1)
     @pl.when(j == 0)
     def _():
-        acc_ref[0:1, :] = jnp.full((1, acc_ref.shape[1]), -jnp.inf, jnp.float32)
-        acc_ref[1:4, :] = jnp.zeros((3, acc_ref.shape[1]), jnp.float32)
+        acc_ref[:, 0:1] = jnp.full((acc_ref.shape[0], 1), -jnp.inf, jnp.float32)
+        acc_ref[:, 1:4] = jnp.zeros((acc_ref.shape[0], 3), jnp.float32)
     rows = rows_ref[:, :width]
-    s = lax.dot_general(head_ref[...], rows, (((1,), (1,)), ((), ())), preferred_element_type=jnp.float32)
-    tn = s.shape[0]
-    top_old = acc_ref[0:1, :]
-    top = jnp.maximum(top_old, jnp.max(s, axis=0, keepdims=True))
+    s = jnp.dot(rows, head_ref[...], preferred_element_type=jnp.float32)
+    tn = s.shape[1]
+    top_old = acc_ref[:, 0:1]
+    top = jnp.maximum(top_old, jnp.max(s, axis=1, keepdims=True))
     scale = jnp.exp(top_old - top)
     e = jnp.exp(s - top)
-    total = acc_ref[1:2, :] * scale + jnp.sum(e, axis=0, keepdims=True)
-    weighted = acc_ref[2:3, :] * scale + jnp.sum(e * s, axis=0, keepdims=True)
-    col = lax.broadcasted_iota(jnp.int32, s.shape, 0) + j * tn
-    picked = acc_ref[3:4, :] + jnp.sum(jnp.where(col == ids_ref[...], s, 0.0), axis=0, keepdims=True)
-    acc_ref[0:1, :] = top
-    acc_ref[1:2, :] = total
-    acc_ref[2:3, :] = weighted
-    acc_ref[3:4, :] = picked
+    total = acc_ref[:, 1:2] * scale + jnp.sum(e, axis=1, keepdims=True)
+    weighted = acc_ref[:, 2:3] * scale + jnp.sum(e * s, axis=1, keepdims=True)
+    col = lax.broadcasted_iota(jnp.int32, s.shape, 1) + j * tn
+    picked = acc_ref[:, 3:4] + jnp.sum(jnp.where(col == ids_ref[...], s, 0.0), axis=1, keepdims=True)
+    acc_ref[:, 0:1] = top
+    acc_ref[:, 1:2] = total
+    acc_ref[:, 2:3] = weighted
+    acc_ref[:, 3:4] = picked
     @pl.when(j == pl.num_programs(1) - 1)
     def _():
         out_ref[...] = acc_ref[...]
 
-def pallas_stats(block, head_t, ids, tm):
+def pallas_stats(block, head, ids, tm):
     n, cols = block.shape
-    vocab, width = head_t.shape
+    width, vocab = head.shape
     out = pl.pallas_call(
         functools.partial(stats_kernel, width=width),
-        out_shape=jax.ShapeDtypeStruct((8, n), jnp.float32),
+        out_shape=jax.ShapeDtypeStruct((n, 128), jnp.float32),
         grid=(n // tm, vocab // TN),
         in_specs=[
-            pl.BlockSpec((1, tm), lambda i, j: (0, i)),
+            pl.BlockSpec((tm, 1), lambda i, j: (i, 0)),
             pl.BlockSpec((tm, cols), lambda i, j: (i, 0)),
-            pl.BlockSpec((TN, width), lambda i, j: (j, 0)),
+            pl.BlockSpec((width, TN), lambda i, j: (0, j)),
         ],
-        out_specs=pl.BlockSpec((8, tm), lambda i, j: (0, i)),
-        scratch_shapes=[pltpu.VMEM((8, tm), jnp.float32)],
+        out_specs=pl.BlockSpec((tm, 128), lambda i, j: (i, 0)),
+        scratch_shapes=[pltpu.VMEM((tm, 128), jnp.float32)],
         compiler_params=pltpu.CompilerParams(dimension_semantics=("arbitrary", "arbitrary")),
         cost_estimate=pl.CostEstimate(flops=2 * n * width * vocab, transcendentals=n * vocab,
                                       bytes_accessed=vocab * width * 2 * (n // tm) + n * cols * 2),
-    )(ids.reshape(1, n), block, head_t)
-    return out[:4]
-
-
-def block_stats(block, head_t, position):
-    width = head_t.shape[1]
-    shard_width = head_t.shape[0]
+    )(ids.reshape(n, 1), block, head)
+    return out[:, :4].T
+
+
+def block_stats(block, head, position):
+    width = head.shape[0]
+    shard_width = head.shape[1]
     meta = block[:, width:width + 2].astype(jnp.int32)
     ids = meta[:, 0] * 256 + meta[:, 1] - position * shard_width
-    return pallas_stats(block, head_t, ids, TM)
+    return pallas_stats(block, head, ids, TM)
 
 
 def shards(hidden, norm_gain, head, targets, bounds):
@@ -158,8 +158,7 @@
     meta = meta.at[:, 0].set(ids // 256).at[:, 1].set(ids % 256).at[:, 2].set(live_count)
     own = jnp.concatenate([normed, meta.astype(jnp.bfloat16)], axis=1)
 
-    head_t = head.T
-    stats = lambda block: block_stats(block, head_t, position)
+    stats = lambda block: block_stats(block, head, position)
     left = shift(own, 0, 1, reqs, vocs)
     right = shift(own, 0, -1, reqs, vocs)
     far_a = shift(left[:HALF], 0, 1, reqs, vocs)

time: 142 us -> 151 us (1.063)
  local copies, waits for them, and re-layouts: 30.1 us -> 19.6 us
  waiting for transfers between devices: 21.3 us -> 30.9 us
  Pallas kernels: 39.6 us -> 48.4 us
  other arithmetic: 18.3 us -> 20 us
    unnamed x18 -> x19, local copies, waits for them, and re-layouts: 17.8 us -> 5.39 us
    pallas_call x3, Pallas kernels: 39.6 us -> 48.4 us  [pallas_stats(): pl.pallas_call(functools.partial(stats_kernel, width=width), out_shape=ja...]
    ppermute x8, waiting for transfers between devices: 4.55 us -> 12.9 us  [shift(): return lax.ppermute(value, AXES, pairs)]
    transpose x0 -> x4, local copies, waits for them, and re-layouts: none -> 3.75 us  [pallas_stats(): return out[:, :4].T]
    sub x3 -> x0, local copies, waits for them, and re-layouts: 1.97 us -> none  [block_stats(): ids = meta[:, 0] * 256 + meta[:, 1] - position * shard_width]
    sub x3, other arithmetic: 0.75 us -> 2.56 us  [block_stats(): ids = meta[:, 0] * 256 + meta[:, 1] - position * shard_width]
  transfers between devices with their start and end apart: 15 -> 15, of which waited for: 10 -> 12; matrix products, arithmetic and copies ran while one was open for 16% -> 8% of each run, Pallas kernels for 21% -> 8%
where the time goes in v6:
time: 151 us; the launch traced here: 150 us
  Pallas kernels  48.4 us (32%)
  waiting for transfers between devices  30.9 us (20%)
  starting transfers between devices  23.4 us (15%)
  other arithmetic  20 us (13%)
  local copies, waits for them, and re-layouts  19.6 us (13%)
  between operations  7.38 us (5%)
    pallas_call x3, Pallas kernels, pallas_stats(): pl.pallas_call(functools.partial(stats_kernel, width=width), out_shape=ja...  48.4 us
    ppermute x7, waiting for transfers between devices, butterfly(): other = lax.ppermute(value, axis, [(i, i ^ step) for i in range(size)])  18 us
    ppermute x8, starting transfers between devices, shift(): return lax.ppermute(value, AXES, pairs)  14.3 us
    ppermute x8, waiting for transfers between devices, shift(): return lax.ppermute(value, AXES, pairs)  12.9 us
    ppermute x7, starting transfers between devices, butterfly(): other = lax.ppermute(value, axis, [(i, i ^ step) for i in range(size)])  9.1 us
    unnamed x19, local copies, waits for them, and re-layouts  5.39 us
    another operation x5, other arithmetic  4.79 us
    transpose x4, local copies, waits for them, and re-layouts, pallas_stats(): return out[:, :4].T  3.75 us
  transfers between devices with their start and end apart: 15, of which 12 were waited for; matrix products, arithmetic and copies ran while one was open for 8% of the time, Pallas kernels for 8%

profile of v6, /device:TPU:0, one launch (start us, length us, event | category | flops | bytes accessed | tf_op | source)
XLA Modules:
  0.0 149.8 jit_solution(16981905262541474094)
XLA Ops:
  0.6 0.6 compare_reduce_fusion.1
  1.3 0.6 compare_reduce_fusion.2
  1.9 0.7 compare_reduce_fusion
  2.6 1.3 fusion.34
  5.9 2.0 %fusion.29 = (s32[96,1]{0,1:T(1,128)S(1)}, s32[96,1]{0,1:T(1,128)S(1)}) fusion(pred[]{:T(512)} %compare_reduce_fusion.1, s32[128]{0:T(128)} %param.15, s32[]{:T(128)S(6)} %select_n.296, pred[]{:T(512)} %compare_reduce_fusion.2), kind=kLoop, calls=%fused_computation.161 | loop fusion | flops 2016 | bytes 1158 | tf_op jit(solution)/shard_map/reshape.233
  9.8 0.8 slice_select_fusion
  10.5 0.3 scatter.14
  10.9 1.2 fusion
  12.1 1.1 fusion.2
  13.2 2.1 %collective-permute-start = (bf16[96,1664]{1,0:T(8,128)(2,1)S(1)}, bf16[96,1664]{1,0:T(8,128)(2,1)S(1)}, u32[]{:S(2)}, u32[]{:S(2)}) collective-permute-start(bf16[96,1664]{1,0:T(8,128)(2,1)S(1)} %get-tuple-element.75), channel_id=1, source_target_pairs={{0,1},{1,2},{2,3},{3,0},{4,5},{5,6},{6,7},{7,4},{8,9},{9,10},{10,1... | collective-permute-start | bytes 958472 | tf_op jit(solution)/shard_map/ppermute | solution.py:83
  15.3 2.2 %collective-permute-start.1 = (bf16[96,1664]{1,0:T(8,128)(2,1)S(1)}, bf16[96,1664]{1,0:T(8,128)(2,1)S(1)}, u32[]{:S(2)}, u32[]{:S(2)}) collective-permute-start(bf16[96,1664]{1,0:T(8,128)(2,1)S(1)} %get-tuple-element.75), channel_id=1, source_target_pairs={{0,3},{1,0},{2,1},{3,2},{4,7},{5,4},{6,5},{7,6},{8,11},{9,8},{10,9... | collective-permute-start | bytes 958472 | tf_op jit(solution)/shard_map/ppermute | solution.py:83
  17.6 0.7 gather_fusion.1
  18.3 0.7 gather_fusion
  18.9 0.7 constant_dynamic-update-slice_fusion.7
  19.7 2.6 %collective-permute-done.1 = bf16[96,1664]{1,0:T(8,128)(2,1)S(1)} collective-permute-done((bf16[96,1664]{1,0:T(8,128)(2,1)S(1)}, bf16[96,1664]{1,0:T(8,128)(2,1)S(1)}, u32[]{:S(2)}, u32[]{:S(2)}) %collective-permute-start.1) | collective-permute-done | bytes 319520 | tf_op jit(solution)/shard_map/ppermute | solution.py:83
  22.3 3.5 %collective-permute-start.3 = (bf16[48,1664]{1,0:T(8,128)(2,1)S(1)}, bf16[48,1664]{1,0:T(8,128)(2,1)S(1)}, u32[]{:S(2)}, u32[]{:S(2)}) collective-permute-start(bf16[48,1664]{1,0:T(8,128)(2,1)S(1)} %slice.277), channel_id=1, source_target_pairs={{0,3},{1,0},{2,1},{3,2},{4,7},{5,4},{6,5},{7,6},{8,11},{9,8},{10,9... | collective-permute-start | bytes 479240 | tf_op jit(solution)/shard_map/ppermute | solution.py:83
  25.9 0.7 constant_dynamic-update-slice_fusion.6
  26.7 1.9 %collective-permute-done.3 = bf16[48,1664]{1,0:T(8,128)(2,1)S(1)} collective-permute-done((bf16[48,1664]{1,0:T(8,128)(2,1)S(1)}, bf16[48,1664]{1,0:T(8,128)(2,1)S(1)}, u32[]{:S(2)}, u32[]{:S(2)}) %collective-permute-start.3) | collective-permute-done | bytes 159776 | tf_op jit(solution)/shard_map/ppermute | solution.py:83
  28.6 3.8 %collective-permute-done.2 = bf16[48,1664]{1,0:T(8,128)(2,1)S(1)} collective-permute-done((bf16[48,1664]{1,0:T(8,128)(2,1)S(1)}, bf16[48,1664]{1,0:T(8,128)(2,1)S(1)}, u32[]{:S(2)}, u32[]{:S(2)}) %collective-permute-start.2) | collective-permute-done | bytes 159776 | tf_op jit(solution)/shard_map/ppermute | solution.py:83
  32.4 1.3 pad_maximum_fusion.1
  33.7 1.5 collective-permute-start.4
  35.2 1.7 %collective-permute-start.5 = (bf16[4,96,1664]{2,1,0:T(8,128)(2,1)}, bf16[4,96,1664]{2,1,0:T(8,128)(2,1)S(1)}, u32[]{:S(2)}, u32[]{:S(2)}) collective-permute-start(bf16[4,96,1664]{2,1,0:T(8,128)(2,1)} %pad_maximum_fusion.1), channel_id=1, source_target_pairs={{0,12},{1,13},{2,14},{3,15},{4,0},{5,1},{6,2},{7,3},{8,4},{9,5},{1... | collective-permute-start | bytes 3833864 | tf_op jit(solution)/shard_map/ppermute | solution.py:83
  36.9 0.7 constant_dynamic-update-slice_fusion.5
  37.7 0.9 slice_convert_fusion.2
  38.6 0.8 fusion.5.ids_ref
  39.4 12.6 %shard_map.93 = f32[384,128]{1,0:T(8,128)} custom-call(s32[384,1]{1,0:T(8,128)} %fusion.5.ids_ref, bf16[384,1664]{1,0:T(8,128)(2,1)} %bitcast.10.rows_ref, bf16[1536,3072]{1,0:T(8,128)(2,1)} %head_ref.5), custom_call_target="tpu_custom_call" | custom-call | flops 3623878656 | bytes 10715136 | tf_op jit(solution)/shard_map/pallas_call | solution.py:116
  52.0 0.9 slice_bitcast_fusion.2
  53.0 0.8 constant_dynamic-update-slice_fusion.4
  53.7 0.9 slice.226
  54.9 1.0 slice.227
  55.9 0.7 copy-done.1
  56.7 0.9 fusion.3.ids_ref
  57.6 23.1 %shard_map.94 = f32[768,128]{1,0:T(8,128)} custom-call(s32[768,1]{1,0:T(8,128)} %fusion.3.ids_ref, bf16[768,1664]{1,0:T(8,128)(2,1)} %bitcast.42, bf16[1536,3072]{1,0:T(8,128)(2,1)} %head_ref.5), custom_call_target="tpu_custom_call" | custom-call | flops 7247757312 | bytes 21430272 | tf_op jit(solution)/shard_map/pallas_call | solution.py:116
  80.7 1.3 collective-permute-start.6
  82.0 2.0 %collective-permute-start.7 = (bf16[4,48,1664]{2,1,0:T(8,128)(2,1)}, bf16[4,48,1664]{2,1,0:T(8,128)(2,1)}, u32[]{:S(2)}, u32[]{:S(2)}) collective-permute-start(bf16[4,48,1664]{2,1,0:T(8,128)(2,1)} %slice.227), channel_id=1, source_target_pairs={{0,12},{1,13},{2,14},{3,15},{4,0},{5,1},{6,2},{7,3},{8,4},{9,5},{1... | collective-permute-start | bytes 1916936 | tf_op jit(solution)/shard_map/ppermute | solution.py:83
  83.9 1.8 %slice_bitcast_fusion = f32[4,768]{0,1:T(8,128)} fusion(f32[768,128]{1,0:T(8,128)} %shard_map.94), kind=kLoop, calls=%fused_computation.12 | loop fusion | bytes 24576 | tf_op jit(solution)/shard_map/transpose | solution.py:131
  85.8 1.2 constant_dynamic-update-slice_fusion.3
  87.0 1.2 constant_dynamic-update-slice_fusion.2
  88.2 4.4 %collective-permute-done.6 = bf16[4,48,1664]{2,1,0:T(8,128)(2,1)S(1)} collective-permute-done((bf16[4,48,1664]{2,1,0:T(8,128)(2,1)}, bf16[4,48,1664]{2,1,0:T(8,128)(2,1)S(1)}, u32[]{:S(2)}, u32[]{:S(2)}) %collective-permute-start.6) | collective-permute-done | bytes 639008 | tf_op jit(solution)/shard_map/ppermute | solution.py:83
  92.7 0.9 constant_dynamic-update-slice_fusion.1
  93.6 1.2 pad_maximum_fusion.2
  94.7 2.5 %constant_dynamic-update-slice_fusion = bf16[16,96,1664]{2,1,0:T(8,128)(2,1)} fusion(bf16[16,96,1664]{2,1,0:T(8,128)(2,1)} %constant_dynamic-update-slice_fusion.1, bf16[4,48,1664]{2,1,0:T(8,128)(2,1)} %collective-permute-done.7), kind=kLoop, calls=%fused_computation.34 | loop fusion | bytes 1277952 | tf_op jit(solution)/shard_map/concatenate | solution.py:180
  97.2 1.2 fusion.6
  98.4 0.7 gather_fusion.3
  99.1 0.6 fusion.31
  99.8 0.8 fusion.4.ids_ref
  100.6 12.7 %shard_map.95 = f32[384,128]{1,0:T(8,128)} custom-call(s32[384,1]{1,0:T(8,128)} %fusion.4.ids_ref, bf16[384,1664]{1,0:T(8,128)(2,1)} %bitcast.46, bf16[1536,3072]{1,0:T(8,128)(2,1)} %head_ref.5), custom_call_target="tpu_custom_call" | custom-call | flops 3623878656 | bytes 10715136 | tf_op jit(solution)/shard_map/pallas_call | solution.py:116
  113.3 0.9 slice_bitcast_fusion.1
  114.6 0.6 gather_fusion.2
  115.6 3.8 %collective-permute-done.8 = f32[4,1536]{1,0:T(4,128)S(1)} collective-permute-done((f32[4,1536]{1,0:T(4,128)S(1)}, f32[4,1536]{1,0:T(4,128)S(1)}, u32[]{:S(2)}, u32[]{:S(2)}) %collective-permute-start.8) | collective-permute-done | bytes 24608 | tf_op jit(solution)/shard_map/ppermute | solution.py:36
  119.6 5.3 %collective-permute-done.9 = f32[4,1536]{1,0:T(4,128)S(1)} collective-permute-done((f32[4,1536]{1,0:T(4,128)S(1)}, f32[4,1536]{1,0:T(4,128)S(1)}, u32[]{:S(2)}, u32[]{:S(2)}) %collective-permute-start.9) | collective-permute-done | bytes 24608 | tf_op jit(solution)/shard_map/ppermute | solution.py:36
  125.1 1.4 collective-permute-start.10
  126.5 2.5 %collective-permute-done.10 = f32[4,1536]{1,0:T(4,128)S(1)} collective-permute-done((f32[4,1536]{1,0:T(4,128)S(1)}, f32[4,1536]{1,0:T(4,128)S(1)}, u32[]{:S(2)}, u32[]{:S(2)}) %collective-permute-start.10) | collective-permute-done | bytes 24608 | tf_op jit(solution)/shard_map/ppermute | solution.py:36
  129.1 2.7 %collective-permute-start.11 = (f32[4,1536]{1,0:T(4,128)S(1)}, f32[4,1536]{1,0:T(4,128)S(1)}, u32[]{:S(2)}, u32[]{:S(2)}) collective-permute-start(f32[4,1536]{1,0:T(4,128)S(1)} %pad_maximum_fusion.7), channel_id=1, source_target_pairs={{0,8},{1,9},{2,10},{3,11},{4,12},{5,13},{6,14},{7,15},{8,0},{9,1},... | collective-permute-start | bytes 73736 | tf_op jit(solution)/shard_map/ppermute | solution.py:36
  132.7 1.9 %collective-permute-done.11 = f32[4,1536]{1,0:T(4,128)S(1)} collective-permute-done((f32[4,1536]{1,0:T(4,128)S(1)}, f32[4,1536]{1,0:T(4,128)S(1)}, u32[]{:S(2)}, u32[]{:S(2)}) %collective-permute-start.11) | collective-permute-done | bytes 24608 | tf_op jit(solution)/shard_map/ppermute | solution.py:36
  134.6 0.8 select_reduce_fusion
  135.3 0.7 pad_maximum_fusion.8
  136.7 0.6 collective-permute-done.12
  137.2 0.7 fusion.19
  138.0 1.6 %collective-permute-start.13 = (f32[2]{0:T(128)S(1)}, f32[2]{0:T(128)S(1)}, u32[]{:S(2)}, u32[]{:S(2)}) collective-permute-start(f32[2]{0:T(128)S(1)} %fusion.19), channel_id=1, source_target_pairs={{0,32},{16,48},{32,0},{48,16},{64,96},{80,112},{96,64},{112,80},{1... | collective-permute-start | bytes 32 | tf_op jit(solution)/shard_map/ppermute | solution.py:36
  139.5 2.0 %collective-permute-done.13 = f32[2]{0:T(128)S(1)} collective-permute-done((f32[2]{0:T(128)S(1)}, f32[2]{0:T(128)S(1)}, u32[]{:S(2)}, u32[]{:S(2)}) %collective-permute-start.13) | collective-permute-done | bytes 40 | tf_op jit(solution)/shard_map/ppermute | solution.py:36
  141.6 3.2 %collective-permute-start.14 = (f32[2]{0:T(128)S(1)}, f32[2]{0:T(128)S(1)}, u32[]{:S(2)}, u32[]{:S(2)}) collective-permute-start(f32[2]{0:T(128)S(1)} %fusion.18), channel_id=1, source_target_pairs={{0,64},{16,80},{32,96},{48,112},{64,0},{80,16},{96,32},{112,48},{1... | collective-permute-start | bytes 32 | tf_op jit(solution)/shard_map/ppermute | solution.py:36
  144.7 1.9 %collective-permute-done.14 = f32[2]{0:T(128)S(1)} collective-permute-done((f32[2]{0:T(128)S(1)}, f32[2]{0:T(128)S(1)}, u32[]{:S(2)}, u32[]{:S(2)}) %collective-permute-start.14) | collective-permute-done | bytes 40 | tf_op jit(solution)/shard_map/ppermute | solution.py:36
  146.6 0.6 fusion.33
  (74 shorter events, 3.3 us)
Async XLA Ops:
  0.6 17.0 %copy-start = (s32[4]{0:T(128)S(1)}, s32[4]{0:T(128)}, u32[]{:S(2)}) copy-start(s32[4]{0:T(128)} %constant.242.clone) | copy-start | bytes 52
  13.2 12.6 %collective-permute-start = (bf16[96,1664]{1,0:T(8,128)(2,1)S(1)}, bf16[96,1664]{1,0:T(8,128)(2,1)S(1)}, u32[]{:S(2)}, u32[]{:S(2)}) collective-permute-start(bf16[96,1664]{1,0:T(8,128)(2,1)S(1)} %get-tuple-element.75), channel_id=1, source_target_pairs={{0,1},{1,2},{2,3},{3,0},{4,5},{5,6},{6,7},{7,4},{8,9},{9,10},{10,1... | collective-permute-start | bytes 958472 | tf_op jit(solution)/shard_map/ppermute | solution.py:83
  15.3 7.0 %collective-permute-start.1 = (bf16[96,1664]{1,0:T(8,128)(2,1)S(1)}, bf16[96,1664]{1,0:T(8,128)(2,1)S(1)}, u32[]{:S(2)}, u32[]{:S(2)}) collective-permute-start(bf16[96,1664]{1,0:T(8,128)(2,1)S(1)} %get-tuple-element.75), channel_id=1, source_target_pairs={{0,3},{1,0},{2,1},{3,2},{4,7},{5,4},{6,5},{7,6},{8,11},{9,8},{10,9... | collective-permute-start | bytes 958472 | tf_op jit(solution)/shard_map/ppermute | solution.py:83
  22.3 6.3 %collective-permute-start.3 = (bf16[48,1664]{1,0:T(8,128)(2,1)S(1)}, bf16[48,1664]{1,0:T(8,128)(2,1)S(1)}, u32[]{:S(2)}, u32[]{:S(2)}) collective-permute-start(bf16[48,1664]{1,0:T(8,128)(2,1)S(1)} %slice.277), channel_id=1, source_target_pairs={{0,3},{1,0},{2,1},{3,2},{4,7},{5,4},{6,5},{7,6},{8,11},{9,8},{10,9... | collective-permute-start | bytes 479240 | tf_op jit(solution)/shard_map/ppermute | solution.py:83
  25.8 6.6 %collective-permute-start.2 = (bf16[48,1664]{1,0:T(8,128)(2,1)S(1)}, bf16[48,1664]{1,0:T(8,128)(2,1)S(1)}, u32[]{:S(2)}, u32[]{:S(2)}) collective-permute-start(bf16[48,1664]{1,0:T(8,128)(2,1)S(1)} %slice.276), channel_id=1, source_target_pairs={{0,1},{1,2},{2,3},{3,0},{4,5},{5,6},{6,7},{7,4},{8,9},{9,10},{10,1... | collective-permute-start | bytes 479240 | tf_op jit(solution)/shard_map/ppermute | solution.py:83
  33.7 20.0 %collective-permute-start.4 = (bf16[4,96,1664]{2,1,0:T(8,128)(2,1)}, bf16[4,96,1664]{2,1,0:T(8,128)(2,1)S(1)}, u32[]{:S(2)}, u32[]{:S(2)}) collective-permute-start(bf16[4,96,1664]{2,1,0:T(8,128)(2,1)} %pad_maximum_fusion.1), channel_id=1, source_target_pairs={{0,4},{1,5},{2,6},{3,7},{4,8},{5,9},{6,10},{7,11},{8,12},{9,13},{1... | collective-permute-start | bytes 3833864 | tf_op jit(solution)/shard_map/ppermute | solution.py:83
  35.2 18.5 %collective-permute-start.5 = (bf16[4,96,1664]{2,1,0:T(8,128)(2,1)}, bf16[4,96,1664]{2,1,0:T(8,128)(2,1)S(1)}, u32[]{:S(2)}, u32[]{:S(2)}) collective-permute-start(bf16[4,96,1664]{2,1,0:T(8,128)(2,1)} %pad_maximum_fusion.1), channel_id=1, source_target_pairs={{0,12},{1,13},{2,14},{3,15},{4,0},{5,1},{6,2},{7,3},{8,4},{9,5},{1... | collective-permute-start | bytes 3833864 | tf_op jit(solution)/shard_map/ppermute | solution.py:83
  54.9 1.7 %copy-start.1 = (bf16[8,96,1664]{2,1,0:T(8,128)(2,1)}, bf16[8,96,1664]{2,1,0:T(8,128)(2,1)S(1)}, u32[]{:S(2)}) copy-start(bf16[8,96,1664]{2,1,0:T(8,128)(2,1)S(1)} %pad_maximum_fusion) | copy-start | bytes 7667716
  80.7 11.8 %collective-permute-start.6 = (bf16[4,48,1664]{2,1,0:T(8,128)(2,1)}, bf16[4,48,1664]{2,1,0:T(8,128)(2,1)S(1)}, u32[]{:S(2)}, u32[]{:S(2)}) collective-permute-start(bf16[4,48,1664]{2,1,0:T(8,128)(2,1)} %slice.226), channel_id=1, source_target_pairs={{0,4},{1,5},{2,6},{3,7},{4,8},{5,9},{6,10},{7,11},{8,12},{9,13},{1... | collective-permute-start | bytes 1916936 | tf_op jit(solution)/shard_map/ppermute | solution.py:83
  82.0 10.7 %collective-permute-start.7 = (bf16[4,48,1664]{2,1,0:T(8,128)(2,1)}, bf16[4,48,1664]{2,1,0:T(8,128)(2,1)}, u32[]{:S(2)}, u32[]{:S(2)}) collective-permute-start(bf16[4,48,1664]{2,1,0:T(8,128)(2,1)} %slice.227), channel_id=1, source_target_pairs={{0,12},{1,13},{2,14},{3,15},{4,0},{5,1},{6,2},{7,3},{8,4},{9,5},{1... | collective-permute-start | bytes 1916936 | tf_op jit(solution)/shard_map/ppermute | solution.py:83
  94.7 5.8 %copy-start.3 = (bf16[4,96,1664]{2,1,0:T(8,128)(2,1)}, bf16[4,96,1664]{2,1,0:T(8,128)(2,1)S(1)}, u32[]{:S(2)}) copy-start(bf16[4,96,1664]{2,1,0:T(8,128)(2,1)S(1)} %pad_maximum_fusion.2) | copy-start | bytes 3833860
  100.6 13.7 %copy-start.2 = (f32[4,768]{0,1:T(8,128)S(1)}, f32[4,768]{0,1:T(8,128)}, u32[]{:S(2)}) copy-start(f32[4,768]{0,1:T(8,128)} %slice_bitcast_fusion) | copy-start | bytes 36868
  115.5 3.9 %collective-permute-start.8 = (f32[4,1536]{1,0:T(4,128)S(1)}, f32[4,1536]{1,0:T(4,128)S(1)}, u32[]{:S(2)}, u32[]{:S(2)}) collective-permute-start(f32[4,1536]{1,0:T(4,128)S(1)} %broadcast_select_fusion), channel_id=1, source_target_pairs={{0,1},{1,0},{2,3},{3,2},{4,5},{5,4},{6,7},{7,6},{8,9},{9,8},{10,11... | collective-permute-start | bytes 73736 | tf_op jit(solution)/shard_map/ppermute | solution.py:36
  119.5 5.4 %collective-permute-start.9 = (f32[4,1536]{1,0:T(4,128)S(1)}, f32[4,1536]{1,0:T(4,128)S(1)}, u32[]{:S(2)}, u32[]{:S(2)}) collective-permute-start(f32[4,1536]{1,0:T(4,128)S(1)} %pad_maximum_fusion.5), channel_id=1, source_target_pairs={{0,2},{1,3},{2,0},{3,1},{4,6},{5,7},{6,4},{7,5},{8,10},{9,11},{10,... | collective-permute-start | bytes 73736 | tf_op jit(solution)/shard_map/ppermute | solution.py:36
  125.1 3.9 %collective-permute-start.10 = (f32[4,1536]{1,0:T(4,128)S(1)}, f32[4,1536]{1,0:T(4,128)S(1)}, u32[]{:S(2)}, u32[]{:S(2)}) collective-permute-start(f32[4,1536]{1,0:T(4,128)S(1)} %pad_maximum_fusion.6), channel_id=1, source_target_pairs={{0,4},{1,5},{2,6},{3,7},{4,0},{5,1},{6,2},{7,3},{8,12},{9,13},{10,... | collective-permute-start | bytes 73736 | tf_op jit(solution)/shard_map/ppermute | solution.py:36
  129.1 5.4 %collective-permute-start.11 = (f32[4,1536]{1,0:T(4,128)S(1)}, f32[4,1536]{1,0:T(4,128)S(1)}, u32[]{:S(2)}, u32[]{:S(2)}) collective-permute-start(f32[4,1536]{1,0:T(4,128)S(1)} %pad_maximum_fusion.7), channel_id=1, source_target_pairs={{0,8},{1,9},{2,10},{3,11},{4,12},{5,13},{6,14},{7,15},{8,0},{9,1},... | collective-permute-start | bytes 73736 | tf_op jit(solution)/shard_map/ppermute | solution.py:36
  136.1 1.2 collective-permute-start.12
  136.3 12.3 %copy-start.5 = (f32[128]{0:T(128)}, f32[128]{0:T(128)S(1)}, u32[]{:S(2)}) copy-start(f32[128]{0:T(128)S(1)} %fusion.28) | copy-start | bytes 1540
  136.5 12.1 %copy-start.6 = (f32[128]{0:T(128)}, f32[128]{0:T(128)S(1)}, u32[]{:S(2)}) copy-start(f32[128]{0:T(128)S(1)} %fusion.27) | copy-start | bytes 1540
  136.7 12.0 %copy-start.4 = (f32[128]{0:T(128)}, f32[128]{0:T(128)S(1)}, u32[]{:S(2)}) copy-start(f32[128]{0:T(128)S(1)} %select_dynamic-update-slice_fusion) | copy-start | bytes 1540
  138.0 3.6 %collective-permute-start.13 = (f32[2]{0:T(128)S(1)}, f32[2]{0:T(128)S(1)}, u32[]{:S(2)}, u32[]{:S(2)}) collective-permute-start(f32[2]{0:T(128)S(1)} %fusion.19), channel_id=1, source_target_pairs={{0,32},{16,48},{32,0},{48,16},{64,96},{80,112},{96,64},{112,80},{1... | collective-permute-start | bytes 32 | tf_op jit(solution)/shard_map/ppermute | solution.py:36
  141.6 5.1 %collective-permute-start.14 = (f32[2]{0:T(128)S(1)}, f32[2]{0:T(128)S(1)}, u32[]{:S(2)}, u32[]{:S(2)}) collective-permute-start(f32[2]{0:T(128)S(1)} %fusion.18), channel_id=1, source_target_pairs={{0,64},{16,80},{32,96},{48,112},{64,0},{80,16},{96,32},{112,48},{1... | collective-permute-start | bytes 32 | tf_op jit(solution)/shard_map/ppermute | solution.py:36

commit v7 on v4

--- a/solution.py
+++ b/solution.py
@@ -110,29 +110,36 @@
     meansq = jnp.mean(values * values, axis=-1, keepdims=True)
     normed = (values * lax.rsqrt(meansq + 1e-05) * norm_gain).astype(jnp.bfloat16)
     ids = lax.dynamic_slice_in_dim(targets, start, LIVE, 0)
-    meta = jnp.zeros((LIVE, EXTRA), jnp.int32)
-    meta = meta.at[:, 0].set(ids // 256).at[:, 1].set(ids % 256).at[:, 2].set(live_count)
+    column = lax.broadcasted_iota(jnp.int32, (LIVE, EXTRA), 1)
+    meta = jnp.where(column == 0, ids[:, None] // 256, ids[:, None] % 256)
+    meta = jnp.where(column == 2, live_count, jnp.where(column < 2, meta, 0))
     own = jnp.concatenate([normed, meta.astype(jnp.bfloat16)], axis=1)
 
     stats = lambda block: block_stats(block, head, position)
+    count_of = lambda block: block[..., :1, width + 2].reshape(-1).astype(jnp.int32)
     left = shift(own, 0, 1, reqs, vocs)
     right = shift(own, 0, -1, reqs, vocs)
+    part_own = stats(own)
+    part_own, left, right = lax.optimization_barrier((part_own, left, right))
     far_a = shift(left[:HALF], 0, 1, reqs, vocs)
     far_b = shift(right[HALF:], 0, -1, reqs, vocs)
     far = jnp.concatenate([far_a, far_b])
     line = jnp.stack([own, left, right, far])
     line_left = shift(line, 1, 1, reqs, vocs)
     line_right = shift(line, 1, -1, reqs, vocs)
-    part_line = stats(line.reshape(-1, own.shape[1]))
+    part_near = stats(line[1:].reshape(-1, own.shape[1]))
+    part_near, line_left, line_right = lax.optimization_barrier((part_near, line_left, line_right))
     line_far_a = shift(line_left[:, :HALF], 1, 1, reqs, vocs)
     line_far_b = shift(line_right[:, HALF:], 1, -1, reqs, vocs)
     part_lines = stats(jnp.concatenate([line_left, line_right]).reshape(-1, own.shape[1]))
+    part_lines, line_far_a, line_far_b = lax.optimization_barrier((part_lines, line_far_a, line_far_b))
     line_far = jnp.concatenate([line_far_a, line_far_b], axis=1)
     part_line_far = stats(line_far.reshape(-1, own.shape[1]))
-    processed = jnp.concatenate([part_line, part_lines, part_line_far], axis=1)
+    processed = jnp.concatenate([part_own, part_near, part_lines, part_line_far], axis=1)
     processed = processed.reshape(4, vocs, LIVE)
-    blocks = jnp.concatenate([line, line_left, line_right, line_far])
-    processed_counts = blocks[:, 0, width + 2].astype(jnp.int32)
+    processed_counts = jnp.concatenate(
+        [count_of(line), count_of(line_left), count_of(line_right), count_of(line_far)]
+    )
 
     source = jnp.arange(vocs, dtype=jnp.int32)
     slot_of = jnp.array([0, 2, 3, 1], jnp.int32)

time: 134 us -> 133 us (level)
  waiting for transfers between devices: 29.8 us -> 38.8 us
  other arithmetic: 31.8 us -> 23.1 us
  matrix products: 25.7 us -> 33.1 us
  local copies, waits for them, and re-layouts: 16.9 us -> 12.1 us
  starting transfers between devices: 22 us -> 18.1 us
    ppermute x8, waiting for transfers between devices: 10.4 us -> 18 us  [shift(): return lax.ppermute(value, AXES, pairs)]
    dot_general x3 -> x4, matrix products: 25.7 us -> 33.1 us  [block_stats(): logits = jnp.dot(rows_in, head, preferred_element_type=jnp.float32)]
    another operation x5 -> x4, other arithmetic: 4.79 us -> 0.06 us  [block_stats(): return jnp.stack([top, total, weighted, picked])]
    unnamed x26 -> x19, local copies, waits for them, and re-layouts: 5.06 us -> 1.2 us
    reduce_sum x3 -> x4, other arithmetic: 15.2 us -> 12.1 us  [block_stats(): total = jnp.sum(expo, axis=-1)]
    slice x0 -> x4, local copies, waits for them, and re-layouts: none -> 2.84 us  [shards(): block[..., :1, width + 2].reshape(-1).astype(jnp.int32)]
    ppermute x8, starting transfers between devices: 14.3 us -> 11.8 us  [shift(): return lax.ppermute(value, AXES, pairs)]
    concatenate x1, local copies, waits for them, and re-layouts: 1.99 us -> 0.1 us  [shards(): jnp.concatenate([part_own, part_near, part_lines, part_line_far], axis=1)]
  transfers between devices with their start and end apart: 15 -> 15, of which waited for: 12 -> 14; matrix products, arithmetic and copies ran while one was open for 21% -> 19% of each run, Pallas kernels for 0% -> 0%
where the time goes in v7:
time: 133 us
  waiting for transfers between devices  38.8 us (29%)
  matrix products  33.1 us (25%)
  other arithmetic  23.1 us (17%)
  starting transfers between devices  18.1 us (14%)
  local copies, waits for them, and re-layouts  12.1 us (9%)
  between operations  7.59 us (6%)
    dot_general x4, matrix products, block_stats(): logits = jnp.dot(rows_in, head, preferred_element_type=jnp.float32)  33.1 us
    ppermute x7, waiting for transfers between devices, butterfly(): other = lax.ppermute(value, axis, [(i, i ^ step) for i in range(size)])  20.8 us
    ppermute x8, waiting for transfers between devices, shift(): return lax.ppermute(value, AXES, pairs)  18 us
    reduce_sum x4, other arithmetic, block_stats(): total = jnp.sum(expo, axis=-1)  12.1 us
    ppermute x8, starting transfers between devices, shift(): return lax.ppermute(value, AXES, pairs)  11.8 us
    ppermute x7, starting transfers between devices, butterfly(): other = lax.ppermute(value, axis, [(i, i ^ step) for i in range(size)])  6.3 us
    slice x4, local copies, waits for them, and re-layouts, shards(): block[..., :1, width + 2].reshape(-1).astype(jnp.int32)  2.84 us
  transfers between devices with their start and end apart: 15, of which 14 were waited for; matrix products, arithmetic and copies ran while one was open for 19% of the time, Pallas kernels for 0%

profile of v7, /device:TPU:0, one launch (start us, length us, event | category | flops | bytes accessed | tf_op | source)
XLA Modules:
  0.0 132.8 jit_solution(1196854831109875048)
XLA Ops:
  0.7 1.3 fusion.46
  5.2 1.2 fusion.10
  6.4 0.7 and_select_fusion.1
  7.1 1.1 fusion.12
  8.3 0.1 select_convert_fusion
  8.4 4.2 %collective-permute-start.1 = (bf16[96,1664]{1,0:T(8,128)(2,1)S(1)}, bf16[96,1664]{1,0:T(8,128)(2,1)S(1)}, u32[]{:S(2)}, u32[]{:S(2)}) collective-permute-start(bf16[96,1664]{1,0:T(8,128)(2,1)S(1)} %get-tuple-element.59), channel_id=1, source_target_pairs={{0,3},{1,0},{2,1},{3,2},{4,7},{5,4},{6,5},{7,6},{8,11},{9,8},{10,9... | collective-permute-start | bytes 958472 | tf_op jit(solution)/shard_map/ppermute | solution.py:79
  12.7 5.4 %fusion.47 = (f32[96]{0:T(128)S(1)}, f32[96,3072]{1,0:T(8,128)S(1)}) fusion(bf16[96,1536]{1,0:T(8,128)(2,1)S(1)} %fusion.12, bf16[1536,3072]{1,0:T(8,128)(2,1)} %param.8), kind=kOutput, calls=%fused_computation.190 | convolution fusion | flops 906264448 | bytes 10912128 | tf_op jit(solution)/shard_map/dot_general | solution.py:89
  18.1 0.2 fusion.14
  18.4 0.7 gather_fusion
  19.0 0.7 gather_fusion.1
  19.7 0.5 fusion.7
  20.2 0.6 collective-permute-done
  20.9 2.7 %collective-permute-start.3 = (bf16[48,1664]{1,0:T(8,128)(2,1)S(1)}, bf16[48,1664]{1,0:T(8,128)(2,1)S(1)}, u32[]{:S(2)}, u32[]{:S(2)}) collective-permute-start(bf16[48,1664]{1,0:T(8,128)(2,1)S(1)} %slice.193), channel_id=1, source_target_pairs={{0,3},{1,0},{2,1},{3,2},{4,7},{5,4},{6,5},{7,6},{8,11},{9,8},{10,9... | collective-permute-start | bytes 479240 | tf_op jit(solution)/shard_map/ppermute | solution.py:79
  23.6 2.8 %collective-permute-done.3 = bf16[48,1664]{1,0:T(8,128)(2,1)S(1)} collective-permute-done((bf16[48,1664]{1,0:T(8,128)(2,1)S(1)}, bf16[48,1664]{1,0:T(8,128)(2,1)S(1)}, u32[]{:S(2)}, u32[]{:S(2)}) %collective-permute-start.3) | collective-permute-done | bytes 159776 | tf_op jit(solution)/shard_map/ppermute | solution.py:79
  26.4 3.7 %collective-permute-done.2 = bf16[48,1664]{1,0:T(8,128)(2,1)S(1)} collective-permute-done((bf16[48,1664]{1,0:T(8,128)(2,1)S(1)}, bf16[48,1664]{1,0:T(8,128)(2,1)S(1)}, u32[]{:S(2)}, u32[]{:S(2)}) %collective-permute-start.2) | collective-permute-done | bytes 159776 | tf_op jit(solution)/shard_map/ppermute | solution.py:79
  30.1 0.1 pad_maximum_fusion.3
  30.2 1.2 pad_maximum_fusion.1
  31.5 2.8 %collective-permute-start.5 = (bf16[4,96,1664]{2,1,0:T(8,128)(2,1)}, bf16[4,96,1664]{2,1,0:T(8,128)(2,1)}, u32[]{:S(2)}, u32[]{:S(2)}) collective-permute-start(bf16[4,96,1664]{2,1,0:T(8,128)(2,1)} %pad_maximum_fusion.1), channel_id=1, source_target_pairs={{0,12},{1,13},{2,14},{3,15},{4,0},{5,1},{6,2},{7,3},{8,4},{9,5},{1... | collective-permute-start | bytes 3833864 | tf_op jit(solution)/shard_map/ppermute | solution.py:79
  34.2 5.6 %fusion.48 = (f32[288]{0:T(512)S(1)}, f32[288,3072]{1,0:T(8,128)S(1)}) fusion(bf16[1536,3072]{1,0:T(8,128)(2,1)} %param.8, bf16[288,1664]{1,0:T(8,128)(2,1)S(1)} %bitcast.43), kind=kOutput, calls=%fused_computation.191 | convolution fusion | flops 2718793472 | bytes 13862016 | tf_op jit(solution)/shard_map/dot_general | solution.py:89
  39.9 0.6 slice.258
  40.5 1.0 copy.18
  41.5 1.3 %fusion.2 = (f32[288]{0:T(512)S(1)}, f32[288]{0:T(512)S(1)}, f32[288]{0:T(512)S(1)}) fusion(f32[288,3072]{1,0:T(8,128)S(1)} %get-tuple-element.83, f32[288]{0:T(512)S(1)} %get-tuple-element.82, s32[288]{0:T(512)S(1)} %fusion.26), kind=kLoop, calls=%fused_computation.18 | loop fusion | flops 6192288 | bytes 3544704 | tf_op jit(solution)/shard_map/reduce_sum | solution.py:92
  42.9 0.9 slice_reduce_fusion.6
  43.8 5.5 %collective-permute-done.5 = bf16[4,96,1664]{2,1,0:T(8,128)(2,1)} collective-permute-done((bf16[4,96,1664]{2,1,0:T(8,128)(2,1)}, bf16[4,96,1664]{2,1,0:T(8,128)(2,1)}, u32[]{:S(2)}, u32[]{:S(2)}) %collective-permute-start.5) | collective-permute-done | bytes 1277984 | tf_op jit(solution)/shard_map/ppermute | solution.py:79
  49.3 3.7 %collective-permute-done.4 = bf16[4,96,1664]{2,1,0:T(8,128)(2,1)} collective-permute-done((bf16[4,96,1664]{2,1,0:T(8,128)(2,1)}, bf16[4,96,1664]{2,1,0:T(8,128)(2,1)}, u32[]{:S(2)}, u32[]{:S(2)}) %collective-permute-start.4) | collective-permute-done | bytes 1277984 | tf_op jit(solution)/shard_map/ppermute | solution.py:79
  53.0 1.1 slice.202
  54.1 1.1 slice.203
  55.3 1.9 %pad_maximum_fusion = bf16[8,96,1664]{2,1,0:T(8,128)(2,1)S(1)} fusion(bf16[4,96,1664]{2,1,0:T(8,128)(2,1)} %collective-permute-done.5, bf16[4,96,1664]{2,1,0:T(8,128)(2,1)} %collective-permute-done.4), kind=kLoop, calls=%fused_computation.19 | loop fusion | flops 1277952 | bytes 5111808 | tf_op jit(solution)/shard_map/concatenate | solution.py:134
  57.3 12.3 %fusion.49 = (f32[768]{0:T(1024)S(1)}, f32[768,3072]{1,0:T(8,128)}) fusion(bf16[1536,3072]{1,0:T(8,128)(2,1)} %param.8, bf16[768,1664]{1,0:T(8,128)(2,1)S(1)} %bitcast.36), kind=kOutput, calls=%fused_computation.192 | convolution fusion | flops 7250115584 | bytes 21236736 | tf_op jit(solution)/shard_map/dot_general | solution.py:89
  69.6 0.1 copy.19
  69.8 2.0 %collective-permute-start.6 = (bf16[4,48,1664]{2,1,0:T(8,128)(2,1)S(1)}, bf16[4,48,1664]{2,1,0:T(8,128)(2,1)S(1)}, u32[]{:S(2)}, u32[]{:S(2)}) collective-permute-start(bf16[4,48,1664]{2,1,0:T(8,128)(2,1)S(1)} %slice.202), channel_id=1, source_target_pairs={{0,4},{1,5},{2,6},{3,7},{4,8},{5,9},{6,10},{7,11},{8,12},{9,13},{1... | collective-permute-start | bytes 1916936 | tf_op jit(solution)/shard_map/ppermute | solution.py:79
  71.9 6.3 %fusion = (f32[768]{0:T(1024)S(1)}, f32[768]{0:T(1024)S(1)}, f32[768]{0:T(1024)S(1)}) fusion(f32[768,3072]{1,0:T(8,128)} %get-tuple-element.85, f32[768]{0:T(1024)S(1)} %get-tuple-element.84, s32[768]{0:T(1024)S(1)} %fusion.23), kind=kLoop, calls=%fused_computation.8 | loop fusion | flops 16512768 | bytes 9452544 | tf_op jit(solution)/shard_map/reduce_sum | solution.py:92
  78.2 0.9 slice_reduce_fusion.9
  79.1 0.9 slice_reduce_fusion.8
  80.0 0.2 collective-permute-done.7
  80.2 1.5 %collective-permute-done.6 = bf16[4,48,1664]{2,1,0:T(8,128)(2,1)S(1)} collective-permute-done((bf16[4,48,1664]{2,1,0:T(8,128)(2,1)S(1)}, bf16[4,48,1664]{2,1,0:T(8,128)(2,1)S(1)}, u32[]{:S(2)}, u32[]{:S(2)}) %collective-permute-start.6) | collective-permute-done | bytes 639008 | tf_op jit(solution)/shard_map/ppermute | solution.py:79
  81.7 0.2 slice_reduce_fusion.7
  81.9 0.1 pad_maximum_fusion.2
  82.0 9.8 %fusion.50 = (f32[384]{0:T(512)S(1)}, f32[384,3072]{1,0:T(8,128)}) fusion(bf16[1536,3072]{1,0:T(8,128)(2,1)} %param.8, bf16[384,1664]{1,0:T(8,128)(2,1)S(1)} %bitcast.42), kind=kOutput, calls=%fused_computation.193 | convolution fusion | flops 3625057792 | bytes 15336960 | tf_op jit(solution)/shard_map/dot_general | solution.py:89
  91.9 0.7 gather_fusion.3
  92.6 0.6 fusion.43
  93.3 0.1 broadcast_in_dim.82
  93.5 4.0 %fusion.1 = (f32[384]{0:T(512)S(1)}, f32[384]{0:T(512)S(1)}, f32[384]{0:T(512)S(1)}) fusion(f32[384,3072]{1,0:T(8,128)} %get-tuple-element.87, f32[384]{0:T(512)S(1)} %get-tuple-element.86, s32[384]{0:T(512)S(1)} %fusion.27), kind=kLoop, calls=%fused_computation.13 | loop fusion | flops 8256384 | bytes 4726272 | tf_op jit(solution)/shard_map/reduce_sum | solution.py:92
  97.6 0.1 concatenate.26
  97.8 0.6 gather_fusion.2
  98.4 0.1 gather.19
  98.6 3.8 %collective-permute-done.8 = f32[4,1536]{1,0:T(4,128)S(1)} collective-permute-done((f32[4,1536]{1,0:T(4,128)S(1)}, f32[4,1536]{1,0:T(4,128)S(1)}, u32[]{:S(2)}, u32[]{:S(2)}) %collective-permute-start.8) | collective-permute-done | bytes 24608 | tf_op jit(solution)/shard_map/ppermute | solution.py:32
  102.6 5.3 %collective-permute-done.9 = f32[4,1536]{1,0:T(4,128)S(1)} collective-permute-done((f32[4,1536]{1,0:T(4,128)S(1)}, f32[4,1536]{1,0:T(4,128)S(1)}, u32[]{:S(2)}, u32[]{:S(2)}) %collective-permute-start.9) | collective-permute-done | bytes 24608 | tf_op jit(solution)/shard_map/ppermute | solution.py:32
  108.1 0.6 collective-permute-start.10
  108.7 3.3 %collective-permute-done.10 = f32[4,1536]{1,0:T(4,128)S(1)} collective-permute-done((f32[4,1536]{1,0:T(4,128)S(1)}, f32[4,1536]{1,0:T(4,128)S(1)}, u32[]{:S(2)}, u32[]{:S(2)}) %collective-permute-start.10) | collective-permute-done | bytes 24608 | tf_op jit(solution)/shard_map/ppermute | solution.py:32
  112.2 0.7 collective-permute-start.11
  113.6 3.9 %collective-permute-done.11 = f32[4,1536]{1,0:T(4,128)S(1)} collective-permute-done((f32[4,1536]{1,0:T(4,128)S(1)}, f32[4,1536]{1,0:T(4,128)S(1)}, u32[]{:S(2)}, u32[]{:S(2)}) %collective-permute-start.11) | collective-permute-done | bytes 24608 | tf_op jit(solution)/shard_map/ppermute | solution.py:32
  117.6 0.8 select_reduce_fusion.4
  118.4 0.7 pad_maximum_fusion.12
  119.1 0.2 fusion.41
  119.3 0.2 fusion.40
  119.5 0.2 select_dynamic-update-slice_fusion
  119.7 0.6 collective-permute-done.12
  120.3 0.7 fusion.32
  121.0 1.6 %collective-permute-start.13 = (f32[2]{0:T(128)S(1)}, f32[2]{0:T(128)S(1)}, u32[]{:S(2)}, u32[]{:S(2)}) collective-permute-start(f32[2]{0:T(128)S(1)} %fusion.32), channel_id=1, source_target_pairs={{0,32},{16,48},{32,0},{48,16},{64,96},{80,112},{96,64},{112,80},{1... | collective-permute-start | bytes 32 | tf_op jit(solution)/shard_map/ppermute | solution.py:32
  122.6 2.0 %collective-permute-done.13 = f32[2]{0:T(128)S(1)} collective-permute-done((f32[2]{0:T(128)S(1)}, f32[2]{0:T(128)S(1)}, u32[]{:S(2)}, u32[]{:S(2)}) %collective-permute-start.13) | collective-permute-done | bytes 40 | tf_op jit(solution)/shard_map/ppermute | solution.py:32
  124.6 3.2 %collective-permute-start.14 = (f32[2]{0:T(128)S(1)}, f32[2]{0:T(128)S(1)}, u32[]{:S(2)}, u32[]{:S(2)}) collective-permute-start(f32[2]{0:T(128)S(1)} %fusion.31), channel_id=1, source_target_pairs={{0,64},{16,80},{32,96},{48,112},{64,0},{80,16},{96,32},{112,48},{1... | collective-permute-start | bytes 32 | tf_op jit(solution)/shard_map/ppermute | solution.py:32
  127.8 1.9 %collective-permute-done.14 = f32[2]{0:T(128)S(1)} collective-permute-done((f32[2]{0:T(128)S(1)}, f32[2]{0:T(128)S(1)}, u32[]{:S(2)}, u32[]{:S(2)}) %collective-permute-start.14) | collective-permute-done | bytes 40 | tf_op jit(solution)/shard_map/ppermute | solution.py:32
  129.6 0.6 fusion.45
  (90 shorter events, 1.7 us)
Async XLA Ops:
  8.4 11.8 %collective-permute-start.1 = (bf16[96,1664]{1,0:T(8,128)(2,1)S(1)}, bf16[96,1664]{1,0:T(8,128)(2,1)S(1)}, u32[]{:S(2)}, u32[]{:S(2)}) collective-permute-start(bf16[96,1664]{1,0:T(8,128)(2,1)S(1)} %get-tuple-element.59), channel_id=1, source_target_pairs={{0,3},{1,0},{2,1},{3,2},{4,7},{5,4},{6,5},{7,6},{8,11},{9,8},{10,9... | collective-permute-start | bytes 958472 | tf_op jit(solution)/shard_map/ppermute | solution.py:79
  12.7 8.2 %collective-permute-start = (bf16[96,1664]{1,0:T(8,128)(2,1)S(1)}, bf16[96,1664]{1,0:T(8,128)(2,1)S(1)}, u32[]{:S(2)}, u32[]{:S(2)}) collective-permute-start(bf16[96,1664]{1,0:T(8,128)(2,1)S(1)} %get-tuple-element.59), channel_id=1, source_target_pairs={{0,1},{1,2},{2,3},{3,0},{4,5},{5,6},{6,7},{7,4},{8,9},{9,10},{10,1... | collective-permute-start | bytes 958472 | tf_op jit(solution)/shard_map/ppermute | solution.py:79
  12.7 5.6 %copy-start = (s32[4]{0:T(128)S(1)}, s32[4]{0:T(128)}, u32[]{:S(2)}) copy-start(s32[4]{0:T(128)} %constant.170.clone) | copy-start | bytes 52
  19.0 12.5 %copy-start.1 = (s32[16]{0:T(128)}, s32[16]{0:T(128)S(1)}, u32[]{:S(2)}) copy-start(s32[16]{0:T(128)S(1)} %gather_fusion) | copy-start | bytes 196
  19.7 11.8 %copy-start.3 = (s32[16]{0:T(128)}, s32[16]{0:T(128)S(1)}, u32[]{:S(2)}) copy-start(s32[16]{0:T(128)S(1)} %gather_fusion.1) | copy-start | bytes 196
  20.9 5.5 %collective-permute-start.3 = (bf16[48,1664]{1,0:T(8,128)(2,1)S(1)}, bf16[48,1664]{1,0:T(8,128)(2,1)S(1)}, u32[]{:S(2)}, u32[]{:S(2)}) collective-permute-start(bf16[48,1664]{1,0:T(8,128)(2,1)S(1)} %slice.193), channel_id=1, source_target_pairs={{0,3},{1,0},{2,1},{3,2},{4,7},{5,4},{6,5},{7,6},{8,11},{9,8},{10,9... | collective-permute-start | bytes 479240 | tf_op jit(solution)/shard_map/ppermute | solution.py:79
  23.6 6.5 %collective-permute-start.2 = (bf16[48,1664]{1,0:T(8,128)(2,1)S(1)}, bf16[48,1664]{1,0:T(8,128)(2,1)S(1)}, u32[]{:S(2)}, u32[]{:S(2)}) collective-permute-start(bf16[48,1664]{1,0:T(8,128)(2,1)S(1)} %slice.192), channel_id=1, source_target_pairs={{0,1},{1,2},{2,3},{3,0},{4,5},{5,6},{6,7},{7,4},{8,9},{9,10},{10,1... | collective-permute-start | bytes 479240 | tf_op jit(solution)/shard_map/ppermute | solution.py:79
  31.5 17.9 %collective-permute-start.5 = (bf16[4,96,1664]{2,1,0:T(8,128)(2,1)}, bf16[4,96,1664]{2,1,0:T(8,128)(2,1)}, u32[]{:S(2)}, u32[]{:S(2)}) collective-permute-start(bf16[4,96,1664]{2,1,0:T(8,128)(2,1)} %pad_maximum_fusion.1), channel_id=1, source_target_pairs={{0,12},{1,13},{2,14},{3,15},{4,0},{5,1},{6,2},{7,3},{8,4},{9,5},{1... | collective-permute-start | bytes 3833864 | tf_op jit(solution)/shard_map/ppermute | solution.py:79
  34.2 18.8 %collective-permute-start.4 = (bf16[4,96,1664]{2,1,0:T(8,128)(2,1)}, bf16[4,96,1664]{2,1,0:T(8,128)(2,1)}, u32[]{:S(2)}, u32[]{:S(2)}) collective-permute-start(bf16[4,96,1664]{2,1,0:T(8,128)(2,1)} %pad_maximum_fusion.1), channel_id=1, source_target_pairs={{0,4},{1,5},{2,6},{3,7},{4,8},{5,9},{6,10},{7,11},{8,12},{9,13},{1... | collective-permute-start | bytes 3833864 | tf_op jit(solution)/shard_map/ppermute | solution.py:79
  69.8 10.5 %collective-permute-start.7 = (bf16[4,48,1664]{2,1,0:T(8,128)(2,1)S(1)}, bf16[4,48,1664]{2,1,0:T(8,128)(2,1)S(1)}, u32[]{:S(2)}, u32[]{:S(2)}) collective-permute-start(bf16[4,48,1664]{2,1,0:T(8,128)(2,1)S(1)} %slice.203), channel_id=1, source_target_pairs={{0,12},{1,13},{2,14},{3,15},{4,0},{5,1},{6,2},{7,3},{8,4},{9,5},{1... | collective-permute-start | bytes 1916936 | tf_op jit(solution)/shard_map/ppermute | solution.py:79
  69.8 11.9 %collective-permute-start.6 = (bf16[4,48,1664]{2,1,0:T(8,128)(2,1)S(1)}, bf16[4,48,1664]{2,1,0:T(8,128)(2,1)S(1)}, u32[]{:S(2)}, u32[]{:S(2)}) collective-permute-start(bf16[4,48,1664]{2,1,0:T(8,128)(2,1)S(1)} %slice.202), channel_id=1, source_target_pairs={{0,4},{1,5},{2,6},{3,7},{4,8},{5,9},{6,10},{7,11},{8,12},{9,13},{1... | collective-permute-start | bytes 1916936 | tf_op jit(solution)/shard_map/ppermute | solution.py:79
  82.0 10.5 %copy-start.2 = (s32[16]{0:T(128)S(1)}, s32[16]{0:T(128)}, u32[]{:S(2)}) copy-start(s32[16]{0:T(128)} %copy-done.1) | copy-start | bytes 196
  82.0 10.5 %copy-start.4 = (s32[16]{0:T(128)S(1)}, s32[16]{0:T(128)}, u32[]{:S(2)}) copy-start(s32[16]{0:T(128)} %copy-done.3) | copy-start | bytes 196
  98.5 3.9 %collective-permute-start.8 = (f32[4,1536]{1,0:T(4,128)S(1)}, f32[4,1536]{1,0:T(4,128)S(1)}, u32[]{:S(2)}, u32[]{:S(2)}) collective-permute-start(f32[4,1536]{1,0:T(4,128)S(1)} %broadcast_select_fusion), channel_id=1, source_target_pairs={{0,1},{1,0},{2,3},{3,2},{4,5},{5,4},{6,7},{7,6},{8,9},{9,8},{10,11... | collective-permute-start | bytes 73736 | tf_op jit(solution)/shard_map/ppermute | solution.py:32
  102.5 5.4 %collective-permute-start.9 = (f32[4,1536]{1,0:T(4,128)S(1)}, f32[4,1536]{1,0:T(4,128)S(1)}, u32[]{:S(2)}, u32[]{:S(2)}) collective-permute-start(f32[4,1536]{1,0:T(4,128)S(1)} %pad_maximum_fusion.5), channel_id=1, source_target_pairs={{0,2},{1,3},{2,0},{3,1},{4,6},{5,7},{6,4},{7,5},{8,10},{9,11},{10,... | collective-permute-start | bytes 73736 | tf_op jit(solution)/shard_map/ppermute | solution.py:32
  108.1 3.9 %collective-permute-start.10 = (f32[4,1536]{1,0:T(4,128)S(1)}, f32[4,1536]{1,0:T(4,128)S(1)}, u32[]{:S(2)}, u32[]{:S(2)}) collective-permute-start(f32[4,1536]{1,0:T(4,128)S(1)} %pad_maximum_fusion.6), channel_id=1, source_target_pairs={{0,4},{1,5},{2,6},{3,7},{4,0},{5,1},{6,2},{7,3},{8,12},{9,13},{10,... | collective-permute-start | bytes 73736 | tf_op jit(solution)/shard_map/ppermute | solution.py:32
  112.2 5.4 %collective-permute-start.11 = (f32[4,1536]{1,0:T(4,128)S(1)}, f32[4,1536]{1,0:T(4,128)S(1)}, u32[]{:S(2)}, u32[]{:S(2)}) collective-permute-start(f32[4,1536]{1,0:T(4,128)S(1)} %pad_maximum_fusion.7), channel_id=1, source_target_pairs={{0,8},{1,9},{2,10},{3,11},{4,12},{5,13},{6,14},{7,15},{8,0},{9,1},... | collective-permute-start | bytes 73736 | tf_op jit(solution)/shard_map/ppermute | solution.py:32
  119.1 1.2 collective-permute-start.12
  119.3 12.3 %copy-start.6 = (f32[128]{0:T(128)}, f32[128]{0:T(128)S(1)}, u32[]{:S(2)}) copy-start(f32[128]{0:T(128)S(1)} %fusion.41) | copy-start | bytes 1540
  119.5 12.1 %copy-start.7 = (f32[128]{0:T(128)}, f32[128]{0:T(128)S(1)}, u32[]{:S(2)}) copy-start(f32[128]{0:T(128)S(1)} %fusion.40) | copy-start | bytes 1540
  119.7 12.0 %copy-start.5 = (f32[128]{0:T(128)}, f32[128]{0:T(128)S(1)}, u32[]{:S(2)}) copy-start(f32[128]{0:T(128)S(1)} %select_dynamic-update-slice_fusion) | copy-start | bytes 1540
  121.0 3.6 %collective-permute-start.13 = (f32[2]{0:T(128)S(1)}, f32[2]{0:T(128)S(1)}, u32[]{:S(2)}, u32[]{:S(2)}) collective-permute-start(f32[2]{0:T(128)S(1)} %fusion.32), channel_id=1, source_target_pairs={{0,32},{16,48},{32,0},{48,16},{64,96},{80,112},{96,64},{112,80},{1... | collective-permute-start | bytes 32 | tf_op jit(solution)/shard_map/ppermute | solution.py:32
  124.6 5.1 %collective-permute-start.14 = (f32[2]{0:T(128)S(1)}, f32[2]{0:T(128)S(1)}, u32[]{:S(2)}, u32[]{:S(2)}) collective-permute-start(f32[2]{0:T(128)S(1)} %fusion.31), channel_id=1, source_target_pairs={{0,64},{16,80},{32,96},{48,112},{64,0},{80,16},{96,32},{112,48},{1... | collective-permute-start | bytes 32 | tf_op jit(solution)/shard_map/ppermute | solution.py:32

commit v8 on v7

--- a/solution.py
+++ b/solution.py
@@ -116,27 +116,25 @@
     own = jnp.concatenate([normed, meta.astype(jnp.bfloat16)], axis=1)
 
     stats = lambda block: block_stats(block, head, position)
-    count_of = lambda block: block[..., :1, width + 2].reshape(-1).astype(jnp.int32)
     left = shift(own, 0, 1, reqs, vocs)
     right = shift(own, 0, -1, reqs, vocs)
     part_own = stats(own)
-    part_own, left, right = lax.optimization_barrier((part_own, left, right))
     far_a = shift(left[:HALF], 0, 1, reqs, vocs)
     far_b = shift(right[HALF:], 0, -1, reqs, vocs)
+    part_near = stats(jnp.concatenate([left, right]))
     far = jnp.concatenate([far_a, far_b])
     line = jnp.stack([own, left, right, far])
     line_left = shift(line, 1, 1, reqs, vocs)
     line_right = shift(line, 1, -1, reqs, vocs)
-    part_near = stats(line[1:].reshape(-1, own.shape[1]))
-    part_near, line_left, line_right = lax.optimization_barrier((part_near, line_left, line_right))
+    part_far = stats(far)
     line_far_a = shift(line_left[:, :HALF], 1, 1, reqs, vocs)
     line_far_b = shift(line_right[:, HALF:], 1, -1, reqs, vocs)
     part_lines = stats(jnp.concatenate([line_left, line_right]).reshape(-1, own.shape[1]))
-    part_lines, line_far_a, line_far_b = lax.optimization_barrier((part_lines, line_far_a, line_far_b))
     line_far = jnp.concatenate([line_far_a, line_far_b], axis=1)
     part_line_far = stats(line_far.reshape(-1, own.shape[1]))
-    processed = jnp.concatenate([part_own, part_near, part_lines, part_line_far], axis=1)
+    processed = jnp.concatenate([part_own, part_near, part_far, part_lines, part_line_far], axis=1)
     processed = processed.reshape(4, vocs, LIVE)
+    count_of = lambda block: block[..., :1, width + 2].reshape(-1).astype(jnp.int32)
     processed_counts = jnp.concatenate(
         [count_of(line), count_of(line_left), count_of(line_right), count_of(line_far)]
     )

time: 133 us -> 130 us (0.977)
  waiting for transfers between devices: 38.8 us -> 43.9 us
  matrix products: 33.1 us -> 29.4 us
  local copies, waits for them, and re-layouts: 12.1 us -> 8.82 us
  other arithmetic: 23.1 us -> 20.8 us
    ppermute x8, waiting for transfers between devices: 18 us -> 23.6 us  [shift(): return lax.ppermute(value, AXES, pairs)]
    dot_general x4 -> x5, matrix products: 33.1 us -> 29.4 us  [block_stats(): logits = jnp.dot(rows_in, head, preferred_element_type=jnp.float32)]
    concatenate x1, other arithmetic: 1.95 us -> 0.26 us  [shards(): jnp.concatenate([line_left, line_right]).reshape(-1, own.shape[1])]
    slice x4, local copies, waits for them, and re-layouts: 2.84 us -> 1.43 us  [shards(): block[..., :1, width + 2].reshape(-1).astype(jnp.int32)]
    reduce_sum x4 -> x5, other arithmetic: 12.1 us -> 12.3 us  [block_stats(): total = jnp.sum(expo, axis=-1)]
  transfers between devices with their start and end apart: 15 -> 15, of which waited for: 14 -> 12; matrix products, arithmetic and copies ran while one was open for 19% -> 16% of each run, Pallas kernels for 0% -> 0%
where the time goes in v8:
time: 130 us
  waiting for transfers between devices  43.9 us (34%)
  matrix products  29.4 us (23%)
  other arithmetic  20.8 us (16%)
  starting transfers between devices  19.3 us (15%)
  local copies, waits for them, and re-layouts  8.82 us (7%)
  between operations  7.62 us (6%)
    dot_general x5, matrix products, block_stats(): logits = jnp.dot(rows_in, head, preferred_element_type=jnp.float32)  29.4 us
    ppermute x8, waiting for transfers between devices, shift(): return lax.ppermute(value, AXES, pairs)  23.6 us
    ppermute x7, waiting for transfers between devices, butterfly(): other = lax.ppermute(value, axis, [(i, i ^ step) for i in range(size)])  20.2 us
    reduce_sum x5, other arithmetic, block_stats(): total = jnp.sum(expo, axis=-1)  12.3 us
    ppermute x8, starting transfers between devices, shift(): return lax.ppermute(value, AXES, pairs)  12.2 us
    ppermute x7, starting transfers between devices, butterfly(): other = lax.ppermute(value, axis, [(i, i ^ step) for i in range(size)])  7.03 us
  transfers between devices with their start and end apart: 15, of which 12 were waited for; matrix products, arithmetic and copies ran while one was open for 16% of the time, Pallas kernels for 0%

profile of v8, /device:TPU:0, one launch (start us, length us, event | category | flops | bytes accessed | tf_op | source)
XLA Modules:
  0.0 129.8 jit_solution(8041981377583558609)
XLA Ops:
  0.7 1.3 %fusion.51 = (s32[1,1]{1,0:T(1,128)}, s32[1,1]{1,0:T(1,128)}) fusion(s32[1,2]{1,0:T(1,128)} %param.10), kind=kLoop, calls=%fused_computation.205 | loop fusion | bytes 16 | tf_op jit(solution)/shard_map/slice | solution.py:106
  5.2 1.2 fusion.9
  6.4 0.7 and_select_fusion.1
  7.2 1.1 fusion.11
  8.3 0.1 select_convert_fusion
  8.4 4.2 %collective-permute-start.1 = (bf16[96,1664]{1,0:T(8,128)(2,1)S(1)}, bf16[96,1664]{1,0:T(8,128)(2,1)S(1)}, u32[]{:S(2)}, u32[]{:S(2)}) collective-permute-start(bf16[96,1664]{1,0:T(8,128)(2,1)S(1)} %get-tuple-element.44), channel_id=1, source_target_pairs={{0,3},{1,0},{2,1},{3,2},{4,7},{5,4},{6,5},{7,6},{8,11},{9,8},{10,9... | collective-permute-start | bytes 958472 | tf_op jit(solution)/shard_map/ppermute | solution.py:79
  12.7 0.7 gather_fusion
  13.4 0.7 gather_fusion.1
  14.1 5.6 %fusion.52 = (f32[96]{0:T(128)S(1)}, f32[96,3072]{1,0:T(8,128)S(1)}) fusion(bf16[96,1536]{1,0:T(8,128)(2,1)S(1)} %fusion.11, bf16[1536,3072]{1,0:T(8,128)(2,1)} %param.8), kind=kOutput, calls=%fused_computation.206 | convolution fusion | flops 906264448 | bytes 10912128 | tf_op jit(solution)/shard_map/dot_general | solution.py:89
  19.8 0.2 fusion.21
  19.9 0.5 fusion.8
  20.5 0.4 collective-permute-done
  21.0 2.1 %fusion.53 = (f32[192]{0:T(256)S(1)}, f32[192,3072]{1,0:T(8,128)S(1)}) fusion(bf16[1536,3072]{1,0:T(8,128)(2,1)S(1)} %bitcast.43, bf16[192,1664]{1,0:T(8,128)(2,1)S(1)} %constant_dynamic-update-slice_fusion), kind=kOutput, calls=%fused_computation.207 | convolution fusion | flops 1812528896 | bytes 12387072 | tf_op jit(solution)/shard_map/dot_general | solution.py:89
  23.1 2.9 %collective-permute-start.3 = (bf16[48,1664]{1,0:T(8,128)(2,1)S(1)}, bf16[48,1664]{1,0:T(8,128)(2,1)S(1)}, u32[]{:S(2)}, u32[]{:S(2)}) collective-permute-start(bf16[48,1664]{1,0:T(8,128)(2,1)S(1)} %slice.276), channel_id=1, source_target_pairs={{0,3},{1,0},{2,1},{3,2},{4,7},{5,4},{6,5},{7,6},{8,11},{9,8},{10,9... | collective-permute-start | bytes 479240 | tf_op jit(solution)/shard_map/ppermute | solution.py:79
  26.2 0.2 fusion.17
  26.4 1.0 fusion.4
  27.4 5.2 %collective-permute-done.2 = bf16[48,1664]{1,0:T(8,128)(2,1)S(1)} collective-permute-done((bf16[48,1664]{1,0:T(8,128)(2,1)S(1)}, bf16[48,1664]{1,0:T(8,128)(2,1)S(1)}, u32[]{:S(2)}, u32[]{:S(2)}) %collective-permute-start.2) | collective-permute-done | bytes 159776 | tf_op jit(solution)/shard_map/ppermute | solution.py:79
  32.7 0.2 pad_maximum_fusion.1
  32.9 2.8 %collective-permute-start.5 = (bf16[4,96,1664]{2,1,0:T(8,128)(2,1)S(1)}, bf16[4,96,1664]{2,1,0:T(8,128)(2,1)S(1)}, u32[]{:S(2)}, u32[]{:S(2)}) collective-permute-start(bf16[4,96,1664]{2,1,0:T(8,128)(2,1)S(1)} %pad_maximum_fusion.1), channel_id=1, source_target_pairs={{0,12},{1,13},{2,14},{3,15},{4,0},{5,1},{6,2},{7,3},{8,4},{9,5},{1... | collective-permute-start | bytes 3833864 | tf_op jit(solution)/shard_map/ppermute | solution.py:79
  35.7 0.2 fusion.19
  35.9 1.7 %fusion.54 = (f32[96]{0:T(128)S(1)}, f32[96,3072]{1,0:T(8,128)S(1)}) fusion(bf16[1536,3072]{1,0:T(8,128)(2,1)S(1)} %bitcast.43, bf16[96,1664]{1,0:T(8,128)(2,1)S(1)} %constant_dynamic-update-slice_fusion.2), kind=kOutput, calls=%fused_computation.208 | convolution fusion | flops 906264448 | bytes 10912128 | tf_op jit(solution)/shard_map/dot_general | solution.py:89
  37.6 0.5 fusion.7
  38.2 0.2 slice_reduce_fusion.9
  38.4 12.1 %collective-permute-done.5 = bf16[4,96,1664]{2,1,0:T(8,128)(2,1)S(1)} collective-permute-done((bf16[4,96,1664]{2,1,0:T(8,128)(2,1)S(1)}, bf16[4,96,1664]{2,1,0:T(8,128)(2,1)S(1)}, u32[]{:S(2)}, u32[]{:S(2)}) %collective-permute-start.5) | collective-permute-done | bytes 1277984 | tf_op jit(solution)/shard_map/ppermute | solution.py:79
  50.5 3.7 %collective-permute-done.4 = bf16[4,96,1664]{2,1,0:T(8,128)(2,1)S(1)} collective-permute-done((bf16[4,96,1664]{2,1,0:T(8,128)(2,1)S(1)}, bf16[4,96,1664]{2,1,0:T(8,128)(2,1)S(1)}, u32[]{:S(2)}, u32[]{:S(2)}) %collective-permute-start.4) | collective-permute-done | bytes 1277984 | tf_op jit(solution)/shard_map/ppermute | solution.py:79
  54.2 0.3 pad_maximum_fusion
  54.4 0.8 copy-done.1
  55.2 10.2 %fusion.55 = (f32[768]{0:T(1024)S(1)}, f32[768,3072]{1,0:T(8,128)}) fusion(bf16[1536,3072]{1,0:T(8,128)(2,1)S(1)} %bitcast.43, bf16[768,1664]{1,0:T(8,128)(2,1)S(1)} %bitcast.46), kind=kOutput, calls=%fused_computation.209 | convolution fusion | flops 7250115584 | bytes 21236736 | tf_op jit(solution)/shard_map/dot_general | solution.py:89
  65.6 0.1 copy.16
  65.8 1.1 slice.285
  66.9 2.1 %collective-permute-start.6 = (bf16[4,48,1664]{2,1,0:T(8,128)(2,1)S(1)}, bf16[4,48,1664]{2,1,0:T(8,128)(2,1)S(1)}, u32[]{:S(2)}, u32[]{:S(2)}) collective-permute-start(bf16[4,48,1664]{2,1,0:T(8,128)(2,1)S(1)} %slice.285), channel_id=1, source_target_pairs={{0,4},{1,5},{2,6},{3,7},{4,8},{5,9},{6,10},{7,11},{8,12},{9,13},{1... | collective-permute-start | bytes 1916936 | tf_op jit(solution)/shard_map/ppermute | solution.py:79
  69.0 6.3 %fusion = (f32[768]{0:T(1024)S(1)}, f32[768]{0:T(1024)S(1)}, f32[768]{0:T(1024)S(1)}) fusion(f32[768,3072]{1,0:T(8,128)} %get-tuple-element.72, f32[768]{0:T(1024)S(1)} %get-tuple-element.71, s32[768]{0:T(1024)S(1)} %fusion.30), kind=kLoop, calls=%fused_computation.8 | loop fusion | flops 16512768 | bytes 9452544 | tf_op jit(solution)/shard_map/reduce_sum | solution.py:92
  75.3 0.2 slice_reduce_fusion.7
  75.5 0.9 slice_reduce_fusion.8
  76.4 2.2 %collective-permute-done.6 = bf16[4,48,1664]{2,1,0:T(8,128)(2,1)S(1)} collective-permute-done((bf16[4,48,1664]{2,1,0:T(8,128)(2,1)S(1)}, bf16[4,48,1664]{2,1,0:T(8,128)(2,1)S(1)}, u32[]{:S(2)}, u32[]{:S(2)}) %collective-permute-start.6) | collective-permute-done | bytes 639008 | tf_op jit(solution)/shard_map/ppermute | solution.py:79
  78.6 0.1 pad_maximum_fusion.2
  78.7 9.8 %fusion.56 = (f32[384]{0:T(512)S(1)}, f32[384,3072]{1,0:T(8,128)}) fusion(bf16[1536,3072]{1,0:T(8,128)(2,1)} %param.8, bf16[384,1664]{1,0:T(8,128)(2,1)S(1)} %bitcast.50), kind=kOutput, calls=%fused_computation.210 | convolution fusion | flops 3625057792 | bytes 15336960 | tf_op jit(solution)/shard_map/dot_general | solution.py:89
  88.5 0.2 slice_reduce_fusion.6
  88.7 0.7 gather_fusion.3
  89.4 0.6 fusion.48
  90.1 0.1 broadcast_in_dim.86
  90.3 4.0 %fusion.1 = (f32[384]{0:T(512)S(1)}, f32[384]{0:T(512)S(1)}, f32[384]{0:T(512)S(1)}) fusion(f32[384,3072]{1,0:T(8,128)} %get-tuple-element.74, f32[384]{0:T(512)S(1)} %get-tuple-element.73, s32[384]{0:T(512)S(1)} %fusion.32), kind=kLoop, calls=%fused_computation.13 | loop fusion | flops 8256384 | bytes 4726272 | tf_op jit(solution)/shard_map/reduce_sum | solution.py:92
  94.4 0.1 concatenate.29
  94.6 0.6 gather_fusion.2
  95.2 0.1 gather.19
  95.3 0.3 collective-permute-start.8
  95.6 3.8 %collective-permute-done.8 = f32[4,1536]{1,0:T(4,128)S(1)} collective-permute-done((f32[4,1536]{1,0:T(4,128)S(1)}, f32[4,1536]{1,0:T(4,128)S(1)}, u32[]{:S(2)}, u32[]{:S(2)}) %collective-permute-start.8) | collective-permute-done | bytes 24608 | tf_op jit(solution)/shard_map/ppermute | solution.py:32
  99.7 5.3 %collective-permute-done.9 = f32[4,1536]{1,0:T(4,128)S(1)} collective-permute-done((f32[4,1536]{1,0:T(4,128)S(1)}, f32[4,1536]{1,0:T(4,128)S(1)}, u32[]{:S(2)}, u32[]{:S(2)}) %collective-permute-start.9) | collective-permute-done | bytes 24608 | tf_op jit(solution)/shard_map/ppermute | solution.py:32
  105.1 0.9 collective-permute-start.10
  106.0 3.0 %collective-permute-done.10 = f32[4,1536]{1,0:T(4,128)S(1)} collective-permute-done((f32[4,1536]{1,0:T(4,128)S(1)}, f32[4,1536]{1,0:T(4,128)S(1)}, u32[]{:S(2)}, u32[]{:S(2)}) %collective-permute-start.10) | collective-permute-done | bytes 24608 | tf_op jit(solution)/shard_map/ppermute | solution.py:32
  109.2 0.9 collective-permute-start.11
  110.9 3.7 %collective-permute-done.11 = f32[4,1536]{1,0:T(4,128)S(1)} collective-permute-done((f32[4,1536]{1,0:T(4,128)S(1)}, f32[4,1536]{1,0:T(4,128)S(1)}, u32[]{:S(2)}, u32[]{:S(2)}) %collective-permute-start.11) | collective-permute-done | bytes 24608 | tf_op jit(solution)/shard_map/ppermute | solution.py:32
  114.7 0.8 select_reduce_fusion.5
  115.4 0.7 pad_maximum_fusion.12
  116.2 0.2 fusion.46
  116.4 0.2 fusion.45
  116.5 0.2 select_dynamic-update-slice_fusion
  116.7 0.6 collective-permute-done.12
  117.3 0.7 fusion.37
  118.0 1.6 %collective-permute-start.13 = (f32[2]{0:T(128)S(1)}, f32[2]{0:T(128)S(1)}, u32[]{:S(2)}, u32[]{:S(2)}) collective-permute-start(f32[2]{0:T(128)S(1)} %fusion.37), channel_id=1, source_target_pairs={{0,32},{16,48},{32,0},{48,16},{64,96},{80,112},{96,64},{112,80},{1... | collective-permute-start | bytes 32 | tf_op jit(solution)/shard_map/ppermute | solution.py:32
  119.6 2.0 %collective-permute-done.13 = f32[2]{0:T(128)S(1)} collective-permute-done((f32[2]{0:T(128)S(1)}, f32[2]{0:T(128)S(1)}, u32[]{:S(2)}, u32[]{:S(2)}) %collective-permute-start.13) | collective-permute-done | bytes 40 | tf_op jit(solution)/shard_map/ppermute | solution.py:32
  121.6 3.2 %collective-permute-start.14 = (f32[2]{0:T(128)S(1)}, f32[2]{0:T(128)S(1)}, u32[]{:S(2)}, u32[]{:S(2)}) collective-permute-start(f32[2]{0:T(128)S(1)} %fusion.36), channel_id=1, source_target_pairs={{0,64},{16,80},{32,96},{48,112},{64,0},{80,16},{96,32},{112,48},{1... | collective-permute-start | bytes 32 | tf_op jit(solution)/shard_map/ppermute | solution.py:32
  124.8 1.9 %collective-permute-done.14 = f32[2]{0:T(128)S(1)} collective-permute-done((f32[2]{0:T(128)S(1)}, f32[2]{0:T(128)S(1)}, u32[]{:S(2)}, u32[]{:S(2)}) %collective-permute-start.14) | collective-permute-done | bytes 40 | tf_op jit(solution)/shard_map/ppermute | solution.py:32
  126.7 0.6 fusion.50
  (92 shorter events, 1.8 us)
Async XLA Ops:
  0.6 12.1 %copy-start = (s32[4]{0:T(128)S(1)}, s32[4]{0:T(128)}, u32[]{:S(2)}) copy-start(s32[4]{0:T(128)} %constant.170.clone) | copy-start | bytes 52
  8.4 12.5 %collective-permute-start.1 = (bf16[96,1664]{1,0:T(8,128)(2,1)S(1)}, bf16[96,1664]{1,0:T(8,128)(2,1)S(1)}, u32[]{:S(2)}, u32[]{:S(2)}) collective-permute-start(bf16[96,1664]{1,0:T(8,128)(2,1)S(1)} %get-tuple-element.44), channel_id=1, source_target_pairs={{0,3},{1,0},{2,1},{3,2},{4,7},{5,4},{6,5},{7,6},{8,11},{9,8},{10,9... | collective-permute-start | bytes 958472 | tf_op jit(solution)/shard_map/ppermute | solution.py:79
  12.7 8.2 %collective-permute-start = (bf16[96,1664]{1,0:T(8,128)(2,1)S(1)}, bf16[96,1664]{1,0:T(8,128)(2,1)S(1)}, u32[]{:S(2)}, u32[]{:S(2)}) collective-permute-start(bf16[96,1664]{1,0:T(8,128)(2,1)S(1)} %get-tuple-element.44), channel_id=1, source_target_pairs={{0,1},{1,2},{2,3},{3,0},{4,5},{5,6},{6,7},{7,4},{8,9},{9,10},{10,1... | collective-permute-start | bytes 958472 | tf_op jit(solution)/shard_map/ppermute | solution.py:79
  13.4 7.6 %slice-start = ((s8[9437184]{0:T(1024)(128)(4,1)}), s8[1048576]{0:T(1024)(128)(4,1)S(1)}, s32[]{:S(2)}) async-start(s8[9437184]{0:T(1024)(128)(4,1)} %bitcast.42), calls=%async_computation | async-start | bytes 2097152
  14.1 6.9 %slice-start.1 = ((s8[9437184]{0:T(1024)(128)(4,1)}), s8[4194304]{0:T(1024)(128)(4,1)S(1)}, s32[]{:S(2)}) async-start(s8[9437184]{0:T(1024)(128)(4,1)} %bitcast.42), calls=%async_computation.1 | async-start | bytes 8388608
  14.1 6.9 %slice-start.2 = ((s8[9437184]{0:T(1024)(128)(4,1)}), s8[4194304]{0:T(1024)(128)(4,1)S(1)}, s32[]{:S(2)}) async-start(s8[9437184]{0:T(1024)(128)(4,1)} %bitcast.42), calls=%async_computation.2 | async-start | bytes 8388608
  23.1 9.5 %collective-permute-start.3 = (bf16[48,1664]{1,0:T(8,128)(2,1)S(1)}, bf16[48,1664]{1,0:T(8,128)(2,1)S(1)}, u32[]{:S(2)}, u32[]{:S(2)}) collective-permute-start(bf16[48,1664]{1,0:T(8,128)(2,1)S(1)} %slice.276), channel_id=1, source_target_pairs={{0,3},{1,0},{2,1},{3,2},{4,7},{5,4},{6,5},{7,6},{8,11},{9,8},{10,9... | collective-permute-start | bytes 479240 | tf_op jit(solution)/shard_map/ppermute | solution.py:79
  26.1 6.6 %collective-permute-start.2 = (bf16[48,1664]{1,0:T(8,128)(2,1)S(1)}, bf16[48,1664]{1,0:T(8,128)(2,1)S(1)}, u32[]{:S(2)}, u32[]{:S(2)}) collective-permute-start(bf16[48,1664]{1,0:T(8,128)(2,1)S(1)} %slice.275), channel_id=1, source_target_pairs={{0,1},{1,2},{2,3},{3,0},{4,5},{5,6},{6,7},{7,4},{8,9},{9,10},{10,1... | collective-permute-start | bytes 479240 | tf_op jit(solution)/shard_map/ppermute | solution.py:79
  32.9 17.6 %collective-permute-start.5 = (bf16[4,96,1664]{2,1,0:T(8,128)(2,1)S(1)}, bf16[4,96,1664]{2,1,0:T(8,128)(2,1)S(1)}, u32[]{:S(2)}, u32[]{:S(2)}) collective-permute-start(bf16[4,96,1664]{2,1,0:T(8,128)(2,1)S(1)} %pad_maximum_fusion.1), channel_id=1, source_target_pairs={{0,12},{1,13},{2,14},{3,15},{4,0},{5,1},{6,2},{7,3},{8,4},{9,5},{1... | collective-permute-start | bytes 3833864 | tf_op jit(solution)/shard_map/ppermute | solution.py:79
  35.7 18.5 %collective-permute-start.4 = (bf16[4,96,1664]{2,1,0:T(8,128)(2,1)S(1)}, bf16[4,96,1664]{2,1,0:T(8,128)(2,1)S(1)}, u32[]{:S(2)}, u32[]{:S(2)}) collective-permute-start(bf16[4,96,1664]{2,1,0:T(8,128)(2,1)S(1)} %pad_maximum_fusion.1), channel_id=1, source_target_pairs={{0,4},{1,5},{2,6},{3,7},{4,8},{5,9},{6,10},{7,11},{8,12},{9,13},{1... | collective-permute-start | bytes 3833864 | tf_op jit(solution)/shard_map/ppermute | solution.py:79
  54.2 1.0 copy-start.1
  65.5 10.9 %collective-permute-start.7 = (bf16[4,48,1664]{2,1,0:T(8,128)(2,1)S(1)}, bf16[4,48,1664]{2,1,0:T(8,128)(2,1)S(1)}, u32[]{:S(2)}, u32[]{:S(2)}) collective-permute-start(bf16[4,48,1664]{2,1,0:T(8,128)(2,1)S(1)} %slice.286), channel_id=1, source_target_pairs={{0,12},{1,13},{2,14},{3,15},{4,0},{5,1},{6,2},{7,3},{8,4},{9,5},{1... | collective-permute-start | bytes 1916936 | tf_op jit(solution)/shard_map/ppermute | solution.py:79
  66.9 11.7 %collective-permute-start.6 = (bf16[4,48,1664]{2,1,0:T(8,128)(2,1)S(1)}, bf16[4,48,1664]{2,1,0:T(8,128)(2,1)S(1)}, u32[]{:S(2)}, u32[]{:S(2)}) collective-permute-start(bf16[4,48,1664]{2,1,0:T(8,128)(2,1)S(1)} %slice.285), channel_id=1, source_target_pairs={{0,4},{1,5},{2,6},{3,7},{4,8},{5,9},{6,10},{7,11},{8,12},{9,13},{1... | collective-permute-start | bytes 1916936 | tf_op jit(solution)/shard_map/ppermute | solution.py:79
  95.3 4.1 %collective-permute-start.8 = (f32[4,1536]{1,0:T(4,128)S(1)}, f32[4,1536]{1,0:T(4,128)S(1)}, u32[]{:S(2)}, u32[]{:S(2)}) collective-permute-start(f32[4,1536]{1,0:T(4,128)S(1)} %broadcast_select_fusion), channel_id=1, source_target_pairs={{0,1},{1,0},{2,3},{3,2},{4,5},{5,4},{6,7},{7,6},{8,9},{9,8},{10,11... | collective-permute-start | bytes 73736 | tf_op jit(solution)/shard_map/ppermute | solution.py:32
  99.6 5.4 %collective-permute-start.9 = (f32[4,1536]{1,0:T(4,128)S(1)}, f32[4,1536]{1,0:T(4,128)S(1)}, u32[]{:S(2)}, u32[]{:S(2)}) collective-permute-start(f32[4,1536]{1,0:T(4,128)S(1)} %pad_maximum_fusion.4), channel_id=1, source_target_pairs={{0,2},{1,3},{2,0},{3,1},{4,6},{5,7},{6,4},{7,5},{8,10},{9,11},{10,... | collective-permute-start | bytes 73736 | tf_op jit(solution)/shard_map/ppermute | solution.py:32
  105.1 3.9 %collective-permute-start.10 = (f32[4,1536]{1,0:T(4,128)S(1)}, f32[4,1536]{1,0:T(4,128)S(1)}, u32[]{:S(2)}, u32[]{:S(2)}) collective-permute-start(f32[4,1536]{1,0:T(4,128)S(1)} %pad_maximum_fusion.5), channel_id=1, source_target_pairs={{0,4},{1,5},{2,6},{3,7},{4,0},{5,1},{6,2},{7,3},{8,12},{9,13},{10,... | collective-permute-start | bytes 73736 | tf_op jit(solution)/shard_map/ppermute | solution.py:32
  109.2 5.4 %collective-permute-start.11 = (f32[4,1536]{1,0:T(4,128)S(1)}, f32[4,1536]{1,0:T(4,128)S(1)}, u32[]{:S(2)}, u32[]{:S(2)}) collective-permute-start(f32[4,1536]{1,0:T(4,128)S(1)} %pad_maximum_fusion.6), channel_id=1, source_target_pairs={{0,8},{1,9},{2,10},{3,11},{4,12},{5,13},{6,14},{7,15},{8,0},{9,1},... | collective-permute-start | bytes 73736 | tf_op jit(solution)/shard_map/ppermute | solution.py:32
  116.1 1.2 collective-permute-start.12
  116.3 12.3 %copy-start.3 = (f32[128]{0:T(128)}, f32[128]{0:T(128)S(1)}, u32[]{:S(2)}) copy-start(f32[128]{0:T(128)S(1)} %fusion.46) | copy-start | bytes 1540
  116.5 12.1 %copy-start.4 = (f32[128]{0:T(128)}, f32[128]{0:T(128)S(1)}, u32[]{:S(2)}) copy-start(f32[128]{0:T(128)S(1)} %fusion.45) | copy-start | bytes 1540
  116.7 12.0 %copy-start.2 = (f32[128]{0:T(128)}, f32[128]{0:T(128)S(1)}, u32[]{:S(2)}) copy-start(f32[128]{0:T(128)S(1)} %select_dynamic-update-slice_fusion) | copy-start | bytes 1540
  118.0 3.6 %collective-permute-start.13 = (f32[2]{0:T(128)S(1)}, f32[2]{0:T(128)S(1)}, u32[]{:S(2)}, u32[]{:S(2)}) collective-permute-start(f32[2]{0:T(128)S(1)} %fusion.37), channel_id=1, source_target_pairs={{0,32},{16,48},{32,0},{48,16},{64,96},{80,112},{96,64},{112,80},{1... | collective-permute-start | bytes 32 | tf_op jit(solution)/shard_map/ppermute | solution.py:32
  121.6 5.1 %collective-permute-start.14 = (f32[2]{0:T(128)S(1)}, f32[2]{0:T(128)S(1)}, u32[]{:S(2)}, u32[]{:S(2)}) collective-permute-start(f32[2]{0:T(128)S(1)} %fusion.36), channel_id=1, source_target_pairs={{0,64},{16,80},{32,96},{48,112},{64,0},{80,16},{96,32},{112,48},{1... | collective-permute-start | bytes 32 | tf_op jit(solution)/shard_map/ppermute | solution.py:32

commit v9 on v8

--- a/solution.py
+++ b/solution.py
@@ -119,10 +119,8 @@
     left = shift(own, 0, 1, reqs, vocs)
     right = shift(own, 0, -1, reqs, vocs)
     part_own = stats(own)
-    far_a = shift(left[:HALF], 0, 1, reqs, vocs)
-    far_b = shift(right[HALF:], 0, -1, reqs, vocs)
+    far = shift(own, 0, 2, reqs, vocs)
     part_near = stats(jnp.concatenate([left, right]))
-    far = jnp.concatenate([far_a, far_b])
     line = jnp.stack([own, left, right, far])
     line_left = shift(line, 1, 1, reqs, vocs)
     line_right = shift(line, 1, -1, reqs, vocs)

time: 130 us -> 120 us (0.923)
  waiting for transfers between devices: 43.9 us -> 31.6 us
  starting transfers between devices: 19.3 us -> 21.4 us
    ppermute x8 -> x7, waiting for transfers between devices: 23.6 us -> 14.5 us  [shift(): return lax.ppermute(value, AXES, pairs)]
    ppermute x7, waiting for transfers between devices: 20.2 us -> 17 us  [butterfly(): other = lax.ppermute(value, axis, [(i, i ^ step) for i in range(size)])]
    ppermute x7, starting transfers between devices: 7.03 us -> 10.1 us  [butterfly(): other = lax.ppermute(value, axis, [(i, i ^ step) for i in range(size)])]
    ppermute x8 -> x7, starting transfers between devices: 12.2 us -> 11.3 us  [shift(): return lax.ppermute(value, AXES, pairs)]
  transfers between devices with their start and end apart: 15 -> 14, of which waited for: 12 -> 10; matrix products, arithmetic and copies ran while one was open for 16% -> 19% of each run, Pallas kernels for 0% -> 0%
where the time goes in v9:
time: 120 us
  waiting for transfers between devices  31.6 us (26%)
  matrix products  29.4 us (24%)
  starting transfers between devices  21.4 us (18%)
  other arithmetic  20.8 us (17%)
  local copies, waits for them, and re-layouts  8.76 us (7%)
  between operations  7.57 us (6%)
    dot_general x5, matrix products, block_stats(): logits = jnp.dot(rows_in, head, preferred_element_type=jnp.float32)  29.4 us
    ppermute x7, waiting for transfers between devices, butterfly(): other = lax.ppermute(value, axis, [(i, i ^ step) for i in range(size)])  17 us
    ppermute x7, waiting for transfers between devices, shift(): return lax.ppermute(value, AXES, pairs)  14.5 us
    reduce_sum x5, other arithmetic, block_stats(): total = jnp.sum(expo, axis=-1)  12.3 us
    ppermute x7, starting transfers between devices, shift(): return lax.ppermute(value, AXES, pairs)  11.3 us
    ppermute x7, starting transfers between devices, butterfly(): other = lax.ppermute(value, axis, [(i, i ^ step) for i in range(size)])  10.1 us
  transfers between devices with their start and end apart: 14, of which 10 were waited for; matrix products, arithmetic and copies ran while one was open for 19% of the time, Pallas kernels for 0%

profile of v9, /device:TPU:0, one launch (start us, length us, event | category | flops | bytes accessed | tf_op | source)
XLA Modules:
  0.0 119.5 jit_solution(2056896334948558372)
XLA Ops:
  0.7 1.3 %fusion.51 = (s32[1,1]{1,0:T(1,128)}, s32[1,1]{1,0:T(1,128)}) fusion(s32[1,2]{1,0:T(1,128)} %param.10), kind=kLoop, calls=%fused_computation.203 | loop fusion | bytes 16 | tf_op jit(solution)/shard_map/slice | solution.py:106
  5.2 1.2 fusion.9
  6.4 0.7 and_select_fusion.1
  7.2 1.1 fusion.11
  8.3 0.1 select_convert_fusion
  8.4 4.1 %collective-permute-start.2 = (bf16[96,1664]{1,0:T(8,128)(2,1)S(1)}, bf16[96,1664]{1,0:T(8,128)(2,1)S(1)}, u32[]{:S(2)}, u32[]{:S(2)}) collective-permute-start(bf16[96,1664]{1,0:T(8,128)(2,1)S(1)} %get-tuple-element.44), channel_id=1, source_target_pairs={{0,2},{1,3},{2,0},{3,1},{4,6},{5,7},{6,4},{7,5},{8,10},{9,11},{10,... | collective-permute-start | bytes 958472 | tf_op jit(solution)/shard_map/ppermute | solution.py:79
  12.5 0.7 collective-permute-start.1
  13.2 1.3 %collective-permute-start = (bf16[96,1664]{1,0:T(8,128)(2,1)S(1)}, bf16[96,1664]{1,0:T(8,128)(2,1)S(1)}, u32[]{:S(2)}, u32[]{:S(2)}) collective-permute-start(bf16[96,1664]{1,0:T(8,128)(2,1)S(1)} %get-tuple-element.44), channel_id=1, source_target_pairs={{0,1},{1,2},{2,3},{3,0},{4,5},{5,6},{6,7},{7,4},{8,9},{9,10},{10,1... | collective-permute-start | bytes 958472 | tf_op jit(solution)/shard_map/ppermute | solution.py:79
  14.6 0.7 gather_fusion
  15.3 0.7 gather_fusion.1
  16.0 5.6 %fusion.52 = (f32[96]{0:T(128)S(1)}, f32[96,3072]{1,0:T(8,128)S(1)}) fusion(bf16[96,1536]{1,0:T(8,128)(2,1)S(1)} %fusion.11, bf16[1536,3072]{1,0:T(8,128)(2,1)} %param.8), kind=kOutput, calls=%fused_computation.204 | convolution fusion | flops 906264448 | bytes 10912128 | tf_op jit(solution)/shard_map/dot_general | solution.py:89
  21.6 0.2 fusion.21
  21.8 0.5 fusion.8
  22.4 0.2 pad_maximum_fusion.1
  22.6 2.8 %collective-permute-start.4 = (bf16[4,96,1664]{2,1,0:T(8,128)(2,1)S(1)}, bf16[4,96,1664]{2,1,0:T(8,128)(2,1)S(1)}, u32[]{:S(2)}, u32[]{:S(2)}) collective-permute-start(bf16[4,96,1664]{2,1,0:T(8,128)(2,1)S(1)} %pad_maximum_fusion.1), channel_id=1, source_target_pairs={{0,12},{1,13},{2,14},{3,15},{4,0},{5,1},{6,2},{7,3},{8,4},{9,5},{1... | collective-permute-start | bytes 3833864 | tf_op jit(solution)/shard_map/ppermute | solution.py:79
  25.4 0.2 fusion.19
  25.7 0.2 fusion.17
  25.9 1.7 %fusion.54 = (f32[96]{0:T(128)S(1)}, f32[96,3072]{1,0:T(8,128)S(1)}) fusion(bf16[1536,3072]{1,0:T(8,128)(2,1)S(1)} %bitcast.43, bf16[96,1664]{1,0:T(8,128)(2,1)S(1)} %collective-permute-done.2), kind=kOutput, calls=%fused_computation.206 | convolution fusion | flops 906264448 | bytes 10912128 | tf_op jit(solution)/shard_map/dot_general | solution.py:89
  27.7 0.5 fusion.7
  28.2 2.1 %fusion.53 = (f32[192]{0:T(256)S(1)}, f32[192,3072]{1,0:T(8,128)S(1)}) fusion(bf16[1536,3072]{1,0:T(8,128)(2,1)S(1)} %bitcast.43, bf16[192,1664]{1,0:T(8,128)(2,1)S(1)} %constant_dynamic-update-slice_fusion), kind=kOutput, calls=%fused_computation.205 | convolution fusion | flops 1812528896 | bytes 12387072 | tf_op jit(solution)/shard_map/dot_general | solution.py:89
  30.3 1.0 fusion.4
  31.3 0.2 slice_reduce_fusion.9
  31.5 8.7 %collective-permute-done.4 = bf16[4,96,1664]{2,1,0:T(8,128)(2,1)S(1)} collective-permute-done((bf16[4,96,1664]{2,1,0:T(8,128)(2,1)S(1)}, bf16[4,96,1664]{2,1,0:T(8,128)(2,1)S(1)}, u32[]{:S(2)}, u32[]{:S(2)}) %collective-permute-start.4) | collective-permute-done | bytes 1277984 | tf_op jit(solution)/shard_map/ppermute | solution.py:79
  40.2 3.7 %collective-permute-done.3 = bf16[4,96,1664]{2,1,0:T(8,128)(2,1)S(1)} collective-permute-done((bf16[4,96,1664]{2,1,0:T(8,128)(2,1)S(1)}, bf16[4,96,1664]{2,1,0:T(8,128)(2,1)S(1)}, u32[]{:S(2)}, u32[]{:S(2)}) %collective-permute-start.3) | collective-permute-done | bytes 1277984 | tf_op jit(solution)/shard_map/ppermute | solution.py:79
  43.9 0.3 pad_maximum_fusion
  44.2 0.8 copy-done.1
  44.9 10.2 %fusion.55 = (f32[768]{0:T(1024)S(1)}, f32[768,3072]{1,0:T(8,128)}) fusion(bf16[1536,3072]{1,0:T(8,128)(2,1)S(1)} %bitcast.43, bf16[768,1664]{1,0:T(8,128)(2,1)S(1)} %bitcast.45), kind=kOutput, calls=%fused_computation.207 | convolution fusion | flops 7250115584 | bytes 21236736 | tf_op jit(solution)/shard_map/dot_general | solution.py:89
  55.3 0.1 copy.16
  55.5 1.1 slice.275
  56.6 2.3 %collective-permute-start.5 = (bf16[4,48,1664]{2,1,0:T(8,128)(2,1)S(1)}, bf16[4,48,1664]{2,1,0:T(8,128)(2,1)S(1)}, u32[]{:S(2)}, u32[]{:S(2)}) collective-permute-start(bf16[4,48,1664]{2,1,0:T(8,128)(2,1)S(1)} %slice.275), channel_id=1, source_target_pairs={{0,4},{1,5},{2,6},{3,7},{4,8},{5,9},{6,10},{7,11},{8,12},{9,13},{1... | collective-permute-start | bytes 1916936 | tf_op jit(solution)/shard_map/ppermute | solution.py:79
  58.9 6.3 %fusion = (f32[768]{0:T(1024)S(1)}, f32[768]{0:T(1024)S(1)}, f32[768]{0:T(1024)S(1)}) fusion(f32[768,3072]{1,0:T(8,128)} %get-tuple-element.72, f32[768]{0:T(1024)S(1)} %get-tuple-element.71, s32[768]{0:T(1024)S(1)} %fusion.30), kind=kLoop, calls=%fused_computation.8 | loop fusion | flops 16512768 | bytes 9452544 | tf_op jit(solution)/shard_map/reduce_sum | solution.py:92
  65.3 0.2 slice_reduce_fusion.7
  65.5 0.9 slice_reduce_fusion.8
  66.3 2.2 %collective-permute-done.5 = bf16[4,48,1664]{2,1,0:T(8,128)(2,1)S(1)} collective-permute-done((bf16[4,48,1664]{2,1,0:T(8,128)(2,1)S(1)}, bf16[4,48,1664]{2,1,0:T(8,128)(2,1)S(1)}, u32[]{:S(2)}, u32[]{:S(2)}) %collective-permute-start.5) | collective-permute-done | bytes 639008 | tf_op jit(solution)/shard_map/ppermute | solution.py:79
  68.5 0.1 pad_maximum_fusion.2
  68.6 9.8 %fusion.56 = (f32[384]{0:T(512)S(1)}, f32[384,3072]{1,0:T(8,128)}) fusion(bf16[1536,3072]{1,0:T(8,128)(2,1)} %param.8, bf16[384,1664]{1,0:T(8,128)(2,1)S(1)} %bitcast.48), kind=kOutput, calls=%fused_computation.208 | convolution fusion | flops 3625057792 | bytes 15336960 | tf_op jit(solution)/shard_map/dot_general | solution.py:89
  78.4 0.2 slice_reduce_fusion.6
  78.7 0.7 gather_fusion.3
  79.3 0.6 fusion.48
  80.0 0.1 broadcast_in_dim.86
  80.3 4.0 %fusion.1 = (f32[384]{0:T(512)S(1)}, f32[384]{0:T(512)S(1)}, f32[384]{0:T(512)S(1)}) fusion(f32[384,3072]{1,0:T(8,128)} %get-tuple-element.74, f32[384]{0:T(512)S(1)} %get-tuple-element.73, s32[384]{0:T(512)S(1)} %fusion.32), kind=kLoop, calls=%fused_computation.13 | loop fusion | flops 8256384 | bytes 4726272 | tf_op jit(solution)/shard_map/reduce_sum | solution.py:92
  84.3 0.1 concatenate.25
  84.5 0.6 gather_fusion.2
  85.1 0.1 gather.19
  85.2 1.1 collective-permute-start.7
  86.3 2.8 %collective-permute-done.7 = f32[4,1536]{1,0:T(4,128)S(1)} collective-permute-done((f32[4,1536]{1,0:T(4,128)S(1)}, f32[4,1536]{1,0:T(4,128)S(1)}, u32[]{:S(2)}, u32[]{:S(2)}) %collective-permute-start.7) | collective-permute-done | bytes 24608 | tf_op jit(solution)/shard_map/ppermute | solution.py:32
  89.3 2.3 %collective-permute-start.8 = (f32[4,1536]{1,0:T(4,128)S(1)}, f32[4,1536]{1,0:T(4,128)S(1)}, u32[]{:S(2)}, u32[]{:S(2)}) collective-permute-start(f32[4,1536]{1,0:T(4,128)S(1)} %pad_maximum_fusion.4), channel_id=1, source_target_pairs={{0,2},{1,3},{2,0},{3,1},{4,6},{5,7},{6,4},{7,5},{8,10},{9,11},{10,... | collective-permute-start | bytes 73736 | tf_op jit(solution)/shard_map/ppermute | solution.py:32
  91.6 3.1 %collective-permute-done.8 = f32[4,1536]{1,0:T(4,128)S(1)} collective-permute-done((f32[4,1536]{1,0:T(4,128)S(1)}, f32[4,1536]{1,0:T(4,128)S(1)}, u32[]{:S(2)}, u32[]{:S(2)}) %collective-permute-start.8) | collective-permute-done | bytes 24608 | tf_op jit(solution)/shard_map/ppermute | solution.py:32
  94.9 0.9 collective-permute-start.9
  95.7 3.0 %collective-permute-done.9 = f32[4,1536]{1,0:T(4,128)S(1)} collective-permute-done((f32[4,1536]{1,0:T(4,128)S(1)}, f32[4,1536]{1,0:T(4,128)S(1)}, u32[]{:S(2)}, u32[]{:S(2)}) %collective-permute-start.9) | collective-permute-done | bytes 24608 | tf_op jit(solution)/shard_map/ppermute | solution.py:32
  98.9 0.9 collective-permute-start.10
  100.7 3.7 %collective-permute-done.10 = f32[4,1536]{1,0:T(4,128)S(1)} collective-permute-done((f32[4,1536]{1,0:T(4,128)S(1)}, f32[4,1536]{1,0:T(4,128)S(1)}, u32[]{:S(2)}, u32[]{:S(2)}) %collective-permute-start.10) | collective-permute-done | bytes 24608 | tf_op jit(solution)/shard_map/ppermute | solution.py:32
  104.4 0.8 select_reduce_fusion.5
  105.1 0.7 pad_maximum_fusion.12
  105.9 0.2 fusion.46
  106.1 0.2 fusion.45
  106.3 0.2 select_dynamic-update-slice_fusion
  106.4 0.6 collective-permute-done.11
  107.0 0.7 fusion.37
  107.7 1.6 %collective-permute-start.12 = (f32[2]{0:T(128)S(1)}, f32[2]{0:T(128)S(1)}, u32[]{:S(2)}, u32[]{:S(2)}) collective-permute-start(f32[2]{0:T(128)S(1)} %fusion.37), channel_id=1, source_target_pairs={{0,32},{16,48},{32,0},{48,16},{64,96},{80,112},{96,64},{112,80},{1... | collective-permute-start | bytes 32 | tf_op jit(solution)/shard_map/ppermute | solution.py:32
  109.3 2.0 %collective-permute-done.12 = f32[2]{0:T(128)S(1)} collective-permute-done((f32[2]{0:T(128)S(1)}, f32[2]{0:T(128)S(1)}, u32[]{:S(2)}, u32[]{:S(2)}) %collective-permute-start.12) | collective-permute-done | bytes 40 | tf_op jit(solution)/shard_map/ppermute | solution.py:32
  111.3 3.2 %collective-permute-start.13 = (f32[2]{0:T(128)S(1)}, f32[2]{0:T(128)S(1)}, u32[]{:S(2)}, u32[]{:S(2)}) collective-permute-start(f32[2]{0:T(128)S(1)} %fusion.36), channel_id=1, source_target_pairs={{0,64},{16,80},{32,96},{48,112},{64,0},{80,16},{96,32},{112,48},{1... | collective-permute-start | bytes 32 | tf_op jit(solution)/shard_map/ppermute | solution.py:32
  114.5 1.9 %collective-permute-done.13 = f32[2]{0:T(128)S(1)} collective-permute-done((f32[2]{0:T(128)S(1)}, f32[2]{0:T(128)S(1)}, u32[]{:S(2)}, u32[]{:S(2)}) %collective-permute-start.13) | collective-permute-done | bytes 40 | tf_op jit(solution)/shard_map/ppermute | solution.py:32
  116.4 0.6 fusion.50
  (86 shorter events, 1.6 us)
Async XLA Ops:
  0.6 14.0 %copy-start = (s32[4]{0:T(128)S(1)}, s32[4]{0:T(128)}, u32[]{:S(2)}) copy-start(s32[4]{0:T(128)} %constant.170.clone) | copy-start | bytes 52
  8.4 13.9 %collective-permute-start.2 = (bf16[96,1664]{1,0:T(8,128)(2,1)S(1)}, bf16[96,1664]{1,0:T(8,128)(2,1)S(1)}, u32[]{:S(2)}, u32[]{:S(2)}) collective-permute-start(bf16[96,1664]{1,0:T(8,128)(2,1)S(1)} %get-tuple-element.44), channel_id=1, source_target_pairs={{0,2},{1,3},{2,0},{3,1},{4,6},{5,7},{6,4},{7,5},{8,10},{9,11},{10,... | collective-permute-start | bytes 958472 | tf_op jit(solution)/shard_map/ppermute | solution.py:79
  12.5 9.9 %collective-permute-start.1 = (bf16[96,1664]{1,0:T(8,128)(2,1)S(1)}, bf16[96,1664]{1,0:T(8,128)(2,1)S(1)}, u32[]{:S(2)}, u32[]{:S(2)}) collective-permute-start(bf16[96,1664]{1,0:T(8,128)(2,1)S(1)} %get-tuple-element.44), channel_id=1, source_target_pairs={{0,3},{1,0},{2,1},{3,2},{4,7},{5,4},{6,5},{7,6},{8,11},{9,8},{10,9... | collective-permute-start | bytes 958472 | tf_op jit(solution)/shard_map/ppermute | solution.py:79
  13.2 9.2 %collective-permute-start = (bf16[96,1664]{1,0:T(8,128)(2,1)S(1)}, bf16[96,1664]{1,0:T(8,128)(2,1)S(1)}, u32[]{:S(2)}, u32[]{:S(2)}) collective-permute-start(bf16[96,1664]{1,0:T(8,128)(2,1)S(1)} %get-tuple-element.44), channel_id=1, source_target_pairs={{0,1},{1,2},{2,3},{3,0},{4,5},{5,6},{6,7},{7,4},{8,9},{9,10},{10,1... | collective-permute-start | bytes 958472 | tf_op jit(solution)/shard_map/ppermute | solution.py:79
  15.3 10.6 %slice-start = ((s8[9437184]{0:T(1024)(128)(4,1)}), s8[1048576]{0:T(1024)(128)(4,1)S(1)}, s32[]{:S(2)}) async-start(s8[9437184]{0:T(1024)(128)(4,1)} %bitcast.42), calls=%async_computation | async-start | bytes 2097152
  15.9 10.0 %slice-start.1 = ((s8[9437184]{0:T(1024)(128)(4,1)}), s8[4194304]{0:T(1024)(128)(4,1)S(1)}, s32[]{:S(2)}) async-start(s8[9437184]{0:T(1024)(128)(4,1)} %bitcast.42), calls=%async_computation.1 | async-start | bytes 8388608
  16.0 10.0 %slice-start.2 = ((s8[9437184]{0:T(1024)(128)(4,1)}), s8[4194304]{0:T(1024)(128)(4,1)S(1)}, s32[]{:S(2)}) async-start(s8[9437184]{0:T(1024)(128)(4,1)} %bitcast.42), calls=%async_computation.2 | async-start | bytes 8388608
  22.6 17.6 %collective-permute-start.4 = (bf16[4,96,1664]{2,1,0:T(8,128)(2,1)S(1)}, bf16[4,96,1664]{2,1,0:T(8,128)(2,1)S(1)}, u32[]{:S(2)}, u32[]{:S(2)}) collective-permute-start(bf16[4,96,1664]{2,1,0:T(8,128)(2,1)S(1)} %pad_maximum_fusion.1), channel_id=1, source_target_pairs={{0,12},{1,13},{2,14},{3,15},{4,0},{5,1},{6,2},{7,3},{8,4},{9,5},{1... | collective-permute-start | bytes 3833864 | tf_op jit(solution)/shard_map/ppermute | solution.py:79
  25.4 18.5 %collective-permute-start.3 = (bf16[4,96,1664]{2,1,0:T(8,128)(2,1)S(1)}, bf16[4,96,1664]{2,1,0:T(8,128)(2,1)S(1)}, u32[]{:S(2)}, u32[]{:S(2)}) collective-permute-start(bf16[4,96,1664]{2,1,0:T(8,128)(2,1)S(1)} %pad_maximum_fusion.1), channel_id=1, source_target_pairs={{0,4},{1,5},{2,6},{3,7},{4,8},{5,9},{6,10},{7,11},{8,12},{9,13},{1... | collective-permute-start | bytes 3833864 | tf_op jit(solution)/shard_map/ppermute | solution.py:79
  43.9 1.0 copy-start.1
  55.2 11.1 %collective-permute-start.6 = (bf16[4,48,1664]{2,1,0:T(8,128)(2,1)S(1)}, bf16[4,48,1664]{2,1,0:T(8,128)(2,1)S(1)}, u32[]{:S(2)}, u32[]{:S(2)}) collective-permute-start(bf16[4,48,1664]{2,1,0:T(8,128)(2,1)S(1)} %slice.276), channel_id=1, source_target_pairs={{0,12},{1,13},{2,14},{3,15},{4,0},{5,1},{6,2},{7,3},{8,4},{9,5},{1... | collective-permute-start | bytes 1916936 | tf_op jit(solution)/shard_map/ppermute | solution.py:79
  56.6 11.9 %collective-permute-start.5 = (bf16[4,48,1664]{2,1,0:T(8,128)(2,1)S(1)}, bf16[4,48,1664]{2,1,0:T(8,128)(2,1)S(1)}, u32[]{:S(2)}, u32[]{:S(2)}) collective-permute-start(bf16[4,48,1664]{2,1,0:T(8,128)(2,1)S(1)} %slice.275), channel_id=1, source_target_pairs={{0,4},{1,5},{2,6},{3,7},{4,8},{5,9},{6,10},{7,11},{8,12},{9,13},{1... | collective-permute-start | bytes 1916936 | tf_op jit(solution)/shard_map/ppermute | solution.py:79
  85.2 3.9 %collective-permute-start.7 = (f32[4,1536]{1,0:T(4,128)S(1)}, f32[4,1536]{1,0:T(4,128)S(1)}, u32[]{:S(2)}, u32[]{:S(2)}) collective-permute-start(f32[4,1536]{1,0:T(4,128)S(1)} %broadcast_select_fusion), channel_id=1, source_target_pairs={{0,1},{1,0},{2,3},{3,2},{4,5},{5,4},{6,7},{7,6},{8,9},{9,8},{10,11... | collective-permute-start | bytes 73736 | tf_op jit(solution)/shard_map/ppermute | solution.py:32
  89.3 5.4 %collective-permute-start.8 = (f32[4,1536]{1,0:T(4,128)S(1)}, f32[4,1536]{1,0:T(4,128)S(1)}, u32[]{:S(2)}, u32[]{:S(2)}) collective-permute-start(f32[4,1536]{1,0:T(4,128)S(1)} %pad_maximum_fusion.4), channel_id=1, source_target_pairs={{0,2},{1,3},{2,0},{3,1},{4,6},{5,7},{6,4},{7,5},{8,10},{9,11},{10,... | collective-permute-start | bytes 73736 | tf_op jit(solution)/shard_map/ppermute | solution.py:32
  94.9 3.9 %collective-permute-start.9 = (f32[4,1536]{1,0:T(4,128)S(1)}, f32[4,1536]{1,0:T(4,128)S(1)}, u32[]{:S(2)}, u32[]{:S(2)}) collective-permute-start(f32[4,1536]{1,0:T(4,128)S(1)} %pad_maximum_fusion.5), channel_id=1, source_target_pairs={{0,4},{1,5},{2,6},{3,7},{4,0},{5,1},{6,2},{7,3},{8,12},{9,13},{10,... | collective-permute-start | bytes 73736 | tf_op jit(solution)/shard_map/ppermute | solution.py:32
  98.9 5.4 %collective-permute-start.10 = (f32[4,1536]{1,0:T(4,128)S(1)}, f32[4,1536]{1,0:T(4,128)S(1)}, u32[]{:S(2)}, u32[]{:S(2)}) collective-permute-start(f32[4,1536]{1,0:T(4,128)S(1)} %pad_maximum_fusion.6), channel_id=1, source_target_pairs={{0,8},{1,9},{2,10},{3,11},{4,12},{5,13},{6,14},{7,15},{8,0},{9,1},... | collective-permute-start | bytes 73736 | tf_op jit(solution)/shard_map/ppermute | solution.py:32
  105.8 1.2 collective-permute-start.11
  106.0 12.3 %copy-start.3 = (f32[128]{0:T(128)}, f32[128]{0:T(128)S(1)}, u32[]{:S(2)}) copy-start(f32[128]{0:T(128)S(1)} %fusion.46) | copy-start | bytes 1540
  106.3 12.1 %copy-start.4 = (f32[128]{0:T(128)}, f32[128]{0:T(128)S(1)}, u32[]{:S(2)}) copy-start(f32[128]{0:T(128)S(1)} %fusion.45) | copy-start | bytes 1540
  106.4 12.0 %copy-start.2 = (f32[128]{0:T(128)}, f32[128]{0:T(128)S(1)}, u32[]{:S(2)}) copy-start(f32[128]{0:T(128)S(1)} %select_dynamic-update-slice_fusion) | copy-start | bytes 1540
  107.7 3.6 %collective-permute-start.12 = (f32[2]{0:T(128)S(1)}, f32[2]{0:T(128)S(1)}, u32[]{:S(2)}, u32[]{:S(2)}) collective-permute-start(f32[2]{0:T(128)S(1)} %fusion.37), channel_id=1, source_target_pairs={{0,32},{16,48},{32,0},{48,16},{64,96},{80,112},{96,64},{112,80},{1... | collective-permute-start | bytes 32 | tf_op jit(solution)/shard_map/ppermute | solution.py:32
  111.3 5.1 %collective-permute-start.13 = (f32[2]{0:T(128)S(1)}, f32[2]{0:T(128)S(1)}, u32[]{:S(2)}, u32[]{:S(2)}) collective-permute-start(f32[2]{0:T(128)S(1)} %fusion.36), channel_id=1, source_target_pairs={{0,64},{16,80},{32,96},{48,112},{64,0},{80,16},{96,32},{112,48},{1... | collective-permute-start | bytes 32 | tf_op jit(solution)/shard_map/ppermute | solution.py:32

commit v10 on v9

--- a/solution.py
+++ b/solution.py
@@ -125,11 +125,10 @@
     line_left = shift(line, 1, 1, reqs, vocs)
     line_right = shift(line, 1, -1, reqs, vocs)
     part_far = stats(far)
-    line_far_a = shift(line_left[:, :HALF], 1, 1, reqs, vocs)
-    line_far_b = shift(line_right[:, HALF:], 1, -1, reqs, vocs)
+    line_far = shift(line, 1, 2, reqs, vocs)
+    part_line_far = stats(line_far.reshape(-1, own.shape[1]))
+    part_line_far, line_left, line_right = lax.optimization_barrier((part_line_far, line_left, line_right))
     part_lines = stats(jnp.concatenate([line_left, line_right]).reshape(-1, own.shape[1]))
-    line_far = jnp.concatenate([line_far_a, line_far_b], axis=1)
-    part_line_far = stats(line_far.reshape(-1, own.shape[1]))
     processed = jnp.concatenate([part_own, part_near, part_far, part_lines, part_line_far], axis=1)
     processed = processed.reshape(4, vocs, LIVE)
     count_of = lambda block: block[..., :1, width + 2].reshape(-1).astype(jnp.int32)

time: 120 us -> 129 us (1.075)
  waiting for transfers between devices: 31.6 us -> 38.7 us
  other arithmetic: 20.8 us -> 24.1 us
  matrix products: 29.4 us -> 27.4 us
    ppermute x7 -> x6, waiting for transfers between devices: 14.5 us -> 21.5 us  [shift(): return lax.ppermute(value, AXES, pairs)]
    dot_general x5, matrix products: 29.4 us -> 27.4 us  [block_stats(): logits = jnp.dot(rows_in, head, preferred_element_type=jnp.float32)]
    another operation x2, other arithmetic: 0.24 us -> 2.3 us  [shards(): line = jnp.stack([own, left, right, far])]
    slice x4, local copies, waits for them, and re-layouts: 1.43 us -> 2.82 us  [shards(): block[..., :1, width + 2].reshape(-1).astype(jnp.int32)]
    concatenate x1, other arithmetic: 0.26 us -> 1.56 us  [shards(): jnp.concatenate([line_left, line_right]).reshape(-1, own.shape[1])]
    ppermute x7 -> x6, starting transfers between devices: 11.3 us -> 11.1 us  [shift(): return lax.ppermute(value, AXES, pairs)]
  transfers between devices with their start and end apart: 14 -> 13, of which waited for: 10 -> 8; matrix products, arithmetic and copies ran while one was open for 19% -> 20% of each run, Pallas kernels for 0% -> 0%
where the time goes in v10:
time: 129 us; the launch traced here: 128 us
  waiting for transfers between devices  38.7 us (30%)
  matrix products  27.4 us (21%)
  other arithmetic  24.1 us (19%)
  starting transfers between devices  21.2 us (16%)
  local copies, waits for them, and re-layouts  9.17 us (7%)
  between operations  7.59 us (6%)
    dot_general x5, matrix products, block_stats(): logits = jnp.dot(rows_in, head, preferred_element_type=jnp.float32)  27.4 us
    ppermute x6, waiting for transfers between devices, shift(): return lax.ppermute(value, AXES, pairs)  21.5 us
    ppermute x7, waiting for transfers between devices, butterfly(): other = lax.ppermute(value, axis, [(i, i ^ step) for i in range(size)])  17.2 us
    reduce_sum x5, other arithmetic, block_stats(): total = jnp.sum(expo, axis=-1)  12.4 us
    ppermute x6, starting transfers between devices, shift(): return lax.ppermute(value, AXES, pairs)  11.1 us
    ppermute x7, starting transfers between devices, butterfly(): other = lax.ppermute(value, axis, [(i, i ^ step) for i in range(size)])  10.1 us
    slice x4, local copies, waits for them, and re-layouts, shards(): block[..., :1, width + 2].reshape(-1).astype(jnp.int32)  2.82 us
  transfers between devices with their start and end apart: 13, of which 8 were waited for; matrix products, arithmetic and copies ran while one was open for 20% of the time, Pallas kernels for 0%

profile of v10, /device:TPU:0, one launch (start us, length us, event | category | flops | bytes accessed | tf_op | source)
XLA Modules:
  0.0 128.1 jit_solution(9796864625424189593)
XLA Ops:
  0.7 1.3 %fusion.51 = (s32[1,1]{1,0:T(1,128)}, s32[1,1]{1,0:T(1,128)}) fusion(s32[1,2]{1,0:T(1,128)} %param.10), kind=kLoop, calls=%fused_computation.202 | loop fusion | bytes 16 | tf_op jit(solution)/shard_map/slice | solution.py:106
  5.2 1.2 fusion.9
  6.4 0.7 and_select_fusion.1
  7.2 1.1 fusion.11
  8.3 0.1 select_convert_fusion
  8.4 4.1 %collective-permute-start.2 = (bf16[96,1664]{1,0:T(8,128)(2,1)S(1)}, bf16[96,1664]{1,0:T(8,128)(2,1)S(1)}, u32[]{:S(2)}, u32[]{:S(2)}) collective-permute-start(bf16[96,1664]{1,0:T(8,128)(2,1)S(1)} %get-tuple-element.50), channel_id=1, source_target_pairs={{0,2},{1,3},{2,0},{3,1},{4,6},{5,7},{6,4},{7,5},{8,10},{9,11},{10,... | collective-permute-start | bytes 958472 | tf_op jit(solution)/shard_map/ppermute | solution.py:79
  12.5 0.7 collective-permute-start.1
  13.2 1.3 %collective-permute-start = (bf16[96,1664]{1,0:T(8,128)(2,1)S(1)}, bf16[96,1664]{1,0:T(8,128)(2,1)}, u32[]{:S(2)}, u32[]{:S(2)}) collective-permute-start(bf16[96,1664]{1,0:T(8,128)(2,1)S(1)} %get-tuple-element.50), channel_id=1, source_target_pairs={{0,1},{1,2},{2,3},{3,0},{4,5},{5,6},{6,7},{7,4},{8,9},{9,10},{10,1... | collective-permute-start | bytes 958472 | tf_op jit(solution)/shard_map/ppermute | solution.py:79
  14.6 0.7 gather_fusion
  15.3 0.7 gather_fusion.1
  16.0 5.6 %fusion.53 = (f32[96]{0:T(128)S(1)}, f32[96,3072]{1,0:T(8,128)S(1)}) fusion(bf16[96,1536]{1,0:T(8,128)(2,1)S(1)} %fusion.11, bf16[1536,3072]{1,0:T(8,128)(2,1)} %param.8), kind=kOutput, calls=%fused_computation.204 | convolution fusion | flops 906264448 | bytes 10912128 | tf_op jit(solution)/shard_map/dot_general | solution.py:89
  21.6 0.2 fusion.21
  21.8 0.5 fusion.8
  22.4 2.3 %pad_maximum_fusion.1 = bf16[4,96,1664]{2,1,0:T(8,128)(2,1)} fusion(bf16[1,96,1664]{2,1,0:T(8,128)(2,1)S(1)} %bitcast.46, bf16[1,96,1664]{2,1,0:T(8,128)(2,1)S(1)} %bitcast.47, bf16[1,96,1664]{2,1,0:T(8,128)(2,1)} %bitcast.17, bf16[1,96,1664]{2,1,0:T(8,128)(2,1)S(1)} %get-tuple-element.49), kind=kLoop, calls=%fused_computation.22 | loop fusion | flops 1916928 | bytes 2555904 | tf_op jit(solution)/shard_map/stack | solution.py:124
  24.7 2.8 %collective-permute-start.5 = (bf16[4,96,1664]{2,1,0:T(8,128)(2,1)}, bf16[4,96,1664]{2,1,0:T(8,128)(2,1)S(1)}, u32[]{:S(2)}, u32[]{:S(2)}) collective-permute-start(bf16[4,96,1664]{2,1,0:T(8,128)(2,1)} %pad_maximum_fusion.1), channel_id=1, source_target_pairs={{0,12},{1,13},{2,14},{3,15},{4,0},{5,1},{6,2},{7,3},{8,4},{9,5},{1... | collective-permute-start | bytes 3833864 | tf_op jit(solution)/shard_map/ppermute | solution.py:79
  27.4 2.3 %collective-permute-start.3 = (bf16[4,96,1664]{2,1,0:T(8,128)(2,1)}, bf16[4,96,1664]{2,1,0:T(8,128)(2,1)S(1)}, u32[]{:S(2)}, u32[]{:S(2)}) collective-permute-start(bf16[4,96,1664]{2,1,0:T(8,128)(2,1)} %pad_maximum_fusion.1), channel_id=1, source_target_pairs={{0,8},{1,9},{2,10},{3,11},{4,12},{5,13},{6,14},{7,15},{8,0},{9,1},... | collective-permute-start | bytes 3833864 | tf_op jit(solution)/shard_map/ppermute | solution.py:79
  29.7 0.2 fusion.19
  29.9 1.0 constant_dynamic-update-slice_fusion.1
  30.9 0.2 fusion.17
  31.2 1.7 %fusion.55 = (f32[96]{0:T(128)S(1)}, f32[96,3072]{1,0:T(8,128)S(1)}) fusion(bf16[1536,3072]{1,0:T(8,128)(2,1)S(1)} %bitcast.43, bf16[96,1664]{1,0:T(8,128)(2,1)S(1)} %collective-permute-done.2), kind=kOutput, calls=%fused_computation.206 | convolution fusion | flops 906264448 | bytes 10912128 | tf_op jit(solution)/shard_map/dot_general | solution.py:89
  32.9 0.5 fusion.7
  33.4 2.1 %fusion.54 = (f32[192]{0:T(256)S(1)}, f32[192,3072]{1,0:T(8,128)S(1)}) fusion(bf16[1536,3072]{1,0:T(8,128)(2,1)S(1)} %bitcast.43, bf16[192,1664]{1,0:T(8,128)(2,1)S(1)} %constant_dynamic-update-slice_fusion), kind=kOutput, calls=%fused_computation.205 | convolution fusion | flops 1812528896 | bytes 12387072 | tf_op jit(solution)/shard_map/dot_general | solution.py:89
  35.5 1.0 fusion.4
  36.6 0.9 slice_reduce_fusion.7
  37.5 21.5 %collective-permute-done.3 = bf16[4,96,1664]{2,1,0:T(8,128)(2,1)S(1)} collective-permute-done((bf16[4,96,1664]{2,1,0:T(8,128)(2,1)}, bf16[4,96,1664]{2,1,0:T(8,128)(2,1)S(1)}, u32[]{:S(2)}, u32[]{:S(2)}) %collective-permute-start.3) | collective-permute-done | bytes 1277984 | tf_op jit(solution)/shard_map/ppermute | solution.py:79
  58.9 5.6 %fusion.52 = (f32[384]{0:T(512)S(1)}, f32[384,3072]{1,0:T(8,128)}) fusion(bf16[1536,3072]{1,0:T(8,128)(2,1)S(1)} %bitcast.43, bf16[384,1664]{1,0:T(8,128)(2,1)S(1)} %bitcast.49), kind=kOutput, calls=%fused_computation.203 | convolution fusion | flops 3625057792 | bytes 15336960 | tf_op jit(solution)/shard_map/dot_general | solution.py:89
  64.5 0.1 copy.16
  64.6 4.0 %fusion.1 = (f32[384]{0:T(512)S(1)}, f32[384]{0:T(512)S(1)}, f32[384]{0:T(512)S(1)}) fusion(f32[384,3072]{1,0:T(8,128)} %get-tuple-element.72, f32[384]{0:T(512)S(1)} %get-tuple-element.71, s32[384]{0:T(512)S(1)} %fusion.32), kind=kLoop, calls=%fused_computation.13 | loop fusion | flops 8256384 | bytes 4726272 | tf_op jit(solution)/shard_map/reduce_sum | solution.py:92
  68.7 0.9 slice_reduce_fusion.9
  69.6 0.2 slice_reduce_fusion.8
  69.8 1.6 %pad_maximum_fusion = bf16[8,96,1664]{2,1,0:T(8,128)(2,1)S(1)} fusion(bf16[4,96,1664]{2,1,0:T(8,128)(2,1)S(1)} %collective-permute-done.5, bf16[4,96,1664]{2,1,0:T(8,128)(2,1)} %collective-permute-done.4), kind=kLoop, calls=%fused_computation.14 | loop fusion | flops 1277952 | bytes 5111808 | tf_op jit(solution)/shard_map/concatenate | solution.py:131
  71.4 12.3 %fusion.56 = (f32[768]{0:T(1024)S(1)}, f32[768,3072]{1,0:T(8,128)}) fusion(bf16[1536,3072]{1,0:T(8,128)(2,1)} %param.8, bf16[768,1664]{1,0:T(8,128)(2,1)S(1)} %bitcast.45), kind=kOutput, calls=%fused_computation.207 | convolution fusion | flops 7250115584 | bytes 21236736 | tf_op jit(solution)/shard_map/dot_general | solution.py:89
  83.7 0.9 slice_reduce_fusion.6
  84.6 0.1 maximum_convert_fusion
  84.7 0.7 gather_fusion.3
  85.3 0.6 fusion.48
  86.0 0.1 broadcast_in_dim.86
  86.1 0.1 copy.17
  86.3 6.3 %fusion = (f32[768]{0:T(1024)S(1)}, f32[768]{0:T(1024)S(1)}, f32[768]{0:T(1024)S(1)}) fusion(f32[768,3072]{1,0:T(8,128)} %get-tuple-element.80, f32[768]{0:T(1024)S(1)} %get-tuple-element.79, s32[768]{0:T(1024)S(1)} %fusion.30), kind=kLoop, calls=%fused_computation.8 | loop fusion | flops 16512768 | bytes 9452544 | tf_op jit(solution)/shard_map/reduce_sum | solution.py:92
  92.7 0.1 concatenate.21
  92.8 0.1 reshape.292
  92.9 0.6 gather_fusion.2
  93.5 0.1 gather.19
  93.6 1.3 %collective-permute-start.6 = (f32[4,1536]{1,0:T(4,128)S(1)}, f32[4,1536]{1,0:T(4,128)S(1)}, u32[]{:S(2)}, u32[]{:S(2)}) collective-permute-start(f32[4,1536]{1,0:T(4,128)S(1)} %broadcast_select_fusion), channel_id=1, source_target_pairs={{0,1},{1,0},{2,3},{3,2},{4,5},{5,4},{6,7},{7,6},{8,9},{9,8},{10,11... | collective-permute-start | bytes 73736 | tf_op jit(solution)/shard_map/ppermute | solution.py:32
  94.9 2.8 %collective-permute-done.6 = f32[4,1536]{1,0:T(4,128)S(1)} collective-permute-done((f32[4,1536]{1,0:T(4,128)S(1)}, f32[4,1536]{1,0:T(4,128)S(1)}, u32[]{:S(2)}, u32[]{:S(2)}) %collective-permute-start.6) | collective-permute-done | bytes 24608 | tf_op jit(solution)/shard_map/ppermute | solution.py:32
  97.9 2.5 %collective-permute-start.7 = (f32[4,1536]{1,0:T(4,128)S(1)}, f32[4,1536]{1,0:T(4,128)S(1)}, u32[]{:S(2)}, u32[]{:S(2)}) collective-permute-start(f32[4,1536]{1,0:T(4,128)S(1)} %pad_maximum_fusion.3), channel_id=1, source_target_pairs={{0,2},{1,3},{2,0},{3,1},{4,6},{5,7},{6,4},{7,5},{8,10},{9,11},{10,... | collective-permute-start | bytes 73736 | tf_op jit(solution)/shard_map/ppermute | solution.py:32
  100.3 2.9 %collective-permute-done.7 = f32[4,1536]{1,0:T(4,128)S(1)} collective-permute-done((f32[4,1536]{1,0:T(4,128)S(1)}, f32[4,1536]{1,0:T(4,128)S(1)}, u32[]{:S(2)}, u32[]{:S(2)}) %collective-permute-start.7) | collective-permute-done | bytes 24608 | tf_op jit(solution)/shard_map/ppermute | solution.py:32
  103.4 0.1 collective-permute-start.8
  103.5 3.8 %collective-permute-done.8 = f32[4,1536]{1,0:T(4,128)S(1)} collective-permute-done((f32[4,1536]{1,0:T(4,128)S(1)}, f32[4,1536]{1,0:T(4,128)S(1)}, u32[]{:S(2)}, u32[]{:S(2)}) %collective-permute-start.8) | collective-permute-done | bytes 24608 | tf_op jit(solution)/shard_map/ppermute | solution.py:32
  107.5 1.4 %collective-permute-start.9 = (f32[4,1536]{1,0:T(4,128)S(1)}, f32[4,1536]{1,0:T(4,128)S(1)}, u32[]{:S(2)}, u32[]{:S(2)}) collective-permute-start(f32[4,1536]{1,0:T(4,128)S(1)} %pad_maximum_fusion.5), channel_id=1, source_target_pairs={{0,8},{1,9},{2,10},{3,11},{4,12},{5,13},{6,14},{7,15},{8,0},{9,1},... | collective-permute-start | bytes 73736 | tf_op jit(solution)/shard_map/ppermute | solution.py:32
  109.6 0.1 lt.139
  109.7 3.2 %collective-permute-done.9 = f32[4,1536]{1,0:T(4,128)S(1)} collective-permute-done((f32[4,1536]{1,0:T(4,128)S(1)}, f32[4,1536]{1,0:T(4,128)S(1)}, u32[]{:S(2)}, u32[]{:S(2)}) %collective-permute-start.9) | collective-permute-done | bytes 24608 | tf_op jit(solution)/shard_map/ppermute | solution.py:32
  112.9 0.8 select_reduce_fusion.5
  113.7 0.7 pad_maximum_fusion.11
  114.5 0.2 fusion.46
  114.7 0.2 fusion.45
  114.8 0.2 select_dynamic-update-slice_fusion
  115.0 0.6 collective-permute-done.10
  115.6 0.7 fusion.37
  116.3 1.6 %collective-permute-start.11 = (f32[2]{0:T(128)S(1)}, f32[2]{0:T(128)S(1)}, u32[]{:S(2)}, u32[]{:S(2)}) collective-permute-start(f32[2]{0:T(128)S(1)} %fusion.37), channel_id=1, source_target_pairs={{0,32},{16,48},{32,0},{48,16},{64,96},{80,112},{96,64},{112,80},{1... | collective-permute-start | bytes 32 | tf_op jit(solution)/shard_map/ppermute | solution.py:32
  117.9 2.0 %collective-permute-done.11 = f32[2]{0:T(128)S(1)} collective-permute-done((f32[2]{0:T(128)S(1)}, f32[2]{0:T(128)S(1)}, u32[]{:S(2)}, u32[]{:S(2)}) %collective-permute-start.11) | collective-permute-done | bytes 40 | tf_op jit(solution)/shard_map/ppermute | solution.py:32
  119.9 3.2 %collective-permute-start.12 = (f32[2]{0:T(128)S(1)}, f32[2]{0:T(128)S(1)}, u32[]{:S(2)}, u32[]{:S(2)}) collective-permute-start(f32[2]{0:T(128)S(1)} %fusion.36), channel_id=1, source_target_pairs={{0,64},{16,80},{32,96},{48,112},{64,0},{80,16},{96,32},{112,48},{1... | collective-permute-start | bytes 32 | tf_op jit(solution)/shard_map/ppermute | solution.py:32
  123.1 1.9 %collective-permute-done.12 = f32[2]{0:T(128)S(1)} collective-permute-done((f32[2]{0:T(128)S(1)}, f32[2]{0:T(128)S(1)}, u32[]{:S(2)}, u32[]{:S(2)}) %collective-permute-start.12) | collective-permute-done | bytes 40 | tf_op jit(solution)/shard_map/ppermute | solution.py:32
  125.0 0.6 fusion.50
  (81 shorter events, 1.1 us)
Async XLA Ops:
  0.6 14.0 %copy-start = (s32[4]{0:T(128)S(1)}, s32[4]{0:T(128)}, u32[]{:S(2)}) copy-start(s32[4]{0:T(128)} %constant.170.clone) | copy-start | bytes 52
  8.4 13.9 %collective-permute-start.2 = (bf16[96,1664]{1,0:T(8,128)(2,1)S(1)}, bf16[96,1664]{1,0:T(8,128)(2,1)S(1)}, u32[]{:S(2)}, u32[]{:S(2)}) collective-permute-start(bf16[96,1664]{1,0:T(8,128)(2,1)S(1)} %get-tuple-element.50), channel_id=1, source_target_pairs={{0,2},{1,3},{2,0},{3,1},{4,6},{5,7},{6,4},{7,5},{8,10},{9,11},{10,... | collective-permute-start | bytes 958472 | tf_op jit(solution)/shard_map/ppermute | solution.py:79
  12.5 9.9 %collective-permute-start.1 = (bf16[96,1664]{1,0:T(8,128)(2,1)S(1)}, bf16[96,1664]{1,0:T(8,128)(2,1)S(1)}, u32[]{:S(2)}, u32[]{:S(2)}) collective-permute-start(bf16[96,1664]{1,0:T(8,128)(2,1)S(1)} %get-tuple-element.50), channel_id=1, source_target_pairs={{0,3},{1,0},{2,1},{3,2},{4,7},{5,4},{6,5},{7,6},{8,11},{9,8},{10,9... | collective-permute-start | bytes 958472 | tf_op jit(solution)/shard_map/ppermute | solution.py:79
  13.2 9.2 %collective-permute-start = (bf16[96,1664]{1,0:T(8,128)(2,1)S(1)}, bf16[96,1664]{1,0:T(8,128)(2,1)}, u32[]{:S(2)}, u32[]{:S(2)}) collective-permute-start(bf16[96,1664]{1,0:T(8,128)(2,1)S(1)} %get-tuple-element.50), channel_id=1, source_target_pairs={{0,1},{1,2},{2,3},{3,0},{4,5},{5,6},{6,7},{7,4},{8,9},{9,10},{10,1... | collective-permute-start | bytes 958472 | tf_op jit(solution)/shard_map/ppermute | solution.py:79
  15.3 15.9 %slice-start = ((s8[9437184]{0:T(1024)(128)(4,1)}), s8[1048576]{0:T(1024)(128)(4,1)S(1)}, s32[]{:S(2)}) async-start(s8[9437184]{0:T(1024)(128)(4,1)} %bitcast.42), calls=%async_computation | async-start | bytes 2097152
  15.9 15.2 %slice-start.1 = ((s8[9437184]{0:T(1024)(128)(4,1)}), s8[4194304]{0:T(1024)(128)(4,1)S(1)}, s32[]{:S(2)}) async-start(s8[9437184]{0:T(1024)(128)(4,1)} %bitcast.42), calls=%async_computation.1 | async-start | bytes 8388608
  16.0 15.2 %slice-start.2 = ((s8[9437184]{0:T(1024)(128)(4,1)}), s8[4194304]{0:T(1024)(128)(4,1)S(1)}, s32[]{:S(2)}) async-start(s8[9437184]{0:T(1024)(128)(4,1)} %bitcast.42), calls=%async_computation.2 | async-start | bytes 8388608
  24.7 44.0 %collective-permute-start.5 = (bf16[4,96,1664]{2,1,0:T(8,128)(2,1)}, bf16[4,96,1664]{2,1,0:T(8,128)(2,1)S(1)}, u32[]{:S(2)}, u32[]{:S(2)}) collective-permute-start(bf16[4,96,1664]{2,1,0:T(8,128)(2,1)} %pad_maximum_fusion.1), channel_id=1, source_target_pairs={{0,12},{1,13},{2,14},{3,15},{4,0},{5,1},{6,2},{7,3},{8,4},{9,5},{1... | collective-permute-start | bytes 3833864 | tf_op jit(solution)/shard_map/ppermute | solution.py:79
  27.4 41.3 %collective-permute-start.4 = (bf16[4,96,1664]{2,1,0:T(8,128)(2,1)}, bf16[4,96,1664]{2,1,0:T(8,128)(2,1)}, u32[]{:S(2)}, u32[]{:S(2)}) collective-permute-start(bf16[4,96,1664]{2,1,0:T(8,128)(2,1)} %pad_maximum_fusion.1), channel_id=1, source_target_pairs={{0,4},{1,5},{2,6},{3,7},{4,8},{5,9},{6,10},{7,11},{8,12},{9,13},{1... | collective-permute-start | bytes 3833864 | tf_op jit(solution)/shard_map/ppermute | solution.py:79
  27.4 31.5 %collective-permute-start.3 = (bf16[4,96,1664]{2,1,0:T(8,128)(2,1)}, bf16[4,96,1664]{2,1,0:T(8,128)(2,1)S(1)}, u32[]{:S(2)}, u32[]{:S(2)}) collective-permute-start(bf16[4,96,1664]{2,1,0:T(8,128)(2,1)} %pad_maximum_fusion.1), channel_id=1, source_target_pairs={{0,8},{1,9},{2,10},{3,11},{4,12},{5,13},{6,14},{7,15},{8,0},{9,1},... | collective-permute-start | bytes 3833864 | tf_op jit(solution)/shard_map/ppermute | solution.py:79
  58.9 5.6 %copy-start.1 = (bf16[4,96,1664]{2,1,0:T(8,128)(2,1)}, bf16[4,96,1664]{2,1,0:T(8,128)(2,1)S(1)}, u32[]{:S(2)}) copy-start(bf16[4,96,1664]{2,1,0:T(8,128)(2,1)S(1)} %collective-permute-done.3) | copy-start | bytes 3833860
  93.6 4.1 %collective-permute-start.6 = (f32[4,1536]{1,0:T(4,128)S(1)}, f32[4,1536]{1,0:T(4,128)S(1)}, u32[]{:S(2)}, u32[]{:S(2)}) collective-permute-start(f32[4,1536]{1,0:T(4,128)S(1)} %broadcast_select_fusion), channel_id=1, source_target_pairs={{0,1},{1,0},{2,3},{3,2},{4,5},{5,4},{6,7},{7,6},{8,9},{9,8},{10,11... | collective-permute-start | bytes 73736 | tf_op jit(solution)/shard_map/ppermute | solution.py:32
  97.9 5.4 %collective-permute-start.7 = (f32[4,1536]{1,0:T(4,128)S(1)}, f32[4,1536]{1,0:T(4,128)S(1)}, u32[]{:S(2)}, u32[]{:S(2)}) collective-permute-start(f32[4,1536]{1,0:T(4,128)S(1)} %pad_maximum_fusion.3), channel_id=1, source_target_pairs={{0,2},{1,3},{2,0},{3,1},{4,6},{5,7},{6,4},{7,5},{8,10},{9,11},{10,... | collective-permute-start | bytes 73736 | tf_op jit(solution)/shard_map/ppermute | solution.py:32
  103.4 3.9 %collective-permute-start.8 = (f32[4,1536]{1,0:T(4,128)S(1)}, f32[4,1536]{1,0:T(4,128)S(1)}, u32[]{:S(2)}, u32[]{:S(2)}) collective-permute-start(f32[4,1536]{1,0:T(4,128)S(1)} %pad_maximum_fusion.4), channel_id=1, source_target_pairs={{0,4},{1,5},{2,6},{3,7},{4,0},{5,1},{6,2},{7,3},{8,12},{9,13},{10,... | collective-permute-start | bytes 73736 | tf_op jit(solution)/shard_map/ppermute | solution.py:32
  107.5 5.4 %collective-permute-start.9 = (f32[4,1536]{1,0:T(4,128)S(1)}, f32[4,1536]{1,0:T(4,128)S(1)}, u32[]{:S(2)}, u32[]{:S(2)}) collective-permute-start(f32[4,1536]{1,0:T(4,128)S(1)} %pad_maximum_fusion.5), channel_id=1, source_target_pairs={{0,8},{1,9},{2,10},{3,11},{4,12},{5,13},{6,14},{7,15},{8,0},{9,1},... | collective-permute-start | bytes 73736 | tf_op jit(solution)/shard_map/ppermute | solution.py:32
  114.4 1.2 collective-permute-start.10
  114.6 12.3 %copy-start.3 = (f32[128]{0:T(128)}, f32[128]{0:T(128)S(1)}, u32[]{:S(2)}) copy-start(f32[128]{0:T(128)S(1)} %fusion.46) | copy-start | bytes 1540
  114.8 12.1 %copy-start.4 = (f32[128]{0:T(128)}, f32[128]{0:T(128)S(1)}, u32[]{:S(2)}) copy-start(f32[128]{0:T(128)S(1)} %fusion.45) | copy-start | bytes 1540
  115.0 12.0 %copy-start.2 = (f32[128]{0:T(128)}, f32[128]{0:T(128)S(1)}, u32[]{:S(2)}) copy-start(f32[128]{0:T(128)S(1)} %select_dynamic-update-slice_fusion) | copy-start | bytes 1540
  116.3 3.6 %collective-permute-start.11 = (f32[2]{0:T(128)S(1)}, f32[2]{0:T(128)S(1)}, u32[]{:S(2)}, u32[]{:S(2)}) collective-permute-start(f32[2]{0:T(128)S(1)} %fusion.37), channel_id=1, source_target_pairs={{0,32},{16,48},{32,0},{48,16},{64,96},{80,112},{96,64},{112,80},{1... | collective-permute-start | bytes 32 | tf_op jit(solution)/shard_map/ppermute | solution.py:32
  119.9 5.1 %collective-permute-start.12 = (f32[2]{0:T(128)S(1)}, f32[2]{0:T(128)S(1)}, u32[]{:S(2)}, u32[]{:S(2)}) collective-permute-start(f32[2]{0:T(128)S(1)} %fusion.36), channel_id=1, source_target_pairs={{0,64},{16,80},{32,96},{48,112},{64,0},{80,16},{96,32},{112,48},{1... | collective-permute-start | bytes 32 | tf_op jit(solution)/shard_map/ppermute | solution.py:32

commit v11 on v9

--- a/solution.py
+++ b/solution.py
@@ -122,13 +122,14 @@
     far = shift(own, 0, 2, reqs, vocs)
     part_near = stats(jnp.concatenate([left, right]))
     line = jnp.stack([own, left, right, far])
-    line_left = shift(line, 1, 1, reqs, vocs)
-    line_right = shift(line, 1, -1, reqs, vocs)
+    halves = lambda step: jnp.concatenate(
+        [shift(line[:, :HALF], 1, step, reqs, vocs), shift(line[:, HALF:], 1, step, reqs, vocs)], axis=1
+    )
+    line_left = halves(1)
+    line_right = halves(-1)
     part_far = stats(far)
-    line_far_a = shift(line_left[:, :HALF], 1, 1, reqs, vocs)
-    line_far_b = shift(line_right[:, HALF:], 1, -1, reqs, vocs)
+    line_far = halves(2)
     part_lines = stats(jnp.concatenate([line_left, line_right]).reshape(-1, own.shape[1]))
-    line_far = jnp.concatenate([line_far_a, line_far_b], axis=1)
     part_line_far = stats(line_far.reshape(-1, own.shape[1]))
     processed = jnp.concatenate([part_own, part_near, part_far, part_lines, part_line_far], axis=1)
     processed = processed.reshape(4, vocs, LIVE)

time: 120 us -> 115 us (0.958)
  starting transfers between devices: 21.4 us -> 26.7 us
  waiting for transfers between devices: 31.6 us -> 27.4 us
  matrix products: 29.4 us -> 25.2 us
  local copies, waits for them, and re-layouts: 8.76 us -> 6.69 us
    dot_general x5, matrix products: 29.4 us -> 25.2 us  [block_stats(): logits = jnp.dot(rows_in, head, preferred_element_type=jnp.float32)]
    ppermute x7 -> x9, starting transfers between devices: 11.3 us -> 14.8 us  [shift(): return lax.ppermute(value, AXES, pairs)]
    ppermute x7 -> x9, waiting for transfers between devices: 14.5 us -> 12.2 us  [shift(): return lax.ppermute(value, AXES, pairs)]
    ppermute x7, waiting for transfers between devices: 17 us -> 15.2 us  [butterfly(): other = lax.ppermute(value, axis, [(i, i ^ step) for i in range(size)])]
    ppermute x7, starting transfers between devices: 10.1 us -> 11.9 us  [butterfly(): other = lax.ppermute(value, axis, [(i, i ^ step) for i in range(size)])]
  transfers between devices with their start and end apart: 14 -> 16, of which waited for: 10 -> 9; matrix products, arithmetic and copies ran while one was open for 19% -> 18% of each run, Pallas kernels for 0% -> 0%
where the time goes in v11:
time: 115 us; the launch traced here: 114 us
  waiting for transfers between devices  27.4 us (24%)
  starting transfers between devices  26.7 us (23%)
  matrix products  25.2 us (22%)
  other arithmetic  20.9 us (18%)
  between operations  7.58 us (7%)
  local copies, waits for them, and re-layouts  6.69 us (6%)
    dot_general x5, matrix products, block_stats(): logits = jnp.dot(rows_in, head, preferred_element_type=jnp.float32)  25.2 us
    ppermute x7, waiting for transfers between devices, butterfly(): other = lax.ppermute(value, axis, [(i, i ^ step) for i in range(size)])  15.2 us
    ppermute x9, starting transfers between devices, shift(): return lax.ppermute(value, AXES, pairs)  14.8 us
    reduce_sum x5, other arithmetic, block_stats(): total = jnp.sum(expo, axis=-1)  12.3 us
    ppermute x9, waiting for transfers between devices, shift(): return lax.ppermute(value, AXES, pairs)  12.2 us
    ppermute x7, starting transfers between devices, butterfly(): other = lax.ppermute(value, axis, [(i, i ^ step) for i in range(size)])  11.9 us
  transfers between devices with their start and end apart: 16, of which 9 were waited for; matrix products, arithmetic and copies ran while one was open for 18% of the time, Pallas kernels for 0%

profile of v11, /device:TPU:0, one launch (start us, length us, event | category | flops | bytes accessed | tf_op | source)
XLA Modules:
  0.0 114.5 jit_solution(13007761809938101652)
XLA Ops:
  0.7 1.3 %fusion.52 = (s32[1,1]{1,0:T(1,128)}, s32[1,1]{1,0:T(1,128)}) fusion(s32[1,2]{1,0:T(1,128)} %param.10), kind=kLoop, calls=%fused_computation.204 | loop fusion | bytes 16 | tf_op jit(solution)/shard_map/slice | solution.py:106
  5.2 1.2 %fusion.9 = f32[96]{0:T(128)S(1)} fusion(bf16[128,1536]{1,0:T(8,128)(2,1)} %param.6, s32[]{:T(128)S(6)} %select_n.329), kind=kLoop, calls=%fused_computation.38 | loop fusion | flops 442272 | bytes 295300 | tf_op jit(solution)/shard_map/reduce_sum | solution.py:110
  6.4 0.7 and_select_fusion.1
  7.2 1.1 fusion.11
  8.3 0.1 select_convert_fusion
  8.4 4.1 %collective-permute-start.2 = (bf16[96,1664]{1,0:T(8,128)(2,1)S(1)}, bf16[96,1664]{1,0:T(8,128)(2,1)S(1)}, u32[]{:S(2)}, u32[]{:S(2)}) collective-permute-start(bf16[96,1664]{1,0:T(8,128)(2,1)S(1)} %get-tuple-element.46), channel_id=1, source_target_pairs={{0,2},{1,3},{2,0},{3,1},{4,6},{5,7},{6,4},{7,5},{8,10},{9,11},{10,... | collective-permute-start | bytes 958472 | tf_op jit(solution)/shard_map/ppermute | solution.py:79
  12.5 0.7 collective-permute-start.1
  13.2 1.3 %collective-permute-start = (bf16[96,1664]{1,0:T(8,128)(2,1)S(1)}, bf16[96,1664]{1,0:T(8,128)(2,1)S(1)}, u32[]{:S(2)}, u32[]{:S(2)}) collective-permute-start(bf16[96,1664]{1,0:T(8,128)(2,1)S(1)} %get-tuple-element.46), channel_id=1, source_target_pairs={{0,1},{1,2},{2,3},{3,0},{4,5},{5,6},{6,7},{7,4},{8,9},{9,10},{10,1... | collective-permute-start | bytes 958472 | tf_op jit(solution)/shard_map/ppermute | solution.py:79
  14.6 1.3 %gather_fusion = s32[16]{0:T(128)S(1)} fusion(s32[4]{0:T(128)} %constant.170.clone, s32[1024]{0:T(1024)S(1)} %pad_clamp_fusion.2), kind=kCustom, calls=%fused_computation | custom fusion | bytes 192 | tf_op jit(solution)/shard_map/gather | solution.py:147
  15.9 0.7 gather_fusion.1
  16.6 5.6 %fusion.53 = (f32[96]{0:T(128)S(1)}, f32[96,3072]{1,0:T(8,128)S(1)}) fusion(bf16[96,1536]{1,0:T(8,128)(2,1)S(1)} %fusion.11, bf16[1536,3072]{1,0:T(8,128)(2,1)} %param.8), kind=kOutput, calls=%fused_computation.205 | convolution fusion | flops 906264448 | bytes 10912128 | tf_op jit(solution)/shard_map/dot_general | solution.py:89
  22.3 0.2 fusion.21
  22.5 0.5 fusion.8
  23.1 0.2 maximum_reduce_fusion
  23.2 0.2 pad_maximum_fusion
  23.4 0.1 fusion.50
  23.5 3.1 %collective-permute-start.7 = (bf16[4,48,1664]{2,1,0:T(8,128)(2,1)S(1)}, bf16[4,48,1664]{2,1,0:T(8,128)(2,1)S(1)}, u32[]{:S(2)}, u32[]{:S(2)}) collective-permute-start(bf16[4,48,1664]{2,1,0:T(8,128)(2,1)S(1)} %get-tuple-element.43), channel_id=1, source_target_pairs={{0,8},{1,9},{2,10},{3,11},{4,12},{5,13},{6,14},{7,15},{8,0},{9,1},... | collective-permute-start | bytes 1916936 | tf_op jit(solution)/shard_map/ppermute | solution.py:79
  26.6 1.2 %collective-permute-start.5 = (bf16[4,48,1664]{2,1,0:T(8,128)(2,1)S(1)}, bf16[4,48,1664]{2,1,0:T(8,128)(2,1)S(1)}, u32[]{:S(2)}, u32[]{:S(2)}) collective-permute-start(bf16[4,48,1664]{2,1,0:T(8,128)(2,1)S(1)} %get-tuple-element.43), channel_id=1, source_target_pairs={{0,12},{1,13},{2,14},{3,15},{4,0},{5,1},{6,2},{7,3},{8,4},{9,5},{1... | collective-permute-start | bytes 1916936 | tf_op jit(solution)/shard_map/ppermute | solution.py:79
  27.8 0.9 collective-permute-start.3
  28.7 0.6 collective-permute-start.8
  29.3 2.6 %collective-permute-start.6 = (bf16[4,48,1664]{2,1,0:T(8,128)(2,1)S(1)}, bf16[4,48,1664]{2,1,0:T(8,128)(2,1)S(1)}, u32[]{:S(2)}, u32[]{:S(2)}) collective-permute-start(bf16[4,48,1664]{2,1,0:T(8,128)(2,1)S(1)} %get-tuple-element.44), channel_id=1, source_target_pairs={{0,12},{1,13},{2,14},{3,15},{4,0},{5,1},{6,2},{7,3},{8,4},{9,5},{1... | collective-permute-start | bytes 1916936 | tf_op jit(solution)/shard_map/ppermute | solution.py:79
  32.1 2.1 %fusion.54 = (f32[192]{0:T(256)S(1)}, f32[192,3072]{1,0:T(8,128)S(1)}) fusion(bf16[1536,3072]{1,0:T(8,128)(2,1)S(1)} %bitcast.43, bf16[192,1664]{1,0:T(8,128)(2,1)S(1)} %constant_dynamic-update-slice_fusion), kind=kOutput, calls=%fused_computation.206 | convolution fusion | flops 1812528896 | bytes 12387072 | tf_op jit(solution)/shard_map/dot_general | solution.py:89
  34.2 0.2 fusion.19
  34.4 1.8 %fusion.55 = (f32[96]{0:T(128)S(1)}, f32[96,3072]{1,0:T(8,128)S(1)}) fusion(bf16[1536,3072]{1,0:T(8,128)(2,1)S(1)} %bitcast.43, bf16[96,1664]{1,0:T(8,128)(2,1)S(1)} %collective-permute-done.2), kind=kOutput, calls=%fused_computation.207 | convolution fusion | flops 906264448 | bytes 10912128 | tf_op jit(solution)/shard_map/dot_general | solution.py:89
  36.2 0.5 fusion.7
  36.7 0.2 fusion.17
  36.9 1.0 fusion.4
  37.9 0.3 collective-permute-start.4
  38.2 11.2 %collective-permute-done.8 = bf16[4,48,1664]{2,1,0:T(8,128)(2,1)S(1)} collective-permute-done((bf16[4,48,1664]{2,1,0:T(8,128)(2,1)S(1)}, bf16[4,48,1664]{2,1,0:T(8,128)(2,1)S(1)}, u32[]{:S(2)}, u32[]{:S(2)}) %collective-permute-start.8) | collective-permute-done | bytes 639008 | tf_op jit(solution)/shard_map/ppermute | solution.py:79
  49.4 0.1 pad_maximum_fusion.1
  49.5 5.7 %fusion.57 = (f32[384]{0:T(512)S(1)}, f32[384,3072]{1,0:T(8,128)}) fusion(bf16[1536,3072]{1,0:T(8,128)(2,1)S(1)} %bitcast.43, bf16[384,1664]{1,0:T(8,128)(2,1)S(1)} %bitcast.53), kind=kOutput, calls=%fused_computation.209 | convolution fusion | flops 3625057792 | bytes 15336960 | tf_op jit(solution)/shard_map/dot_general | solution.py:89
  55.2 1.0 collective-permute-done.6
  56.2 0.2 maximum_maximum_fusion
  56.5 9.9 %fusion.56 = (f32[768]{0:T(1024)S(1)}, f32[768,3072]{1,0:T(8,128)}) fusion(bf16[1536,3072]{1,0:T(8,128)(2,1)S(1)} %bitcast.43, bf16[768,1664]{1,0:T(8,128)(2,1)S(1)} %bitcast.47), kind=kOutput, calls=%fused_computation.208 | convolution fusion | flops 7250115584 | bytes 21236736 | tf_op jit(solution)/shard_map/dot_general | solution.py:89
  66.4 0.2 slice_reduce_fusion.6
  66.6 0.2 slice_reduce_fusion.7
  66.8 0.2 slice_reduce_fusion.8
  67.0 0.7 gather_fusion.3
  67.7 0.6 fusion.48
  68.7 0.1 copy.16
  68.8 4.0 %fusion.1 = (f32[384]{0:T(512)S(1)}, f32[384]{0:T(512)S(1)}, f32[384]{0:T(512)S(1)}) fusion(f32[384,3072]{1,0:T(8,128)} %get-tuple-element.76, f32[384]{0:T(512)S(1)} %get-tuple-element.75, s32[384]{0:T(512)S(1)} %fusion.32), kind=kLoop, calls=%fused_computation.13 | loop fusion | flops 8256384 | bytes 4726272 | tf_op jit(solution)/shard_map/reduce_sum | solution.py:92
  72.9 6.3 %fusion = (f32[768]{0:T(1024)S(1)}, f32[768]{0:T(1024)S(1)}, f32[768]{0:T(1024)S(1)}) fusion(f32[768,3072]{1,0:T(8,128)} %get-tuple-element.74, f32[768]{0:T(1024)S(1)} %get-tuple-element.73, s32[768]{0:T(1024)S(1)} %fusion.30), kind=kLoop, calls=%fused_computation.8 | loop fusion | flops 16512768 | bytes 9452544 | tf_op jit(solution)/shard_map/reduce_sum | solution.py:92
  79.3 0.1 concatenate.33
  79.5 0.6 gather_fusion.2
  80.2 1.1 collective-permute-start.9
  81.3 2.8 %collective-permute-done.9 = f32[4,1536]{1,0:T(4,128)S(1)} collective-permute-done((f32[4,1536]{1,0:T(4,128)S(1)}, f32[4,1536]{1,0:T(4,128)S(1)}, u32[]{:S(2)}, u32[]{:S(2)}) %collective-permute-start.9) | collective-permute-done | bytes 24608 | tf_op jit(solution)/shard_map/ppermute | solution.py:32
  84.2 1.5 %collective-permute-start.10 = (f32[4,1536]{1,0:T(4,128)S(1)}, f32[4,1536]{1,0:T(4,128)S(1)}, u32[]{:S(2)}, u32[]{:S(2)}) collective-permute-start(f32[4,1536]{1,0:T(4,128)S(1)} %pad_maximum_fusion.3), channel_id=1, source_target_pairs={{0,2},{1,3},{2,0},{3,1},{4,6},{5,7},{6,4},{7,5},{8,10},{9,11},{10,... | collective-permute-start | bytes 73736 | tf_op jit(solution)/shard_map/ppermute | solution.py:32
  85.7 4.0 %collective-permute-done.10 = f32[4,1536]{1,0:T(4,128)S(1)} collective-permute-done((f32[4,1536]{1,0:T(4,128)S(1)}, f32[4,1536]{1,0:T(4,128)S(1)}, u32[]{:S(2)}, u32[]{:S(2)}) %collective-permute-start.10) | collective-permute-done | bytes 24608 | tf_op jit(solution)/shard_map/ppermute | solution.py:32
  89.8 1.5 %collective-permute-start.11 = (f32[4,1536]{1,0:T(4,128)S(1)}, f32[4,1536]{1,0:T(4,128)S(1)}, u32[]{:S(2)}, u32[]{:S(2)}) collective-permute-start(f32[4,1536]{1,0:T(4,128)S(1)} %pad_maximum_fusion.4), channel_id=1, source_target_pairs={{0,4},{1,5},{2,6},{3,7},{4,0},{5,1},{6,2},{7,3},{8,12},{9,13},{10,... | collective-permute-start | bytes 73736 | tf_op jit(solution)/shard_map/ppermute | solution.py:32
  91.3 2.4 %collective-permute-done.11 = f32[4,1536]{1,0:T(4,128)S(1)} collective-permute-done((f32[4,1536]{1,0:T(4,128)S(1)}, f32[4,1536]{1,0:T(4,128)S(1)}, u32[]{:S(2)}, u32[]{:S(2)}) %collective-permute-start.11) | collective-permute-done | bytes 24608 | tf_op jit(solution)/shard_map/ppermute | solution.py:32
  93.9 3.1 %collective-permute-start.12 = (f32[4,1536]{1,0:T(4,128)S(1)}, f32[4,1536]{1,0:T(4,128)S(1)}, u32[]{:S(2)}, u32[]{:S(2)}) collective-permute-start(f32[4,1536]{1,0:T(4,128)S(1)} %pad_maximum_fusion.5), channel_id=1, source_target_pairs={{0,8},{1,9},{2,10},{3,11},{4,12},{5,13},{6,14},{7,15},{8,0},{9,1},... | collective-permute-start | bytes 73736 | tf_op jit(solution)/shard_map/ppermute | solution.py:32
  97.7 1.5 %collective-permute-done.12 = f32[4,1536]{1,0:T(4,128)S(1)} collective-permute-done((f32[4,1536]{1,0:T(4,128)S(1)}, f32[4,1536]{1,0:T(4,128)S(1)}, u32[]{:S(2)}, u32[]{:S(2)}) %collective-permute-start.12) | collective-permute-done | bytes 24608 | tf_op jit(solution)/shard_map/ppermute | solution.py:32
  99.3 0.8 select_reduce_fusion.5
  100.1 0.7 pad_maximum_fusion.11
  100.8 0.2 fusion.46
  101.0 0.2 fusion.45
  101.2 0.2 select_dynamic-update-slice_fusion
  101.4 0.6 collective-permute-done.13
  102.0 0.7 fusion.37
  102.7 1.6 %collective-permute-start.14 = (f32[2]{0:T(128)S(1)}, f32[2]{0:T(128)S(1)}, u32[]{:S(2)}, u32[]{:S(2)}) collective-permute-start(f32[2]{0:T(128)S(1)} %fusion.37), channel_id=1, source_target_pairs={{0,32},{16,48},{32,0},{48,16},{64,96},{80,112},{96,64},{112,80},{1... | collective-permute-start | bytes 32 | tf_op jit(solution)/shard_map/ppermute | solution.py:32
  104.3 2.0 %collective-permute-done.14 = f32[2]{0:T(128)S(1)} collective-permute-done((f32[2]{0:T(128)S(1)}, f32[2]{0:T(128)S(1)}, u32[]{:S(2)}, u32[]{:S(2)}) %collective-permute-start.14) | collective-permute-done | bytes 40 | tf_op jit(solution)/shard_map/ppermute | solution.py:32
  106.3 3.2 %collective-permute-start.15 = (f32[2]{0:T(128)S(1)}, f32[2]{0:T(128)S(1)}, u32[]{:S(2)}, u32[]{:S(2)}) collective-permute-start(f32[2]{0:T(128)S(1)} %fusion.36), channel_id=1, source_target_pairs={{0,64},{16,80},{32,96},{48,112},{64,0},{80,16},{96,32},{112,48},{1... | collective-permute-start | bytes 32 | tf_op jit(solution)/shard_map/ppermute | solution.py:32
  109.5 1.9 %collective-permute-done.15 = f32[2]{0:T(128)S(1)} collective-permute-done((f32[2]{0:T(128)S(1)}, f32[2]{0:T(128)S(1)}, u32[]{:S(2)}, u32[]{:S(2)}) %collective-permute-start.15) | collective-permute-done | bytes 40 | tf_op jit(solution)/shard_map/ppermute | solution.py:32
  111.3 0.6 fusion.51
  (87 shorter events, 1.7 us)
Async XLA Ops:
  0.6 15.3 %copy-start = (s32[4]{0:T(128)S(1)}, s32[4]{0:T(128)}, u32[]{:S(2)}) copy-start(s32[4]{0:T(128)} %constant.170.clone) | copy-start | bytes 52
  8.4 14.6 %collective-permute-start.2 = (bf16[96,1664]{1,0:T(8,128)(2,1)S(1)}, bf16[96,1664]{1,0:T(8,128)(2,1)S(1)}, u32[]{:S(2)}, u32[]{:S(2)}) collective-permute-start(bf16[96,1664]{1,0:T(8,128)(2,1)S(1)} %get-tuple-element.46), channel_id=1, source_target_pairs={{0,2},{1,3},{2,0},{3,1},{4,6},{5,7},{6,4},{7,5},{8,10},{9,11},{10,... | collective-permute-start | bytes 958472 | tf_op jit(solution)/shard_map/ppermute | solution.py:79
  12.5 10.5 %collective-permute-start.1 = (bf16[96,1664]{1,0:T(8,128)(2,1)S(1)}, bf16[96,1664]{1,0:T(8,128)(2,1)S(1)}, u32[]{:S(2)}, u32[]{:S(2)}) collective-permute-start(bf16[96,1664]{1,0:T(8,128)(2,1)S(1)} %get-tuple-element.46), channel_id=1, source_target_pairs={{0,3},{1,0},{2,1},{3,2},{4,7},{5,4},{6,5},{7,6},{8,11},{9,8},{10,9... | collective-permute-start | bytes 958472 | tf_op jit(solution)/shard_map/ppermute | solution.py:79
  13.2 9.8 %collective-permute-start = (bf16[96,1664]{1,0:T(8,128)(2,1)S(1)}, bf16[96,1664]{1,0:T(8,128)(2,1)S(1)}, u32[]{:S(2)}, u32[]{:S(2)}) collective-permute-start(bf16[96,1664]{1,0:T(8,128)(2,1)S(1)} %get-tuple-element.46), channel_id=1, source_target_pairs={{0,1},{1,2},{2,3},{3,0},{4,5},{5,6},{6,7},{7,4},{8,9},{9,10},{10,1... | collective-permute-start | bytes 958472 | tf_op jit(solution)/shard_map/ppermute | solution.py:79
  16.6 15.4 %slice-start = ((s8[9437184]{0:T(1024)(128)(4,1)}), s8[4194304]{0:T(1024)(128)(4,1)S(1)}, s32[]{:S(2)}) async-start(s8[9437184]{0:T(1024)(128)(4,1)} %bitcast.42), calls=%async_computation | async-start | bytes 8388608
  16.6 15.4 %slice-start.1 = ((s8[9437184]{0:T(1024)(128)(4,1)}), s8[4194304]{0:T(1024)(128)(4,1)S(1)}, s32[]{:S(2)}) async-start(s8[9437184]{0:T(1024)(128)(4,1)} %bitcast.42), calls=%async_computation.1 | async-start | bytes 8388608
  22.5 9.6 %slice-start.2 = ((s8[9437184]{0:T(1024)(128)(4,1)}), s8[1048576]{0:T(1024)(128)(4,1)S(1)}, s32[]{:S(2)}) async-start(s8[9437184]{0:T(1024)(128)(4,1)} %bitcast.42), calls=%async_computation.2 | async-start | bytes 2097152
  23.5 14.4 %collective-permute-start.7 = (bf16[4,48,1664]{2,1,0:T(8,128)(2,1)S(1)}, bf16[4,48,1664]{2,1,0:T(8,128)(2,1)S(1)}, u32[]{:S(2)}, u32[]{:S(2)}) collective-permute-start(bf16[4,48,1664]{2,1,0:T(8,128)(2,1)S(1)} %get-tuple-element.43), channel_id=1, source_target_pairs={{0,8},{1,9},{2,10},{3,11},{4,12},{5,13},{6,14},{7,15},{8,0},{9,1},... | collective-permute-start | bytes 1916936 | tf_op jit(solution)/shard_map/ppermute | solution.py:79
  26.6 28.6 %collective-permute-start.5 = (bf16[4,48,1664]{2,1,0:T(8,128)(2,1)S(1)}, bf16[4,48,1664]{2,1,0:T(8,128)(2,1)S(1)}, u32[]{:S(2)}, u32[]{:S(2)}) collective-permute-start(bf16[4,48,1664]{2,1,0:T(8,128)(2,1)S(1)} %get-tuple-element.43), channel_id=1, source_target_pairs={{0,12},{1,13},{2,14},{3,15},{4,0},{5,1},{6,2},{7,3},{8,4},{9,5},{1... | collective-permute-start | bytes 1916936 | tf_op jit(solution)/shard_map/ppermute | solution.py:79
  27.8 27.4 %collective-permute-start.3 = (bf16[4,48,1664]{2,1,0:T(8,128)(2,1)S(1)}, bf16[4,48,1664]{2,1,0:T(8,128)(2,1)S(1)}, u32[]{:S(2)}, u32[]{:S(2)}) collective-permute-start(bf16[4,48,1664]{2,1,0:T(8,128)(2,1)S(1)} %get-tuple-element.43), channel_id=1, source_target_pairs={{0,4},{1,5},{2,6},{3,7},{4,8},{5,9},{6,10},{7,11},{8,12},{9,13},{1... | collective-permute-start | bytes 1916936 | tf_op jit(solution)/shard_map/ppermute | solution.py:79
  28.7 20.7 %collective-permute-start.8 = (bf16[4,48,1664]{2,1,0:T(8,128)(2,1)S(1)}, bf16[4,48,1664]{2,1,0:T(8,128)(2,1)S(1)}, u32[]{:S(2)}, u32[]{:S(2)}) collective-permute-start(bf16[4,48,1664]{2,1,0:T(8,128)(2,1)S(1)} %get-tuple-element.44), channel_id=1, source_target_pairs={{0,8},{1,9},{2,10},{3,11},{4,12},{5,13},{6,14},{7,15},{8,0},{9,1},... | collective-permute-start | bytes 1916936 | tf_op jit(solution)/shard_map/ppermute | solution.py:79
  29.3 26.9 %collective-permute-start.6 = (bf16[4,48,1664]{2,1,0:T(8,128)(2,1)S(1)}, bf16[4,48,1664]{2,1,0:T(8,128)(2,1)S(1)}, u32[]{:S(2)}, u32[]{:S(2)}) collective-permute-start(bf16[4,48,1664]{2,1,0:T(8,128)(2,1)S(1)} %get-tuple-element.44), channel_id=1, source_target_pairs={{0,12},{1,13},{2,14},{3,15},{4,0},{5,1},{6,2},{7,3},{8,4},{9,5},{1... | collective-permute-start | bytes 1916936 | tf_op jit(solution)/shard_map/ppermute | solution.py:79
  37.9 18.3 %collective-permute-start.4 = (bf16[4,48,1664]{2,1,0:T(8,128)(2,1)S(1)}, bf16[4,48,1664]{2,1,0:T(8,128)(2,1)S(1)}, u32[]{:S(2)}, u32[]{:S(2)}) collective-permute-start(bf16[4,48,1664]{2,1,0:T(8,128)(2,1)S(1)} %get-tuple-element.44), channel_id=1, source_target_pairs={{0,4},{1,5},{2,6},{3,7},{4,8},{5,9},{6,10},{7,11},{8,12},{9,13},{1... | collective-permute-start | bytes 1916936 | tf_op jit(solution)/shard_map/ppermute | solution.py:79
  80.2 3.9 %collective-permute-start.9 = (f32[4,1536]{1,0:T(4,128)S(1)}, f32[4,1536]{1,0:T(4,128)S(1)}, u32[]{:S(2)}, u32[]{:S(2)}) collective-permute-start(f32[4,1536]{1,0:T(4,128)S(1)} %broadcast_select_fusion), channel_id=1, source_target_pairs={{0,1},{1,0},{2,3},{3,2},{4,5},{5,4},{6,7},{7,6},{8,9},{9,8},{10,11... | collective-permute-start | bytes 73736 | tf_op jit(solution)/shard_map/ppermute | solution.py:32
  84.2 5.4 %collective-permute-start.10 = (f32[4,1536]{1,0:T(4,128)S(1)}, f32[4,1536]{1,0:T(4,128)S(1)}, u32[]{:S(2)}, u32[]{:S(2)}) collective-permute-start(f32[4,1536]{1,0:T(4,128)S(1)} %pad_maximum_fusion.3), channel_id=1, source_target_pairs={{0,2},{1,3},{2,0},{3,1},{4,6},{5,7},{6,4},{7,5},{8,10},{9,11},{10,... | collective-permute-start | bytes 73736 | tf_op jit(solution)/shard_map/ppermute | solution.py:32
  89.8 3.9 %collective-permute-start.11 = (f32[4,1536]{1,0:T(4,128)S(1)}, f32[4,1536]{1,0:T(4,128)S(1)}, u32[]{:S(2)}, u32[]{:S(2)}) collective-permute-start(f32[4,1536]{1,0:T(4,128)S(1)} %pad_maximum_fusion.4), channel_id=1, source_target_pairs={{0,4},{1,5},{2,6},{3,7},{4,0},{5,1},{6,2},{7,3},{8,12},{9,13},{10,... | collective-permute-start | bytes 73736 | tf_op jit(solution)/shard_map/ppermute | solution.py:32
  93.9 5.4 %collective-permute-start.12 = (f32[4,1536]{1,0:T(4,128)S(1)}, f32[4,1536]{1,0:T(4,128)S(1)}, u32[]{:S(2)}, u32[]{:S(2)}) collective-permute-start(f32[4,1536]{1,0:T(4,128)S(1)} %pad_maximum_fusion.5), channel_id=1, source_target_pairs={{0,8},{1,9},{2,10},{3,11},{4,12},{5,13},{6,14},{7,15},{8,0},{9,1},... | collective-permute-start | bytes 73736 | tf_op jit(solution)/shard_map/ppermute | solution.py:32
  100.8 1.2 %collective-permute-start.13 = (f32[2]{0:T(128)S(1)}, f32[2]{0:T(128)S(1)}, u32[]{:S(2)}, u32[]{:S(2)}) collective-permute-start(f32[2]{0:T(128)S(1)} %pad_maximum_fusion.11), channel_id=1, source_target_pairs={{0,16},{16,0},{32,48},{48,32},{64,80},{80,64},{96,112},{112,96},{1... | collective-permute-start | bytes 32 | tf_op jit(solution)/shard_map/ppermute | solution.py:32
  101.0 12.3 %copy-start.2 = (f32[128]{0:T(128)}, f32[128]{0:T(128)S(1)}, u32[]{:S(2)}) copy-start(f32[128]{0:T(128)S(1)} %fusion.46) | copy-start | bytes 1540
  101.2 12.1 %copy-start.3 = (f32[128]{0:T(128)}, f32[128]{0:T(128)S(1)}, u32[]{:S(2)}) copy-start(f32[128]{0:T(128)S(1)} %fusion.45) | copy-start | bytes 1540
  101.4 12.0 %copy-start.1 = (f32[128]{0:T(128)}, f32[128]{0:T(128)S(1)}, u32[]{:S(2)}) copy-start(f32[128]{0:T(128)S(1)} %select_dynamic-update-slice_fusion) | copy-start | bytes 1540
  102.7 3.6 %collective-permute-start.14 = (f32[2]{0:T(128)S(1)}, f32[2]{0:T(128)S(1)}, u32[]{:S(2)}, u32[]{:S(2)}) collective-permute-start(f32[2]{0:T(128)S(1)} %fusion.37), channel_id=1, source_target_pairs={{0,32},{16,48},{32,0},{48,16},{64,96},{80,112},{96,64},{112,80},{1... | collective-permute-start | bytes 32 | tf_op jit(solution)/shard_map/ppermute | solution.py:32
  106.3 5.1 %collective-permute-start.15 = (f32[2]{0:T(128)S(1)}, f32[2]{0:T(128)S(1)}, u32[]{:S(2)}, u32[]{:S(2)}) collective-permute-start(f32[2]{0:T(128)S(1)} %fusion.36), channel_id=1, source_target_pairs={{0,64},{16,80},{32,96},{48,112},{64,0},{80,16},{96,32},{112,48},{1... | collective-permute-start | bytes 32 | tf_op jit(solution)/shard_map/ppermute | solution.py:32

commit v12 on v11

--- a/solution.py
+++ b/solution.py
@@ -116,26 +116,30 @@
     own = jnp.concatenate([normed, meta.astype(jnp.bfloat16)], axis=1)
 
     stats = lambda block: block_stats(block, head, position)
+    flat = lambda blocks: blocks.reshape(-1, own.shape[1])
     left = shift(own, 0, 1, reqs, vocs)
     right = shift(own, 0, -1, reqs, vocs)
+    far = shift(own, 0, 2, reqs, vocs)
+    own_left = shift(own, 1, 1, reqs, vocs)
+    own_right = shift(own, 1, -1, reqs, vocs)
+    own_far = shift(own, 1, 2, reqs, vocs)
     part_own = stats(own)
-    far = shift(own, 0, 2, reqs, vocs)
-    part_near = stats(jnp.concatenate([left, right]))
-    line = jnp.stack([own, left, right, far])
+    rest = jnp.stack([left, right, far])
     halves = lambda step: jnp.concatenate(
-        [shift(line[:, :HALF], 1, step, reqs, vocs), shift(line[:, HALF:], 1, step, reqs, vocs)], axis=1
+        [shift(rest[:, :HALF], 1, step, reqs, vocs), shift(rest[:, HALF:], 1, step, reqs, vocs)], axis=1
     )
-    line_left = halves(1)
-    line_right = halves(-1)
-    part_far = stats(far)
-    line_far = halves(2)
-    part_lines = stats(jnp.concatenate([line_left, line_right]).reshape(-1, own.shape[1]))
-    part_line_far = stats(line_far.reshape(-1, own.shape[1]))
-    processed = jnp.concatenate([part_own, part_near, part_far, part_lines, part_line_far], axis=1)
+    rest_left = halves(1)
+    rest_right = halves(-1)
+    rest_far = halves(2)
+    early = jnp.stack([left, right, far, own_left, own_right, own_far])
+    part_early = stats(flat(early))
+    part_rest_far = stats(flat(rest_far))
+    part_rest_sides = stats(flat(jnp.concatenate([rest_left, rest_right])))
+    processed = jnp.concatenate([part_own, part_early, part_rest_sides, part_rest_far], axis=1)
     processed = processed.reshape(4, vocs, LIVE)
     count_of = lambda block: block[..., :1, width + 2].reshape(-1).astype(jnp.int32)
     processed_counts = jnp.concatenate(
-        [count_of(line), count_of(line_left), count_of(line_right), count_of(line_far)]
+        [count_of(own), count_of(early), count_of(rest_left), count_of(rest_right), count_of(rest_far)]
     )
 
     source = jnp.arange(vocs, dtype=jnp.int32)
@@ -144,7 +148,8 @@
     my_b = jnp.where(core == 0, position // SIDE, position % SIDE)
     src_a = jnp.where(core == 0, source % SIDE, source // SIDE)
     src_b = jnp.where(core == 0, source // SIDE, source % SIDE)
-    where_is = slot_of[(src_b - my_b) % SIDE] * SIDE + slot_of[(src_a - my_a) % SIDE]
+    order = jnp.array([[0, 1, 2, 3], [4, 7, 8, 9], [5, 10, 11, 12], [6, 13, 14, 15]], jnp.int32)
+    where_is = order[slot_of[(src_b - my_b) % SIDE], slot_of[(src_a - my_a) % SIDE]]
     canonical = jnp.take(processed, where_is, axis=1).reshape(4, vocs * LIVE)
     counts = jnp.take(processed_counts, where_is, axis=0)
 

time: 115 us -> 145 us (1.26)
  local copies, waits for them, and re-layouts: 6.69 us -> 25.3 us
  matrix products: 25.2 us -> 30.4 us
  other arithmetic: 20.9 us -> 25.6 us
    dot_general x5 -> x4, matrix products: 25.2 us -> 30.4 us  [block_stats(): logits = jnp.dot(rows_in, head, preferred_element_type=jnp.float32)]
    slice x3 -> x5, local copies, waits for them, and re-layouts: 0.55 us -> 5.62 us  [shards(): block[..., :1, width + 2].reshape(-1).astype(jnp.int32)]
    ppermute x9 -> x12, starting transfers between devices: 14.8 us -> 18.7 us  [shift(): return lax.ppermute(value, AXES, pairs)]
    unnamed x17 -> x36, local copies, waits for them, and re-layouts: 0.26 us -> 4.16 us
    concatenate x2, local copies, waits for them, and re-layouts: 0.13 us -> 3.45 us  [the longest x1 3.34 us: shards(): jnp.concatenate([count_of(own), count_of(early), count_of(rest_left), cou...]
    ppermute x7, starting transfers between devices: 11.9 us -> 9.22 us  [butterfly(): other = lax.ppermute(value, axis, [(i, i ^ step) for i in range(size)])]
    ppermute x7, waiting for transfers between devices: 15.2 us -> 17.8 us  [butterfly(): other = lax.ppermute(value, axis, [(i, i ^ step) for i in range(size)])]
    ppermute x9 -> x12, waiting for transfers between devices: 12.2 us -> 10 us  [shift(): return lax.ppermute(value, AXES, pairs)]
  transfers between devices with their start and end apart: 16 -> 19, of which waited for: 9 -> 9; matrix products, arithmetic and copies ran while one was open for 18% -> 25% of each run, Pallas kernels for 0% -> 0%
where the time goes in v12:
time: 145 us
  matrix products  30.4 us (21%)
  starting transfers between devices  27.9 us (19%)
  waiting for transfers between devices  27.8 us (19%)
  other arithmetic  25.6 us (18%)
  local copies, waits for them, and re-layouts  25.3 us (17%)
  between operations  7.61 us (5%)
    dot_general x4, matrix products, block_stats(): logits = jnp.dot(rows_in, head, preferred_element_type=jnp.float32)  30.4 us
    ppermute x12, starting transfers between devices, shift(): return lax.ppermute(value, AXES, pairs)  18.7 us
    ppermute x7, waiting for transfers between devices, butterfly(): other = lax.ppermute(value, axis, [(i, i ^ step) for i in range(size)])  17.8 us
    reduce_sum x4, other arithmetic, block_stats(): total = jnp.sum(expo, axis=-1)  11.6 us
    ppermute x12, waiting for transfers between devices, shift(): return lax.ppermute(value, AXES, pairs)  10 us
    ppermute x7, starting transfers between devices, butterfly(): other = lax.ppermute(value, axis, [(i, i ^ step) for i in range(size)])  9.22 us
    slice x5, local copies, waits for them, and re-layouts, shards(): block[..., :1, width + 2].reshape(-1).astype(jnp.int32)  5.62 us
    unnamed x36, local copies, waits for them, and re-layouts  4.16 us
  transfers between devices with their start and end apart: 19, of which 9 were waited for; matrix products, arithmetic and copies ran while one was open for 25% of the time, Pallas kernels for 0%

profile of v12, /device:TPU:0, one launch (start us, length us, event | category | flops | bytes accessed | tf_op | source)
XLA Modules:
  0.0 144.7 jit_solution(5314665021704523255)
XLA Ops:
  0.7 1.3 fusion.52
  5.2 1.2 fusion.10
  6.4 0.7 and_select_fusion.1
  7.1 1.1 fusion.12
  8.4 3.2 %collective-permute-start.5 = (bf16[96,1664]{1,0:T(8,128)(2,1)S(1)}, bf16[96,1664]{1,0:T(8,128)(2,1)S(1)}, u32[]{:S(2)}, u32[]{:S(2)}) collective-permute-start(bf16[96,1664]{1,0:T(8,128)(2,1)S(1)} %pad_maximum_fusion.2), channel_id=1, source_target_pairs={{0,8},{1,9},{2,10},{3,11},{4,12},{5,13},{6,14},{7,15},{8,0},{9,1},... | collective-permute-start | bytes 958472 | tf_op jit(solution)/shard_map/ppermute | solution.py:79
  11.6 1.1 collective-permute-start.4
  12.8 3.9 %collective-permute-start.2 = (bf16[96,1664]{1,0:T(8,128)(2,1)S(1)}, bf16[96,1664]{1,0:T(8,128)(2,1)S(1)}, u32[]{:S(2)}, u32[]{:S(2)}) collective-permute-start(bf16[96,1664]{1,0:T(8,128)(2,1)S(1)} %pad_maximum_fusion.2), channel_id=1, source_target_pairs={{0,2},{1,3},{2,0},{3,1},{4,6},{5,7},{6,4},{7,5},{8,10},{9,11},{10,... | collective-permute-start | bytes 958472 | tf_op jit(solution)/shard_map/ppermute | solution.py:79
  16.6 0.7 collective-permute-start.1
  17.4 1.3 collective-permute-start
  19.3 1.3 gather_fusion
  20.6 1.3 gather_fusion.1
  22.0 5.4 %fusion.53 = (f32[96]{0:T(128)S(1)}, f32[96,3072]{1,0:T(8,128)S(1)}) fusion(bf16[96,1536]{1,0:T(8,128)(2,1)S(1)} %fusion.12, bf16[1536,3072]{1,0:T(8,128)(2,1)} %param.9), kind=kOutput, calls=%fused_computation.201 | convolution fusion | flops 906264448 | bytes 10912128 | tf_op jit(solution)/shard_map/dot_general | solution.py:89
  27.4 0.7 gather_fusion.2
  28.8 0.6 pad_maximum_fusion.9
  30.0 0.9 collective-permute-start.3
  31.0 1.1 fusion.50
  32.1 0.6 collective-permute-start.10
  32.7 2.6 %collective-permute-start.8 = (bf16[3,48,1664]{2,1,0:T(8,128)(2,1)}, bf16[3,48,1664]{2,1,0:T(8,128)(2,1)}, u32[]{:S(2)}, u32[]{:S(2)}) collective-permute-start(bf16[3,48,1664]{2,1,0:T(8,128)(2,1)} %get-tuple-element.40), channel_id=1, source_target_pairs={{0,12},{1,13},{2,14},{3,15},{4,0},{5,1},{6,2},{7,3},{8,4},{9,5},{1... | collective-permute-start | bytes 1437704 | tf_op jit(solution)/shard_map/ppermute | solution.py:79
  35.5 7.9 %collective-permute-done.3 = bf16[96,1664]{1,0:T(8,128)(2,1)S(1)} collective-permute-done((bf16[96,1664]{1,0:T(8,128)(2,1)S(1)}, bf16[96,1664]{1,0:T(8,128)(2,1)S(1)}, u32[]{:S(2)}, u32[]{:S(2)}) %collective-permute-start.3) | collective-permute-done | bytes 319520 | tf_op jit(solution)/shard_map/ppermute | solution.py:79
  43.4 1.1 collective-permute-start.11
  44.5 2.3 %collective-permute-start.9 = (bf16[3,48,1664]{2,1,0:T(8,128)(2,1)}, bf16[3,48,1664]{2,1,0:T(8,128)(2,1)}, u32[]{:S(2)}, u32[]{:S(2)}) collective-permute-start(bf16[3,48,1664]{2,1,0:T(8,128)(2,1)} %get-tuple-element.41), channel_id=1, source_target_pairs={{0,12},{1,13},{2,14},{3,15},{4,0},{5,1},{6,2},{7,3},{8,4},{9,5},{1... | collective-permute-start | bytes 1437704 | tf_op jit(solution)/shard_map/ppermute | solution.py:79
  46.9 1.3 copy-done.2
  48.2 10.1 %fusion.54 = (f32[576]{0:T(1024)S(1)}, f32[576,3072]{1,0:T(8,128)}) fusion(bf16[1536,3072]{1,0:T(8,128)(2,1)} %param.9, bf16[576,1664]{1,0:T(8,128)(2,1)S(1)} %bitcast.63), kind=kOutput, calls=%fused_computation.202 | convolution fusion | flops 5437586944 | bytes 18286848 | tf_op jit(solution)/shard_map/dot_general | solution.py:89
  58.5 4.6 %fusion.1 = (f32[576]{0:T(1024)S(1)}, f32[576]{0:T(1024)S(1)}, f32[576]{0:T(1024)S(1)}) fusion(f32[576,3072]{1,0:T(8,128)} %get-tuple-element.65, f32[576]{0:T(1024)S(1)} %get-tuple-element.64, s32[576]{0:T(1024)S(1)} %fusion.24), kind=kLoop, calls=%fused_computation.14 | loop fusion | flops 12384576 | bytes 7089408 | tf_op jit(solution)/shard_map/reduce_sum | solution.py:92
  63.2 1.4 slice_reduce_fusion.6
  64.6 0.9 collective-permute-start.7
  65.6 6.4 %fusion.56 = (f32[288]{0:T(512)}, f32[288,3072]{1,0:T(8,128)S(1)}) fusion(bf16[1536,3072]{1,0:T(8,128)(2,1)} %param.9, bf16[288,1664]{1,0:T(8,128)(2,1)S(1)} %bitcast.59), kind=kOutput, calls=%fused_computation.204 | convolution fusion | flops 2718793472 | bytes 13862016 | tf_op jit(solution)/shard_map/dot_general | solution.py:89
  72.0 0.6 slice.268
  72.6 2.1 %collective-permute-done.7 = bf16[3,48,1664]{2,1,0:T(8,128)(2,1)S(1)} collective-permute-done((bf16[3,48,1664]{2,1,0:T(8,128)(2,1)}, bf16[3,48,1664]{2,1,0:T(8,128)(2,1)S(1)}, u32[]{:S(2)}, u32[]{:S(2)}) %collective-permute-start.7) | collective-permute-done | bytes 479264 | tf_op jit(solution)/shard_map/ppermute | solution.py:79
  74.7 1.5 %maximum_maximum_fusion = bf16[6,96,1664]{2,1,0:T(8,128)(2,1)S(1)} fusion(bf16[3,48,1664]{2,1,0:T(8,128)(2,1)} %collective-permute-done.9, bf16[3,48,1664]{2,1,0:T(8,128)(2,1)} %collective-permute-done.8, bf16[3,48,1664]{2,1,0:T(8,128)(2,1)S(1)} %collective-permute-done.7, bf16[3,48,1664]{2,1,0:T(8,128)(2,1)} %collective-permute-done.6), kind=kLoop, calls=%fused_computation.20 | loop fusion | flops 7667712 | bytes 3833856 | tf_op jit(solution)/shard_map/concatenate | solution.py:137
  76.2 0.7 slice.264
  76.9 8.4 %fusion.55 = (f32[576]{0:T(1024)}, f32[576,3072]{1,0:T(8,128)}) fusion(bf16[1536,3072]{1,0:T(8,128)(2,1)S(1)} %bitcast.53, bf16[576,1664]{1,0:T(8,128)(2,1)S(1)} %bitcast.55), kind=kOutput, calls=%fused_computation.203 | convolution fusion | flops 5437586944 | bytes 18286848 | tf_op jit(solution)/shard_map/dot_general | solution.py:89
  85.3 1.5 %copy.21 = bf16[288,2]{0,1:T(2,128)(2,1)} copy(bf16[288,2]{1,0:T(8,128)(2,1)} %slice.268) | data formatting | bytes 2304
  86.8 0.6 convert_element_type.50
  87.5 0.6 fusion.27
  88.1 1.0 copy.20
  89.1 0.6 fusion.25
  89.7 0.9 slice_reduce_fusion.7
  90.6 1.4 slice_reduce_fusion.8
  92.0 1.4 slice_reduce_fusion.9
  93.3 3.3 %concatenate.34 = bf16[16]{0:T(256)(128)(2,1)} concatenate(bf16[1]{0:T(256)(128)(2,1)} %bitcast.24, bf16[6]{0:T(256)(128)(2,1)} %slice_reduce_fusion.6, bf16[3]{0:T(256)(128)(2,1)} %slice_reduce_fusion.9, bf16[3]{0:T(256)(128)(2,1)} %slice_reduce_fusion.8, bf16[3]{0:T(256)(128)(2,1)S(1)} %slice_reduce_fusion.7), dimensions={0} | concatenate | bytes 64 | tf_op jit(solution)/shard_map/concatenate | solution.py:141
  96.7 0.7 concatenate.35
  97.4 1.3 gather_fusion.4
  98.7 1.8 %fusion.48 = (s32[]{:T(128)}, s32[16]{0:T(128)}, pred[16]{0:T(512)(128)(4,1)S(1)}) fusion(s32[16]{0:T(128)} %gather_fusion.4, s32[16]{0:T(128)} %copy-done.6), kind=kLoop, calls=%fused_computation.196 | loop fusion | flops 127 | bytes 212 | tf_op jit(solution)/shard_map/reduce_sum | solution.py:164
  100.5 0.7 broadcast_in_dim.80
  101.2 0.8 broadcast_in_dim.81
  101.9 0.7 stack.140
  102.6 2.0 %fusion.2 = (f32[288]{0:T(512)S(1)}, f32[288]{0:T(512)S(1)}, f32[288]{0:T(512)S(1)}) fusion(f32[288,3072]{1,0:T(8,128)S(1)} %get-tuple-element.69, f32[288]{0:T(512)} %get-tuple-element.68, s32[288]{0:T(512)} %fusion.27), kind=kLoop, calls=%fused_computation.19 | loop fusion | flops 6192288 | bytes 3544704 | tf_op jit(solution)/shard_map/reduce_sum | solution.py:92
  104.7 4.6 %fusion = (f32[576]{0:T(1024)S(1)}, f32[576]{0:T(1024)S(1)}, f32[576]{0:T(1024)S(1)}) fusion(f32[576,3072]{1,0:T(8,128)} %get-tuple-element.67, f32[576]{0:T(1024)S(1)} %copy-done.4, s32[576]{0:T(1024)S(1)} %copy-done.3), kind=kLoop, calls=%fused_computation.9 | loop fusion | flops 12384576 | bytes 7089408 | tf_op jit(solution)/shard_map/reduce_sum | solution.py:92
  109.6 0.7 gather_fusion.3
  110.4 1.1 collective-permute-start.12
  111.5 2.8 %collective-permute-done.12 = f32[4,1536]{1,0:T(4,128)S(1)} collective-permute-done((f32[4,1536]{1,0:T(4,128)S(1)}, f32[4,1536]{1,0:T(4,128)S(1)}, u32[]{:S(2)}, u32[]{:S(2)}) %collective-permute-start.12) | collective-permute-done | bytes 24608 | tf_op jit(solution)/shard_map/ppermute | solution.py:32
  114.4 1.4 collective-permute-start.13
  115.9 4.0 %collective-permute-done.13 = f32[4,1536]{1,0:T(4,128)S(1)} collective-permute-done((f32[4,1536]{1,0:T(4,128)S(1)}, f32[4,1536]{1,0:T(4,128)S(1)}, u32[]{:S(2)}, u32[]{:S(2)}) %collective-permute-start.13) | collective-permute-done | bytes 24608 | tf_op jit(solution)/shard_map/ppermute | solution.py:32
  120.1 3.8 %collective-permute-done.14 = f32[4,1536]{1,0:T(4,128)S(1)} collective-permute-done((f32[4,1536]{1,0:T(4,128)S(1)}, f32[4,1536]{1,0:T(4,128)S(1)}, u32[]{:S(2)}, u32[]{:S(2)}) %collective-permute-start.14) | collective-permute-done | bytes 24608 | tf_op jit(solution)/shard_map/ppermute | solution.py:32
  124.1 1.8 %collective-permute-start.15 = (f32[4,1536]{1,0:T(4,128)S(1)}, f32[4,1536]{1,0:T(4,128)S(1)}, u32[]{:S(2)}, u32[]{:S(2)}) collective-permute-start(f32[4,1536]{1,0:T(4,128)S(1)} %pad_maximum_fusion.5), channel_id=1, source_target_pairs={{0,8},{1,9},{2,10},{3,11},{4,12},{5,13},{6,14},{7,15},{8,0},{9,1},... | collective-permute-start | bytes 73736 | tf_op jit(solution)/shard_map/ppermute | solution.py:32
  126.7 2.8 %collective-permute-done.15 = f32[4,1536]{1,0:T(4,128)S(1)} collective-permute-done((f32[4,1536]{1,0:T(4,128)S(1)}, f32[4,1536]{1,0:T(4,128)S(1)}, u32[]{:S(2)}, u32[]{:S(2)}) %collective-permute-start.15) | collective-permute-done | bytes 24608 | tf_op jit(solution)/shard_map/ppermute | solution.py:32
  129.5 0.8 select_reduce_fusion.4
  130.3 0.7 pad_maximum_fusion.10
  132.2 0.7 fusion.32
  132.9 1.6 %collective-permute-start.17 = (f32[2]{0:T(128)S(1)}, f32[2]{0:T(128)S(1)}, u32[]{:S(2)}, u32[]{:S(2)}) collective-permute-start(f32[2]{0:T(128)S(1)} %fusion.32), channel_id=1, source_target_pairs={{0,32},{16,48},{32,0},{48,16},{64,96},{80,112},{96,64},{112,80},{1... | collective-permute-start | bytes 32 | tf_op jit(solution)/shard_map/ppermute | solution.py:32
  134.5 2.0 %collective-permute-done.17 = f32[2]{0:T(128)S(1)} collective-permute-done((f32[2]{0:T(128)S(1)}, f32[2]{0:T(128)S(1)}, u32[]{:S(2)}, u32[]{:S(2)}) %collective-permute-start.17) | collective-permute-done | bytes 40 | tf_op jit(solution)/shard_map/ppermute | solution.py:32
  136.5 3.2 %collective-permute-start.18 = (f32[2]{0:T(128)S(1)}, f32[2]{0:T(128)S(1)}, u32[]{:S(2)}, u32[]{:S(2)}) collective-permute-start(f32[2]{0:T(128)S(1)} %fusion.31), channel_id=1, source_target_pairs={{0,64},{16,80},{32,96},{48,112},{64,0},{80,16},{96,32},{112,48},{1... | collective-permute-start | bytes 32 | tf_op jit(solution)/shard_map/ppermute | solution.py:32
  139.7 1.9 %collective-permute-done.18 = f32[2]{0:T(128)S(1)} collective-permute-done((f32[2]{0:T(128)S(1)}, f32[2]{0:T(128)S(1)}, u32[]{:S(2)}, u32[]{:S(2)}) %collective-permute-start.18) | collective-permute-done | bytes 40 | tf_op jit(solution)/shard_map/ppermute | solution.py:32
  (116 shorter events, 5.6 us)
Async XLA Ops:
  8.4 36.1 %collective-permute-start.5 = (bf16[96,1664]{1,0:T(8,128)(2,1)S(1)}, bf16[96,1664]{1,0:T(8,128)(2,1)S(1)}, u32[]{:S(2)}, u32[]{:S(2)}) collective-permute-start(bf16[96,1664]{1,0:T(8,128)(2,1)S(1)} %pad_maximum_fusion.2), channel_id=1, source_target_pairs={{0,8},{1,9},{2,10},{3,11},{4,12},{5,13},{6,14},{7,15},{8,0},{9,1},... | collective-permute-start | bytes 958472 | tf_op jit(solution)/shard_map/ppermute | solution.py:79
  11.6 31.8 %collective-permute-start.4 = (bf16[96,1664]{1,0:T(8,128)(2,1)S(1)}, bf16[96,1664]{1,0:T(8,128)(2,1)S(1)}, u32[]{:S(2)}, u32[]{:S(2)}) collective-permute-start(bf16[96,1664]{1,0:T(8,128)(2,1)S(1)} %pad_maximum_fusion.2), channel_id=1, source_target_pairs={{0,12},{1,13},{2,14},{3,15},{4,0},{5,1},{6,2},{7,3},{8,4},{9,5},{1... | collective-permute-start | bytes 958472 | tf_op jit(solution)/shard_map/ppermute | solution.py:79
  12.8 17.2 %collective-permute-start.2 = (bf16[96,1664]{1,0:T(8,128)(2,1)S(1)}, bf16[96,1664]{1,0:T(8,128)(2,1)S(1)}, u32[]{:S(2)}, u32[]{:S(2)}) collective-permute-start(bf16[96,1664]{1,0:T(8,128)(2,1)S(1)} %pad_maximum_fusion.2), channel_id=1, source_target_pairs={{0,2},{1,3},{2,0},{3,1},{4,6},{5,7},{6,4},{7,5},{8,10},{9,11},{10,... | collective-permute-start | bytes 958472 | tf_op jit(solution)/shard_map/ppermute | solution.py:79
  16.6 14.3 %collective-permute-start.1 = (bf16[96,1664]{1,0:T(8,128)(2,1)S(1)}, bf16[96,1664]{1,0:T(8,128)(2,1)S(1)}, u32[]{:S(2)}, u32[]{:S(2)}) collective-permute-start(bf16[96,1664]{1,0:T(8,128)(2,1)S(1)} %pad_maximum_fusion.2), channel_id=1, source_target_pairs={{0,3},{1,0},{2,1},{3,2},{4,7},{5,4},{6,5},{7,6},{8,11},{9,8},{10,9... | collective-permute-start | bytes 958472 | tf_op jit(solution)/shard_map/ppermute | solution.py:79
  17.4 13.6 %collective-permute-start = (bf16[96,1664]{1,0:T(8,128)(2,1)S(1)}, bf16[96,1664]{1,0:T(8,128)(2,1)S(1)}, u32[]{:S(2)}, u32[]{:S(2)}) collective-permute-start(bf16[96,1664]{1,0:T(8,128)(2,1)S(1)} %pad_maximum_fusion.2), channel_id=1, source_target_pairs={{0,1},{1,2},{2,3},{3,0},{4,5},{5,6},{6,7},{7,4},{8,9},{9,10},{10,1... | collective-permute-start | bytes 958472 | tf_op jit(solution)/shard_map/ppermute | solution.py:79
  22.0 5.5 %copy-start = (s32[4,4]{1,0:T(4,128)S(1)}, s32[4,4]{1,0:T(4,128)}, u32[]{:S(2)}) copy-start(s32[4,4]{1,0:T(4,128)} %constant.172.clone) | copy-start | bytes 196
  28.1 4.0 %copy-start.6 = (s32[16]{0:T(128)}, s32[16]{0:T(128)S(1)}, u32[]{:S(2)}) copy-start(s32[16]{0:T(128)S(1)} %gather_fusion.2) | copy-start | bytes 196
  30.0 13.3 %collective-permute-start.3 = (bf16[96,1664]{1,0:T(8,128)(2,1)S(1)}, bf16[96,1664]{1,0:T(8,128)(2,1)S(1)}, u32[]{:S(2)}, u32[]{:S(2)}) collective-permute-start(bf16[96,1664]{1,0:T(8,128)(2,1)S(1)} %pad_maximum_fusion.2), channel_id=1, source_target_pairs={{0,4},{1,5},{2,6},{3,7},{4,8},{5,9},{6,10},{7,11},{8,12},{9,13},{1... | collective-permute-start | bytes 958472 | tf_op jit(solution)/shard_map/ppermute | solution.py:79
  32.1 32.5 %collective-permute-start.10 = (bf16[3,48,1664]{2,1,0:T(8,128)(2,1)}, bf16[3,48,1664]{2,1,0:T(8,128)(2,1)S(1)}, u32[]{:S(2)}, u32[]{:S(2)}) collective-permute-start(bf16[3,48,1664]{2,1,0:T(8,128)(2,1)} %get-tuple-element.40), channel_id=1, source_target_pairs={{0,8},{1,9},{2,10},{3,11},{4,12},{5,13},{6,14},{7,15},{8,0},{9,1},... | collective-permute-start | bytes 1437704 | tf_op jit(solution)/shard_map/ppermute | solution.py:79
  32.7 39.9 %collective-permute-start.8 = (bf16[3,48,1664]{2,1,0:T(8,128)(2,1)}, bf16[3,48,1664]{2,1,0:T(8,128)(2,1)}, u32[]{:S(2)}, u32[]{:S(2)}) collective-permute-start(bf16[3,48,1664]{2,1,0:T(8,128)(2,1)} %get-tuple-element.40), channel_id=1, source_target_pairs={{0,12},{1,13},{2,14},{3,15},{4,0},{5,1},{6,2},{7,3},{8,4},{9,5},{1... | collective-permute-start | bytes 1437704 | tf_op jit(solution)/shard_map/ppermute | solution.py:79
  43.3 29.3 %collective-permute-start.6 = (bf16[3,48,1664]{2,1,0:T(8,128)(2,1)}, bf16[3,48,1664]{2,1,0:T(8,128)(2,1)}, u32[]{:S(2)}, u32[]{:S(2)}) collective-permute-start(bf16[3,48,1664]{2,1,0:T(8,128)(2,1)} %get-tuple-element.40), channel_id=1, source_target_pairs={{0,4},{1,5},{2,6},{3,7},{4,8},{5,9},{6,10},{7,11},{8,12},{9,13},{1... | collective-permute-start | bytes 1437704 | tf_op jit(solution)/shard_map/ppermute | solution.py:79
  43.4 22.1 %collective-permute-start.11 = (bf16[3,48,1664]{2,1,0:T(8,128)(2,1)}, bf16[3,48,1664]{2,1,0:T(8,128)(2,1)S(1)}, u32[]{:S(2)}, u32[]{:S(2)}) collective-permute-start(bf16[3,48,1664]{2,1,0:T(8,128)(2,1)} %get-tuple-element.41), channel_id=1, source_target_pairs={{0,8},{1,9},{2,10},{3,11},{4,12},{5,13},{6,14},{7,15},{8,0},{9,1},... | collective-permute-start | bytes 1437704 | tf_op jit(solution)/shard_map/ppermute | solution.py:79
  44.5 28.1 %collective-permute-start.9 = (bf16[3,48,1664]{2,1,0:T(8,128)(2,1)}, bf16[3,48,1664]{2,1,0:T(8,128)(2,1)}, u32[]{:S(2)}, u32[]{:S(2)}) collective-permute-start(bf16[3,48,1664]{2,1,0:T(8,128)(2,1)} %get-tuple-element.41), channel_id=1, source_target_pairs={{0,12},{1,13},{2,14},{3,15},{4,0},{5,1},{6,2},{7,3},{8,4},{9,5},{1... | collective-permute-start | bytes 1437704 | tf_op jit(solution)/shard_map/ppermute | solution.py:79
  46.9 1.3 copy-start.2
  64.6 0.9 copy-start.1
  64.6 10.1 %collective-permute-start.7 = (bf16[3,48,1664]{2,1,0:T(8,128)(2,1)}, bf16[3,48,1664]{2,1,0:T(8,128)(2,1)S(1)}, u32[]{:S(2)}, u32[]{:S(2)}) collective-permute-start(bf16[3,48,1664]{2,1,0:T(8,128)(2,1)} %get-tuple-element.41), channel_id=1, source_target_pairs={{0,4},{1,5},{2,6},{3,7},{4,8},{5,9},{6,10},{7,11},{8,12},{9,13},{1... | collective-permute-start | bytes 1437704 | tf_op jit(solution)/shard_map/ppermute | solution.py:79
  65.6 11.3 %slice-start = ((s8[9437184]{0:T(1024)(128)(4,1)}), s8[4194304]{0:T(1024)(128)(4,1)S(1)}, s32[]{:S(2)}) async-start(s8[9437184]{0:T(1024)(128)(4,1)} %bitcast.52), calls=%async_computation | async-start | bytes 8388608
  65.6 11.3 %slice-start.1 = ((s8[9437184]{0:T(1024)(128)(4,1)}), s8[4194304]{0:T(1024)(128)(4,1)S(1)}, s32[]{:S(2)}) async-start(s8[9437184]{0:T(1024)(128)(4,1)} %bitcast.52), calls=%async_computation.1 | async-start | bytes 8388608
  65.6 11.3 %slice-start.2 = ((s8[9437184]{0:T(1024)(128)(4,1)}), s8[1048576]{0:T(1024)(128)(4,1)S(1)}, s32[]{:S(2)}) async-start(s8[9437184]{0:T(1024)(128)(4,1)} %bitcast.52), calls=%async_computation.2 | async-start | bytes 2097152
  101.9 2.7 %copy-start.4 = (f32[576]{0:T(1024)S(1)}, f32[576]{0:T(1024)}, u32[]{:S(2)}) copy-start(f32[576]{0:T(1024)} %get-tuple-element.66) | copy-start | bytes 6916
  101.9 2.7 %copy-start.3 = (s32[576]{0:T(1024)S(1)}, s32[576]{0:T(1024)}, u32[]{:S(2)}) copy-start(s32[576]{0:T(1024)} %fusion.25) | copy-start | bytes 6916
  104.6 4.7 %copy-start.5 = (f32[4,96]{1,0:T(4,128)S(1)}, f32[4,96]{1,0:T(4,128)}, u32[]{:S(2)}) copy-start(f32[4,96]{1,0:T(4,128)} %pad_maximum_fusion.9) | copy-start | bytes 4612
  104.7 21.2 %copy-start.7 = (s32[16]{0:T(128)S(1)}, s32[16]{0:T(128)}, u32[]{:S(2)}) copy-start(s32[16]{0:T(128)} %get-tuple-element.24) | copy-start | bytes 196
  110.4 3.9 %collective-permute-start.12 = (f32[4,1536]{1,0:T(4,128)S(1)}, f32[4,1536]{1,0:T(4,128)S(1)}, u32[]{:S(2)}, u32[]{:S(2)}) collective-permute-start(f32[4,1536]{1,0:T(4,128)S(1)} %broadcast_select_fusion), channel_id=1, source_target_pairs={{0,1},{1,0},{2,3},{3,2},{4,5},{5,4},{6,7},{7,6},{8,9},{9,8},{10,11... | collective-permute-start | bytes 73736 | tf_op jit(solution)/shard_map/ppermute | solution.py:32
  114.4 5.4 %collective-permute-start.13 = (f32[4,1536]{1,0:T(4,128)S(1)}, f32[4,1536]{1,0:T(4,128)S(1)}, u32[]{:S(2)}, u32[]{:S(2)}) collective-permute-start(f32[4,1536]{1,0:T(4,128)S(1)} %pad_maximum_fusion.3), channel_id=1, source_target_pairs={{0,2},{1,3},{2,0},{3,1},{4,6},{5,7},{6,4},{7,5},{8,10},{9,11},{10,... | collective-permute-start | bytes 73736 | tf_op jit(solution)/shard_map/ppermute | solution.py:32
  120.0 3.9 %collective-permute-start.14 = (f32[4,1536]{1,0:T(4,128)S(1)}, f32[4,1536]{1,0:T(4,128)S(1)}, u32[]{:S(2)}, u32[]{:S(2)}) collective-permute-start(f32[4,1536]{1,0:T(4,128)S(1)} %pad_maximum_fusion.4), channel_id=1, source_target_pairs={{0,4},{1,5},{2,6},{3,7},{4,0},{5,1},{6,2},{7,3},{8,12},{9,13},{10,... | collective-permute-start | bytes 73736 | tf_op jit(solution)/shard_map/ppermute | solution.py:32
  124.1 5.4 %collective-permute-start.15 = (f32[4,1536]{1,0:T(4,128)S(1)}, f32[4,1536]{1,0:T(4,128)S(1)}, u32[]{:S(2)}, u32[]{:S(2)}) collective-permute-start(f32[4,1536]{1,0:T(4,128)S(1)} %pad_maximum_fusion.5), channel_id=1, source_target_pairs={{0,8},{1,9},{2,10},{3,11},{4,12},{5,13},{6,14},{7,15},{8,0},{9,1},... | collective-permute-start | bytes 73736 | tf_op jit(solution)/shard_map/ppermute | solution.py:32
  131.0 1.2 collective-permute-start.16
  131.2 12.3 %copy-start.9 = (f32[128]{0:T(128)}, f32[128]{0:T(128)S(1)}, u32[]{:S(2)}) copy-start(f32[128]{0:T(128)S(1)} %fusion.46) | copy-start | bytes 1540
  131.4 12.1 %copy-start.10 = (f32[128]{0:T(128)}, f32[128]{0:T(128)S(1)}, u32[]{:S(2)}) copy-start(f32[128]{0:T(128)S(1)} %fusion.45) | copy-start | bytes 1540
  131.6 12.0 %copy-start.8 = (f32[128]{0:T(128)}, f32[128]{0:T(128)S(1)}, u32[]{:S(2)}) copy-start(f32[128]{0:T(128)S(1)} %select_dynamic-update-slice_fusion) | copy-start | bytes 1540
  132.9 3.6 %collective-permute-start.17 = (f32[2]{0:T(128)S(1)}, f32[2]{0:T(128)S(1)}, u32[]{:S(2)}, u32[]{:S(2)}) collective-permute-start(f32[2]{0:T(128)S(1)} %fusion.32), channel_id=1, source_target_pairs={{0,32},{16,48},{32,0},{48,16},{64,96},{80,112},{96,64},{112,80},{1... | collective-permute-start | bytes 32 | tf_op jit(solution)/shard_map/ppermute | solution.py:32
  136.5 5.1 %collective-permute-start.18 = (f32[2]{0:T(128)S(1)}, f32[2]{0:T(128)S(1)}, u32[]{:S(2)}, u32[]{:S(2)}) collective-permute-start(f32[2]{0:T(128)S(1)} %fusion.31), channel_id=1, source_target_pairs={{0,64},{16,80},{32,96},{48,112},{64,0},{80,16},{96,32},{112,48},{1... | collective-permute-start | bytes 32 | tf_op jit(solution)/shard_map/ppermute | solution.py:32

commit v13 on v11

--- a/solution.py
+++ b/solution.py
@@ -24,12 +24,12 @@
     )
 
 
-def butterfly(value, axis, combine):
+def butterfly(value, axis, combine, flips):
     size = lax.axis_size(axis)
     index = lax.axis_index(axis)
     step = 1
-    while step < size:
-        other = lax.ppermute(value, axis, [(i, i ^ step) for i in range(size)])
+    for flip in flips:
+        other = lax.ppermute(value, axis, [(i, i ^ flip) for i in range(size)])
         upper = (index & step) != 0
         first = jnp.where(upper, other, value)
         second = jnp.where(upper, value, other)
@@ -148,7 +148,7 @@
     canonical = jnp.take(processed, where_is, axis=1).reshape(4, vocs * LIVE)
     counts = jnp.take(processed_counts, where_is, axis=0)
 
-    merged = butterfly(canonical, "voc", combine_stats)
+    merged = butterfly(canonical, "voc", combine_stats, (1, 3, 4, 12))
     top, total, weighted, picked = merged[0], merged[1], merged[2], merged[3]
     lse = top + jnp.log(total)
     row_entropy = lse - weighted / total
@@ -157,7 +157,7 @@
     group_live = slot[None, :] < counts[:, None]
     group_entropy = jnp.where(group_live, row_entropy.reshape(vocs, LIVE), 0.0)
     totals = jnp.stack([jnp.sum(group_entropy), jnp.sum(counts).astype(jnp.float32)])
-    totals = butterfly(totals, "req", lambda a, b: a + b)
+    totals = butterfly(totals, "req", lambda a, b: a + b, (1, 2, 6))
     mean_entropy = (totals[0] / totals[1]).reshape(1)
     mine = lambda a: lax.dynamic_slice_in_dim(a, position * LIVE, LIVE, 0)
     live = slot < live_count

time: 115 us -> 114 us (level)
  no operation moved by 1% of the time
where the time goes in v13:
time: 114 us
  starting transfers between devices  26.6 us (23%)
  waiting for transfers between devices  26.5 us (23%)
  matrix products  25.2 us (22%)
  other arithmetic  20.9 us (18%)
  between operations  7.58 us (7%)
  local copies, waits for them, and re-layouts  6.69 us (6%)
    dot_general x5, matrix products, block_stats(): logits = jnp.dot(rows_in, head, preferred_element_type=jnp.float32)  25.2 us
    ppermute x9, starting transfers between devices, shift(): return lax.ppermute(value, AXES, pairs)  14.8 us
    ppermute x7, waiting for transfers between devices, butterfly(): other = lax.ppermute(value, axis, [(i, i ^ flip) for i in range(size)])  14.3 us
    reduce_sum x5, other arithmetic, block_stats(): total = jnp.sum(expo, axis=-1)  12.3 us
    ppermute x9, waiting for transfers between devices, shift(): return lax.ppermute(value, AXES, pairs)  12.2 us
    ppermute x7, starting transfers between devices, butterfly(): other = lax.ppermute(value, axis, [(i, i ^ flip) for i in range(size)])  11.9 us
  transfers between devices with their start and end apart: 16, of which 9 were waited for; matrix products, arithmetic and copies ran while one was open for 18% of the time, Pallas kernels for 0%

profile of v13, /device:TPU:0, one launch (start us, length us, event | category | flops | bytes accessed | tf_op | source)
XLA Modules:
  0.0 113.6 jit_solution(15811950765967031682)
XLA Ops:
  0.7 1.3 %fusion.52 = (s32[1,1]{1,0:T(1,128)}, s32[1,1]{1,0:T(1,128)}) fusion(s32[1,2]{1,0:T(1,128)} %param.10), kind=kLoop, calls=%fused_computation.204 | loop fusion | bytes 16 | tf_op jit(solution)/shard_map/slice | solution.py:106
  5.2 1.2 %fusion.9 = f32[96]{0:T(128)S(1)} fusion(bf16[128,1536]{1,0:T(8,128)(2,1)} %param.6, s32[]{:T(128)S(6)} %select_n.329), kind=kLoop, calls=%fused_computation.38 | loop fusion | flops 442272 | bytes 295300 | tf_op jit(solution)/shard_map/reduce_sum | solution.py:110
  6.4 0.7 and_select_fusion.1
  7.2 1.1 fusion.11
  8.3 0.1 select_convert_fusion
  8.4 4.1 %collective-permute-start.2 = (bf16[96,1664]{1,0:T(8,128)(2,1)S(1)}, bf16[96,1664]{1,0:T(8,128)(2,1)S(1)}, u32[]{:S(2)}, u32[]{:S(2)}) collective-permute-start(bf16[96,1664]{1,0:T(8,128)(2,1)S(1)} %get-tuple-element.46), channel_id=1, source_target_pairs={{0,2},{1,3},{2,0},{3,1},{4,6},{5,7},{6,4},{7,5},{8,10},{9,11},{10,... | collective-permute-start | bytes 958472 | tf_op jit(solution)/shard_map/ppermute | solution.py:79
  12.5 0.7 collective-permute-start.1
  13.2 1.3 %collective-permute-start = (bf16[96,1664]{1,0:T(8,128)(2,1)S(1)}, bf16[96,1664]{1,0:T(8,128)(2,1)S(1)}, u32[]{:S(2)}, u32[]{:S(2)}) collective-permute-start(bf16[96,1664]{1,0:T(8,128)(2,1)S(1)} %get-tuple-element.46), channel_id=1, source_target_pairs={{0,1},{1,2},{2,3},{3,0},{4,5},{5,6},{6,7},{7,4},{8,9},{9,10},{10,1... | collective-permute-start | bytes 958472 | tf_op jit(solution)/shard_map/ppermute | solution.py:79
  14.6 1.3 %gather_fusion = s32[16]{0:T(128)S(1)} fusion(s32[4]{0:T(128)} %constant.170.clone, s32[1024]{0:T(1024)S(1)} %pad_clamp_fusion.2), kind=kCustom, calls=%fused_computation | custom fusion | bytes 192 | tf_op jit(solution)/shard_map/gather | solution.py:147
  15.9 0.7 gather_fusion.1
  16.6 5.6 %fusion.53 = (f32[96]{0:T(128)S(1)}, f32[96,3072]{1,0:T(8,128)S(1)}) fusion(bf16[96,1536]{1,0:T(8,128)(2,1)S(1)} %fusion.11, bf16[1536,3072]{1,0:T(8,128)(2,1)} %param.8), kind=kOutput, calls=%fused_computation.205 | convolution fusion | flops 906264448 | bytes 10912128 | tf_op jit(solution)/shard_map/dot_general | solution.py:89
  22.3 0.2 fusion.21
  22.5 0.5 fusion.8
  23.1 0.2 maximum_reduce_fusion
  23.2 0.2 pad_maximum_fusion
  23.4 0.1 fusion.50
  23.5 3.1 %collective-permute-start.7 = (bf16[4,48,1664]{2,1,0:T(8,128)(2,1)S(1)}, bf16[4,48,1664]{2,1,0:T(8,128)(2,1)S(1)}, u32[]{:S(2)}, u32[]{:S(2)}) collective-permute-start(bf16[4,48,1664]{2,1,0:T(8,128)(2,1)S(1)} %get-tuple-element.43), channel_id=1, source_target_pairs={{0,8},{1,9},{2,10},{3,11},{4,12},{5,13},{6,14},{7,15},{8,0},{9,1},... | collective-permute-start | bytes 1916936 | tf_op jit(solution)/shard_map/ppermute | solution.py:79
  26.6 1.2 %collective-permute-start.5 = (bf16[4,48,1664]{2,1,0:T(8,128)(2,1)S(1)}, bf16[4,48,1664]{2,1,0:T(8,128)(2,1)S(1)}, u32[]{:S(2)}, u32[]{:S(2)}) collective-permute-start(bf16[4,48,1664]{2,1,0:T(8,128)(2,1)S(1)} %get-tuple-element.43), channel_id=1, source_target_pairs={{0,12},{1,13},{2,14},{3,15},{4,0},{5,1},{6,2},{7,3},{8,4},{9,5},{1... | collective-permute-start | bytes 1916936 | tf_op jit(solution)/shard_map/ppermute | solution.py:79
  27.8 0.9 collective-permute-start.3
  28.7 0.6 collective-permute-start.8
  29.3 2.6 %collective-permute-start.6 = (bf16[4,48,1664]{2,1,0:T(8,128)(2,1)S(1)}, bf16[4,48,1664]{2,1,0:T(8,128)(2,1)S(1)}, u32[]{:S(2)}, u32[]{:S(2)}) collective-permute-start(bf16[4,48,1664]{2,1,0:T(8,128)(2,1)S(1)} %get-tuple-element.44), channel_id=1, source_target_pairs={{0,12},{1,13},{2,14},{3,15},{4,0},{5,1},{6,2},{7,3},{8,4},{9,5},{1... | collective-permute-start | bytes 1916936 | tf_op jit(solution)/shard_map/ppermute | solution.py:79
  32.1 2.1 %fusion.54 = (f32[192]{0:T(256)S(1)}, f32[192,3072]{1,0:T(8,128)S(1)}) fusion(bf16[1536,3072]{1,0:T(8,128)(2,1)S(1)} %bitcast.43, bf16[192,1664]{1,0:T(8,128)(2,1)S(1)} %constant_dynamic-update-slice_fusion), kind=kOutput, calls=%fused_computation.206 | convolution fusion | flops 1812528896 | bytes 12387072 | tf_op jit(solution)/shard_map/dot_general | solution.py:89
  34.2 0.2 fusion.19
  34.4 1.8 %fusion.55 = (f32[96]{0:T(128)S(1)}, f32[96,3072]{1,0:T(8,128)S(1)}) fusion(bf16[1536,3072]{1,0:T(8,128)(2,1)S(1)} %bitcast.43, bf16[96,1664]{1,0:T(8,128)(2,1)S(1)} %collective-permute-done.2), kind=kOutput, calls=%fused_computation.207 | convolution fusion | flops 906264448 | bytes 10912128 | tf_op jit(solution)/shard_map/dot_general | solution.py:89
  36.2 0.5 fusion.7
  36.7 0.2 fusion.17
  36.9 1.0 fusion.4
  37.9 0.3 collective-permute-start.4
  38.2 11.2 %collective-permute-done.8 = bf16[4,48,1664]{2,1,0:T(8,128)(2,1)S(1)} collective-permute-done((bf16[4,48,1664]{2,1,0:T(8,128)(2,1)S(1)}, bf16[4,48,1664]{2,1,0:T(8,128)(2,1)S(1)}, u32[]{:S(2)}, u32[]{:S(2)}) %collective-permute-start.8) | collective-permute-done | bytes 639008 | tf_op jit(solution)/shard_map/ppermute | solution.py:79
  49.4 0.1 pad_maximum_fusion.1
  49.5 5.7 %fusion.57 = (f32[384]{0:T(512)S(1)}, f32[384,3072]{1,0:T(8,128)}) fusion(bf16[1536,3072]{1,0:T(8,128)(2,1)S(1)} %bitcast.43, bf16[384,1664]{1,0:T(8,128)(2,1)S(1)} %bitcast.53), kind=kOutput, calls=%fused_computation.209 | convolution fusion | flops 3625057792 | bytes 15336960 | tf_op jit(solution)/shard_map/dot_general | solution.py:89
  55.2 1.0 collective-permute-done.6
  56.2 0.2 maximum_maximum_fusion
  56.5 9.9 %fusion.56 = (f32[768]{0:T(1024)S(1)}, f32[768,3072]{1,0:T(8,128)}) fusion(bf16[1536,3072]{1,0:T(8,128)(2,1)S(1)} %bitcast.43, bf16[768,1664]{1,0:T(8,128)(2,1)S(1)} %bitcast.47), kind=kOutput, calls=%fused_computation.208 | convolution fusion | flops 7250115584 | bytes 21236736 | tf_op jit(solution)/shard_map/dot_general | solution.py:89
  66.4 0.2 slice_reduce_fusion.6
  66.6 0.2 slice_reduce_fusion.7
  66.8 0.2 slice_reduce_fusion.8
  67.0 0.7 gather_fusion.3
  67.7 0.6 fusion.48
  68.7 0.1 copy.16
  68.8 4.0 %fusion.1 = (f32[384]{0:T(512)S(1)}, f32[384]{0:T(512)S(1)}, f32[384]{0:T(512)S(1)}) fusion(f32[384,3072]{1,0:T(8,128)} %get-tuple-element.76, f32[384]{0:T(512)S(1)} %get-tuple-element.75, s32[384]{0:T(512)S(1)} %fusion.32), kind=kLoop, calls=%fused_computation.13 | loop fusion | flops 8256384 | bytes 4726272 | tf_op jit(solution)/shard_map/reduce_sum | solution.py:92
  72.9 6.3 %fusion = (f32[768]{0:T(1024)S(1)}, f32[768]{0:T(1024)S(1)}, f32[768]{0:T(1024)S(1)}) fusion(f32[768,3072]{1,0:T(8,128)} %get-tuple-element.74, f32[768]{0:T(1024)S(1)} %get-tuple-element.73, s32[768]{0:T(1024)S(1)} %fusion.30), kind=kLoop, calls=%fused_computation.8 | loop fusion | flops 16512768 | bytes 9452544 | tf_op jit(solution)/shard_map/reduce_sum | solution.py:92
  79.3 0.1 concatenate.33
  79.5 0.6 gather_fusion.2
  80.2 1.1 collective-permute-start.9
  81.3 2.8 %collective-permute-done.9 = f32[4,1536]{1,0:T(4,128)S(1)} collective-permute-done((f32[4,1536]{1,0:T(4,128)S(1)}, f32[4,1536]{1,0:T(4,128)S(1)}, u32[]{:S(2)}, u32[]{:S(2)}) %collective-permute-start.9) | collective-permute-done | bytes 24608 | tf_op jit(solution)/shard_map/ppermute | solution.py:32
  84.2 2.0 %collective-permute-start.10 = (f32[4,1536]{1,0:T(4,128)S(1)}, f32[4,1536]{1,0:T(4,128)S(1)}, u32[]{:S(2)}, u32[]{:S(2)}) collective-permute-start(f32[4,1536]{1,0:T(4,128)S(1)} %pad_maximum_fusion.3), channel_id=1, source_target_pairs={{0,3},{1,2},{2,1},{3,0},{4,7},{5,6},{6,5},{7,4},{8,11},{9,10},{10,... | collective-permute-start | bytes 73736 | tf_op jit(solution)/shard_map/ppermute | solution.py:32
  86.2 3.1 %collective-permute-done.10 = f32[4,1536]{1,0:T(4,128)S(1)} collective-permute-done((f32[4,1536]{1,0:T(4,128)S(1)}, f32[4,1536]{1,0:T(4,128)S(1)}, u32[]{:S(2)}, u32[]{:S(2)}) %collective-permute-start.10) | collective-permute-done | bytes 24608 | tf_op jit(solution)/shard_map/ppermute | solution.py:32
  89.5 1.5 %collective-permute-start.11 = (f32[4,1536]{1,0:T(4,128)S(1)}, f32[4,1536]{1,0:T(4,128)S(1)}, u32[]{:S(2)}, u32[]{:S(2)}) collective-permute-start(f32[4,1536]{1,0:T(4,128)S(1)} %pad_maximum_fusion.4), channel_id=1, source_target_pairs={{0,4},{1,5},{2,6},{3,7},{4,0},{5,1},{6,2},{7,3},{8,12},{9,13},{10,... | collective-permute-start | bytes 73736 | tf_op jit(solution)/shard_map/ppermute | solution.py:32
  91.0 2.4 %collective-permute-done.11 = f32[4,1536]{1,0:T(4,128)S(1)} collective-permute-done((f32[4,1536]{1,0:T(4,128)S(1)}, f32[4,1536]{1,0:T(4,128)S(1)}, u32[]{:S(2)}, u32[]{:S(2)}) %collective-permute-start.11) | collective-permute-done | bytes 24608 | tf_op jit(solution)/shard_map/ppermute | solution.py:32
  93.6 2.7 %collective-permute-start.12 = (f32[4,1536]{1,0:T(4,128)S(1)}, f32[4,1536]{1,0:T(4,128)S(1)}, u32[]{:S(2)}, u32[]{:S(2)}) collective-permute-start(f32[4,1536]{1,0:T(4,128)S(1)} %pad_maximum_fusion.5), channel_id=1, source_target_pairs={{0,12},{1,13},{2,14},{3,15},{4,8},{5,9},{6,10},{7,11},{8,4},{9,5},... | collective-permute-start | bytes 73736 | tf_op jit(solution)/shard_map/ppermute | solution.py:32
  97.0 1.6 %collective-permute-done.12 = f32[4,1536]{1,0:T(4,128)S(1)} collective-permute-done((f32[4,1536]{1,0:T(4,128)S(1)}, f32[4,1536]{1,0:T(4,128)S(1)}, u32[]{:S(2)}, u32[]{:S(2)}) %collective-permute-start.12) | collective-permute-done | bytes 24608 | tf_op jit(solution)/shard_map/ppermute | solution.py:32
  98.7 0.8 select_reduce_fusion.5
  99.5 0.7 pad_maximum_fusion.11
  100.2 0.2 fusion.46
  100.4 0.2 fusion.45
  100.6 0.2 select_dynamic-update-slice_fusion
  100.8 0.6 collective-permute-done.13
  101.4 0.7 fusion.37
  102.1 1.6 %collective-permute-start.14 = (f32[2]{0:T(128)S(1)}, f32[2]{0:T(128)S(1)}, u32[]{:S(2)}, u32[]{:S(2)}) collective-permute-start(f32[2]{0:T(128)S(1)} %fusion.37), channel_id=1, source_target_pairs={{0,32},{16,48},{32,0},{48,16},{64,96},{80,112},{96,64},{112,80},{1... | collective-permute-start | bytes 32 | tf_op jit(solution)/shard_map/ppermute | solution.py:32
  103.7 2.0 %collective-permute-done.14 = f32[2]{0:T(128)S(1)} collective-permute-done((f32[2]{0:T(128)S(1)}, f32[2]{0:T(128)S(1)}, u32[]{:S(2)}, u32[]{:S(2)}) %collective-permute-start.14) | collective-permute-done | bytes 40 | tf_op jit(solution)/shard_map/ppermute | solution.py:32
  105.7 3.0 %collective-permute-start.15 = (f32[2]{0:T(128)S(1)}, f32[2]{0:T(128)S(1)}, u32[]{:S(2)}, u32[]{:S(2)}) collective-permute-start(f32[2]{0:T(128)S(1)} %fusion.36), channel_id=1, source_target_pairs={{0,96},{16,112},{32,64},{48,80},{64,32},{80,48},{96,0},{112,16},{1... | collective-permute-start | bytes 32 | tf_op jit(solution)/shard_map/ppermute | solution.py:32
  108.7 1.8 %collective-permute-done.15 = f32[2]{0:T(128)S(1)} collective-permute-done((f32[2]{0:T(128)S(1)}, f32[2]{0:T(128)S(1)}, u32[]{:S(2)}, u32[]{:S(2)}) %collective-permute-start.15) | collective-permute-done | bytes 40 | tf_op jit(solution)/shard_map/ppermute | solution.py:32
  110.5 0.6 fusion.51
  (87 shorter events, 1.7 us)
Async XLA Ops:
  0.6 15.3 %copy-start = (s32[4]{0:T(128)S(1)}, s32[4]{0:T(128)}, u32[]{:S(2)}) copy-start(s32[4]{0:T(128)} %constant.170.clone) | copy-start | bytes 52
  8.4 14.6 %collective-permute-start.2 = (bf16[96,1664]{1,0:T(8,128)(2,1)S(1)}, bf16[96,1664]{1,0:T(8,128)(2,1)S(1)}, u32[]{:S(2)}, u32[]{:S(2)}) collective-permute-start(bf16[96,1664]{1,0:T(8,128)(2,1)S(1)} %get-tuple-element.46), channel_id=1, source_target_pairs={{0,2},{1,3},{2,0},{3,1},{4,6},{5,7},{6,4},{7,5},{8,10},{9,11},{10,... | collective-permute-start | bytes 958472 | tf_op jit(solution)/shard_map/ppermute | solution.py:79
  12.5 10.5 %collective-permute-start.1 = (bf16[96,1664]{1,0:T(8,128)(2,1)S(1)}, bf16[96,1664]{1,0:T(8,128)(2,1)S(1)}, u32[]{:S(2)}, u32[]{:S(2)}) collective-permute-start(bf16[96,1664]{1,0:T(8,128)(2,1)S(1)} %get-tuple-element.46), channel_id=1, source_target_pairs={{0,3},{1,0},{2,1},{3,2},{4,7},{5,4},{6,5},{7,6},{8,11},{9,8},{10,9... | collective-permute-start | bytes 958472 | tf_op jit(solution)/shard_map/ppermute | solution.py:79
  13.2 9.8 %collective-permute-start = (bf16[96,1664]{1,0:T(8,128)(2,1)S(1)}, bf16[96,1664]{1,0:T(8,128)(2,1)S(1)}, u32[]{:S(2)}, u32[]{:S(2)}) collective-permute-start(bf16[96,1664]{1,0:T(8,128)(2,1)S(1)} %get-tuple-element.46), channel_id=1, source_target_pairs={{0,1},{1,2},{2,3},{3,0},{4,5},{5,6},{6,7},{7,4},{8,9},{9,10},{10,1... | collective-permute-start | bytes 958472 | tf_op jit(solution)/shard_map/ppermute | solution.py:79
  16.6 15.4 %slice-start = ((s8[9437184]{0:T(1024)(128)(4,1)}), s8[4194304]{0:T(1024)(128)(4,1)S(1)}, s32[]{:S(2)}) async-start(s8[9437184]{0:T(1024)(128)(4,1)} %bitcast.42), calls=%async_computation | async-start | bytes 8388608
  16.6 15.4 %slice-start.1 = ((s8[9437184]{0:T(1024)(128)(4,1)}), s8[4194304]{0:T(1024)(128)(4,1)S(1)}, s32[]{:S(2)}) async-start(s8[9437184]{0:T(1024)(128)(4,1)} %bitcast.42), calls=%async_computation.1 | async-start | bytes 8388608
  22.5 9.6 %slice-start.2 = ((s8[9437184]{0:T(1024)(128)(4,1)}), s8[1048576]{0:T(1024)(128)(4,1)S(1)}, s32[]{:S(2)}) async-start(s8[9437184]{0:T(1024)(128)(4,1)} %bitcast.42), calls=%async_computation.2 | async-start | bytes 2097152
  23.5 14.4 %collective-permute-start.7 = (bf16[4,48,1664]{2,1,0:T(8,128)(2,1)S(1)}, bf16[4,48,1664]{2,1,0:T(8,128)(2,1)S(1)}, u32[]{:S(2)}, u32[]{:S(2)}) collective-permute-start(bf16[4,48,1664]{2,1,0:T(8,128)(2,1)S(1)} %get-tuple-element.43), channel_id=1, source_target_pairs={{0,8},{1,9},{2,10},{3,11},{4,12},{5,13},{6,14},{7,15},{8,0},{9,1},... | collective-permute-start | bytes 1916936 | tf_op jit(solution)/shard_map/ppermute | solution.py:79
  26.6 28.6 %collective-permute-start.5 = (bf16[4,48,1664]{2,1,0:T(8,128)(2,1)S(1)}, bf16[4,48,1664]{2,1,0:T(8,128)(2,1)S(1)}, u32[]{:S(2)}, u32[]{:S(2)}) collective-permute-start(bf16[4,48,1664]{2,1,0:T(8,128)(2,1)S(1)} %get-tuple-element.43), channel_id=1, source_target_pairs={{0,12},{1,13},{2,14},{3,15},{4,0},{5,1},{6,2},{7,3},{8,4},{9,5},{1... | collective-permute-start | bytes 1916936 | tf_op jit(solution)/shard_map/ppermute | solution.py:79
  27.8 27.4 %collective-permute-start.3 = (bf16[4,48,1664]{2,1,0:T(8,128)(2,1)S(1)}, bf16[4,48,1664]{2,1,0:T(8,128)(2,1)S(1)}, u32[]{:S(2)}, u32[]{:S(2)}) collective-permute-start(bf16[4,48,1664]{2,1,0:T(8,128)(2,1)S(1)} %get-tuple-element.43), channel_id=1, source_target_pairs={{0,4},{1,5},{2,6},{3,7},{4,8},{5,9},{6,10},{7,11},{8,12},{9,13},{1... | collective-permute-start | bytes 1916936 | tf_op jit(solution)/shard_map/ppermute | solution.py:79
  28.7 20.7 %collective-permute-start.8 = (bf16[4,48,1664]{2,1,0:T(8,128)(2,1)S(1)}, bf16[4,48,1664]{2,1,0:T(8,128)(2,1)S(1)}, u32[]{:S(2)}, u32[]{:S(2)}) collective-permute-start(bf16[4,48,1664]{2,1,0:T(8,128)(2,1)S(1)} %get-tuple-element.44), channel_id=1, source_target_pairs={{0,8},{1,9},{2,10},{3,11},{4,12},{5,13},{6,14},{7,15},{8,0},{9,1},... | collective-permute-start | bytes 1916936 | tf_op jit(solution)/shard_map/ppermute | solution.py:79
  29.3 26.9 %collective-permute-start.6 = (bf16[4,48,1664]{2,1,0:T(8,128)(2,1)S(1)}, bf16[4,48,1664]{2,1,0:T(8,128)(2,1)S(1)}, u32[]{:S(2)}, u32[]{:S(2)}) collective-permute-start(bf16[4,48,1664]{2,1,0:T(8,128)(2,1)S(1)} %get-tuple-element.44), channel_id=1, source_target_pairs={{0,12},{1,13},{2,14},{3,15},{4,0},{5,1},{6,2},{7,3},{8,4},{9,5},{1... | collective-permute-start | bytes 1916936 | tf_op jit(solution)/shard_map/ppermute | solution.py:79
  37.9 18.3 %collective-permute-start.4 = (bf16[4,48,1664]{2,1,0:T(8,128)(2,1)S(1)}, bf16[4,48,1664]{2,1,0:T(8,128)(2,1)S(1)}, u32[]{:S(2)}, u32[]{:S(2)}) collective-permute-start(bf16[4,48,1664]{2,1,0:T(8,128)(2,1)S(1)} %get-tuple-element.44), channel_id=1, source_target_pairs={{0,4},{1,5},{2,6},{3,7},{4,8},{5,9},{6,10},{7,11},{8,12},{9,13},{1... | collective-permute-start | bytes 1916936 | tf_op jit(solution)/shard_map/ppermute | solution.py:79
  80.2 3.9 %collective-permute-start.9 = (f32[4,1536]{1,0:T(4,128)S(1)}, f32[4,1536]{1,0:T(4,128)S(1)}, u32[]{:S(2)}, u32[]{:S(2)}) collective-permute-start(f32[4,1536]{1,0:T(4,128)S(1)} %broadcast_select_fusion), channel_id=1, source_target_pairs={{0,1},{1,0},{2,3},{3,2},{4,5},{5,4},{6,7},{7,6},{8,9},{9,8},{10,11... | collective-permute-start | bytes 73736 | tf_op jit(solution)/shard_map/ppermute | solution.py:32
  84.2 5.1 %collective-permute-start.10 = (f32[4,1536]{1,0:T(4,128)S(1)}, f32[4,1536]{1,0:T(4,128)S(1)}, u32[]{:S(2)}, u32[]{:S(2)}) collective-permute-start(f32[4,1536]{1,0:T(4,128)S(1)} %pad_maximum_fusion.3), channel_id=1, source_target_pairs={{0,3},{1,2},{2,1},{3,0},{4,7},{5,6},{6,5},{7,4},{8,11},{9,10},{10,... | collective-permute-start | bytes 73736 | tf_op jit(solution)/shard_map/ppermute | solution.py:32
  89.5 3.9 %collective-permute-start.11 = (f32[4,1536]{1,0:T(4,128)S(1)}, f32[4,1536]{1,0:T(4,128)S(1)}, u32[]{:S(2)}, u32[]{:S(2)}) collective-permute-start(f32[4,1536]{1,0:T(4,128)S(1)} %pad_maximum_fusion.4), channel_id=1, source_target_pairs={{0,4},{1,5},{2,6},{3,7},{4,0},{5,1},{6,2},{7,3},{8,12},{9,13},{10,... | collective-permute-start | bytes 73736 | tf_op jit(solution)/shard_map/ppermute | solution.py:32
  93.6 5.1 %collective-permute-start.12 = (f32[4,1536]{1,0:T(4,128)S(1)}, f32[4,1536]{1,0:T(4,128)S(1)}, u32[]{:S(2)}, u32[]{:S(2)}) collective-permute-start(f32[4,1536]{1,0:T(4,128)S(1)} %pad_maximum_fusion.5), channel_id=1, source_target_pairs={{0,12},{1,13},{2,14},{3,15},{4,8},{5,9},{6,10},{7,11},{8,4},{9,5},... | collective-permute-start | bytes 73736 | tf_op jit(solution)/shard_map/ppermute | solution.py:32
  100.2 1.2 %collective-permute-start.13 = (f32[2]{0:T(128)S(1)}, f32[2]{0:T(128)S(1)}, u32[]{:S(2)}, u32[]{:S(2)}) collective-permute-start(f32[2]{0:T(128)S(1)} %pad_maximum_fusion.11), channel_id=1, source_target_pairs={{0,16},{16,0},{32,48},{48,32},{64,80},{80,64},{96,112},{112,96},{1... | collective-permute-start | bytes 32 | tf_op jit(solution)/shard_map/ppermute | solution.py:32
  100.4 12.0 %copy-start.2 = (f32[128]{0:T(128)}, f32[128]{0:T(128)S(1)}, u32[]{:S(2)}) copy-start(f32[128]{0:T(128)S(1)} %fusion.46) | copy-start | bytes 1540
  100.6 11.8 %copy-start.3 = (f32[128]{0:T(128)}, f32[128]{0:T(128)S(1)}, u32[]{:S(2)}) copy-start(f32[128]{0:T(128)S(1)} %fusion.45) | copy-start | bytes 1540
  100.8 11.7 %copy-start.1 = (f32[128]{0:T(128)}, f32[128]{0:T(128)S(1)}, u32[]{:S(2)}) copy-start(f32[128]{0:T(128)S(1)} %select_dynamic-update-slice_fusion) | copy-start | bytes 1540
  102.1 3.6 %collective-permute-start.14 = (f32[2]{0:T(128)S(1)}, f32[2]{0:T(128)S(1)}, u32[]{:S(2)}, u32[]{:S(2)}) collective-permute-start(f32[2]{0:T(128)S(1)} %fusion.37), channel_id=1, source_target_pairs={{0,32},{16,48},{32,0},{48,16},{64,96},{80,112},{96,64},{112,80},{1... | collective-permute-start | bytes 32 | tf_op jit(solution)/shard_map/ppermute | solution.py:32
  105.7 4.8 %collective-permute-start.15 = (f32[2]{0:T(128)S(1)}, f32[2]{0:T(128)S(1)}, u32[]{:S(2)}, u32[]{:S(2)}) collective-permute-start(f32[2]{0:T(128)S(1)} %fusion.36), channel_id=1, source_target_pairs={{0,96},{16,112},{32,64},{48,80},{64,32},{80,48},{96,0},{112,16},{1... | collective-permute-start | bytes 32 | tf_op jit(solution)/shard_map/ppermute | solution.py:32

commit v14 on v13

--- a/solution.py
+++ b/solution.py
@@ -85,13 +85,14 @@
     rows_in = block[:, :width]
     meta = block[:, width:width + 2].astype(jnp.int32)
     ids = meta[:, 0] * 256 + meta[:, 1] - position * shard_width
-    columns = jnp.arange(shard_width, dtype=jnp.int32)
     logits = jnp.dot(rows_in, head, preferred_element_type=jnp.float32)
     top = jnp.max(logits, axis=-1)
     expo = jnp.exp(logits - top[:, None])
     total = jnp.sum(expo, axis=-1)
     weighted = jnp.sum(expo * logits, axis=-1)
-    picked = jnp.sum(jnp.where(columns[None, :] == ids[:, None], logits, 0.0), axis=-1)
+    inside = (ids >= 0) & (ids < shard_width)
+    value = jnp.take_along_axis(logits, jnp.clip(ids, 0, shard_width - 1)[:, None], axis=1)[:, 0]
+    picked = jnp.where(inside, value, 0.0)
     return jnp.stack([top, total, weighted, picked])
 
 

time: 114 us -> 150 us (1.32)
  local copies, waits for them, and re-layouts: 6.69 us -> 37.3 us
  matrix products: 25.2 us -> 37.2 us
  waiting for transfers between devices: 26.5 us -> 18.3 us
  other arithmetic: 20.9 us -> 22.5 us
    gather x0 -> x5, local copies, waits for them, and re-layouts: none -> 23.2 us  [block_stats(): jnp.take_along_axis(logits, jnp.clip(ids, 0, shard_width - 1)[:, None], a...]
    dot_general x5, matrix products: 25.2 us -> 37.2 us  [block_stats(): logits = jnp.dot(rows_in, head, preferred_element_type=jnp.float32)]
    ppermute x9, waiting for transfers between devices: 12.2 us -> 2.69 us  [shift(): return lax.ppermute(value, AXES, pairs)]
    slice x1 -> x2, local copies, waits for them, and re-layouts: 0.1 us -> 3.23 us  [shards(): line[:, :HALF]]
    slice x0 -> x1, local copies, waits for them, and re-layouts: none -> 2.48 us  [shards(): line[:, HALF:]]
    reduce_sum x5, other arithmetic: 12.3 us -> 10 us  [block_stats(): total = jnp.sum(expo, axis=-1)]
  transfers between devices with their start and end apart: 16 -> 16, of which waited for: 9 -> 9; matrix products, arithmetic and copies ran while one was open for 18% -> 27% of each run, Pallas kernels for 0% -> 0%
where the time goes in v14:
time: 150 us; the launch traced here: 148 us
  local copies, waits for them, and re-layouts  37.3 us (25%)
  matrix products  37.2 us (25%)
  starting transfers between devices  25.2 us (17%)
  other arithmetic  22.5 us (15%)
  waiting for transfers between devices  18.3 us (12%)
  between operations  7.75 us (5%)
    dot_general x5, matrix products, block_stats(): logits = jnp.dot(rows_in, head, preferred_element_type=jnp.float32)  37.2 us
    gather x5, local copies, waits for them, and re-layouts, block_stats(): jnp.take_along_axis(logits, jnp.clip(ids, 0, shard_width - 1)[:, None], a...  23.2 us
    ppermute x7, waiting for transfers between devices, butterfly(): other = lax.ppermute(value, axis, [(i, i ^ flip) for i in range(size)])  15.6 us
    ppermute x9, starting transfers between devices, shift(): return lax.ppermute(value, AXES, pairs)  14.6 us
    ppermute x7, starting transfers between devices, butterfly(): other = lax.ppermute(value, axis, [(i, i ^ flip) for i in range(size)])  10.6 us
    reduce_sum x5, other arithmetic, block_stats(): total = jnp.sum(expo, axis=-1)  10 us
    slice x2, local copies, waits for them, and re-layouts, shards(): line[:, :HALF]  3.23 us
  transfers between devices with their start and end apart: 16, of which 9 were waited for; matrix products, arithmetic and copies ran while one was open for 27% of the time, Pallas kernels for 0%

profile of v14, /device:TPU:0, one launch (start us, length us, event | category | flops | bytes accessed | tf_op | source)
XLA Modules:
  0.0 148.3 jit_solution(3024317530825288144)
XLA Ops:
  0.7 1.3 fusion.74
  5.2 0.7 and_select_fusion.11
  6.1 0.2 copy.60
  6.3 0.2 fusion.12
  6.6 1.0 fusion.14
  7.7 1.0 fusion.66
  8.7 4.0 %collective-permute-start.2 = (bf16[96,1664]{0,1:T(8,128)(2,1)}, bf16[96,1664]{0,1:T(8,128)(2,1)S(1)}, u32[]{:S(2)}, u32[]{:S(2)}) collective-permute-start(bf16[96,1664]{0,1:T(8,128)(2,1)} %get-tuple-element.52), channel_id=1, source_target_pairs={{0,2},{1,3},{2,0},{3,1},{4,6},{5,7},{6,4},{7,5},{8,10},{9,11},{10,... | collective-permute-start | bytes 958472 | tf_op jit(solution)/shard_map/ppermute | solution.py:79
  12.7 0.7 collective-permute-start.1
  13.4 1.3 collective-permute-start
  14.8 0.7 gather_fusion
  15.4 0.7 gather_fusion.1
  16.1 5.5 %fusion.75 = (f32[96]{0:T(128)S(1)}, f32[96,3072]{1,0:T(8,128)S(1)}) fusion(bf16[96,1536]{0,1:T(8,128)(2,1)S(1)} %fusion.14, bf16[1536,3072]{1,0:T(8,128)(2,1)} %param.10), kind=kOutput, calls=%fused_computation.245 | convolution fusion | flops 906264448 | bytes 10912128 | tf_op jit(solution)/shard_map/dot_general | solution.py:88
  21.6 0.4 fusion.8
  22.1 2.5 %collective-permute-done.1 = bf16[96,1664]{0,1:T(8,128)(2,1)S(1)} collective-permute-done((bf16[96,1664]{0,1:T(8,128)(2,1)}, bf16[96,1664]{0,1:T(8,128)(2,1)S(1)}, u32[]{:S(2)}, u32[]{:S(2)}) %collective-permute-start.1) | collective-permute-done | bytes 319520 | tf_op jit(solution)/shard_map/ppermute | solution.py:79
  24.7 0.6 copy-done.2
  25.5 0.5 pad_maximum_fusion
  26.0 1.8 %fusion.72 = (bf16[4,48,1664]{1,2,0:T(8,128)(2,1)S(1)}, bf16[4,48,1664]{1,2,0:T(8,128)(2,1)}) fusion(bf16[4,96,1664]{1,2,0:T(8,128)(2,1)S(1)} %pad_maximum_fusion), kind=kLoop, calls=%fused_computation.242 | loop fusion | bytes 2555904 | tf_op jit(solution)/shard_map/slice | solution.py:127
  27.8 2.5 %copy.51 = bf16[4,48,1664]{2,1,0:T(8,128)(2,1)} copy(bf16[4,48,1664]{1,2,0:T(8,128)(2,1)} %get-tuple-element.50) | data formatting | bytes 1277952 | tf_op jit(solution)/shard_map/slice | solution.py:127
  30.2 3.0 %collective-permute-start.8 = (bf16[4,48,1664]{2,1,0:T(8,128)(2,1)}, bf16[4,48,1664]{2,1,0:T(8,128)(2,1)}, u32[]{:S(2)}, u32[]{:S(2)}) collective-permute-start(bf16[4,48,1664]{2,1,0:T(8,128)(2,1)} %copy.51), channel_id=1, source_target_pairs={{0,8},{1,9},{2,10},{3,11},{4,12},{5,13},{6,14},{7,15},{8,0},{9,1},... | collective-permute-start | bytes 1916936 | tf_op jit(solution)/shard_map/ppermute | solution.py:79
  33.3 1.1 collective-permute-start.6
  34.4 0.9 collective-permute-start.4
  35.3 1.4 copy.50
  36.7 0.6 collective-permute-start.7
  37.4 2.6 %collective-permute-start.5 = (bf16[4,48,1664]{2,1,0:T(8,128)(2,1)}, bf16[4,48,1664]{2,1,0:T(8,128)(2,1)}, u32[]{:S(2)}, u32[]{:S(2)}) collective-permute-start(bf16[4,48,1664]{2,1,0:T(8,128)(2,1)} %copy.50), channel_id=1, source_target_pairs={{0,12},{1,13},{2,14},{3,15},{4,0},{5,1},{6,2},{7,3},{8,4},{9,5},{1... | collective-permute-start | bytes 1916936 | tf_op jit(solution)/shard_map/ppermute | solution.py:79
  40.0 0.7 slice_convert_fusion
  40.7 0.8 fusion.42
  41.6 1.5 gather_fusion.7
  43.0 5.6 %fusion.77 = (f32[96]{0:T(128)S(1)}, f32[96,3072]{1,0:T(8,128)S(1)}) fusion(bf16[1536,3072]{1,0:T(8,128)(2,1)} %param.10, bf16[96,1664]{0,1:T(8,128)(2,1)} %copy-done.5), kind=kOutput, calls=%fused_computation.247 | convolution fusion | flops 906264448 | bytes 11010432 | tf_op jit(solution)/shard_map/dot_general | solution.py:88
  48.7 1.5 %gather_fusion.8 = f32[96]{0:T(128)S(1)} fusion(f32[96,3072]{1,0:T(8,128)S(1)} %get-tuple-element.80, s32[96]{0:T(128)S(1)} %get-tuple-element.87), kind=kCustom, calls=%fused_computation.1.clone | custom fusion | bytes 1536 | tf_op jit(solution)/shard_map/jit(take_along_axis)/gather | solution.py:94
  50.2 0.4 fusion.7
  50.6 6.1 %fusion.76 = (f32[192]{0:T(256)S(1)}, f32[192,3072]{1,0:T(8,128)S(1)}) fusion(bf16[1536,3072]{1,0:T(8,128)(2,1)} %param.10, bf16[96,1664]{0,1:T(8,128)(2,1)} %copy-done.4, bf16[96,1664]{0,1:T(8,128)(2,1)S(1)} %copy-done.3), kind=kOutput, calls=%fused_computation.246 | convolution fusion | flops 1813708544 | bytes 12436224 | tf_op jit(solution)/shard_map/dot_general | solution.py:88
  56.7 1.9 %gather_fusion.4 = f32[192]{0:T(256)S(1)} fusion(f32[192,3072]{1,0:T(8,128)S(1)} %get-tuple-element.78, s32[192]{0:T(256)S(1)} %bitcast.85), kind=kCustom, calls=%fused_computation.6 | custom fusion | bytes 3072 | tf_op jit(solution)/shard_map/jit(take_along_axis)/gather | solution.py:94
  58.7 0.7 fusion.4
  59.4 0.3 collective-permute-start.3
  59.7 1.4 pad_maximum_fusion.1
  61.1 10.0 %fusion.79 = (f32[384]{0:T(512)S(1)}, f32[384,3072]{1,0:T(8,128)}) fusion(bf16[1536,3072]{1,0:T(8,128)(2,1)} %param.10, bf16[384,1664]{1,0:T(8,128)(2,1)S(1)} %bitcast.95), kind=kOutput, calls=%fused_computation.249 | convolution fusion | flops 3625057792 | bytes 15336960 | tf_op jit(solution)/shard_map/dot_general | solution.py:88
  71.3 1.7 %maximum_maximum_fusion = bf16[8,96,1664]{2,1,0:T(8,128)(2,1)S(1)} fusion(bf16[4,48,1664]{2,1,0:T(8,128)(2,1)} %collective-permute-done.6, bf16[4,48,1664]{2,1,0:T(8,128)(2,1)} %collective-permute-done.5, bf16[4,48,1664]{2,1,0:T(8,128)(2,1)} %collective-permute-done.4, bf16[4,48,1664]{2,1,0:T(8,128)(2,1)S(1)} %collective-permute-done.3), kind=kLoop, calls=%fused_computation.15 | loop fusion | flops 10223616 | bytes 5111808 | tf_op jit(solution)/shard_map/concatenate | solution.py:133
  73.0 9.9 %fusion.78 = (f32[768]{0:T(1024)S(1)}, f32[768,3072]{1,0:T(8,128)}) fusion(bf16[1536,3072]{1,0:T(8,128)(2,1)S(1)} %bitcast.84, bf16[768,1664]{1,0:T(8,128)(2,1)S(1)} %bitcast.93), kind=kOutput, calls=%fused_computation.248 | convolution fusion | flops 7250115584 | bytes 21236736 | tf_op jit(solution)/shard_map/dot_general | solution.py:88
  83.1 0.9 slice_reduce_fusion.6
  84.0 0.9 slice_reduce_fusion.7
  85.2 0.7 gather_fusion.3
  85.9 0.6 fusion.67
  86.9 3.5 %fusion.1 = (f32[384]{0:T(512)S(1)}, f32[384]{0:T(512)S(1)}) fusion(f32[384,3072]{1,0:T(8,128)} %get-tuple-element.84, f32[384]{0:T(512)S(1)} %get-tuple-element.83), kind=kLoop, calls=%fused_computation.14 | loop fusion | flops 4717824 | bytes 4723200 | tf_op jit(solution)/shard_map/reduce_sum | solution.py:91
  90.4 6.5 %gather_fusion.6 = f32[384]{0:T(512)S(1)} fusion(f32[384,3072]{1,0:T(8,128)} %get-tuple-element.84, s32[384]{0:T(512)S(1)} %fusion.34), kind=kCustom, calls=%fused_computation.8 | custom fusion | bytes 6144 | tf_op jit(solution)/shard_map/jit(take_along_axis)/gather | solution.py:94
  97.0 5.0 %fusion = (f32[768]{0:T(1024)S(1)}, f32[768]{0:T(1024)S(1)}) fusion(f32[768,3072]{1,0:T(8,128)} %get-tuple-element.82, f32[768]{0:T(1024)S(1)} %get-tuple-element.81), kind=kLoop, calls=%fused_computation.11 | loop fusion | flops 9435648 | bytes 9446400 | tf_op jit(solution)/shard_map/reduce_sum | solution.py:91
  102.0 11.9 %gather_fusion.5 = f32[768]{0:T(1024)S(1)} fusion(f32[768,3072]{1,0:T(8,128)} %get-tuple-element.82, s32[768]{0:T(1024)S(1)} %fusion.28), kind=kCustom, calls=%fused_computation.7 | custom fusion | bytes 12288 | tf_op jit(solution)/shard_map/jit(take_along_axis)/gather | solution.py:94
  114.2 0.6 gather_fusion.2
  114.9 0.4 collective-permute-start.9
  115.3 3.5 %collective-permute-done.9 = f32[4,1536]{1,0:T(4,128)S(1)} collective-permute-done((f32[4,1536]{1,0:T(4,128)S(1)}, f32[4,1536]{1,0:T(4,128)S(1)}, u32[]{:S(2)}, u32[]{:S(2)}) %collective-permute-start.9) | collective-permute-done | bytes 24608 | tf_op jit(solution)/shard_map/ppermute | solution.py:32
  118.9 1.9 %collective-permute-start.10 = (f32[4,1536]{1,0:T(4,128)S(1)}, f32[4,1536]{1,0:T(4,128)S(1)}, u32[]{:S(2)}, u32[]{:S(2)}) collective-permute-start(f32[4,1536]{1,0:T(4,128)S(1)} %pad_maximum_fusion.3), channel_id=1, source_target_pairs={{0,3},{1,2},{2,1},{3,0},{4,7},{5,6},{6,5},{7,4},{8,11},{9,10},{10,... | collective-permute-start | bytes 73736 | tf_op jit(solution)/shard_map/ppermute | solution.py:32
  120.8 3.2 %collective-permute-done.10 = f32[4,1536]{1,0:T(4,128)S(1)} collective-permute-done((f32[4,1536]{1,0:T(4,128)S(1)}, f32[4,1536]{1,0:T(4,128)S(1)}, u32[]{:S(2)}, u32[]{:S(2)}) %collective-permute-start.10) | collective-permute-done | bytes 24608 | tf_op jit(solution)/shard_map/ppermute | solution.py:32
  124.2 0.3 collective-permute-start.11
  124.5 3.6 %collective-permute-done.11 = f32[4,1536]{1,0:T(4,128)S(1)} collective-permute-done((f32[4,1536]{1,0:T(4,128)S(1)}, f32[4,1536]{1,0:T(4,128)S(1)}, u32[]{:S(2)}, u32[]{:S(2)}) %collective-permute-start.11) | collective-permute-done | bytes 24608 | tf_op jit(solution)/shard_map/ppermute | solution.py:32
  128.3 3.0 %collective-permute-start.12 = (f32[4,1536]{1,0:T(4,128)S(1)}, f32[4,1536]{1,0:T(4,128)S(1)}, u32[]{:S(2)}, u32[]{:S(2)}) collective-permute-start(f32[4,1536]{1,0:T(4,128)S(1)} %pad_maximum_fusion.5), channel_id=1, source_target_pairs={{0,12},{1,13},{2,14},{3,15},{4,8},{5,9},{6,10},{7,11},{8,4},{9,5},... | collective-permute-start | bytes 73736 | tf_op jit(solution)/shard_map/ppermute | solution.py:32
  132.1 1.3 collective-permute-done.12
  133.4 0.8 select_reduce_fusion
  134.2 0.7 pad_maximum_fusion.12
  135.5 0.6 collective-permute-done.13
  136.1 0.7 fusion.48
  136.8 1.7 %collective-permute-start.14 = (f32[2]{0:T(128)S(1)}, f32[2]{0:T(128)S(1)}, u32[]{:S(2)}, u32[]{:S(2)}) collective-permute-start(f32[2]{0:T(128)S(1)} %fusion.48), channel_id=1, source_target_pairs={{0,32},{16,48},{32,0},{48,16},{64,96},{80,112},{96,64},{112,80},{1... | collective-permute-start | bytes 32 | tf_op jit(solution)/shard_map/ppermute | solution.py:32
  138.5 1.9 %collective-permute-done.14 = f32[2]{0:T(128)S(1)} collective-permute-done((f32[2]{0:T(128)S(1)}, f32[2]{0:T(128)S(1)}, u32[]{:S(2)}, u32[]{:S(2)}) %collective-permute-start.14) | collective-permute-done | bytes 40 | tf_op jit(solution)/shard_map/ppermute | solution.py:32
  140.4 3.3 %collective-permute-start.15 = (f32[2]{0:T(128)S(1)}, f32[2]{0:T(128)S(1)}, u32[]{:S(2)}, u32[]{:S(2)}) collective-permute-start(f32[2]{0:T(128)S(1)} %fusion.47), channel_id=1, source_target_pairs={{0,96},{16,112},{32,64},{48,80},{64,32},{80,48},{96,0},{112,16},{1... | collective-permute-start | bytes 32 | tf_op jit(solution)/shard_map/ppermute | solution.py:32
  143.6 1.5 %collective-permute-done.15 = f32[2]{0:T(128)S(1)} collective-permute-done((f32[2]{0:T(128)S(1)}, f32[2]{0:T(128)S(1)}, u32[]{:S(2)}, u32[]{:S(2)}) %collective-permute-start.15) | collective-permute-done | bytes 40 | tf_op jit(solution)/shard_map/ppermute | solution.py:32
  145.2 0.6 fusion.73
  (124 shorter events, 3.3 us)
Async XLA Ops:
  0.6 5.4 %copy-start = (bf16[128,1536]{1,0:T(8,128)(2,1)S(1)}, bf16[128,1536]{1,0:T(8,128)(2,1)}, u32[]{:S(2)}) copy-start(bf16[128,1536]{1,0:T(8,128)(2,1)} %param.8) | copy-start | bytes 1179652
  0.6 14.1 %copy-start.1 = (s32[4]{0:T(128)S(1)}, s32[4]{0:T(128)}, u32[]{:S(2)}) copy-start(s32[4]{0:T(128)} %constant.226.clone) | copy-start | bytes 52
  8.7 13.4 %collective-permute-start.2 = (bf16[96,1664]{0,1:T(8,128)(2,1)}, bf16[96,1664]{0,1:T(8,128)(2,1)S(1)}, u32[]{:S(2)}, u32[]{:S(2)}) collective-permute-start(bf16[96,1664]{0,1:T(8,128)(2,1)} %get-tuple-element.52), channel_id=1, source_target_pairs={{0,2},{1,3},{2,0},{3,1},{4,6},{5,7},{6,4},{7,5},{8,10},{9,11},{10,... | collective-permute-start | bytes 958472 | tf_op jit(solution)/shard_map/ppermute | solution.py:79
  12.7 11.9 %collective-permute-start.1 = (bf16[96,1664]{0,1:T(8,128)(2,1)}, bf16[96,1664]{0,1:T(8,128)(2,1)S(1)}, u32[]{:S(2)}, u32[]{:S(2)}) collective-permute-start(bf16[96,1664]{0,1:T(8,128)(2,1)} %get-tuple-element.52), channel_id=1, source_target_pairs={{0,3},{1,0},{2,1},{3,2},{4,7},{5,4},{6,5},{7,6},{8,11},{9,8},{10,9... | collective-permute-start | bytes 958472 | tf_op jit(solution)/shard_map/ppermute | solution.py:79
  13.4 11.2 %collective-permute-start = (bf16[96,1664]{0,1:T(8,128)(2,1)}, bf16[96,1664]{0,1:T(8,128)(2,1)S(1)}, u32[]{:S(2)}, u32[]{:S(2)}) collective-permute-start(bf16[96,1664]{0,1:T(8,128)(2,1)} %get-tuple-element.52), channel_id=1, source_target_pairs={{0,1},{1,2},{2,3},{3,0},{4,5},{5,6},{6,7},{7,4},{8,9},{9,10},{10,1... | collective-permute-start | bytes 958472 | tf_op jit(solution)/shard_map/ppermute | solution.py:79
  16.1 8.5 %copy-start.6 = (bf16[1,96,1664]{1,2,0:T(8,128)(2,1)S(1)}, bf16[1,96,1664]{1,2,0:T(8,128)(2,1)}, u32[]{:S(2)}) copy-start(bf16[1,96,1664]{1,2,0:T(8,128)(2,1)} %get-tuple-element.51) | copy-start | bytes 958468
  22.0 2.7 %copy-start.5 = (bf16[96,1664]{0,1:T(8,128)(2,1)}, bf16[96,1664]{0,1:T(8,128)(2,1)S(1)}, u32[]{:S(2)}) copy-start(bf16[96,1664]{0,1:T(8,128)(2,1)S(1)} %collective-permute-done.2) | copy-start | bytes 958468
  24.6 0.8 copy-start.2
  24.6 0.9 copy-start.4
  30.2 29.1 %collective-permute-start.8 = (bf16[4,48,1664]{2,1,0:T(8,128)(2,1)}, bf16[4,48,1664]{2,1,0:T(8,128)(2,1)}, u32[]{:S(2)}, u32[]{:S(2)}) collective-permute-start(bf16[4,48,1664]{2,1,0:T(8,128)(2,1)} %copy.51), channel_id=1, source_target_pairs={{0,8},{1,9},{2,10},{3,11},{4,12},{5,13},{6,14},{7,15},{8,0},{9,1},... | collective-permute-start | bytes 1916936 | tf_op jit(solution)/shard_map/ppermute | solution.py:79
  33.3 37.9 %collective-permute-start.6 = (bf16[4,48,1664]{2,1,0:T(8,128)(2,1)}, bf16[4,48,1664]{2,1,0:T(8,128)(2,1)}, u32[]{:S(2)}, u32[]{:S(2)}) collective-permute-start(bf16[4,48,1664]{2,1,0:T(8,128)(2,1)} %copy.51), channel_id=1, source_target_pairs={{0,12},{1,13},{2,14},{3,15},{4,0},{5,1},{6,2},{7,3},{8,4},{9,5},{1... | collective-permute-start | bytes 1916936 | tf_op jit(solution)/shard_map/ppermute | solution.py:79
  34.4 36.8 %collective-permute-start.4 = (bf16[4,48,1664]{2,1,0:T(8,128)(2,1)}, bf16[4,48,1664]{2,1,0:T(8,128)(2,1)}, u32[]{:S(2)}, u32[]{:S(2)}) collective-permute-start(bf16[4,48,1664]{2,1,0:T(8,128)(2,1)} %copy.51), channel_id=1, source_target_pairs={{0,4},{1,5},{2,6},{3,7},{4,8},{5,9},{6,10},{7,11},{8,12},{9,13},{1... | collective-permute-start | bytes 1916936 | tf_op jit(solution)/shard_map/ppermute | solution.py:79
  36.7 23.0 %collective-permute-start.7 = (bf16[4,48,1664]{2,1,0:T(8,128)(2,1)}, bf16[4,48,1664]{2,1,0:T(8,128)(2,1)}, u32[]{:S(2)}, u32[]{:S(2)}) collective-permute-start(bf16[4,48,1664]{2,1,0:T(8,128)(2,1)} %copy.50), channel_id=1, source_target_pairs={{0,8},{1,9},{2,10},{3,11},{4,12},{5,13},{6,14},{7,15},{8,0},{9,1},... | collective-permute-start | bytes 1916936 | tf_op jit(solution)/shard_map/ppermute | solution.py:79
  37.4 33.8 %collective-permute-start.5 = (bf16[4,48,1664]{2,1,0:T(8,128)(2,1)}, bf16[4,48,1664]{2,1,0:T(8,128)(2,1)}, u32[]{:S(2)}, u32[]{:S(2)}) collective-permute-start(bf16[4,48,1664]{2,1,0:T(8,128)(2,1)} %copy.50), channel_id=1, source_target_pairs={{0,12},{1,13},{2,14},{3,15},{4,0},{5,1},{6,2},{7,3},{8,4},{9,5},{1... | collective-permute-start | bytes 1916936 | tf_op jit(solution)/shard_map/ppermute | solution.py:79
  43.0 7.6 %copy-start.3 = (bf16[96,1664]{0,1:T(8,128)(2,1)S(1)}, bf16[96,1664]{0,1:T(8,128)(2,1)}, u32[]{:S(2)}) copy-start(bf16[96,1664]{0,1:T(8,128)(2,1)} %copy-done.2) | copy-start | bytes 958468
  56.7 2.7 %copy-start.7 = (bf16[4,48,1664]{2,1,0:T(8,128)(2,1)S(1)}, bf16[4,48,1664]{2,1,0:T(8,128)(2,1)}, u32[]{:S(2)}) copy-start(bf16[4,48,1664]{2,1,0:T(8,128)(2,1)} %copy.50) | copy-start | bytes 1916932
  59.4 11.9 %collective-permute-start.3 = (bf16[4,48,1664]{2,1,0:T(8,128)(2,1)S(1)}, bf16[4,48,1664]{2,1,0:T(8,128)(2,1)S(1)}, u32[]{:S(2)}, u32[]{:S(2)}) collective-permute-start(bf16[4,48,1664]{2,1,0:T(8,128)(2,1)S(1)} %copy-done.7), channel_id=1, source_target_pairs={{0,4},{1,5},{2,6},{3,7},{4,8},{5,9},{6,10},{7,11},{8,12},{9,13},{1... | collective-permute-start | bytes 1916936 | tf_op jit(solution)/shard_map/ppermute | solution.py:79
  61.1 11.9 %slice-start = ((s8[9437184]{0:T(1024)(128)(4,1)}), s8[4194304]{0:T(1024)(128)(4,1)S(1)}, s32[]{:S(2)}) async-start(s8[9437184]{0:T(1024)(128)(4,1)} %bitcast.83), calls=%async_computation | async-start | bytes 8388608
  61.1 11.9 %slice-start.1 = ((s8[9437184]{0:T(1024)(128)(4,1)}), s8[4194304]{0:T(1024)(128)(4,1)S(1)}, s32[]{:S(2)}) async-start(s8[9437184]{0:T(1024)(128)(4,1)} %bitcast.83), calls=%async_computation.1 | async-start | bytes 8388608
  61.1 11.9 %slice-start.2 = ((s8[9437184]{0:T(1024)(128)(4,1)}), s8[1048576]{0:T(1024)(128)(4,1)S(1)}, s32[]{:S(2)}) async-start(s8[9437184]{0:T(1024)(128)(4,1)} %bitcast.83), calls=%async_computation.2 | async-start | bytes 2097152
  114.9 3.9 %collective-permute-start.9 = (f32[4,1536]{1,0:T(4,128)S(1)}, f32[4,1536]{1,0:T(4,128)S(1)}, u32[]{:S(2)}, u32[]{:S(2)}) collective-permute-start(f32[4,1536]{1,0:T(4,128)S(1)} %broadcast_select_fusion), channel_id=1, source_target_pairs={{0,1},{1,0},{2,3},{3,2},{4,5},{5,4},{6,7},{7,6},{8,9},{9,8},{10,11... | collective-permute-start | bytes 73736 | tf_op jit(solution)/shard_map/ppermute | solution.py:32
  118.9 5.1 %collective-permute-start.10 = (f32[4,1536]{1,0:T(4,128)S(1)}, f32[4,1536]{1,0:T(4,128)S(1)}, u32[]{:S(2)}, u32[]{:S(2)}) collective-permute-start(f32[4,1536]{1,0:T(4,128)S(1)} %pad_maximum_fusion.3), channel_id=1, source_target_pairs={{0,3},{1,2},{2,1},{3,0},{4,7},{5,6},{6,5},{7,4},{8,11},{9,10},{10,... | collective-permute-start | bytes 73736 | tf_op jit(solution)/shard_map/ppermute | solution.py:32
  124.2 3.9 %collective-permute-start.11 = (f32[4,1536]{1,0:T(4,128)S(1)}, f32[4,1536]{1,0:T(4,128)S(1)}, u32[]{:S(2)}, u32[]{:S(2)}) collective-permute-start(f32[4,1536]{1,0:T(4,128)S(1)} %pad_maximum_fusion.4), channel_id=1, source_target_pairs={{0,4},{1,5},{2,6},{3,7},{4,0},{5,1},{6,2},{7,3},{8,12},{9,13},{10,... | collective-permute-start | bytes 73736 | tf_op jit(solution)/shard_map/ppermute | solution.py:32
  128.3 5.1 %collective-permute-start.12 = (f32[4,1536]{1,0:T(4,128)S(1)}, f32[4,1536]{1,0:T(4,128)S(1)}, u32[]{:S(2)}, u32[]{:S(2)}) collective-permute-start(f32[4,1536]{1,0:T(4,128)S(1)} %pad_maximum_fusion.5), channel_id=1, source_target_pairs={{0,12},{1,13},{2,14},{3,15},{4,8},{5,9},{6,10},{7,11},{8,4},{9,5},... | collective-permute-start | bytes 73736 | tf_op jit(solution)/shard_map/ppermute | solution.py:32
  134.9 1.2 collective-permute-start.13
  135.1 12.1 %copy-start.9 = (f32[128]{0:T(128)}, f32[128]{0:T(128)S(1)}, u32[]{:S(2)}) copy-start(f32[128]{0:T(128)S(1)} %fusion.57) | copy-start | bytes 1540
  135.3 11.9 %copy-start.10 = (f32[128]{0:T(128)}, f32[128]{0:T(128)S(1)}, u32[]{:S(2)}) copy-start(f32[128]{0:T(128)S(1)} %fusion.56) | copy-start | bytes 1540
  135.5 11.7 %copy-start.8 = (f32[128]{0:T(128)}, f32[128]{0:T(128)S(1)}, u32[]{:S(2)}) copy-start(f32[128]{0:T(128)S(1)} %select_dynamic-update-slice_fusion) | copy-start | bytes 1540
  136.8 3.6 %collective-permute-start.14 = (f32[2]{0:T(128)S(1)}, f32[2]{0:T(128)S(1)}, u32[]{:S(2)}, u32[]{:S(2)}) collective-permute-start(f32[2]{0:T(128)S(1)} %fusion.48), channel_id=1, source_target_pairs={{0,32},{16,48},{32,0},{48,16},{64,96},{80,112},{96,64},{112,80},{1... | collective-permute-start | bytes 32 | tf_op jit(solution)/shard_map/ppermute | solution.py:32
  140.4 4.8 %collective-permute-start.15 = (f32[2]{0:T(128)S(1)}, f32[2]{0:T(128)S(1)}, u32[]{:S(2)}, u32[]{:S(2)}) collective-permute-start(f32[2]{0:T(128)S(1)} %fusion.47), channel_id=1, source_target_pairs={{0,96},{16,112},{32,64},{48,80},{64,32},{80,48},{96,0},{112,16},{1... | collective-permute-start | bytes 32 | tf_op jit(solution)/shard_map/ppermute | solution.py:32

commit v15 on v13

--- a/solution.py
+++ b/solution.py
@@ -105,10 +105,10 @@
     start = bounds[0, 0]
     finish = bounds[0, 1]
     live_count = finish - start
-    rows = lax.dynamic_slice_in_dim(hidden, start, LIVE, 0)
-    values = rows.astype(jnp.float32)
+    values = hidden.astype(jnp.float32)
     meansq = jnp.mean(values * values, axis=-1, keepdims=True)
-    normed = (values * lax.rsqrt(meansq + 1e-05) * norm_gain).astype(jnp.bfloat16)
+    normed_all = (values * lax.rsqrt(meansq + 1e-05) * norm_gain).astype(jnp.bfloat16)
+    normed = lax.dynamic_slice_in_dim(normed_all, start, LIVE, 0)
     ids = lax.dynamic_slice_in_dim(targets, start, LIVE, 0)
     column = lax.broadcasted_iota(jnp.int32, (LIVE, EXTRA), 1)
     meta = jnp.where(column == 0, ids[:, None] // 256, ids[:, None] % 256)

time: 114 us -> 114 us (level)
  no operation moved by 1% of the time
where the time goes in v15:
time: 114 us
  starting transfers between devices  26.9 us (24%)
  waiting for transfers between devices  26.2 us (23%)
  matrix products  25.2 us (22%)
  other arithmetic  21.7 us (19%)
  between operations  7.59 us (7%)
  local copies, waits for them, and re-layouts  6.11 us (5%)
    dot_general x5, matrix products, block_stats(): logits = jnp.dot(rows_in, head, preferred_element_type=jnp.float32)  25.2 us
    ppermute x9, starting transfers between devices, shift(): return lax.ppermute(value, AXES, pairs)  14.7 us
    ppermute x7, waiting for transfers between devices, butterfly(): other = lax.ppermute(value, axis, [(i, i ^ flip) for i in range(size)])  14 us
    reduce_sum x5, other arithmetic, block_stats(): total = jnp.sum(expo, axis=-1)  12.3 us
    ppermute x9, waiting for transfers between devices, shift(): return lax.ppermute(value, AXES, pairs)  12.2 us
    ppermute x7, starting transfers between devices, butterfly(): other = lax.ppermute(value, axis, [(i, i ^ flip) for i in range(size)])  12.2 us
  transfers between devices with their start and end apart: 16, of which 9 were waited for; matrix products, arithmetic and copies ran while one was open for 18% of the time, Pallas kernels for 0%

profile of v15, /device:TPU:0, one launch (start us, length us, event | category | flops | bytes accessed | tf_op | source)
XLA Modules:
  0.0 113.8 jit_solution(10556674368578499056)
XLA Ops:
  0.7 1.2 %multiply_reduce_fusion.5 = f32[128]{0:T(128)S(1)} fusion(bf16[128,1536]{1,0:T(8,128)(2,1)} %param.6), kind=kLoop, calls=%fused_computation.36 | loop fusion | flops 589696 | bytes 393728 | tf_op jit(solution)/shard_map/reduce_sum | solution.py:109
  1.8 1.1 convert_element_type.43
  2.9 1.3 %fusion.51 = (s32[1,1]{1,0:T(1,128)}, s32[1,1]{1,0:T(1,128)}) fusion(s32[1,2]{1,0:T(1,128)} %param.10), kind=kLoop, calls=%fused_computation.203 | loop fusion | bytes 16 | tf_op jit(solution)/shard_map/slice | solution.py:106
  7.5 0.7 and_select_fusion.1
  8.3 0.8 fusion.12
  9.1 0.1 select_convert_fusion
  9.3 4.1 %collective-permute-start.2 = (bf16[96,1664]{1,0:T(8,128)(2,1)S(1)}, bf16[96,1664]{1,0:T(8,128)(2,1)S(1)}, u32[]{:S(2)}, u32[]{:S(2)}) collective-permute-start(bf16[96,1664]{1,0:T(8,128)(2,1)S(1)} %get-tuple-element.46), channel_id=1, source_target_pairs={{0,2},{1,3},{2,0},{3,1},{4,6},{5,7},{6,4},{7,5},{8,10},{9,11},{10,... | collective-permute-start | bytes 958472 | tf_op jit(solution)/shard_map/ppermute | solution.py:79
  13.3 0.7 collective-permute-start.1
  14.0 1.3 %collective-permute-start = (bf16[96,1664]{1,0:T(8,128)(2,1)S(1)}, bf16[96,1664]{1,0:T(8,128)(2,1)S(1)}, u32[]{:S(2)}, u32[]{:S(2)}) collective-permute-start(bf16[96,1664]{1,0:T(8,128)(2,1)S(1)} %get-tuple-element.46), channel_id=1, source_target_pairs={{0,1},{1,2},{2,3},{3,0},{4,5},{5,6},{6,7},{7,4},{8,9},{9,10},{10,1... | collective-permute-start | bytes 958472 | tf_op jit(solution)/shard_map/ppermute | solution.py:79
  15.4 0.7 gather_fusion
  16.1 0.7 gather_fusion.1
  16.8 5.6 %fusion.52 = (f32[96]{0:T(128)S(1)}, f32[96,3072]{1,0:T(8,128)S(1)}) fusion(bf16[96,1536]{1,0:T(8,128)(2,1)S(1)} %fusion.12, bf16[1536,3072]{1,0:T(8,128)(2,1)} %param.8), kind=kOutput, calls=%fused_computation.204 | convolution fusion | flops 906264448 | bytes 10912128 | tf_op jit(solution)/shard_map/dot_general | solution.py:89
  22.4 0.2 fusion.20
  22.6 0.5 fusion.8
  23.2 0.2 maximum_reduce_fusion
  23.4 0.2 pad_maximum_fusion
  23.6 0.1 fusion.49
  23.7 3.1 %collective-permute-start.7 = (bf16[4,48,1664]{2,1,0:T(8,128)(2,1)S(1)}, bf16[4,48,1664]{2,1,0:T(8,128)(2,1)S(1)}, u32[]{:S(2)}, u32[]{:S(2)}) collective-permute-start(bf16[4,48,1664]{2,1,0:T(8,128)(2,1)S(1)} %get-tuple-element.43), channel_id=1, source_target_pairs={{0,8},{1,9},{2,10},{3,11},{4,12},{5,13},{6,14},{7,15},{8,0},{9,1},... | collective-permute-start | bytes 1916936 | tf_op jit(solution)/shard_map/ppermute | solution.py:79
  26.8 1.1 collective-permute-start.5
  27.9 0.9 collective-permute-start.3
  28.8 0.6 collective-permute-start.8
  29.5 2.6 %collective-permute-start.6 = (bf16[4,48,1664]{2,1,0:T(8,128)(2,1)S(1)}, bf16[4,48,1664]{2,1,0:T(8,128)(2,1)S(1)}, u32[]{:S(2)}, u32[]{:S(2)}) collective-permute-start(bf16[4,48,1664]{2,1,0:T(8,128)(2,1)S(1)} %get-tuple-element.44), channel_id=1, source_target_pairs={{0,12},{1,13},{2,14},{3,15},{4,0},{5,1},{6,2},{7,3},{8,4},{9,5},{1... | collective-permute-start | bytes 1916936 | tf_op jit(solution)/shard_map/ppermute | solution.py:79
  32.2 2.1 %fusion.53 = (f32[192]{0:T(256)S(1)}, f32[192,3072]{1,0:T(8,128)S(1)}) fusion(bf16[1536,3072]{1,0:T(8,128)(2,1)S(1)} %bitcast.43, bf16[192,1664]{1,0:T(8,128)(2,1)S(1)} %constant_dynamic-update-slice_fusion), kind=kOutput, calls=%fused_computation.205 | convolution fusion | flops 1812528896 | bytes 12387072 | tf_op jit(solution)/shard_map/dot_general | solution.py:89
  34.4 0.2 fusion.18
  34.5 1.8 %fusion.54 = (f32[96]{0:T(128)S(1)}, f32[96,3072]{1,0:T(8,128)S(1)}) fusion(bf16[1536,3072]{1,0:T(8,128)(2,1)S(1)} %bitcast.43, bf16[96,1664]{1,0:T(8,128)(2,1)S(1)} %collective-permute-done.2), kind=kOutput, calls=%fused_computation.206 | convolution fusion | flops 906264448 | bytes 10912128 | tf_op jit(solution)/shard_map/dot_general | solution.py:89
  36.3 0.5 fusion.7
  36.9 0.2 fusion.16
  37.1 1.0 fusion.4
  38.1 0.3 collective-permute-start.4
  38.4 11.2 %collective-permute-done.8 = bf16[4,48,1664]{2,1,0:T(8,128)(2,1)S(1)} collective-permute-done((bf16[4,48,1664]{2,1,0:T(8,128)(2,1)S(1)}, bf16[4,48,1664]{2,1,0:T(8,128)(2,1)S(1)}, u32[]{:S(2)}, u32[]{:S(2)}) %collective-permute-start.8) | collective-permute-done | bytes 639008 | tf_op jit(solution)/shard_map/ppermute | solution.py:79
  49.6 5.7 %fusion.56 = (f32[384]{0:T(512)S(1)}, f32[384,3072]{1,0:T(8,128)}) fusion(bf16[1536,3072]{1,0:T(8,128)(2,1)S(1)} %bitcast.43, bf16[384,1664]{1,0:T(8,128)(2,1)S(1)} %bitcast.53), kind=kOutput, calls=%fused_computation.208 | convolution fusion | flops 3625057792 | bytes 15336960 | tf_op jit(solution)/shard_map/dot_general | solution.py:89
  55.4 1.0 collective-permute-done.6
  56.4 0.2 maximum_maximum_fusion
  56.6 9.9 %fusion.55 = (f32[768]{0:T(1024)S(1)}, f32[768,3072]{1,0:T(8,128)}) fusion(bf16[1536,3072]{1,0:T(8,128)(2,1)S(1)} %bitcast.43, bf16[768,1664]{1,0:T(8,128)(2,1)S(1)} %bitcast.47), kind=kOutput, calls=%fused_computation.207 | convolution fusion | flops 7250115584 | bytes 21236736 | tf_op jit(solution)/shard_map/dot_general | solution.py:89
  66.6 0.2 slice_reduce_fusion.6
  66.8 0.2 slice_reduce_fusion.7
  66.9 0.2 slice_reduce_fusion.8
  67.2 0.7 gather_fusion.3
  67.9 0.6 fusion.47
  68.8 0.1 copy.16
  69.0 4.0 %fusion.1 = (f32[384]{0:T(512)S(1)}, f32[384]{0:T(512)S(1)}, f32[384]{0:T(512)S(1)}) fusion(f32[384,3072]{1,0:T(8,128)} %get-tuple-element.76, f32[384]{0:T(512)S(1)} %get-tuple-element.75, s32[384]{0:T(512)S(1)} %fusion.31), kind=kLoop, calls=%fused_computation.13 | loop fusion | flops 8256384 | bytes 4726272 | tf_op jit(solution)/shard_map/reduce_sum | solution.py:92
  73.0 6.3 %fusion = (f32[768]{0:T(1024)S(1)}, f32[768]{0:T(1024)S(1)}, f32[768]{0:T(1024)S(1)}) fusion(f32[768,3072]{1,0:T(8,128)} %get-tuple-element.74, f32[768]{0:T(1024)S(1)} %get-tuple-element.73, s32[768]{0:T(1024)S(1)} %fusion.29), kind=kLoop, calls=%fused_computation.8 | loop fusion | flops 16512768 | bytes 9452544 | tf_op jit(solution)/shard_map/reduce_sum | solution.py:92
  79.4 0.1 concatenate.33
  79.6 0.6 gather_fusion.2
  80.4 1.1 collective-permute-start.9
  81.5 2.8 %collective-permute-done.9 = f32[4,1536]{1,0:T(4,128)S(1)} collective-permute-done((f32[4,1536]{1,0:T(4,128)S(1)}, f32[4,1536]{1,0:T(4,128)S(1)}, u32[]{:S(2)}, u32[]{:S(2)}) %collective-permute-start.9) | collective-permute-done | bytes 24608 | tf_op jit(solution)/shard_map/ppermute | solution.py:32
  84.4 2.3 %collective-permute-start.10 = (f32[4,1536]{1,0:T(4,128)S(1)}, f32[4,1536]{1,0:T(4,128)S(1)}, u32[]{:S(2)}, u32[]{:S(2)}) collective-permute-start(f32[4,1536]{1,0:T(4,128)S(1)} %pad_maximum_fusion.3), channel_id=1, source_target_pairs={{0,3},{1,2},{2,1},{3,0},{4,7},{5,6},{6,5},{7,4},{8,11},{9,10},{10,... | collective-permute-start | bytes 73736 | tf_op jit(solution)/shard_map/ppermute | solution.py:32
  86.7 2.8 %collective-permute-done.10 = f32[4,1536]{1,0:T(4,128)S(1)} collective-permute-done((f32[4,1536]{1,0:T(4,128)S(1)}, f32[4,1536]{1,0:T(4,128)S(1)}, u32[]{:S(2)}, u32[]{:S(2)}) %collective-permute-start.10) | collective-permute-done | bytes 24608 | tf_op jit(solution)/shard_map/ppermute | solution.py:32
  89.7 1.5 %collective-permute-start.11 = (f32[4,1536]{1,0:T(4,128)S(1)}, f32[4,1536]{1,0:T(4,128)S(1)}, u32[]{:S(2)}, u32[]{:S(2)}) collective-permute-start(f32[4,1536]{1,0:T(4,128)S(1)} %pad_maximum_fusion.4), channel_id=1, source_target_pairs={{0,4},{1,5},{2,6},{3,7},{4,0},{5,1},{6,2},{7,3},{8,12},{9,13},{10,... | collective-permute-start | bytes 73736 | tf_op jit(solution)/shard_map/ppermute | solution.py:32
  91.2 2.4 %collective-permute-done.11 = f32[4,1536]{1,0:T(4,128)S(1)} collective-permute-done((f32[4,1536]{1,0:T(4,128)S(1)}, f32[4,1536]{1,0:T(4,128)S(1)}, u32[]{:S(2)}, u32[]{:S(2)}) %collective-permute-start.11) | collective-permute-done | bytes 24608 | tf_op jit(solution)/shard_map/ppermute | solution.py:32
  93.7 2.7 %collective-permute-start.12 = (f32[4,1536]{1,0:T(4,128)S(1)}, f32[4,1536]{1,0:T(4,128)S(1)}, u32[]{:S(2)}, u32[]{:S(2)}) collective-permute-start(f32[4,1536]{1,0:T(4,128)S(1)} %pad_maximum_fusion.5), channel_id=1, source_target_pairs={{0,12},{1,13},{2,14},{3,15},{4,8},{5,9},{6,10},{7,11},{8,4},{9,5},... | collective-permute-start | bytes 73736 | tf_op jit(solution)/shard_map/ppermute | solution.py:32
  97.2 1.6 %collective-permute-done.12 = f32[4,1536]{1,0:T(4,128)S(1)} collective-permute-done((f32[4,1536]{1,0:T(4,128)S(1)}, f32[4,1536]{1,0:T(4,128)S(1)}, u32[]{:S(2)}, u32[]{:S(2)}) %collective-permute-start.12) | collective-permute-done | bytes 24608 | tf_op jit(solution)/shard_map/ppermute | solution.py:32
  98.9 0.8 select_reduce_fusion.5
  99.6 0.7 pad_maximum_fusion.11
  100.4 0.2 fusion.45
  100.6 0.2 fusion.44
  100.8 0.2 select_dynamic-update-slice_fusion
  101.0 0.6 collective-permute-done.13
  101.5 0.7 fusion.36
  102.3 1.6 %collective-permute-start.14 = (f32[2]{0:T(128)S(1)}, f32[2]{0:T(128)S(1)}, u32[]{:S(2)}, u32[]{:S(2)}) collective-permute-start(f32[2]{0:T(128)S(1)} %fusion.36), channel_id=1, source_target_pairs={{0,32},{16,48},{32,0},{48,16},{64,96},{80,112},{96,64},{112,80},{1... | collective-permute-start | bytes 32 | tf_op jit(solution)/shard_map/ppermute | solution.py:32
  103.9 2.0 %collective-permute-done.14 = f32[2]{0:T(128)S(1)} collective-permute-done((f32[2]{0:T(128)S(1)}, f32[2]{0:T(128)S(1)}, u32[]{:S(2)}, u32[]{:S(2)}) %collective-permute-start.14) | collective-permute-done | bytes 40 | tf_op jit(solution)/shard_map/ppermute | solution.py:32
  105.9 3.0 %collective-permute-start.15 = (f32[2]{0:T(128)S(1)}, f32[2]{0:T(128)S(1)}, u32[]{:S(2)}, u32[]{:S(2)}) collective-permute-start(f32[2]{0:T(128)S(1)} %fusion.35), channel_id=1, source_target_pairs={{0,96},{16,112},{32,64},{48,80},{64,32},{80,48},{96,0},{112,16},{1... | collective-permute-start | bytes 32 | tf_op jit(solution)/shard_map/ppermute | solution.py:32
  108.9 1.8 %collective-permute-done.15 = f32[2]{0:T(128)S(1)} collective-permute-done((f32[2]{0:T(128)S(1)}, f32[2]{0:T(128)S(1)}, u32[]{:S(2)}, u32[]{:S(2)}) %collective-permute-start.15) | collective-permute-done | bytes 40 | tf_op jit(solution)/shard_map/ppermute | solution.py:32
  110.6 0.6 fusion.50
  (89 shorter events, 1.8 us)
Async XLA Ops:
  0.6 14.8 %copy-start = (s32[4]{0:T(128)S(1)}, s32[4]{0:T(128)}, u32[]{:S(2)}) copy-start(s32[4]{0:T(128)} %constant.170.clone) | copy-start | bytes 52
  9.3 13.9 %collective-permute-start.2 = (bf16[96,1664]{1,0:T(8,128)(2,1)S(1)}, bf16[96,1664]{1,0:T(8,128)(2,1)S(1)}, u32[]{:S(2)}, u32[]{:S(2)}) collective-permute-start(bf16[96,1664]{1,0:T(8,128)(2,1)S(1)} %get-tuple-element.46), channel_id=1, source_target_pairs={{0,2},{1,3},{2,0},{3,1},{4,6},{5,7},{6,4},{7,5},{8,10},{9,11},{10,... | collective-permute-start | bytes 958472 | tf_op jit(solution)/shard_map/ppermute | solution.py:79
  13.3 9.9 %collective-permute-start.1 = (bf16[96,1664]{1,0:T(8,128)(2,1)S(1)}, bf16[96,1664]{1,0:T(8,128)(2,1)S(1)}, u32[]{:S(2)}, u32[]{:S(2)}) collective-permute-start(bf16[96,1664]{1,0:T(8,128)(2,1)S(1)} %get-tuple-element.46), channel_id=1, source_target_pairs={{0,3},{1,0},{2,1},{3,2},{4,7},{5,4},{6,5},{7,6},{8,11},{9,8},{10,9... | collective-permute-start | bytes 958472 | tf_op jit(solution)/shard_map/ppermute | solution.py:79
  14.0 9.2 %collective-permute-start = (bf16[96,1664]{1,0:T(8,128)(2,1)S(1)}, bf16[96,1664]{1,0:T(8,128)(2,1)S(1)}, u32[]{:S(2)}, u32[]{:S(2)}) collective-permute-start(bf16[96,1664]{1,0:T(8,128)(2,1)S(1)} %get-tuple-element.46), channel_id=1, source_target_pairs={{0,1},{1,2},{2,3},{3,0},{4,5},{5,6},{6,7},{7,4},{8,9},{9,10},{10,1... | collective-permute-start | bytes 958472 | tf_op jit(solution)/shard_map/ppermute | solution.py:79
  16.8 15.4 %slice-start = ((s8[9437184]{0:T(1024)(128)(4,1)}), s8[4194304]{0:T(1024)(128)(4,1)S(1)}, s32[]{:S(2)}) async-start(s8[9437184]{0:T(1024)(128)(4,1)} %bitcast.42), calls=%async_computation | async-start | bytes 8388608
  16.8 15.4 %slice-start.1 = ((s8[9437184]{0:T(1024)(128)(4,1)}), s8[4194304]{0:T(1024)(128)(4,1)S(1)}, s32[]{:S(2)}) async-start(s8[9437184]{0:T(1024)(128)(4,1)} %bitcast.42), calls=%async_computation.1 | async-start | bytes 8388608
  22.6 9.6 %slice-start.2 = ((s8[9437184]{0:T(1024)(128)(4,1)}), s8[1048576]{0:T(1024)(128)(4,1)S(1)}, s32[]{:S(2)}) async-start(s8[9437184]{0:T(1024)(128)(4,1)} %bitcast.42), calls=%async_computation.2 | async-start | bytes 2097152
  23.7 14.4 %collective-permute-start.7 = (bf16[4,48,1664]{2,1,0:T(8,128)(2,1)S(1)}, bf16[4,48,1664]{2,1,0:T(8,128)(2,1)S(1)}, u32[]{:S(2)}, u32[]{:S(2)}) collective-permute-start(bf16[4,48,1664]{2,1,0:T(8,128)(2,1)S(1)} %get-tuple-element.43), channel_id=1, source_target_pairs={{0,8},{1,9},{2,10},{3,11},{4,12},{5,13},{6,14},{7,15},{8,0},{9,1},... | collective-permute-start | bytes 1916936 | tf_op jit(solution)/shard_map/ppermute | solution.py:79
  26.8 28.6 %collective-permute-start.5 = (bf16[4,48,1664]{2,1,0:T(8,128)(2,1)S(1)}, bf16[4,48,1664]{2,1,0:T(8,128)(2,1)S(1)}, u32[]{:S(2)}, u32[]{:S(2)}) collective-permute-start(bf16[4,48,1664]{2,1,0:T(8,128)(2,1)S(1)} %get-tuple-element.43), channel_id=1, source_target_pairs={{0,12},{1,13},{2,14},{3,15},{4,0},{5,1},{6,2},{7,3},{8,4},{9,5},{1... | collective-permute-start | bytes 1916936 | tf_op jit(solution)/shard_map/ppermute | solution.py:79
  27.9 27.4 %collective-permute-start.3 = (bf16[4,48,1664]{2,1,0:T(8,128)(2,1)S(1)}, bf16[4,48,1664]{2,1,0:T(8,128)(2,1)S(1)}, u32[]{:S(2)}, u32[]{:S(2)}) collective-permute-start(bf16[4,48,1664]{2,1,0:T(8,128)(2,1)S(1)} %get-tuple-element.43), channel_id=1, source_target_pairs={{0,4},{1,5},{2,6},{3,7},{4,8},{5,9},{6,10},{7,11},{8,12},{9,13},{1... | collective-permute-start | bytes 1916936 | tf_op jit(solution)/shard_map/ppermute | solution.py:79
  28.8 20.7 %collective-permute-start.8 = (bf16[4,48,1664]{2,1,0:T(8,128)(2,1)S(1)}, bf16[4,48,1664]{2,1,0:T(8,128)(2,1)S(1)}, u32[]{:S(2)}, u32[]{:S(2)}) collective-permute-start(bf16[4,48,1664]{2,1,0:T(8,128)(2,1)S(1)} %get-tuple-element.44), channel_id=1, source_target_pairs={{0,8},{1,9},{2,10},{3,11},{4,12},{5,13},{6,14},{7,15},{8,0},{9,1},... | collective-permute-start | bytes 1916936 | tf_op jit(solution)/shard_map/ppermute | solution.py:79
  29.5 26.9 %collective-permute-start.6 = (bf16[4,48,1664]{2,1,0:T(8,128)(2,1)S(1)}, bf16[4,48,1664]{2,1,0:T(8,128)(2,1)S(1)}, u32[]{:S(2)}, u32[]{:S(2)}) collective-permute-start(bf16[4,48,1664]{2,1,0:T(8,128)(2,1)S(1)} %get-tuple-element.44), channel_id=1, source_target_pairs={{0,12},{1,13},{2,14},{3,15},{4,0},{5,1},{6,2},{7,3},{8,4},{9,5},{1... | collective-permute-start | bytes 1916936 | tf_op jit(solution)/shard_map/ppermute | solution.py:79
  38.1 18.3 %collective-permute-start.4 = (bf16[4,48,1664]{2,1,0:T(8,128)(2,1)S(1)}, bf16[4,48,1664]{2,1,0:T(8,128)(2,1)S(1)}, u32[]{:S(2)}, u32[]{:S(2)}) collective-permute-start(bf16[4,48,1664]{2,1,0:T(8,128)(2,1)S(1)} %get-tuple-element.44), channel_id=1, source_target_pairs={{0,4},{1,5},{2,6},{3,7},{4,8},{5,9},{6,10},{7,11},{8,12},{9,13},{1... | collective-permute-start | bytes 1916936 | tf_op jit(solution)/shard_map/ppermute | solution.py:79
  80.4 3.9 %collective-permute-start.9 = (f32[4,1536]{1,0:T(4,128)S(1)}, f32[4,1536]{1,0:T(4,128)S(1)}, u32[]{:S(2)}, u32[]{:S(2)}) collective-permute-start(f32[4,1536]{1,0:T(4,128)S(1)} %broadcast_select_fusion), channel_id=1, source_target_pairs={{0,1},{1,0},{2,3},{3,2},{4,5},{5,4},{6,7},{7,6},{8,9},{9,8},{10,11... | collective-permute-start | bytes 73736 | tf_op jit(solution)/shard_map/ppermute | solution.py:32
  84.4 5.1 %collective-permute-start.10 = (f32[4,1536]{1,0:T(4,128)S(1)}, f32[4,1536]{1,0:T(4,128)S(1)}, u32[]{:S(2)}, u32[]{:S(2)}) collective-permute-start(f32[4,1536]{1,0:T(4,128)S(1)} %pad_maximum_fusion.3), channel_id=1, source_target_pairs={{0,3},{1,2},{2,1},{3,0},{4,7},{5,6},{6,5},{7,4},{8,11},{9,10},{10,... | collective-permute-start | bytes 73736 | tf_op jit(solution)/shard_map/ppermute | solution.py:32
  89.7 3.9 %collective-permute-start.11 = (f32[4,1536]{1,0:T(4,128)S(1)}, f32[4,1536]{1,0:T(4,128)S(1)}, u32[]{:S(2)}, u32[]{:S(2)}) collective-permute-start(f32[4,1536]{1,0:T(4,128)S(1)} %pad_maximum_fusion.4), channel_id=1, source_target_pairs={{0,4},{1,5},{2,6},{3,7},{4,0},{5,1},{6,2},{7,3},{8,12},{9,13},{10,... | collective-permute-start | bytes 73736 | tf_op jit(solution)/shard_map/ppermute | solution.py:32
  93.7 5.1 %collective-permute-start.12 = (f32[4,1536]{1,0:T(4,128)S(1)}, f32[4,1536]{1,0:T(4,128)S(1)}, u32[]{:S(2)}, u32[]{:S(2)}) collective-permute-start(f32[4,1536]{1,0:T(4,128)S(1)} %pad_maximum_fusion.5), channel_id=1, source_target_pairs={{0,12},{1,13},{2,14},{3,15},{4,8},{5,9},{6,10},{7,11},{8,4},{9,5},... | collective-permute-start | bytes 73736 | tf_op jit(solution)/shard_map/ppermute | solution.py:32
  100.4 1.2 %collective-permute-start.13 = (f32[2]{0:T(128)S(1)}, f32[2]{0:T(128)S(1)}, u32[]{:S(2)}, u32[]{:S(2)}) collective-permute-start(f32[2]{0:T(128)S(1)} %pad_maximum_fusion.11), channel_id=1, source_target_pairs={{0,16},{16,0},{32,48},{48,32},{64,80},{80,64},{96,112},{112,96},{1... | collective-permute-start | bytes 32 | tf_op jit(solution)/shard_map/ppermute | solution.py:32
  100.6 12.0 %copy-start.2 = (f32[128]{0:T(128)}, f32[128]{0:T(128)S(1)}, u32[]{:S(2)}) copy-start(f32[128]{0:T(128)S(1)} %fusion.45) | copy-start | bytes 1540
  100.8 11.8 %copy-start.3 = (f32[128]{0:T(128)}, f32[128]{0:T(128)S(1)}, u32[]{:S(2)}) copy-start(f32[128]{0:T(128)S(1)} %fusion.44) | copy-start | bytes 1540
  101.0 11.7 %copy-start.1 = (f32[128]{0:T(128)}, f32[128]{0:T(128)S(1)}, u32[]{:S(2)}) copy-start(f32[128]{0:T(128)S(1)} %select_dynamic-update-slice_fusion) | copy-start | bytes 1540
  102.3 3.6 %collective-permute-start.14 = (f32[2]{0:T(128)S(1)}, f32[2]{0:T(128)S(1)}, u32[]{:S(2)}, u32[]{:S(2)}) collective-permute-start(f32[2]{0:T(128)S(1)} %fusion.36), channel_id=1, source_target_pairs={{0,32},{16,48},{32,0},{48,16},{64,96},{80,112},{96,64},{112,80},{1... | collective-permute-start | bytes 32 | tf_op jit(solution)/shard_map/ppermute | solution.py:32
  105.9 4.8 %collective-permute-start.15 = (f32[2]{0:T(128)S(1)}, f32[2]{0:T(128)S(1)}, u32[]{:S(2)}, u32[]{:S(2)}) collective-permute-start(f32[2]{0:T(128)S(1)} %fusion.35), channel_id=1, source_target_pairs={{0,96},{16,112},{32,64},{48,80},{64,32},{80,48},{96,0},{112,16},{1... | collective-permute-start | bytes 32 | tf_op jit(solution)/shard_map/ppermute | solution.py:32

commit v16 on v15

--- a/solution.py
+++ b/solution.py
@@ -108,8 +108,15 @@
     values = hidden.astype(jnp.float32)
     meansq = jnp.mean(values * values, axis=-1, keepdims=True)
     normed_all = (values * lax.rsqrt(meansq + 1e-05) * norm_gain).astype(jnp.bfloat16)
-    normed = lax.dynamic_slice_in_dim(normed_all, start, LIVE, 0)
-    ids = lax.dynamic_slice_in_dim(targets, start, LIVE, 0)
+    pick = (
+        lax.broadcasted_iota(jnp.int32, (LIVE, slots), 1)
+        == lax.broadcasted_iota(jnp.int32, (LIVE, slots), 0) + start
+    )
+    normed = jnp.dot(pick.astype(jnp.bfloat16), normed_all, preferred_element_type=jnp.float32)
+    normed = normed.astype(jnp.bfloat16)
+    ids = jnp.dot(
+        pick.astype(jnp.float32), targets.astype(jnp.float32), precision=lax.Precision.HIGHEST
+    ).astype(jnp.int32)
     column = lax.broadcasted_iota(jnp.int32, (LIVE, EXTRA), 1)
     meta = jnp.where(column == 0, ids[:, None] // 256, ids[:, None] % 256)
     meta = jnp.where(column == 2, live_count, jnp.where(column < 2, meta, 0))

time: 114 us -> 112 us (0.982)
  matrix products: 25.2 us -> 27.4 us
  other arithmetic: 21.7 us -> 19.7 us
  waiting for transfers between devices: 26.2 us -> 24.3 us
    dot_general x0 -> x2, matrix products: none -> 2.21 us  [the longest x1 1.31 us: shards(): jnp.dot(pick.astype(jnp.bfloat16), normed_all, preferred_element_type=jnp...]
    ppermute x7, waiting for transfers between devices: 14 us -> 12.1 us  [butterfly(): other = lax.ppermute(value, axis, [(i, i ^ flip) for i in range(size)])]
    convert_element_type x2 -> x0, other arithmetic: 1.89 us -> none  [the longest x1 1.07 us: shards(): values = hidden.astype(jnp.float32)]
where the time goes in v16:
time: 112 us
  matrix products  27.4 us (24%)
  starting transfers between devices  26.9 us (24%)
  waiting for transfers between devices  24.3 us (22%)
  other arithmetic  19.7 us (18%)
  between operations  7.61 us (7%)
  local copies, waits for them, and re-layouts  6.03 us (5%)
    dot_general x5, matrix products, block_stats(): logits = jnp.dot(rows_in, head, preferred_element_type=jnp.float32)  25.2 us
    ppermute x9, starting transfers between devices, shift(): return lax.ppermute(value, AXES, pairs)  14.7 us
    reduce_sum x5, other arithmetic, block_stats(): total = jnp.sum(expo, axis=-1)  12.3 us
    ppermute x9, waiting for transfers between devices, shift(): return lax.ppermute(value, AXES, pairs)  12.2 us
    ppermute x7, starting transfers between devices, butterfly(): other = lax.ppermute(value, axis, [(i, i ^ flip) for i in range(size)])  12.2 us
    ppermute x7, waiting for transfers between devices, butterfly(): other = lax.ppermute(value, axis, [(i, i ^ flip) for i in range(size)])  12.1 us
  transfers between devices with their start and end apart: 16, of which 9 were waited for; matrix products, arithmetic and copies ran while one was open for 18% of the time, Pallas kernels for 0%

profile of v16, /device:TPU:0, one launch (start us, length us, event | category | flops | bytes accessed | tf_op | source)
XLA Modules:
  0.0 112.0 jit_solution(2063974362724777477)
XLA Ops:
  0.7 1.2 %fusion.10 = f32[128]{0:T(128)S(1)} fusion(bf16[128,1536]{1,0:T(8,128)(2,1)} %param.6), kind=kLoop, calls=%fused_computation.41 | loop fusion | flops 589696 | bytes 393728 | tf_op jit(solution)/shard_map/reduce_sum | solution.py:109
  1.8 1.3 %fusion.58 = (s32[1,1]{1,0:T(1,128)}, s32[1,1]{1,0:T(1,128)}) fusion(s32[1,2]{1,0:T(1,128)} %param.10), kind=kLoop, calls=%fused_computation.214 | loop fusion | bytes 16 | tf_op jit(solution)/shard_map/slice | solution.py:106
  3.2 0.6 iota_add_fusion
  5.1 0.9 and_select_fusion.1
  6.0 1.3 %convolution_convert_fusion = bf16[96,1536]{1,0:T(8,128)(2,1)S(1)} fusion(bf16[128,1536]{1,0:T(8,128)(2,1)} %param.6, f32[1536]{0:T(1024)} %param.7, f32[128]{0:T(128)S(1)} %add_rsqrt_fusion, s32[96]{0:T(128)S(1)} %iota_add_fusion), kind=kOutput, calls=%fused_computation.22 | convolution fusion | flops 38694912 | bytes 695168 | tf_op jit(solution)/shard_map/dot_general | solution.py:115
  7.3 0.1 select_convert_fusion
  7.5 4.1 %collective-permute-start.2 = (bf16[96,1664]{1,0:T(8,128)(2,1)S(1)}, bf16[96,1664]{1,0:T(8,128)(2,1)S(1)}, u32[]{:S(2)}, u32[]{:S(2)}) collective-permute-start(bf16[96,1664]{1,0:T(8,128)(2,1)S(1)} %get-tuple-element.44), channel_id=1, source_target_pairs={{0,2},{1,3},{2,0},{3,1},{4,6},{5,7},{6,4},{7,5},{8,10},{9,11},{10,... | collective-permute-start | bytes 958472 | tf_op jit(solution)/shard_map/ppermute | solution.py:79
  11.6 0.7 collective-permute-start.1
  12.3 1.3 %collective-permute-start = (bf16[96,1664]{1,0:T(8,128)(2,1)S(1)}, bf16[96,1664]{1,0:T(8,128)(2,1)S(1)}, u32[]{:S(2)}, u32[]{:S(2)}) collective-permute-start(bf16[96,1664]{1,0:T(8,128)(2,1)S(1)} %get-tuple-element.44), channel_id=1, source_target_pairs={{0,1},{1,2},{2,3},{3,0},{4,5},{5,6},{6,7},{7,4},{8,9},{9,10},{10,1... | collective-permute-start | bytes 958472 | tf_op jit(solution)/shard_map/ppermute | solution.py:79
  13.7 0.7 gather_fusion
  14.3 0.7 gather_fusion.1
  15.0 5.6 %fusion.59 = (f32[96]{0:T(128)S(1)}, f32[96,3072]{1,0:T(8,128)S(1)}) fusion(bf16[96,1536]{1,0:T(8,128)(2,1)S(1)} %convolution_convert_fusion, bf16[1536,3072]{1,0:T(8,128)(2,1)} %param.8), kind=kOutput, calls=%fused_computation.215 | convolution fusion | flops 906264448 | bytes 10912128 | tf_op jit(solution)/shard_map/dot_general | solution.py:89
  20.7 0.2 fusion.25
  20.9 0.5 fusion.8
  21.4 0.2 maximum_reduce_fusion
  21.6 0.2 pad_maximum_fusion
  21.8 0.1 fusion.56
  21.9 3.1 %collective-permute-start.7 = (bf16[4,48,1664]{2,1,0:T(8,128)(2,1)S(1)}, bf16[4,48,1664]{2,1,0:T(8,128)(2,1)S(1)}, u32[]{:S(2)}, u32[]{:S(2)}) collective-permute-start(bf16[4,48,1664]{2,1,0:T(8,128)(2,1)S(1)} %get-tuple-element.41), channel_id=1, source_target_pairs={{0,8},{1,9},{2,10},{3,11},{4,12},{5,13},{6,14},{7,15},{8,0},{9,1},... | collective-permute-start | bytes 1916936 | tf_op jit(solution)/shard_map/ppermute | solution.py:79
  25.0 1.1 %collective-permute-start.5 = (bf16[4,48,1664]{2,1,0:T(8,128)(2,1)S(1)}, bf16[4,48,1664]{2,1,0:T(8,128)(2,1)S(1)}, u32[]{:S(2)}, u32[]{:S(2)}) collective-permute-start(bf16[4,48,1664]{2,1,0:T(8,128)(2,1)S(1)} %get-tuple-element.41), channel_id=1, source_target_pairs={{0,12},{1,13},{2,14},{3,15},{4,0},{5,1},{6,2},{7,3},{8,4},{9,5},{1... | collective-permute-start | bytes 1916936 | tf_op jit(solution)/shard_map/ppermute | solution.py:79
  26.2 0.9 collective-permute-start.3
  27.1 0.6 collective-permute-start.8
  27.7 2.6 %collective-permute-start.6 = (bf16[4,48,1664]{2,1,0:T(8,128)(2,1)S(1)}, bf16[4,48,1664]{2,1,0:T(8,128)(2,1)S(1)}, u32[]{:S(2)}, u32[]{:S(2)}) collective-permute-start(bf16[4,48,1664]{2,1,0:T(8,128)(2,1)S(1)} %get-tuple-element.42), channel_id=1, source_target_pairs={{0,12},{1,13},{2,14},{3,15},{4,0},{5,1},{6,2},{7,3},{8,4},{9,5},{1... | collective-permute-start | bytes 1916936 | tf_op jit(solution)/shard_map/ppermute | solution.py:79
  30.5 2.1 %fusion.60 = (f32[192]{0:T(256)S(1)}, f32[192,3072]{1,0:T(8,128)S(1)}) fusion(bf16[1536,3072]{1,0:T(8,128)(2,1)S(1)} %bitcast.52, bf16[192,1664]{1,0:T(8,128)(2,1)S(1)} %constant_dynamic-update-slice_fusion), kind=kOutput, calls=%fused_computation.216 | convolution fusion | flops 1812528896 | bytes 12387072 | tf_op jit(solution)/shard_map/dot_general | solution.py:89
  32.6 0.2 fusion.23
  32.8 1.8 %fusion.61 = (f32[96]{0:T(128)S(1)}, f32[96,3072]{1,0:T(8,128)S(1)}) fusion(bf16[1536,3072]{1,0:T(8,128)(2,1)S(1)} %bitcast.52, bf16[96,1664]{1,0:T(8,128)(2,1)S(1)} %collective-permute-done.2), kind=kOutput, calls=%fused_computation.217 | convolution fusion | flops 906264448 | bytes 10912128 | tf_op jit(solution)/shard_map/dot_general | solution.py:89
  34.6 0.5 fusion.7
  35.1 0.2 fusion.21
  35.3 1.0 fusion.4
  36.3 0.3 collective-permute-start.4
  36.6 11.2 %collective-permute-done.8 = bf16[4,48,1664]{2,1,0:T(8,128)(2,1)S(1)} collective-permute-done((bf16[4,48,1664]{2,1,0:T(8,128)(2,1)S(1)}, bf16[4,48,1664]{2,1,0:T(8,128)(2,1)S(1)}, u32[]{:S(2)}, u32[]{:S(2)}) %collective-permute-start.8) | collective-permute-done | bytes 639008 | tf_op jit(solution)/shard_map/ppermute | solution.py:79
  47.9 5.7 %fusion.63 = (f32[384]{0:T(512)S(1)}, f32[384,3072]{1,0:T(8,128)}) fusion(bf16[1536,3072]{1,0:T(8,128)(2,1)S(1)} %bitcast.52, bf16[384,1664]{1,0:T(8,128)(2,1)S(1)} %bitcast.62), kind=kOutput, calls=%fused_computation.219 | convolution fusion | flops 3625057792 | bytes 15336960 | tf_op jit(solution)/shard_map/dot_general | solution.py:89
  53.6 1.0 collective-permute-done.6
  54.6 0.2 maximum_maximum_fusion
  54.9 9.9 %fusion.62 = (f32[768]{0:T(1024)S(1)}, f32[768,3072]{1,0:T(8,128)}) fusion(bf16[1536,3072]{1,0:T(8,128)(2,1)S(1)} %bitcast.52, bf16[768,1664]{1,0:T(8,128)(2,1)S(1)} %bitcast.56), kind=kOutput, calls=%fused_computation.218 | convolution fusion | flops 7250115584 | bytes 21236736 | tf_op jit(solution)/shard_map/dot_general | solution.py:89
  64.8 0.2 slice_reduce_fusion.6
  65.0 0.2 slice_reduce_fusion.7
  65.2 0.2 slice_reduce_fusion.8
  65.4 0.7 gather_fusion.3
  66.1 0.6 fusion.54
  67.0 0.1 copy.16
  67.2 4.0 %fusion.1 = (f32[384]{0:T(512)S(1)}, f32[384]{0:T(512)S(1)}, f32[384]{0:T(512)S(1)}) fusion(f32[384,3072]{1,0:T(8,128)} %get-tuple-element.76, f32[384]{0:T(512)S(1)} %get-tuple-element.75, s32[384]{0:T(512)S(1)} %fusion.38), kind=kLoop, calls=%fused_computation.13 | loop fusion | flops 8256384 | bytes 4726272 | tf_op jit(solution)/shard_map/reduce_sum | solution.py:92
  71.3 6.3 %fusion = (f32[768]{0:T(1024)S(1)}, f32[768]{0:T(1024)S(1)}, f32[768]{0:T(1024)S(1)}) fusion(f32[768,3072]{1,0:T(8,128)} %get-tuple-element.74, f32[768]{0:T(1024)S(1)} %get-tuple-element.73, s32[768]{0:T(1024)S(1)} %fusion.36), kind=kLoop, calls=%fused_computation.8 | loop fusion | flops 16512768 | bytes 9452544 | tf_op jit(solution)/shard_map/reduce_sum | solution.py:92
  77.7 0.1 concatenate.33
  77.9 0.6 gather_fusion.2
  78.6 1.1 collective-permute-start.9
  79.7 2.8 %collective-permute-done.9 = f32[4,1536]{1,0:T(4,128)S(1)} collective-permute-done((f32[4,1536]{1,0:T(4,128)S(1)}, f32[4,1536]{1,0:T(4,128)S(1)}, u32[]{:S(2)}, u32[]{:S(2)}) %collective-permute-start.9) | collective-permute-done | bytes 24608 | tf_op jit(solution)/shard_map/ppermute | solution.py:32
  82.6 2.3 %collective-permute-start.10 = (f32[4,1536]{1,0:T(4,128)S(1)}, f32[4,1536]{1,0:T(4,128)S(1)}, u32[]{:S(2)}, u32[]{:S(2)}) collective-permute-start(f32[4,1536]{1,0:T(4,128)S(1)} %pad_maximum_fusion.3), channel_id=1, source_target_pairs={{0,3},{1,2},{2,1},{3,0},{4,7},{5,6},{6,5},{7,4},{8,11},{9,10},{10,... | collective-permute-start | bytes 73736 | tf_op jit(solution)/shard_map/ppermute | solution.py:32
  84.9 2.8 %collective-permute-done.10 = f32[4,1536]{1,0:T(4,128)S(1)} collective-permute-done((f32[4,1536]{1,0:T(4,128)S(1)}, f32[4,1536]{1,0:T(4,128)S(1)}, u32[]{:S(2)}, u32[]{:S(2)}) %collective-permute-start.10) | collective-permute-done | bytes 24608 | tf_op jit(solution)/shard_map/ppermute | solution.py:32
  87.9 1.5 %collective-permute-start.11 = (f32[4,1536]{1,0:T(4,128)S(1)}, f32[4,1536]{1,0:T(4,128)S(1)}, u32[]{:S(2)}, u32[]{:S(2)}) collective-permute-start(f32[4,1536]{1,0:T(4,128)S(1)} %pad_maximum_fusion.4), channel_id=1, source_target_pairs={{0,4},{1,5},{2,6},{3,7},{4,0},{5,1},{6,2},{7,3},{8,12},{9,13},{10,... | collective-permute-start | bytes 73736 | tf_op jit(solution)/shard_map/ppermute | solution.py:32
  91.4 0.4 collective-permute-done.11
  92.0 2.7 %collective-permute-start.12 = (f32[4,1536]{1,0:T(4,128)S(1)}, f32[4,1536]{1,0:T(4,128)S(1)}, u32[]{:S(2)}, u32[]{:S(2)}) collective-permute-start(f32[4,1536]{1,0:T(4,128)S(1)} %pad_maximum_fusion.5), channel_id=1, source_target_pairs={{0,12},{1,13},{2,14},{3,15},{4,8},{5,9},{6,10},{7,11},{8,4},{9,5},... | collective-permute-start | bytes 73736 | tf_op jit(solution)/shard_map/ppermute | solution.py:32
  95.4 1.6 %collective-permute-done.12 = f32[4,1536]{1,0:T(4,128)S(1)} collective-permute-done((f32[4,1536]{1,0:T(4,128)S(1)}, f32[4,1536]{1,0:T(4,128)S(1)}, u32[]{:S(2)}, u32[]{:S(2)}) %collective-permute-start.12) | collective-permute-done | bytes 24608 | tf_op jit(solution)/shard_map/ppermute | solution.py:32
  97.1 0.8 select_reduce_fusion.5
  97.9 0.7 pad_maximum_fusion.11
  98.6 0.2 fusion.52
  98.8 0.2 fusion.51
  99.0 0.2 select_dynamic-update-slice_fusion
  99.2 0.6 collective-permute-done.13
  99.8 0.7 fusion.43
  100.5 1.6 %collective-permute-start.14 = (f32[2]{0:T(128)S(1)}, f32[2]{0:T(128)S(1)}, u32[]{:S(2)}, u32[]{:S(2)}) collective-permute-start(f32[2]{0:T(128)S(1)} %fusion.43), channel_id=1, source_target_pairs={{0,32},{16,48},{32,0},{48,16},{64,96},{80,112},{96,64},{112,80},{1... | collective-permute-start | bytes 32 | tf_op jit(solution)/shard_map/ppermute | solution.py:32
  102.1 2.0 %collective-permute-done.14 = f32[2]{0:T(128)S(1)} collective-permute-done((f32[2]{0:T(128)S(1)}, f32[2]{0:T(128)S(1)}, u32[]{:S(2)}, u32[]{:S(2)}) %collective-permute-start.14) | collective-permute-done | bytes 40 | tf_op jit(solution)/shard_map/ppermute | solution.py:32
  104.1 3.0 %collective-permute-start.15 = (f32[2]{0:T(128)S(1)}, f32[2]{0:T(128)S(1)}, u32[]{:S(2)}, u32[]{:S(2)}) collective-permute-start(f32[2]{0:T(128)S(1)} %fusion.42), channel_id=1, source_target_pairs={{0,96},{16,112},{32,64},{48,80},{64,32},{80,48},{96,0},{112,16},{1... | collective-permute-start | bytes 32 | tf_op jit(solution)/shard_map/ppermute | solution.py:32
  107.1 1.8 %collective-permute-done.15 = f32[2]{0:T(128)S(1)} collective-permute-done((f32[2]{0:T(128)S(1)}, f32[2]{0:T(128)S(1)}, u32[]{:S(2)}, u32[]{:S(2)}) %collective-permute-start.15) | collective-permute-done | bytes 40 | tf_op jit(solution)/shard_map/ppermute | solution.py:32
  108.9 0.6 fusion.57
  (87 shorter events, 1.7 us)
Async XLA Ops:
  0.6 13.0 %copy-start = (s32[4]{0:T(128)S(1)}, s32[4]{0:T(128)}, u32[]{:S(2)}) copy-start(s32[4]{0:T(128)} %constant.170.clone) | copy-start | bytes 52
  7.5 13.9 %collective-permute-start.2 = (bf16[96,1664]{1,0:T(8,128)(2,1)S(1)}, bf16[96,1664]{1,0:T(8,128)(2,1)S(1)}, u32[]{:S(2)}, u32[]{:S(2)}) collective-permute-start(bf16[96,1664]{1,0:T(8,128)(2,1)S(1)} %get-tuple-element.44), channel_id=1, source_target_pairs={{0,2},{1,3},{2,0},{3,1},{4,6},{5,7},{6,4},{7,5},{8,10},{9,11},{10,... | collective-permute-start | bytes 958472 | tf_op jit(solution)/shard_map/ppermute | solution.py:79
  11.6 9.9 %collective-permute-start.1 = (bf16[96,1664]{1,0:T(8,128)(2,1)S(1)}, bf16[96,1664]{1,0:T(8,128)(2,1)S(1)}, u32[]{:S(2)}, u32[]{:S(2)}) collective-permute-start(bf16[96,1664]{1,0:T(8,128)(2,1)S(1)} %get-tuple-element.44), channel_id=1, source_target_pairs={{0,3},{1,0},{2,1},{3,2},{4,7},{5,4},{6,5},{7,6},{8,11},{9,8},{10,9... | collective-permute-start | bytes 958472 | tf_op jit(solution)/shard_map/ppermute | solution.py:79
  12.3 9.2 %collective-permute-start = (bf16[96,1664]{1,0:T(8,128)(2,1)S(1)}, bf16[96,1664]{1,0:T(8,128)(2,1)S(1)}, u32[]{:S(2)}, u32[]{:S(2)}) collective-permute-start(bf16[96,1664]{1,0:T(8,128)(2,1)S(1)} %get-tuple-element.44), channel_id=1, source_target_pairs={{0,1},{1,2},{2,3},{3,0},{4,5},{5,6},{6,7},{7,4},{8,9},{9,10},{10,1... | collective-permute-start | bytes 958472 | tf_op jit(solution)/shard_map/ppermute | solution.py:79
  15.0 15.4 %slice-start = ((s8[9437184]{0:T(1024)(128)(4,1)}), s8[4194304]{0:T(1024)(128)(4,1)S(1)}, s32[]{:S(2)}) async-start(s8[9437184]{0:T(1024)(128)(4,1)} %bitcast.51), calls=%async_computation | async-start | bytes 8388608
  15.0 15.4 %slice-start.1 = ((s8[9437184]{0:T(1024)(128)(4,1)}), s8[4194304]{0:T(1024)(128)(4,1)S(1)}, s32[]{:S(2)}) async-start(s8[9437184]{0:T(1024)(128)(4,1)} %bitcast.51), calls=%async_computation.1 | async-start | bytes 8388608
  20.8 9.6 %slice-start.2 = ((s8[9437184]{0:T(1024)(128)(4,1)}), s8[1048576]{0:T(1024)(128)(4,1)S(1)}, s32[]{:S(2)}) async-start(s8[9437184]{0:T(1024)(128)(4,1)} %bitcast.51), calls=%async_computation.2 | async-start | bytes 2097152
  21.9 14.4 %collective-permute-start.7 = (bf16[4,48,1664]{2,1,0:T(8,128)(2,1)S(1)}, bf16[4,48,1664]{2,1,0:T(8,128)(2,1)S(1)}, u32[]{:S(2)}, u32[]{:S(2)}) collective-permute-start(bf16[4,48,1664]{2,1,0:T(8,128)(2,1)S(1)} %get-tuple-element.41), channel_id=1, source_target_pairs={{0,8},{1,9},{2,10},{3,11},{4,12},{5,13},{6,14},{7,15},{8,0},{9,1},... | collective-permute-start | bytes 1916936 | tf_op jit(solution)/shard_map/ppermute | solution.py:79
  25.0 28.6 %collective-permute-start.5 = (bf16[4,48,1664]{2,1,0:T(8,128)(2,1)S(1)}, bf16[4,48,1664]{2,1,0:T(8,128)(2,1)S(1)}, u32[]{:S(2)}, u32[]{:S(2)}) collective-permute-start(bf16[4,48,1664]{2,1,0:T(8,128)(2,1)S(1)} %get-tuple-element.41), channel_id=1, source_target_pairs={{0,12},{1,13},{2,14},{3,15},{4,0},{5,1},{6,2},{7,3},{8,4},{9,5},{1... | collective-permute-start | bytes 1916936 | tf_op jit(solution)/shard_map/ppermute | solution.py:79
  26.2 27.4 %collective-permute-start.3 = (bf16[4,48,1664]{2,1,0:T(8,128)(2,1)S(1)}, bf16[4,48,1664]{2,1,0:T(8,128)(2,1)S(1)}, u32[]{:S(2)}, u32[]{:S(2)}) collective-permute-start(bf16[4,48,1664]{2,1,0:T(8,128)(2,1)S(1)} %get-tuple-element.41), channel_id=1, source_target_pairs={{0,4},{1,5},{2,6},{3,7},{4,8},{5,9},{6,10},{7,11},{8,12},{9,13},{1... | collective-permute-start | bytes 1916936 | tf_op jit(solution)/shard_map/ppermute | solution.py:79
  27.1 20.7 %collective-permute-start.8 = (bf16[4,48,1664]{2,1,0:T(8,128)(2,1)S(1)}, bf16[4,48,1664]{2,1,0:T(8,128)(2,1)S(1)}, u32[]{:S(2)}, u32[]{:S(2)}) collective-permute-start(bf16[4,48,1664]{2,1,0:T(8,128)(2,1)S(1)} %get-tuple-element.42), channel_id=1, source_target_pairs={{0,8},{1,9},{2,10},{3,11},{4,12},{5,13},{6,14},{7,15},{8,0},{9,1},... | collective-permute-start | bytes 1916936 | tf_op jit(solution)/shard_map/ppermute | solution.py:79
  27.7 26.9 %collective-permute-start.6 = (bf16[4,48,1664]{2,1,0:T(8,128)(2,1)S(1)}, bf16[4,48,1664]{2,1,0:T(8,128)(2,1)S(1)}, u32[]{:S(2)}, u32[]{:S(2)}) collective-permute-start(bf16[4,48,1664]{2,1,0:T(8,128)(2,1)S(1)} %get-tuple-element.42), channel_id=1, source_target_pairs={{0,12},{1,13},{2,14},{3,15},{4,0},{5,1},{6,2},{7,3},{8,4},{9,5},{1... | collective-permute-start | bytes 1916936 | tf_op jit(solution)/shard_map/ppermute | solution.py:79
  36.3 18.3 %collective-permute-start.4 = (bf16[4,48,1664]{2,1,0:T(8,128)(2,1)S(1)}, bf16[4,48,1664]{2,1,0:T(8,128)(2,1)S(1)}, u32[]{:S(2)}, u32[]{:S(2)}) collective-permute-start(bf16[4,48,1664]{2,1,0:T(8,128)(2,1)S(1)} %get-tuple-element.42), channel_id=1, source_target_pairs={{0,4},{1,5},{2,6},{3,7},{4,8},{5,9},{6,10},{7,11},{8,12},{9,13},{1... | collective-permute-start | bytes 1916936 | tf_op jit(solution)/shard_map/ppermute | solution.py:79
  78.6 3.9 %collective-permute-start.9 = (f32[4,1536]{1,0:T(4,128)S(1)}, f32[4,1536]{1,0:T(4,128)S(1)}, u32[]{:S(2)}, u32[]{:S(2)}) collective-permute-start(f32[4,1536]{1,0:T(4,128)S(1)} %broadcast_select_fusion), channel_id=1, source_target_pairs={{0,1},{1,0},{2,3},{3,2},{4,5},{5,4},{6,7},{7,6},{8,9},{9,8},{10,11... | collective-permute-start | bytes 73736 | tf_op jit(solution)/shard_map/ppermute | solution.py:32
  82.6 5.1 %collective-permute-start.10 = (f32[4,1536]{1,0:T(4,128)S(1)}, f32[4,1536]{1,0:T(4,128)S(1)}, u32[]{:S(2)}, u32[]{:S(2)}) collective-permute-start(f32[4,1536]{1,0:T(4,128)S(1)} %pad_maximum_fusion.3), channel_id=1, source_target_pairs={{0,3},{1,2},{2,1},{3,0},{4,7},{5,6},{6,5},{7,4},{8,11},{9,10},{10,... | collective-permute-start | bytes 73736 | tf_op jit(solution)/shard_map/ppermute | solution.py:32
  87.9 3.9 %collective-permute-start.11 = (f32[4,1536]{1,0:T(4,128)S(1)}, f32[4,1536]{1,0:T(4,128)S(1)}, u32[]{:S(2)}, u32[]{:S(2)}) collective-permute-start(f32[4,1536]{1,0:T(4,128)S(1)} %pad_maximum_fusion.4), channel_id=1, source_target_pairs={{0,4},{1,5},{2,6},{3,7},{4,0},{5,1},{6,2},{7,3},{8,12},{9,13},{10,... | collective-permute-start | bytes 73736 | tf_op jit(solution)/shard_map/ppermute | solution.py:32
  92.0 5.1 %collective-permute-start.12 = (f32[4,1536]{1,0:T(4,128)S(1)}, f32[4,1536]{1,0:T(4,128)S(1)}, u32[]{:S(2)}, u32[]{:S(2)}) collective-permute-start(f32[4,1536]{1,0:T(4,128)S(1)} %pad_maximum_fusion.5), channel_id=1, source_target_pairs={{0,12},{1,13},{2,14},{3,15},{4,8},{5,9},{6,10},{7,11},{8,4},{9,5},... | collective-permute-start | bytes 73736 | tf_op jit(solution)/shard_map/ppermute | solution.py:32
  98.6 1.2 %collective-permute-start.13 = (f32[2]{0:T(128)S(1)}, f32[2]{0:T(128)S(1)}, u32[]{:S(2)}, u32[]{:S(2)}) collective-permute-start(f32[2]{0:T(128)S(1)} %pad_maximum_fusion.11), channel_id=1, source_target_pairs={{0,16},{16,0},{32,48},{48,32},{64,80},{80,64},{96,112},{112,96},{1... | collective-permute-start | bytes 32 | tf_op jit(solution)/shard_map/ppermute | solution.py:32
  98.8 12.0 %copy-start.2 = (f32[128]{0:T(128)}, f32[128]{0:T(128)S(1)}, u32[]{:S(2)}) copy-start(f32[128]{0:T(128)S(1)} %fusion.52) | copy-start | bytes 1540
  99.0 11.8 %copy-start.3 = (f32[128]{0:T(128)}, f32[128]{0:T(128)S(1)}, u32[]{:S(2)}) copy-start(f32[128]{0:T(128)S(1)} %fusion.51) | copy-start | bytes 1540
  99.2 11.7 %copy-start.1 = (f32[128]{0:T(128)}, f32[128]{0:T(128)S(1)}, u32[]{:S(2)}) copy-start(f32[128]{0:T(128)S(1)} %select_dynamic-update-slice_fusion) | copy-start | bytes 1540
  100.5 3.6 %collective-permute-start.14 = (f32[2]{0:T(128)S(1)}, f32[2]{0:T(128)S(1)}, u32[]{:S(2)}, u32[]{:S(2)}) collective-permute-start(f32[2]{0:T(128)S(1)} %fusion.43), channel_id=1, source_target_pairs={{0,32},{16,48},{32,0},{48,16},{64,96},{80,112},{96,64},{112,80},{1... | collective-permute-start | bytes 32 | tf_op jit(solution)/shard_map/ppermute | solution.py:32
  104.1 4.8 %collective-permute-start.15 = (f32[2]{0:T(128)S(1)}, f32[2]{0:T(128)S(1)}, u32[]{:S(2)}, u32[]{:S(2)}) collective-permute-start(f32[2]{0:T(128)S(1)} %fusion.42), channel_id=1, source_target_pairs={{0,96},{16,112},{32,64},{48,80},{64,32},{80,48},{96,0},{112,16},{1... | collective-permute-start | bytes 32 | tf_op jit(solution)/shard_map/ppermute | solution.py:32

commit v17 on v16

--- a/solution.py
+++ b/solution.py
@@ -123,10 +123,13 @@
     own = jnp.concatenate([normed, meta.astype(jnp.bfloat16)], axis=1)
 
     stats = lambda block: block_stats(block, head, position)
-    left = shift(own, 0, 1, reqs, vocs)
-    right = shift(own, 0, -1, reqs, vocs)
+    split = lambda step: jnp.concatenate(
+        [shift(own[:HALF], 0, step, reqs, vocs), shift(own[HALF:], 0, step, reqs, vocs)]
+    )
+    left = split(1)
+    right = split(-1)
     part_own = stats(own)
-    far = shift(own, 0, 2, reqs, vocs)
+    far = split(2)
     part_near = stats(jnp.concatenate([left, right]))
     line = jnp.stack([own, left, right, far])
     halves = lambda step: jnp.concatenate(

time: 112 us -> 131 us (1.17)
  waiting for transfers between devices: 24.3 us -> 34.4 us
  starting transfers between devices: 26.9 us -> 35.1 us
    ppermute x9 -> x12, starting transfers between devices: 14.7 us -> 26.6 us  [shift(): return lax.ppermute(value, AXES, pairs)]
    ppermute x9 -> x12, waiting for transfers between devices: 12.2 us -> 18.6 us  [shift(): return lax.ppermute(value, AXES, pairs)]
    ppermute x7, starting transfers between devices: 12.2 us -> 8.5 us  [butterfly(): other = lax.ppermute(value, axis, [(i, i ^ flip) for i in range(size)])]
    ppermute x7, waiting for transfers between devices: 12.1 us -> 15.7 us  [butterfly(): other = lax.ppermute(value, axis, [(i, i ^ flip) for i in range(size)])]
  transfers between devices with their start and end apart: 16 -> 19, of which waited for: 9 -> 10; matrix products, arithmetic and copies ran while one was open for 18% -> 16% of each run, Pallas kernels for 0% -> 0%
where the time goes in v17:
time: 131 us; the launch traced here: 130 us
  starting transfers between devices  35.1 us (27%)
  waiting for transfers between devices  34.4 us (26%)
  matrix products  27.4 us (21%)
  other arithmetic  19.8 us (15%)
  between operations  7.67 us (6%)
  local copies, waits for them, and re-layouts  6.09 us (5%)
    ppermute x12, starting transfers between devices, shift(): return lax.ppermute(value, AXES, pairs)  26.6 us
    dot_general x5, matrix products, block_stats(): logits = jnp.dot(rows_in, head, preferred_element_type=jnp.float32)  25.2 us
    ppermute x12, waiting for transfers between devices, shift(): return lax.ppermute(value, AXES, pairs)  18.6 us
    ppermute x7, waiting for transfers between devices, butterfly(): other = lax.ppermute(value, axis, [(i, i ^ flip) for i in range(size)])  15.7 us
    reduce_sum x5, other arithmetic, block_stats(): total = jnp.sum(expo, axis=-1)  12.3 us
    ppermute x7, starting transfers between devices, butterfly(): other = lax.ppermute(value, axis, [(i, i ^ flip) for i in range(size)])  8.5 us
  transfers between devices with their start and end apart: 19, of which 10 were waited for; matrix products, arithmetic and copies ran while one was open for 16% of the time, Pallas kernels for 0%

profile of v17, /device:TPU:0, one launch (start us, length us, event | category | flops | bytes accessed | tf_op | source)
XLA Modules:
  0.0 130.4 jit_solution(18017491645301085259)
XLA Ops:
  0.7 1.2 fusion.10
  1.8 1.3 %fusion.60 = (s32[1,1]{1,0:T(1,128)}, s32[1,1]{1,0:T(1,128)}) fusion(s32[1,2]{1,0:T(1,128)} %param.10), kind=kLoop, calls=%fused_computation.226 | loop fusion | bytes 16 | tf_op jit(solution)/shard_map/slice | solution.py:106
  3.2 0.6 iota_add_fusion
  5.1 0.9 and_select_fusion.1
  6.0 1.3 %convolution_convert_fusion = bf16[96,1536]{1,0:T(8,128)(2,1)S(1)} fusion(bf16[128,1536]{1,0:T(8,128)(2,1)} %param.6, f32[1536]{0:T(1024)} %param.7, f32[128]{0:T(128)S(1)} %add_rsqrt_fusion, s32[96]{0:T(128)S(1)} %iota_add_fusion), kind=kOutput, calls=%fused_computation.22 | convolution fusion | flops 38694912 | bytes 695168 | tf_op jit(solution)/shard_map/dot_general | solution.py:115
  7.5 4.1 %collective-permute-start.5 = (bf16[48,1664]{1,0:T(8,128)(2,1)S(1)}, bf16[48,1664]{1,0:T(8,128)(2,1)S(1)}, u32[]{:S(2)}, u32[]{:S(2)}) collective-permute-start(bf16[48,1664]{1,0:T(8,128)(2,1)S(1)} %get-tuple-element.43), channel_id=1, source_target_pairs={{0,2},{1,3},{2,0},{3,1},{4,6},{5,7},{6,4},{7,5},{8,10},{9,11},{10,... | collective-permute-start | bytes 479240 | tf_op jit(solution)/shard_map/ppermute | solution.py:79
  11.5 0.7 collective-permute-start.3
  12.2 1.3 %collective-permute-start.1 = (bf16[48,1664]{1,0:T(8,128)(2,1)S(1)}, bf16[48,1664]{1,0:T(8,128)(2,1)S(1)}, u32[]{:S(2)}, u32[]{:S(2)}) collective-permute-start(bf16[48,1664]{1,0:T(8,128)(2,1)S(1)} %get-tuple-element.43), channel_id=1, source_target_pairs={{0,1},{1,2},{2,3},{3,0},{4,5},{5,6},{6,7},{7,4},{8,9},{9,10},{10,1... | collective-permute-start | bytes 479240 | tf_op jit(solution)/shard_map/ppermute | solution.py:79
  13.6 1.1 collective-permute-start.4
  14.6 2.6 %collective-permute-start.2 = (bf16[48,1664]{1,0:T(8,128)(2,1)S(1)}, bf16[48,1664]{1,0:T(8,128)(2,1)S(1)}, u32[]{:S(2)}, u32[]{:S(2)}) collective-permute-start(bf16[48,1664]{1,0:T(8,128)(2,1)S(1)} %get-tuple-element.44), channel_id=1, source_target_pairs={{0,3},{1,0},{2,1},{3,2},{4,7},{5,4},{6,5},{7,6},{8,11},{9,8},{10,9... | collective-permute-start | bytes 479240 | tf_op jit(solution)/shard_map/ppermute | solution.py:79
  17.4 0.7 gather_fusion
  18.0 0.7 gather_fusion.1
  18.7 5.6 %fusion.61 = (f32[96]{0:T(128)S(1)}, f32[96,3072]{1,0:T(8,128)S(1)}) fusion(bf16[96,1536]{1,0:T(8,128)(2,1)S(1)} %convolution_convert_fusion, bf16[1536,3072]{1,0:T(8,128)(2,1)} %param.8), kind=kOutput, calls=%fused_computation.227 | convolution fusion | flops 906264448 | bytes 10912128 | tf_op jit(solution)/shard_map/dot_general | solution.py:89
  24.4 0.2 fusion.28
  24.6 0.5 fusion.8
  25.3 6.4 %collective-permute-done = bf16[48,1664]{1,0:T(8,128)(2,1)S(1)} collective-permute-done((bf16[48,1664]{1,0:T(8,128)(2,1)S(1)}, bf16[48,1664]{1,0:T(8,128)(2,1)S(1)}, u32[]{:S(2)}, u32[]{:S(2)}) %collective-permute-start) | collective-permute-done | bytes 159776 | tf_op jit(solution)/shard_map/ppermute | solution.py:79
  31.8 0.2 maximum_reduce_fusion
  32.0 0.2 pad_maximum_fusion
  32.3 10.7 %collective-permute-start.10 = (bf16[4,48,1664]{2,1,0:T(8,128)(2,1)S(1)}, bf16[4,48,1664]{2,1,0:T(8,128)(2,1)S(1)}, u32[]{:S(2)}, u32[]{:S(2)}) collective-permute-start(bf16[4,48,1664]{2,1,0:T(8,128)(2,1)S(1)} %get-tuple-element.41), channel_id=1, source_target_pairs={{0,8},{1,9},{2,10},{3,11},{4,12},{5,13},{6,14},{7,15},{8,0},{9,1},... | collective-permute-start | bytes 1916936 | tf_op jit(solution)/shard_map/ppermute | solution.py:79
  42.9 1.3 collective-permute-start.8
  44.2 0.7 collective-permute-start.6
  45.0 1.2 collective-permute-start.11
  46.1 2.6 %collective-permute-start.9 = (bf16[4,48,1664]{2,1,0:T(8,128)(2,1)S(1)}, bf16[4,48,1664]{2,1,0:T(8,128)(2,1)S(1)}, u32[]{:S(2)}, u32[]{:S(2)}) collective-permute-start(bf16[4,48,1664]{2,1,0:T(8,128)(2,1)S(1)} %get-tuple-element.42), channel_id=1, source_target_pairs={{0,12},{1,13},{2,14},{3,15},{4,0},{5,1},{6,2},{7,3},{8,4},{9,5},{1... | collective-permute-start | bytes 1916936 | tf_op jit(solution)/shard_map/ppermute | solution.py:79
  48.8 1.8 %fusion.63 = (f32[96]{0:T(128)S(1)}, f32[96,3072]{1,0:T(8,128)S(1)}) fusion(bf16[1536,3072]{1,0:T(8,128)(2,1)S(1)} %bitcast.54, bf16[96,1664]{1,0:T(8,128)(2,1)S(1)} %constant_dynamic-update-slice_fusion.4), kind=kOutput, calls=%fused_computation.229 | convolution fusion | flops 906264448 | bytes 10912128 | tf_op jit(solution)/shard_map/dot_general | solution.py:89
  50.7 2.1 %fusion.62 = (f32[192]{0:T(256)S(1)}, f32[192,3072]{1,0:T(8,128)S(1)}) fusion(bf16[1536,3072]{1,0:T(8,128)(2,1)S(1)} %bitcast.54, bf16[192,1664]{1,0:T(8,128)(2,1)S(1)} %constant_dynamic-update-slice_fusion), kind=kOutput, calls=%fused_computation.228 | convolution fusion | flops 1812528896 | bytes 12387072 | tf_op jit(solution)/shard_map/dot_general | solution.py:89
  52.8 0.2 fusion.26
  53.0 0.5 fusion.7
  53.5 0.2 fusion.24
  53.7 1.0 fusion.4
  54.8 0.3 collective-permute-start.7
  55.0 10.1 %collective-permute-done.11 = bf16[4,48,1664]{2,1,0:T(8,128)(2,1)S(1)} collective-permute-done((bf16[4,48,1664]{2,1,0:T(8,128)(2,1)S(1)}, bf16[4,48,1664]{2,1,0:T(8,128)(2,1)S(1)}, u32[]{:S(2)}, u32[]{:S(2)}) %collective-permute-start.11) | collective-permute-done | bytes 639008 | tf_op jit(solution)/shard_map/ppermute | solution.py:79
  65.2 0.1 pad_maximum_fusion.1
  65.3 5.7 %fusion.65 = (f32[384]{0:T(512)S(1)}, f32[384,3072]{1,0:T(8,128)}) fusion(bf16[1536,3072]{1,0:T(8,128)(2,1)S(1)} %bitcast.54, bf16[384,1664]{1,0:T(8,128)(2,1)S(1)} %bitcast.60), kind=kOutput, calls=%fused_computation.231 | convolution fusion | flops 3625057792 | bytes 15336960 | tf_op jit(solution)/shard_map/dot_general | solution.py:89
  71.0 2.1 %collective-permute-done.9 = bf16[4,48,1664]{2,1,0:T(8,128)(2,1)S(1)} collective-permute-done((bf16[4,48,1664]{2,1,0:T(8,128)(2,1)S(1)}, bf16[4,48,1664]{2,1,0:T(8,128)(2,1)S(1)}, u32[]{:S(2)}, u32[]{:S(2)}) %collective-permute-start.9) | collective-permute-done | bytes 639008 | tf_op jit(solution)/shard_map/ppermute | solution.py:79
  73.1 0.2 maximum_maximum_fusion
  73.3 9.9 %fusion.64 = (f32[768]{0:T(1024)S(1)}, f32[768,3072]{1,0:T(8,128)}) fusion(bf16[1536,3072]{1,0:T(8,128)(2,1)S(1)} %bitcast.54, bf16[768,1664]{1,0:T(8,128)(2,1)S(1)} %bitcast.58), kind=kOutput, calls=%fused_computation.230 | convolution fusion | flops 7250115584 | bytes 21236736 | tf_op jit(solution)/shard_map/dot_general | solution.py:89
  83.2 0.2 slice_reduce_fusion.6
  83.4 0.2 slice_reduce_fusion.7
  83.6 0.2 slice_reduce_fusion.8
  83.9 0.7 gather_fusion.3
  84.5 0.6 fusion.56
  85.5 0.1 copy.16
  85.7 4.0 %fusion.1 = (f32[384]{0:T(512)S(1)}, f32[384]{0:T(512)S(1)}, f32[384]{0:T(512)S(1)}) fusion(f32[384,3072]{1,0:T(8,128)} %get-tuple-element.76, f32[384]{0:T(512)S(1)} %get-tuple-element.75, s32[384]{0:T(512)S(1)} %fusion.41), kind=kLoop, calls=%fused_computation.13 | loop fusion | flops 8256384 | bytes 4726272 | tf_op jit(solution)/shard_map/reduce_sum | solution.py:92
  89.7 6.3 %fusion = (f32[768]{0:T(1024)S(1)}, f32[768]{0:T(1024)S(1)}, f32[768]{0:T(1024)S(1)}) fusion(f32[768,3072]{1,0:T(8,128)} %get-tuple-element.74, f32[768]{0:T(1024)S(1)} %get-tuple-element.73, s32[768]{0:T(1024)S(1)} %fusion.39), kind=kLoop, calls=%fused_computation.8 | loop fusion | flops 16512768 | bytes 9452544 | tf_op jit(solution)/shard_map/reduce_sum | solution.py:92
  96.1 0.1 concatenate.46
  96.3 0.6 gather_fusion.2
  97.1 3.8 %collective-permute-done.12 = f32[4,1536]{1,0:T(4,128)S(1)} collective-permute-done((f32[4,1536]{1,0:T(4,128)S(1)}, f32[4,1536]{1,0:T(4,128)S(1)}, u32[]{:S(2)}, u32[]{:S(2)}) %collective-permute-start.12) | collective-permute-done | bytes 24608 | tf_op jit(solution)/shard_map/ppermute | solution.py:32
  101.2 5.0 %collective-permute-done.13 = f32[4,1536]{1,0:T(4,128)S(1)} collective-permute-done((f32[4,1536]{1,0:T(4,128)S(1)}, f32[4,1536]{1,0:T(4,128)S(1)}, u32[]{:S(2)}, u32[]{:S(2)}) %collective-permute-start.13) | collective-permute-done | bytes 24608 | tf_op jit(solution)/shard_map/ppermute | solution.py:32
  106.3 1.0 collective-permute-start.14
  109.3 0.9 collective-permute-done.14
  110.4 2.7 %collective-permute-start.15 = (f32[4,1536]{1,0:T(4,128)S(1)}, f32[4,1536]{1,0:T(4,128)S(1)}, u32[]{:S(2)}, u32[]{:S(2)}) collective-permute-start(f32[4,1536]{1,0:T(4,128)S(1)} %pad_maximum_fusion.5), channel_id=1, source_target_pairs={{0,12},{1,13},{2,14},{3,15},{4,8},{5,9},{6,10},{7,11},{8,4},{9,5},... | collective-permute-start | bytes 73736 | tf_op jit(solution)/shard_map/ppermute | solution.py:32
  113.9 1.6 %collective-permute-done.15 = f32[4,1536]{1,0:T(4,128)S(1)} collective-permute-done((f32[4,1536]{1,0:T(4,128)S(1)}, f32[4,1536]{1,0:T(4,128)S(1)}, u32[]{:S(2)}, u32[]{:S(2)}) %collective-permute-start.15) | collective-permute-done | bytes 24608 | tf_op jit(solution)/shard_map/ppermute | solution.py:32
  115.6 0.8 select_reduce_fusion.5
  116.3 0.7 pad_maximum_fusion.11
  117.1 0.2 fusion.55
  117.3 0.2 fusion.54
  117.5 0.2 select_dynamic-update-slice_fusion
  117.6 0.6 collective-permute-done.16
  118.2 0.7 fusion.46
  118.9 1.6 %collective-permute-start.17 = (f32[2]{0:T(128)S(1)}, f32[2]{0:T(128)S(1)}, u32[]{:S(2)}, u32[]{:S(2)}) collective-permute-start(f32[2]{0:T(128)S(1)} %fusion.46), channel_id=1, source_target_pairs={{0,32},{16,48},{32,0},{48,16},{64,96},{80,112},{96,64},{112,80},{1... | collective-permute-start | bytes 32 | tf_op jit(solution)/shard_map/ppermute | solution.py:32
  120.5 2.0 %collective-permute-done.17 = f32[2]{0:T(128)S(1)} collective-permute-done((f32[2]{0:T(128)S(1)}, f32[2]{0:T(128)S(1)}, u32[]{:S(2)}, u32[]{:S(2)}) %collective-permute-start.17) | collective-permute-done | bytes 40 | tf_op jit(solution)/shard_map/ppermute | solution.py:32
  122.5 3.0 %collective-permute-start.18 = (f32[2]{0:T(128)S(1)}, f32[2]{0:T(128)S(1)}, u32[]{:S(2)}, u32[]{:S(2)}) collective-permute-start(f32[2]{0:T(128)S(1)} %fusion.45), channel_id=1, source_target_pairs={{0,96},{16,112},{32,64},{48,80},{64,32},{80,48},{96,0},{112,16},{1... | collective-permute-start | bytes 32 | tf_op jit(solution)/shard_map/ppermute | solution.py:32
  125.5 1.8 %collective-permute-done.18 = f32[2]{0:T(128)S(1)} collective-permute-done((f32[2]{0:T(128)S(1)}, f32[2]{0:T(128)S(1)}, u32[]{:S(2)}, u32[]{:S(2)}) %collective-permute-start.18) | collective-permute-done | bytes 40 | tf_op jit(solution)/shard_map/ppermute | solution.py:32
  127.3 0.6 fusion.59
  (100 shorter events, 2.2 us)
Async XLA Ops:
  0.6 16.7 %copy-start = (s32[4]{0:T(128)S(1)}, s32[4]{0:T(128)}, u32[]{:S(2)}) copy-start(s32[4]{0:T(128)} %constant.170.clone) | copy-start | bytes 52
  7.5 17.8 %collective-permute-start.5 = (bf16[48,1664]{1,0:T(8,128)(2,1)S(1)}, bf16[48,1664]{1,0:T(8,128)(2,1)S(1)}, u32[]{:S(2)}, u32[]{:S(2)}) collective-permute-start(bf16[48,1664]{1,0:T(8,128)(2,1)S(1)} %get-tuple-element.43), channel_id=1, source_target_pairs={{0,2},{1,3},{2,0},{3,1},{4,6},{5,7},{6,4},{7,5},{8,10},{9,11},{10,... | collective-permute-start | bytes 479240 | tf_op jit(solution)/shard_map/ppermute | solution.py:79
  11.5 20.2 %collective-permute-start.3 = (bf16[48,1664]{1,0:T(8,128)(2,1)S(1)}, bf16[48,1664]{1,0:T(8,128)(2,1)S(1)}, u32[]{:S(2)}, u32[]{:S(2)}) collective-permute-start(bf16[48,1664]{1,0:T(8,128)(2,1)S(1)} %get-tuple-element.43), channel_id=1, source_target_pairs={{0,3},{1,0},{2,1},{3,2},{4,7},{5,4},{6,5},{7,6},{8,11},{9,8},{10,9... | collective-permute-start | bytes 479240 | tf_op jit(solution)/shard_map/ppermute | solution.py:79
  12.2 13.0 %collective-permute-start.1 = (bf16[48,1664]{1,0:T(8,128)(2,1)S(1)}, bf16[48,1664]{1,0:T(8,128)(2,1)S(1)}, u32[]{:S(2)}, u32[]{:S(2)}) collective-permute-start(bf16[48,1664]{1,0:T(8,128)(2,1)S(1)} %get-tuple-element.43), channel_id=1, source_target_pairs={{0,1},{1,2},{2,3},{3,0},{4,5},{5,6},{6,7},{7,4},{8,9},{9,10},{10,1... | collective-permute-start | bytes 479240 | tf_op jit(solution)/shard_map/ppermute | solution.py:79
  13.6 11.5 %collective-permute-start.4 = (bf16[48,1664]{1,0:T(8,128)(2,1)S(1)}, bf16[48,1664]{1,0:T(8,128)(2,1)S(1)}, u32[]{:S(2)}, u32[]{:S(2)}) collective-permute-start(bf16[48,1664]{1,0:T(8,128)(2,1)S(1)} %get-tuple-element.44), channel_id=1, source_target_pairs={{0,2},{1,3},{2,0},{3,1},{4,6},{5,7},{6,4},{7,5},{8,10},{9,11},{10,... | collective-permute-start | bytes 479240 | tf_op jit(solution)/shard_map/ppermute | solution.py:79
  14.6 17.1 %collective-permute-start.2 = (bf16[48,1664]{1,0:T(8,128)(2,1)S(1)}, bf16[48,1664]{1,0:T(8,128)(2,1)S(1)}, u32[]{:S(2)}, u32[]{:S(2)}) collective-permute-start(bf16[48,1664]{1,0:T(8,128)(2,1)S(1)} %get-tuple-element.44), channel_id=1, source_target_pairs={{0,3},{1,0},{2,1},{3,2},{4,7},{5,4},{6,5},{7,6},{8,11},{9,8},{10,9... | collective-permute-start | bytes 479240 | tf_op jit(solution)/shard_map/ppermute | solution.py:79
  18.7 30.1 %slice-start = ((s8[9437184]{0:T(1024)(128)(4,1)}), s8[4194304]{0:T(1024)(128)(4,1)S(1)}, s32[]{:S(2)}) async-start(s8[9437184]{0:T(1024)(128)(4,1)} %bitcast.53), calls=%async_computation | async-start | bytes 8388608
  18.7 30.1 %slice-start.1 = ((s8[9437184]{0:T(1024)(128)(4,1)}), s8[4194304]{0:T(1024)(128)(4,1)S(1)}, s32[]{:S(2)}) async-start(s8[9437184]{0:T(1024)(128)(4,1)} %bitcast.53), calls=%async_computation.1 | async-start | bytes 8388608
  24.6 24.2 %slice-start.2 = ((s8[9437184]{0:T(1024)(128)(4,1)}), s8[1048576]{0:T(1024)(128)(4,1)S(1)}, s32[]{:S(2)}) async-start(s8[9437184]{0:T(1024)(128)(4,1)} %bitcast.53), calls=%async_computation.2 | async-start | bytes 2097152
  25.1 6.6 %collective-permute-start = (bf16[48,1664]{1,0:T(8,128)(2,1)S(1)}, bf16[48,1664]{1,0:T(8,128)(2,1)S(1)}, u32[]{:S(2)}, u32[]{:S(2)}) collective-permute-start(bf16[48,1664]{1,0:T(8,128)(2,1)S(1)} %get-tuple-element.44), channel_id=1, source_target_pairs={{0,1},{1,2},{2,3},{3,0},{4,5},{5,6},{6,7},{7,4},{8,9},{9,10},{10,1... | collective-permute-start | bytes 479240 | tf_op jit(solution)/shard_map/ppermute | solution.py:79
  32.3 22.5 %collective-permute-start.10 = (bf16[4,48,1664]{2,1,0:T(8,128)(2,1)S(1)}, bf16[4,48,1664]{2,1,0:T(8,128)(2,1)S(1)}, u32[]{:S(2)}, u32[]{:S(2)}) collective-permute-start(bf16[4,48,1664]{2,1,0:T(8,128)(2,1)S(1)} %get-tuple-element.41), channel_id=1, source_target_pairs={{0,8},{1,9},{2,10},{3,11},{4,12},{5,13},{6,14},{7,15},{8,0},{9,1},... | collective-permute-start | bytes 1916936 | tf_op jit(solution)/shard_map/ppermute | solution.py:79
  42.9 28.1 %collective-permute-start.8 = (bf16[4,48,1664]{2,1,0:T(8,128)(2,1)S(1)}, bf16[4,48,1664]{2,1,0:T(8,128)(2,1)S(1)}, u32[]{:S(2)}, u32[]{:S(2)}) collective-permute-start(bf16[4,48,1664]{2,1,0:T(8,128)(2,1)S(1)} %get-tuple-element.41), channel_id=1, source_target_pairs={{0,12},{1,13},{2,14},{3,15},{4,0},{5,1},{6,2},{7,3},{8,4},{9,5},{1... | collective-permute-start | bytes 1916936 | tf_op jit(solution)/shard_map/ppermute | solution.py:79
  44.2 26.8 %collective-permute-start.6 = (bf16[4,48,1664]{2,1,0:T(8,128)(2,1)S(1)}, bf16[4,48,1664]{2,1,0:T(8,128)(2,1)S(1)}, u32[]{:S(2)}, u32[]{:S(2)}) collective-permute-start(bf16[4,48,1664]{2,1,0:T(8,128)(2,1)S(1)} %get-tuple-element.41), channel_id=1, source_target_pairs={{0,4},{1,5},{2,6},{3,7},{4,8},{5,9},{6,10},{7,11},{8,12},{9,13},{1... | collective-permute-start | bytes 1916936 | tf_op jit(solution)/shard_map/ppermute | solution.py:79
  45.0 20.2 %collective-permute-start.11 = (bf16[4,48,1664]{2,1,0:T(8,128)(2,1)S(1)}, bf16[4,48,1664]{2,1,0:T(8,128)(2,1)S(1)}, u32[]{:S(2)}, u32[]{:S(2)}) collective-permute-start(bf16[4,48,1664]{2,1,0:T(8,128)(2,1)S(1)} %get-tuple-element.42), channel_id=1, source_target_pairs={{0,8},{1,9},{2,10},{3,11},{4,12},{5,13},{6,14},{7,15},{8,0},{9,1},... | collective-permute-start | bytes 1916936 | tf_op jit(solution)/shard_map/ppermute | solution.py:79
  46.1 26.9 %collective-permute-start.9 = (bf16[4,48,1664]{2,1,0:T(8,128)(2,1)S(1)}, bf16[4,48,1664]{2,1,0:T(8,128)(2,1)S(1)}, u32[]{:S(2)}, u32[]{:S(2)}) collective-permute-start(bf16[4,48,1664]{2,1,0:T(8,128)(2,1)S(1)} %get-tuple-element.42), channel_id=1, source_target_pairs={{0,12},{1,13},{2,14},{3,15},{4,0},{5,1},{6,2},{7,3},{8,4},{9,5},{1... | collective-permute-start | bytes 1916936 | tf_op jit(solution)/shard_map/ppermute | solution.py:79
  54.8 18.3 %collective-permute-start.7 = (bf16[4,48,1664]{2,1,0:T(8,128)(2,1)S(1)}, bf16[4,48,1664]{2,1,0:T(8,128)(2,1)S(1)}, u32[]{:S(2)}, u32[]{:S(2)}) collective-permute-start(bf16[4,48,1664]{2,1,0:T(8,128)(2,1)S(1)} %get-tuple-element.42), channel_id=1, source_target_pairs={{0,4},{1,5},{2,6},{3,7},{4,8},{5,9},{6,10},{7,11},{8,12},{9,13},{1... | collective-permute-start | bytes 1916936 | tf_op jit(solution)/shard_map/ppermute | solution.py:79
  97.0 3.9 %collective-permute-start.12 = (f32[4,1536]{1,0:T(4,128)S(1)}, f32[4,1536]{1,0:T(4,128)S(1)}, u32[]{:S(2)}, u32[]{:S(2)}) collective-permute-start(f32[4,1536]{1,0:T(4,128)S(1)} %broadcast_select_fusion), channel_id=1, source_target_pairs={{0,1},{1,0},{2,3},{3,2},{4,5},{5,4},{6,7},{7,6},{8,9},{9,8},{10,11... | collective-permute-start | bytes 73736 | tf_op jit(solution)/shard_map/ppermute | solution.py:32
  101.1 5.1 %collective-permute-start.13 = (f32[4,1536]{1,0:T(4,128)S(1)}, f32[4,1536]{1,0:T(4,128)S(1)}, u32[]{:S(2)}, u32[]{:S(2)}) collective-permute-start(f32[4,1536]{1,0:T(4,128)S(1)} %pad_maximum_fusion.3), channel_id=1, source_target_pairs={{0,3},{1,2},{2,1},{3,0},{4,7},{5,6},{6,5},{7,4},{8,11},{9,10},{10,... | collective-permute-start | bytes 73736 | tf_op jit(solution)/shard_map/ppermute | solution.py:32
  106.3 3.9 %collective-permute-start.14 = (f32[4,1536]{1,0:T(4,128)S(1)}, f32[4,1536]{1,0:T(4,128)S(1)}, u32[]{:S(2)}, u32[]{:S(2)}) collective-permute-start(f32[4,1536]{1,0:T(4,128)S(1)} %pad_maximum_fusion.4), channel_id=1, source_target_pairs={{0,4},{1,5},{2,6},{3,7},{4,0},{5,1},{6,2},{7,3},{8,12},{9,13},{10,... | collective-permute-start | bytes 73736 | tf_op jit(solution)/shard_map/ppermute | solution.py:32
  110.4 5.1 %collective-permute-start.15 = (f32[4,1536]{1,0:T(4,128)S(1)}, f32[4,1536]{1,0:T(4,128)S(1)}, u32[]{:S(2)}, u32[]{:S(2)}) collective-permute-start(f32[4,1536]{1,0:T(4,128)S(1)} %pad_maximum_fusion.5), channel_id=1, source_target_pairs={{0,12},{1,13},{2,14},{3,15},{4,8},{5,9},{6,10},{7,11},{8,4},{9,5},... | collective-permute-start | bytes 73736 | tf_op jit(solution)/shard_map/ppermute | solution.py:32
  117.0 1.2 collective-permute-start.16
  117.2 12.0 %copy-start.2 = (f32[128]{0:T(128)}, f32[128]{0:T(128)S(1)}, u32[]{:S(2)}) copy-start(f32[128]{0:T(128)S(1)} %fusion.55) | copy-start | bytes 1540
  117.5 11.8 %copy-start.3 = (f32[128]{0:T(128)}, f32[128]{0:T(128)S(1)}, u32[]{:S(2)}) copy-start(f32[128]{0:T(128)S(1)} %fusion.54) | copy-start | bytes 1540
  117.6 11.7 %copy-start.1 = (f32[128]{0:T(128)}, f32[128]{0:T(128)S(1)}, u32[]{:S(2)}) copy-start(f32[128]{0:T(128)S(1)} %select_dynamic-update-slice_fusion) | copy-start | bytes 1540
  118.9 3.6 %collective-permute-start.17 = (f32[2]{0:T(128)S(1)}, f32[2]{0:T(128)S(1)}, u32[]{:S(2)}, u32[]{:S(2)}) collective-permute-start(f32[2]{0:T(128)S(1)} %fusion.46), channel_id=1, source_target_pairs={{0,32},{16,48},{32,0},{48,16},{64,96},{80,112},{96,64},{112,80},{1... | collective-permute-start | bytes 32 | tf_op jit(solution)/shard_map/ppermute | solution.py:32
  122.5 4.8 %collective-permute-start.18 = (f32[2]{0:T(128)S(1)}, f32[2]{0:T(128)S(1)}, u32[]{:S(2)}, u32[]{:S(2)}) collective-permute-start(f32[2]{0:T(128)S(1)} %fusion.45), channel_id=1, source_target_pairs={{0,96},{16,112},{32,64},{48,80},{64,32},{80,48},{96,0},{112,16},{1... | collective-permute-start | bytes 32 | tf_op jit(solution)/shard_map/ppermute | solution.py:32

commit v18 on v16

--- a/solution.py
+++ b/solution.py
@@ -135,8 +135,10 @@
     line_left = halves(1)
     line_right = halves(-1)
     part_far = stats(far)
+    part_near, part_far, line = lax.optimization_barrier((part_near, part_far, line))
     line_far = halves(2)
     part_lines = stats(jnp.concatenate([line_left, line_right]).reshape(-1, own.shape[1]))
+    part_lines, line_far = lax.optimization_barrier((part_lines, line_far))
     part_line_far = stats(line_far.reshape(-1, own.shape[1]))
     processed = jnp.concatenate([part_own, part_near, part_far, part_lines, part_line_far], axis=1)
     processed = processed.reshape(4, vocs, LIVE)

time: 112 us -> 127 us (1.13)
  waiting for transfers between devices: 24.3 us -> 34 us
  matrix products: 27.4 us -> 31.6 us
  starting transfers between devices: 26.9 us -> 24.1 us
  local copies, waits for them, and re-layouts: 6.03 us -> 8.04 us
    ppermute x9, waiting for transfers between devices: 12.2 us -> 17.9 us  [shift(): return lax.ppermute(value, AXES, pairs)]
    dot_general x5, matrix products: 25.2 us -> 29.4 us  [block_stats(): logits = jnp.dot(rows_in, head, preferred_element_type=jnp.float32)]
    ppermute x7, starting transfers between devices: 12.2 us -> 8.17 us  [butterfly(): other = lax.ppermute(value, axis, [(i, i ^ flip) for i in range(size)])]
    ppermute x7, waiting for transfers between devices: 12.1 us -> 16.1 us  [butterfly(): other = lax.ppermute(value, axis, [(i, i ^ flip) for i in range(size)])]
  transfers between devices with their start and end apart: 16 -> 16, of which waited for: 9 -> 9; matrix products, arithmetic and copies ran while one was open for 18% -> 26% of each run, Pallas kernels for 0% -> 0%
where the time goes in v18:
time: 127 us; the launch traced here: 126 us
  waiting for transfers between devices  34 us (27%)
  matrix products  31.6 us (25%)
  starting transfers between devices  24.1 us (19%)
  other arithmetic  20.6 us (16%)
  local copies, waits for them, and re-layouts  8.04 us (6%)
  between operations  7.63 us (6%)
    dot_general x5, matrix products, block_stats(): logits = jnp.dot(rows_in, head, preferred_element_type=jnp.float32)  29.4 us
    ppermute x9, waiting for transfers between devices, shift(): return lax.ppermute(value, AXES, pairs)  17.9 us
    ppermute x7, waiting for transfers between devices, butterfly(): other = lax.ppermute(value, axis, [(i, i ^ flip) for i in range(size)])  16.1 us
    ppermute x9, starting transfers between devices, shift(): return lax.ppermute(value, AXES, pairs)  16 us
    reduce_sum x5, other arithmetic, block_stats(): total = jnp.sum(expo, axis=-1)  12.3 us
    ppermute x7, starting transfers between devices, butterfly(): other = lax.ppermute(value, axis, [(i, i ^ flip) for i in range(size)])  8.17 us
  transfers between devices with their start and end apart: 16, of which 9 were waited for; matrix products, arithmetic and copies ran while one was open for 26% of the time, Pallas kernels for 0%

profile of v18, /device:TPU:0, one launch (start us, length us, event | category | flops | bytes accessed | tf_op | source)
XLA Modules:
  0.0 126.0 jit_solution(11317603293776636442)
XLA Ops:
  0.7 1.2 fusion.10
  1.8 1.3 %fusion.59 = (s32[1,1]{1,0:T(1,128)}, s32[1,1]{1,0:T(1,128)}) fusion(s32[1,2]{1,0:T(1,128)} %param.10), kind=kLoop, calls=%fused_computation.215 | loop fusion | bytes 16 | tf_op jit(solution)/shard_map/slice | solution.py:106
  3.2 0.6 iota_add_fusion
  5.1 0.9 and_select_fusion.1
  6.0 1.3 %convolution_convert_fusion = bf16[96,1536]{1,0:T(8,128)(2,1)S(1)} fusion(bf16[128,1536]{1,0:T(8,128)(2,1)} %param.6, f32[1536]{0:T(1024)} %param.7, f32[128]{0:T(128)S(1)} %add_rsqrt_fusion, s32[96]{0:T(128)S(1)} %iota_add_fusion), kind=kOutput, calls=%fused_computation.22 | convolution fusion | flops 38694912 | bytes 695168 | tf_op jit(solution)/shard_map/dot_general | solution.py:115
  7.3 0.1 select_convert_fusion
  7.5 4.1 %collective-permute-start.2 = (bf16[96,1664]{1,0:T(8,128)(2,1)S(1)}, bf16[96,1664]{1,0:T(8,128)(2,1)S(1)}, u32[]{:S(2)}, u32[]{:S(2)}) collective-permute-start(bf16[96,1664]{1,0:T(8,128)(2,1)S(1)} %get-tuple-element.56), channel_id=1, source_target_pairs={{0,2},{1,3},{2,0},{3,1},{4,6},{5,7},{6,4},{7,5},{8,10},{9,11},{10,... | collective-permute-start | bytes 958472 | tf_op jit(solution)/shard_map/ppermute | solution.py:79
  11.6 0.7 collective-permute-start.1
  12.3 1.3 %collective-permute-start = (bf16[96,1664]{1,0:T(8,128)(2,1)S(1)}, bf16[96,1664]{1,0:T(8,128)(2,1)S(1)}, u32[]{:S(2)}, u32[]{:S(2)}) collective-permute-start(bf16[96,1664]{1,0:T(8,128)(2,1)S(1)} %get-tuple-element.56), channel_id=1, source_target_pairs={{0,1},{1,2},{2,3},{3,0},{4,5},{5,6},{6,7},{7,4},{8,9},{9,10},{10,1... | collective-permute-start | bytes 958472 | tf_op jit(solution)/shard_map/ppermute | solution.py:79
  13.7 0.7 gather_fusion
  14.3 0.7 gather_fusion.1
  15.0 5.6 %fusion.63 = (f32[96]{0:T(128)S(1)}, f32[96,3072]{1,0:T(8,128)S(1)}) fusion(bf16[96,1536]{1,0:T(8,128)(2,1)S(1)} %convolution_convert_fusion, bf16[1536,3072]{1,0:T(8,128)(2,1)} %param.8), kind=kOutput, calls=%fused_computation.219 | convolution fusion | flops 906264448 | bytes 10912128 | tf_op jit(solution)/shard_map/dot_general | solution.py:89
  20.6 0.2 fusion.25
  20.8 0.5 fusion.8
  21.4 0.2 pad_maximum_fusion
  21.6 0.1 fusion.57
  21.7 2.8 %collective-permute-start.5 = (bf16[4,48,1664]{2,1,0:T(8,128)(2,1)S(1)}, bf16[4,48,1664]{2,1,0:T(8,128)(2,1)S(1)}, u32[]{:S(2)}, u32[]{:S(2)}) collective-permute-start(bf16[4,48,1664]{2,1,0:T(8,128)(2,1)S(1)} %get-tuple-element.53), channel_id=1, source_target_pairs={{0,12},{1,13},{2,14},{3,15},{4,0},{5,1},{6,2},{7,3},{8,4},{9,5},{1... | collective-permute-start | bytes 1916936 | tf_op jit(solution)/shard_map/ppermute | solution.py:79
  24.6 3.2 %collective-permute-start.6 = (bf16[4,48,1664]{2,1,0:T(8,128)(2,1)S(1)}, bf16[4,48,1664]{2,1,0:T(8,128)(2,1)S(1)}, u32[]{:S(2)}, u32[]{:S(2)}) collective-permute-start(bf16[4,48,1664]{2,1,0:T(8,128)(2,1)S(1)} %get-tuple-element.54), channel_id=1, source_target_pairs={{0,12},{1,13},{2,14},{3,15},{4,0},{5,1},{6,2},{7,3},{8,4},{9,5},{1... | collective-permute-start | bytes 1916936 | tf_op jit(solution)/shard_map/ppermute | solution.py:79
  27.9 2.1 %fusion.61 = (f32[192]{0:T(256)S(1)}, f32[192,3072]{1,0:T(8,128)S(1)}) fusion(bf16[1536,3072]{1,0:T(8,128)(2,1)S(1)} %bitcast.52, bf16[192,1664]{1,0:T(8,128)(2,1)S(1)} %constant_dynamic-update-slice_fusion), kind=kOutput, calls=%fused_computation.217 | convolution fusion | flops 1812528896 | bytes 12387072 | tf_op jit(solution)/shard_map/dot_general | solution.py:89
  30.1 0.2 fusion.23
  30.2 0.2 fusion.21
  30.4 1.7 %fusion.62 = (f32[96]{0:T(128)S(1)}, f32[96,3072]{1,0:T(8,128)S(1)}) fusion(bf16[1536,3072]{1,0:T(8,128)(2,1)S(1)} %bitcast.52, bf16[96,1664]{1,0:T(8,128)(2,1)S(1)} %collective-permute-done.2), kind=kOutput, calls=%fused_computation.218 | convolution fusion | flops 906264448 | bytes 10912128 | tf_op jit(solution)/shard_map/dot_general | solution.py:89
  32.2 0.5 fusion.7
  32.7 1.0 fusion.4
  33.7 1.1 fusion.56
  34.9 1.5 %collective-permute-start.7 = (bf16[4,48,1664]{2,1,0:T(8,128)(2,1)}, bf16[4,48,1664]{2,1,0:T(8,128)(2,1)S(1)}, u32[]{:S(2)}, u32[]{:S(2)}) collective-permute-start(bf16[4,48,1664]{2,1,0:T(8,128)(2,1)} %get-tuple-element.51), channel_id=1, source_target_pairs={{0,8},{1,9},{2,10},{3,11},{4,12},{5,13},{6,14},{7,15},{8,0},{9,1},... | collective-permute-start | bytes 1916936 | tf_op jit(solution)/shard_map/ppermute | solution.py:79
  36.3 0.2 slice_reduce_fusion.9
  36.5 2.3 %collective-permute-start.8 = (bf16[4,48,1664]{2,1,0:T(8,128)(2,1)}, bf16[4,48,1664]{2,1,0:T(8,128)(2,1)}, u32[]{:S(2)}, u32[]{:S(2)}) collective-permute-start(bf16[4,48,1664]{2,1,0:T(8,128)(2,1)} %get-tuple-element.52), channel_id=1, source_target_pairs={{0,8},{1,9},{2,10},{3,11},{4,12},{5,13},{6,14},{7,15},{8,0},{9,1},... | collective-permute-start | bytes 1916936 | tf_op jit(solution)/shard_map/ppermute | solution.py:79
  38.8 0.5 collective-permute-done.6
  39.3 17.4 %collective-permute-done.4 = bf16[4,48,1664]{2,1,0:T(8,128)(2,1)S(1)} collective-permute-done((bf16[4,48,1664]{2,1,0:T(8,128)(2,1)S(1)}, bf16[4,48,1664]{2,1,0:T(8,128)(2,1)S(1)}, u32[]{:S(2)}, u32[]{:S(2)}) %collective-permute-start.4) | collective-permute-done | bytes 639008 | tf_op jit(solution)/shard_map/ppermute | solution.py:79
  56.7 0.2 maximum_maximum_fusion
  57.0 10.2 %fusion.60 = (f32[768]{0:T(1024)S(1)}, f32[768,3072]{1,0:T(8,128)}) fusion(bf16[1536,3072]{1,0:T(8,128)(2,1)S(1)} %bitcast.52, bf16[768,1664]{1,0:T(8,128)(2,1)S(1)} %bitcast.54), kind=kOutput, calls=%fused_computation.216 | convolution fusion | flops 7250115584 | bytes 21236736 | tf_op jit(solution)/shard_map/dot_general | solution.py:89
  67.2 0.1 copy.16
  67.4 6.3 %fusion = (f32[768]{0:T(1024)S(1)}, f32[768]{0:T(1024)S(1)}, f32[768]{0:T(1024)S(1)}) fusion(f32[768,3072]{1,0:T(8,128)} %get-tuple-element.80, f32[768]{0:T(1024)S(1)} %get-tuple-element.79, s32[768]{0:T(1024)S(1)} %fusion.36), kind=kLoop, calls=%fused_computation.8 | loop fusion | flops 16512768 | bytes 9452544 | tf_op jit(solution)/shard_map/reduce_sum | solution.py:92
  73.7 1.2 pad_maximum_fusion.1
  74.9 0.2 slice_reduce_fusion.8
  75.1 9.8 %fusion.64 = (f32[384]{0:T(512)S(1)}, f32[384,3072]{1,0:T(8,128)}) fusion(bf16[1536,3072]{1,0:T(8,128)(2,1)} %param.8, bf16[384,1664]{1,0:T(8,128)(2,1)S(1)} %bitcast.57), kind=kOutput, calls=%fused_computation.220 | convolution fusion | flops 3625057792 | bytes 15336960 | tf_op jit(solution)/shard_map/dot_general | solution.py:89
  84.9 0.2 slice_reduce_fusion.6
  85.1 0.9 slice_reduce_fusion.7
  86.0 0.7 gather_fusion.3
  86.7 0.6 fusion.54
  87.4 0.1 broadcast_in_dim.86
  87.7 4.0 %fusion.1 = (f32[384]{0:T(512)S(1)}, f32[384]{0:T(512)S(1)}, f32[384]{0:T(512)S(1)}) fusion(f32[384,3072]{1,0:T(8,128)} %get-tuple-element.88, f32[384]{0:T(512)S(1)} %get-tuple-element.87, s32[384]{0:T(512)S(1)} %fusion.38), kind=kLoop, calls=%fused_computation.13 | loop fusion | flops 8256384 | bytes 4726272 | tf_op jit(solution)/shard_map/reduce_sum | solution.py:92
  91.7 0.1 concatenate.33
  91.9 0.6 gather_fusion.2
  92.5 0.1 gather.19
  92.6 1.1 collective-permute-start.9
  93.7 2.8 %collective-permute-done.9 = f32[4,1536]{1,0:T(4,128)S(1)} collective-permute-done((f32[4,1536]{1,0:T(4,128)S(1)}, f32[4,1536]{1,0:T(4,128)S(1)}, u32[]{:S(2)}, u32[]{:S(2)}) %collective-permute-start.9) | collective-permute-done | bytes 24608 | tf_op jit(solution)/shard_map/ppermute | solution.py:32
  96.7 2.3 %collective-permute-start.10 = (f32[4,1536]{1,0:T(4,128)S(1)}, f32[4,1536]{1,0:T(4,128)S(1)}, u32[]{:S(2)}, u32[]{:S(2)}) collective-permute-start(f32[4,1536]{1,0:T(4,128)S(1)} %pad_maximum_fusion.3), channel_id=1, source_target_pairs={{0,3},{1,2},{2,1},{3,0},{4,7},{5,6},{6,5},{7,4},{8,11},{9,10},{10,... | collective-permute-start | bytes 73736 | tf_op jit(solution)/shard_map/ppermute | solution.py:32
  98.9 2.9 %collective-permute-done.10 = f32[4,1536]{1,0:T(4,128)S(1)} collective-permute-done((f32[4,1536]{1,0:T(4,128)S(1)}, f32[4,1536]{1,0:T(4,128)S(1)}, u32[]{:S(2)}, u32[]{:S(2)}) %collective-permute-start.10) | collective-permute-done | bytes 24608 | tf_op jit(solution)/shard_map/ppermute | solution.py:32
  104.0 1.9 %collective-permute-done.11 = f32[4,1536]{1,0:T(4,128)S(1)} collective-permute-done((f32[4,1536]{1,0:T(4,128)S(1)}, f32[4,1536]{1,0:T(4,128)S(1)}, u32[]{:S(2)}, u32[]{:S(2)}) %collective-permute-start.11) | collective-permute-done | bytes 24608 | tf_op jit(solution)/shard_map/ppermute | solution.py:32
  106.9 4.2 %collective-permute-done.12 = f32[4,1536]{1,0:T(4,128)S(1)} collective-permute-done((f32[4,1536]{1,0:T(4,128)S(1)}, f32[4,1536]{1,0:T(4,128)S(1)}, u32[]{:S(2)}, u32[]{:S(2)}) %collective-permute-start.12) | collective-permute-done | bytes 24608 | tf_op jit(solution)/shard_map/ppermute | solution.py:32
  111.1 0.8 select_reduce_fusion.5
  111.9 0.7 pad_maximum_fusion.11
  112.7 0.2 fusion.52
  112.9 0.2 fusion.51
  113.0 0.2 select_dynamic-update-slice_fusion
  113.2 0.6 collective-permute-done.13
  113.8 0.7 fusion.43
  114.5 1.6 %collective-permute-start.14 = (f32[2]{0:T(128)S(1)}, f32[2]{0:T(128)S(1)}, u32[]{:S(2)}, u32[]{:S(2)}) collective-permute-start(f32[2]{0:T(128)S(1)} %fusion.43), channel_id=1, source_target_pairs={{0,32},{16,48},{32,0},{48,16},{64,96},{80,112},{96,64},{112,80},{1... | collective-permute-start | bytes 32 | tf_op jit(solution)/shard_map/ppermute | solution.py:32
  116.1 2.0 %collective-permute-done.14 = f32[2]{0:T(128)S(1)} collective-permute-done((f32[2]{0:T(128)S(1)}, f32[2]{0:T(128)S(1)}, u32[]{:S(2)}, u32[]{:S(2)}) %collective-permute-start.14) | collective-permute-done | bytes 40 | tf_op jit(solution)/shard_map/ppermute | solution.py:32
  118.1 3.0 %collective-permute-start.15 = (f32[2]{0:T(128)S(1)}, f32[2]{0:T(128)S(1)}, u32[]{:S(2)}, u32[]{:S(2)}) collective-permute-start(f32[2]{0:T(128)S(1)} %fusion.42), channel_id=1, source_target_pairs={{0,96},{16,112},{32,64},{48,80},{64,32},{80,48},{96,0},{112,16},{1... | collective-permute-start | bytes 32 | tf_op jit(solution)/shard_map/ppermute | solution.py:32
  121.1 1.8 %collective-permute-done.15 = f32[2]{0:T(128)S(1)} collective-permute-done((f32[2]{0:T(128)S(1)}, f32[2]{0:T(128)S(1)}, u32[]{:S(2)}, u32[]{:S(2)}) %collective-permute-start.15) | collective-permute-done | bytes 40 | tf_op jit(solution)/shard_map/ppermute | solution.py:32
  122.9 0.6 fusion.58
  (90 shorter events, 1.6 us)
Async XLA Ops:
  0.6 13.0 %copy-start = (s32[4]{0:T(128)S(1)}, s32[4]{0:T(128)}, u32[]{:S(2)}) copy-start(s32[4]{0:T(128)} %constant.170.clone) | copy-start | bytes 52
  7.5 13.9 %collective-permute-start.2 = (bf16[96,1664]{1,0:T(8,128)(2,1)S(1)}, bf16[96,1664]{1,0:T(8,128)(2,1)S(1)}, u32[]{:S(2)}, u32[]{:S(2)}) collective-permute-start(bf16[96,1664]{1,0:T(8,128)(2,1)S(1)} %get-tuple-element.56), channel_id=1, source_target_pairs={{0,2},{1,3},{2,0},{3,1},{4,6},{5,7},{6,4},{7,5},{8,10},{9,11},{10,... | collective-permute-start | bytes 958472 | tf_op jit(solution)/shard_map/ppermute | solution.py:79
  11.6 9.9 %collective-permute-start.1 = (bf16[96,1664]{1,0:T(8,128)(2,1)S(1)}, bf16[96,1664]{1,0:T(8,128)(2,1)S(1)}, u32[]{:S(2)}, u32[]{:S(2)}) collective-permute-start(bf16[96,1664]{1,0:T(8,128)(2,1)S(1)} %get-tuple-element.56), channel_id=1, source_target_pairs={{0,3},{1,0},{2,1},{3,2},{4,7},{5,4},{6,5},{7,6},{8,11},{9,8},{10,9... | collective-permute-start | bytes 958472 | tf_op jit(solution)/shard_map/ppermute | solution.py:79
  12.3 9.2 %collective-permute-start = (bf16[96,1664]{1,0:T(8,128)(2,1)S(1)}, bf16[96,1664]{1,0:T(8,128)(2,1)S(1)}, u32[]{:S(2)}, u32[]{:S(2)}) collective-permute-start(bf16[96,1664]{1,0:T(8,128)(2,1)S(1)} %get-tuple-element.56), channel_id=1, source_target_pairs={{0,1},{1,2},{2,3},{3,0},{4,5},{5,6},{6,7},{7,4},{8,9},{9,10},{10,1... | collective-permute-start | bytes 958472 | tf_op jit(solution)/shard_map/ppermute | solution.py:79
  14.3 13.6 %slice-start = ((s8[9437184]{0:T(1024)(128)(4,1)}), s8[1048576]{0:T(1024)(128)(4,1)S(1)}, s32[]{:S(2)}) async-start(s8[9437184]{0:T(1024)(128)(4,1)} %bitcast.51), calls=%async_computation | async-start | bytes 2097152
  15.0 12.9 %slice-start.1 = ((s8[9437184]{0:T(1024)(128)(4,1)}), s8[4194304]{0:T(1024)(128)(4,1)S(1)}, s32[]{:S(2)}) async-start(s8[9437184]{0:T(1024)(128)(4,1)} %bitcast.51), calls=%async_computation.1 | async-start | bytes 8388608
  15.0 12.9 %slice-start.2 = ((s8[9437184]{0:T(1024)(128)(4,1)}), s8[4194304]{0:T(1024)(128)(4,1)S(1)}, s32[]{:S(2)}) async-start(s8[9437184]{0:T(1024)(128)(4,1)} %bitcast.51), calls=%async_computation.2 | async-start | bytes 8388608
  21.7 14.8 %collective-permute-start.5 = (bf16[4,48,1664]{2,1,0:T(8,128)(2,1)S(1)}, bf16[4,48,1664]{2,1,0:T(8,128)(2,1)S(1)}, u32[]{:S(2)}, u32[]{:S(2)}) collective-permute-start(bf16[4,48,1664]{2,1,0:T(8,128)(2,1)S(1)} %get-tuple-element.53), channel_id=1, source_target_pairs={{0,12},{1,13},{2,14},{3,15},{4,0},{5,1},{6,2},{7,3},{8,4},{9,5},{1... | collective-permute-start | bytes 1916936 | tf_op jit(solution)/shard_map/ppermute | solution.py:79
  24.6 14.3 %collective-permute-start.3 = (bf16[4,48,1664]{2,1,0:T(8,128)(2,1)S(1)}, bf16[4,48,1664]{2,1,0:T(8,128)(2,1)S(1)}, u32[]{:S(2)}, u32[]{:S(2)}) collective-permute-start(bf16[4,48,1664]{2,1,0:T(8,128)(2,1)S(1)} %get-tuple-element.53), channel_id=1, source_target_pairs={{0,4},{1,5},{2,6},{3,7},{4,8},{5,9},{6,10},{7,11},{8,12},{9,13},{1... | collective-permute-start | bytes 1916936 | tf_op jit(solution)/shard_map/ppermute | solution.py:79
  24.6 14.8 %collective-permute-start.6 = (bf16[4,48,1664]{2,1,0:T(8,128)(2,1)S(1)}, bf16[4,48,1664]{2,1,0:T(8,128)(2,1)S(1)}, u32[]{:S(2)}, u32[]{:S(2)}) collective-permute-start(bf16[4,48,1664]{2,1,0:T(8,128)(2,1)S(1)} %get-tuple-element.54), channel_id=1, source_target_pairs={{0,12},{1,13},{2,14},{3,15},{4,0},{5,1},{6,2},{7,3},{8,4},{9,5},{1... | collective-permute-start | bytes 1916936 | tf_op jit(solution)/shard_map/ppermute | solution.py:79
  27.8 28.9 %collective-permute-start.4 = (bf16[4,48,1664]{2,1,0:T(8,128)(2,1)S(1)}, bf16[4,48,1664]{2,1,0:T(8,128)(2,1)S(1)}, u32[]{:S(2)}, u32[]{:S(2)}) collective-permute-start(bf16[4,48,1664]{2,1,0:T(8,128)(2,1)S(1)} %get-tuple-element.54), channel_id=1, source_target_pairs={{0,4},{1,5},{2,6},{3,7},{4,8},{5,9},{6,10},{7,11},{8,12},{9,13},{1... | collective-permute-start | bytes 1916936 | tf_op jit(solution)/shard_map/ppermute | solution.py:79
  34.9 38.9 %collective-permute-start.7 = (bf16[4,48,1664]{2,1,0:T(8,128)(2,1)}, bf16[4,48,1664]{2,1,0:T(8,128)(2,1)S(1)}, u32[]{:S(2)}, u32[]{:S(2)}) collective-permute-start(bf16[4,48,1664]{2,1,0:T(8,128)(2,1)} %get-tuple-element.51), channel_id=1, source_target_pairs={{0,8},{1,9},{2,10},{3,11},{4,12},{5,13},{6,14},{7,15},{8,0},{9,1},... | collective-permute-start | bytes 1916936 | tf_op jit(solution)/shard_map/ppermute | solution.py:79
  36.5 37.2 %collective-permute-start.8 = (bf16[4,48,1664]{2,1,0:T(8,128)(2,1)}, bf16[4,48,1664]{2,1,0:T(8,128)(2,1)}, u32[]{:S(2)}, u32[]{:S(2)}) collective-permute-start(bf16[4,48,1664]{2,1,0:T(8,128)(2,1)} %get-tuple-element.52), channel_id=1, source_target_pairs={{0,8},{1,9},{2,10},{3,11},{4,12},{5,13},{6,14},{7,15},{8,0},{9,1},... | collective-permute-start | bytes 1916936 | tf_op jit(solution)/shard_map/ppermute | solution.py:79
  38.8 18.1 %copy-start.1 = (bf16[4,48,1664]{2,1,0:T(8,128)(2,1)}, bf16[4,48,1664]{2,1,0:T(8,128)(2,1)S(1)}, u32[]{:S(2)}) copy-start(bf16[4,48,1664]{2,1,0:T(8,128)(2,1)S(1)} %collective-permute-done.3) | copy-start | bytes 1916932
  92.6 3.9 %collective-permute-start.9 = (f32[4,1536]{1,0:T(4,128)S(1)}, f32[4,1536]{1,0:T(4,128)S(1)}, u32[]{:S(2)}, u32[]{:S(2)}) collective-permute-start(f32[4,1536]{1,0:T(4,128)S(1)} %broadcast_select_fusion), channel_id=1, source_target_pairs={{0,1},{1,0},{2,3},{3,2},{4,5},{5,4},{6,7},{7,6},{8,9},{9,8},{10,11... | collective-permute-start | bytes 73736 | tf_op jit(solution)/shard_map/ppermute | solution.py:32
  96.7 5.1 %collective-permute-start.10 = (f32[4,1536]{1,0:T(4,128)S(1)}, f32[4,1536]{1,0:T(4,128)S(1)}, u32[]{:S(2)}, u32[]{:S(2)}) collective-permute-start(f32[4,1536]{1,0:T(4,128)S(1)} %pad_maximum_fusion.3), channel_id=1, source_target_pairs={{0,3},{1,2},{2,1},{3,0},{4,7},{5,6},{6,5},{7,4},{8,11},{9,10},{10,... | collective-permute-start | bytes 73736 | tf_op jit(solution)/shard_map/ppermute | solution.py:32
  101.9 3.9 %collective-permute-start.11 = (f32[4,1536]{1,0:T(4,128)S(1)}, f32[4,1536]{1,0:T(4,128)S(1)}, u32[]{:S(2)}, u32[]{:S(2)}) collective-permute-start(f32[4,1536]{1,0:T(4,128)S(1)} %pad_maximum_fusion.4), channel_id=1, source_target_pairs={{0,4},{1,5},{2,6},{3,7},{4,0},{5,1},{6,2},{7,3},{8,12},{9,13},{10,... | collective-permute-start | bytes 73736 | tf_op jit(solution)/shard_map/ppermute | solution.py:32
  106.0 5.1 %collective-permute-start.12 = (f32[4,1536]{1,0:T(4,128)S(1)}, f32[4,1536]{1,0:T(4,128)S(1)}, u32[]{:S(2)}, u32[]{:S(2)}) collective-permute-start(f32[4,1536]{1,0:T(4,128)S(1)} %pad_maximum_fusion.5), channel_id=1, source_target_pairs={{0,12},{1,13},{2,14},{3,15},{4,8},{5,9},{6,10},{7,11},{8,4},{9,5},... | collective-permute-start | bytes 73736 | tf_op jit(solution)/shard_map/ppermute | solution.py:32
  112.6 1.2 collective-permute-start.13
  112.8 12.0 %copy-start.3 = (f32[128]{0:T(128)}, f32[128]{0:T(128)S(1)}, u32[]{:S(2)}) copy-start(f32[128]{0:T(128)S(1)} %fusion.52) | copy-start | bytes 1540
  113.0 11.8 %copy-start.4 = (f32[128]{0:T(128)}, f32[128]{0:T(128)S(1)}, u32[]{:S(2)}) copy-start(f32[128]{0:T(128)S(1)} %fusion.51) | copy-start | bytes 1540
  113.2 11.7 %copy-start.2 = (f32[128]{0:T(128)}, f32[128]{0:T(128)S(1)}, u32[]{:S(2)}) copy-start(f32[128]{0:T(128)S(1)} %select_dynamic-update-slice_fusion) | copy-start | bytes 1540
  114.5 3.6 %collective-permute-start.14 = (f32[2]{0:T(128)S(1)}, f32[2]{0:T(128)S(1)}, u32[]{:S(2)}, u32[]{:S(2)}) collective-permute-start(f32[2]{0:T(128)S(1)} %fusion.43), channel_id=1, source_target_pairs={{0,32},{16,48},{32,0},{48,16},{64,96},{80,112},{96,64},{112,80},{1... | collective-permute-start | bytes 32 | tf_op jit(solution)/shard_map/ppermute | solution.py:32
  118.1 4.8 %collective-permute-start.15 = (f32[2]{0:T(128)S(1)}, f32[2]{0:T(128)S(1)}, u32[]{:S(2)}, u32[]{:S(2)}) collective-permute-start(f32[2]{0:T(128)S(1)} %fusion.42), channel_id=1, source_target_pairs={{0,96},{16,112},{32,64},{48,80},{64,32},{80,48},{96,0},{112,16},{1... | collective-permute-start | bytes 32 | tf_op jit(solution)/shard_map/ppermute | solution.py:32

commit v19 on v16

--- a/solution.py
+++ b/solution.py
@@ -164,7 +164,7 @@
     group_live = slot[None, :] < counts[:, None]
     group_entropy = jnp.where(group_live, row_entropy.reshape(vocs, LIVE), 0.0)
     totals = jnp.stack([jnp.sum(group_entropy), jnp.sum(counts).astype(jnp.float32)])
-    totals = butterfly(totals, "req", lambda a, b: a + b, (1, 2, 6))
+    totals = lax.psum(totals, "req")
     mean_entropy = (totals[0] / totals[1]).reshape(1)
     mine = lambda a: lax.dynamic_slice_in_dim(a, position * LIVE, LIVE, 0)
     live = slot < live_count

time: 112 us -> 117 us (1.045)
  blocking collectives: 0 us -> 12.4 us
  starting transfers between devices: 26.9 us -> 22.3 us
  waiting for transfers between devices: 24.3 us -> 20.6 us
    psum x0 -> x1, blocking collectives: none -> 12.4 us  [shards(): totals = lax.psum(totals, 'req')]
    ppermute x7 -> x4, starting transfers between devices: 12.2 us -> 7.55 us  [butterfly(): other = lax.ppermute(value, axis, [(i, i ^ flip) for i in range(size)])]
    ppermute x7 -> x4, waiting for transfers between devices: 12.1 us -> 8.38 us  [butterfly(): other = lax.ppermute(value, axis, [(i, i ^ flip) for i in range(size)])]
  transfers between devices with their start and end apart: 16 -> 13, of which waited for: 9 -> 6; matrix products, arithmetic and copies ran while one was open for 18% -> 17% of each run, Pallas kernels for 0% -> 0%
where the time goes in v19:
time: 117 us; the launch traced here: 116 us
  matrix products  27.4 us (23%)
  starting transfers between devices  22.3 us (19%)
  waiting for transfers between devices  20.6 us (18%)
  other arithmetic  19 us (16%)
  blocking collectives  12.4 us (11%)
  between operations  7.54 us (6%)
  local copies, waits for them, and re-layouts  6.86 us (6%)
    dot_general x5, matrix products, block_stats(): logits = jnp.dot(rows_in, head, preferred_element_type=jnp.float32)  25.2 us
    ppermute x9, starting transfers between devices, shift(): return lax.ppermute(value, AXES, pairs)  14.7 us
    psum x1, blocking collectives, shards(): totals = lax.psum(totals, 'req')  12.4 us
    reduce_sum x5, other arithmetic, block_stats(): total = jnp.sum(expo, axis=-1)  12.3 us
    ppermute x9, waiting for transfers between devices, shift(): return lax.ppermute(value, AXES, pairs)  12.2 us
    ppermute x4, waiting for transfers between devices, butterfly(): other = lax.ppermute(value, axis, [(i, i ^ flip) for i in range(size)])  8.38 us
    ppermute x4, starting transfers between devices, butterfly(): other = lax.ppermute(value, axis, [(i, i ^ flip) for i in range(size)])  7.55 us
  transfers between devices with their start and end apart: 13, of which 6 were waited for; matrix products, arithmetic and copies ran while one was open for 17% of the time, Pallas kernels for 0%

profile of v19, /device:TPU:0, one launch (start us, length us, event | category | flops | bytes accessed | tf_op | source)
XLA Modules:
  0.0 116.1 jit_solution(14975297905655274118)
XLA Ops:
  0.7 1.2 fusion.10
  1.8 1.3 %fusion.55 = (s32[1,1]{1,0:T(1,128)}, s32[1,1]{1,0:T(1,128)}) fusion(s32[1,2]{1,0:T(1,128)} %param.10), kind=kLoop, calls=%fused_computation.205 | loop fusion | bytes 16 | tf_op jit(solution)/shard_map/slice | solution.py:106
  3.2 0.6 iota_add_fusion
  5.1 0.9 and_select_fusion.1
  6.0 1.3 %convolution_convert_fusion = bf16[96,1536]{1,0:T(8,128)(2,1)S(1)} fusion(bf16[128,1536]{1,0:T(8,128)(2,1)} %param.6, f32[1536]{0:T(1024)} %param.7, f32[128]{0:T(128)S(1)} %add_rsqrt_fusion, s32[96]{0:T(128)S(1)} %iota_add_fusion), kind=kOutput, calls=%fused_computation.22 | convolution fusion | flops 38694912 | bytes 695168 | tf_op jit(solution)/shard_map/dot_general | solution.py:115
  7.3 0.1 select_convert_fusion
  7.5 4.1 %collective-permute-start.2 = (bf16[96,1664]{1,0:T(8,128)(2,1)S(1)}, bf16[96,1664]{1,0:T(8,128)(2,1)S(1)}, u32[]{:S(2)}, u32[]{:S(2)}) collective-permute-start(bf16[96,1664]{1,0:T(8,128)(2,1)S(1)} %get-tuple-element.44), channel_id=1, source_target_pairs={{0,2},{1,3},{2,0},{3,1},{4,6},{5,7},{6,4},{7,5},{8,10},{9,11},{10,... | collective-permute-start | bytes 958472 | tf_op jit(solution)/shard_map/ppermute | solution.py:79
  11.6 0.7 collective-permute-start.1
  12.3 1.3 %collective-permute-start = (bf16[96,1664]{1,0:T(8,128)(2,1)S(1)}, bf16[96,1664]{1,0:T(8,128)(2,1)S(1)}, u32[]{:S(2)}, u32[]{:S(2)}) collective-permute-start(bf16[96,1664]{1,0:T(8,128)(2,1)S(1)} %get-tuple-element.44), channel_id=1, source_target_pairs={{0,1},{1,2},{2,3},{3,0},{4,5},{5,6},{6,7},{7,4},{8,9},{9,10},{10,1... | collective-permute-start | bytes 958472 | tf_op jit(solution)/shard_map/ppermute | solution.py:79
  13.7 0.7 gather_fusion
  14.3 0.7 gather_fusion.1
  15.0 5.6 %fusion.56 = (f32[96]{0:T(128)S(1)}, f32[96,3072]{1,0:T(8,128)S(1)}) fusion(bf16[96,1536]{1,0:T(8,128)(2,1)S(1)} %convolution_convert_fusion, bf16[1536,3072]{1,0:T(8,128)(2,1)} %param.8), kind=kOutput, calls=%fused_computation.206 | convolution fusion | flops 906264448 | bytes 10912128 | tf_op jit(solution)/shard_map/dot_general | solution.py:89
  20.7 0.2 fusion.25
  20.9 0.5 fusion.8
  21.4 0.2 maximum_reduce_fusion
  21.6 0.2 pad_maximum_fusion
  21.8 0.1 fusion.53
  21.9 3.1 %collective-permute-start.7 = (bf16[4,48,1664]{2,1,0:T(8,128)(2,1)S(1)}, bf16[4,48,1664]{2,1,0:T(8,128)(2,1)S(1)}, u32[]{:S(2)}, u32[]{:S(2)}) collective-permute-start(bf16[4,48,1664]{2,1,0:T(8,128)(2,1)S(1)} %get-tuple-element.41), channel_id=1, source_target_pairs={{0,8},{1,9},{2,10},{3,11},{4,12},{5,13},{6,14},{7,15},{8,0},{9,1},... | collective-permute-start | bytes 1916936 | tf_op jit(solution)/shard_map/ppermute | solution.py:79
  25.0 1.1 collective-permute-start.5
  26.2 0.9 collective-permute-start.3
  27.1 0.6 collective-permute-start.8
  27.7 2.6 %collective-permute-start.6 = (bf16[4,48,1664]{2,1,0:T(8,128)(2,1)S(1)}, bf16[4,48,1664]{2,1,0:T(8,128)(2,1)S(1)}, u32[]{:S(2)}, u32[]{:S(2)}) collective-permute-start(bf16[4,48,1664]{2,1,0:T(8,128)(2,1)S(1)} %get-tuple-element.42), channel_id=1, source_target_pairs={{0,12},{1,13},{2,14},{3,15},{4,0},{5,1},{6,2},{7,3},{8,4},{9,5},{1... | collective-permute-start | bytes 1916936 | tf_op jit(solution)/shard_map/ppermute | solution.py:79
  30.5 2.1 %fusion.57 = (f32[192]{0:T(256)S(1)}, f32[192,3072]{1,0:T(8,128)S(1)}) fusion(bf16[1536,3072]{1,0:T(8,128)(2,1)S(1)} %bitcast.52, bf16[192,1664]{1,0:T(8,128)(2,1)S(1)} %constant_dynamic-update-slice_fusion), kind=kOutput, calls=%fused_computation.207 | convolution fusion | flops 1812528896 | bytes 12387072 | tf_op jit(solution)/shard_map/dot_general | solution.py:89
  32.6 0.2 fusion.23
  32.8 1.8 %fusion.58 = (f32[96]{0:T(128)S(1)}, f32[96,3072]{1,0:T(8,128)S(1)}) fusion(bf16[1536,3072]{1,0:T(8,128)(2,1)S(1)} %bitcast.52, bf16[96,1664]{1,0:T(8,128)(2,1)S(1)} %collective-permute-done.2), kind=kOutput, calls=%fused_computation.208 | convolution fusion | flops 906264448 | bytes 10912128 | tf_op jit(solution)/shard_map/dot_general | solution.py:89
  34.6 0.5 fusion.7
  35.1 0.2 fusion.21
  35.3 1.0 fusion.4
  36.3 0.3 collective-permute-start.4
  36.6 11.2 %collective-permute-done.8 = bf16[4,48,1664]{2,1,0:T(8,128)(2,1)S(1)} collective-permute-done((bf16[4,48,1664]{2,1,0:T(8,128)(2,1)S(1)}, bf16[4,48,1664]{2,1,0:T(8,128)(2,1)S(1)}, u32[]{:S(2)}, u32[]{:S(2)}) %collective-permute-start.8) | collective-permute-done | bytes 639008 | tf_op jit(solution)/shard_map/ppermute | solution.py:79
  47.8 0.1 pad_maximum_fusion.1
  47.9 5.7 %fusion.60 = (f32[384]{0:T(512)S(1)}, f32[384,3072]{1,0:T(8,128)}) fusion(bf16[1536,3072]{1,0:T(8,128)(2,1)S(1)} %bitcast.52, bf16[384,1664]{1,0:T(8,128)(2,1)S(1)} %bitcast.62), kind=kOutput, calls=%fused_computation.210 | convolution fusion | flops 3625057792 | bytes 15336960 | tf_op jit(solution)/shard_map/dot_general | solution.py:89
  53.6 1.0 collective-permute-done.6
  54.6 0.2 maximum_maximum_fusion
  54.9 9.9 %fusion.59 = (f32[768]{0:T(1024)S(1)}, f32[768,3072]{1,0:T(8,128)}) fusion(bf16[1536,3072]{1,0:T(8,128)(2,1)S(1)} %bitcast.52, bf16[768,1664]{1,0:T(8,128)(2,1)S(1)} %bitcast.56), kind=kOutput, calls=%fused_computation.209 | convolution fusion | flops 7250115584 | bytes 21236736 | tf_op jit(solution)/shard_map/dot_general | solution.py:89
  64.8 0.2 slice_reduce_fusion.6
  65.0 0.2 slice_reduce_fusion.7
  65.2 0.2 slice_reduce_fusion.8
  65.4 0.7 gather_fusion.3
  66.1 0.6 fusion.51
  67.0 0.1 copy.16
  67.2 4.0 %fusion.1 = (f32[384]{0:T(512)S(1)}, f32[384]{0:T(512)S(1)}, f32[384]{0:T(512)S(1)}) fusion(f32[384,3072]{1,0:T(8,128)} %get-tuple-element.76, f32[384]{0:T(512)S(1)} %get-tuple-element.75, s32[384]{0:T(512)S(1)} %fusion.38), kind=kLoop, calls=%fused_computation.13 | loop fusion | flops 8256384 | bytes 4726272 | tf_op jit(solution)/shard_map/reduce_sum | solution.py:92
  71.3 6.3 %fusion = (f32[768]{0:T(1024)S(1)}, f32[768]{0:T(1024)S(1)}, f32[768]{0:T(1024)S(1)}) fusion(f32[768,3072]{1,0:T(8,128)} %get-tuple-element.74, f32[768]{0:T(1024)S(1)} %get-tuple-element.73, s32[768]{0:T(1024)S(1)} %fusion.36), kind=kLoop, calls=%fused_computation.8 | loop fusion | flops 16512768 | bytes 9452544 | tf_op jit(solution)/shard_map/reduce_sum | solution.py:92
  77.7 0.1 concatenate.33
  77.9 0.6 gather_fusion.2
  78.5 0.1 gather.19
  78.6 1.1 collective-permute-start.9
  79.7 2.8 %collective-permute-done.9 = f32[4,1536]{1,0:T(4,128)S(1)} collective-permute-done((f32[4,1536]{1,0:T(4,128)S(1)}, f32[4,1536]{1,0:T(4,128)S(1)}, u32[]{:S(2)}, u32[]{:S(2)}) %collective-permute-start.9) | collective-permute-done | bytes 24608 | tf_op jit(solution)/shard_map/ppermute | solution.py:32
  82.6 2.3 %collective-permute-start.10 = (f32[4,1536]{1,0:T(4,128)S(1)}, f32[4,1536]{1,0:T(4,128)S(1)}, u32[]{:S(2)}, u32[]{:S(2)}) collective-permute-start(f32[4,1536]{1,0:T(4,128)S(1)} %pad_maximum_fusion.3), channel_id=1, source_target_pairs={{0,3},{1,2},{2,1},{3,0},{4,7},{5,6},{6,5},{7,4},{8,11},{9,10},{10,... | collective-permute-start | bytes 73736 | tf_op jit(solution)/shard_map/ppermute | solution.py:32
  84.9 2.8 %collective-permute-done.10 = f32[4,1536]{1,0:T(4,128)S(1)} collective-permute-done((f32[4,1536]{1,0:T(4,128)S(1)}, f32[4,1536]{1,0:T(4,128)S(1)}, u32[]{:S(2)}, u32[]{:S(2)}) %collective-permute-start.10) | collective-permute-done | bytes 24608 | tf_op jit(solution)/shard_map/ppermute | solution.py:32
  87.9 1.5 %collective-permute-start.11 = (f32[4,1536]{1,0:T(4,128)S(1)}, f32[4,1536]{1,0:T(4,128)S(1)}, u32[]{:S(2)}, u32[]{:S(2)}) collective-permute-start(f32[4,1536]{1,0:T(4,128)S(1)} %pad_maximum_fusion.4), channel_id=1, source_target_pairs={{0,4},{1,5},{2,6},{3,7},{4,0},{5,1},{6,2},{7,3},{8,12},{9,13},{10,... | collective-permute-start | bytes 73736 | tf_op jit(solution)/shard_map/ppermute | solution.py:32
  90.7 1.1 collective-permute-done.11
  92.0 2.7 %collective-permute-start.12 = (f32[4,1536]{1,0:T(4,128)S(1)}, f32[4,1536]{1,0:T(4,128)S(1)}, u32[]{:S(2)}, u32[]{:S(2)}) collective-permute-start(f32[4,1536]{1,0:T(4,128)S(1)} %pad_maximum_fusion.5), channel_id=1, source_target_pairs={{0,12},{1,13},{2,14},{3,15},{4,8},{5,9},{6,10},{7,11},{8,4},{9,5},... | collective-permute-start | bytes 73736 | tf_op jit(solution)/shard_map/ppermute | solution.py:32
  95.4 1.6 %collective-permute-done.12 = f32[4,1536]{1,0:T(4,128)S(1)} collective-permute-done((f32[4,1536]{1,0:T(4,128)S(1)}, f32[4,1536]{1,0:T(4,128)S(1)}, u32[]{:S(2)}, u32[]{:S(2)}) %collective-permute-start.12) | collective-permute-done | bytes 24608 | tf_op jit(solution)/shard_map/ppermute | solution.py:32
  97.1 0.8 select_reduce_fusion.5
  97.9 0.7 pad_maximum_fusion.11
  99.2 12.4 %psum.7 = f32[2]{0:T(128)S(1)} all-reduce(f32[2]{0:T(128)S(1)} %pad_maximum_fusion.11), channel_id=1, replica_groups=mesh['req'=8,'voc'=16] {'req'}, use_global_device_ids=true, to_apply=%region_23.24 | all-reduce | flops 2 | bytes 16 | tf_op jit(solution)/shard_map/psum | solution.py:167
  111.7 0.6 fusion.54
  113.6 0.2 fusion.49
  113.8 0.2 fusion.48
  114.0 0.2 select_dynamic-update-slice_fusion
  114.1 0.1 copy-done.2
  114.3 0.2 copy-done.3
  114.5 0.5 copy-done.1
  (79 shorter events, 1.5 us)
Async XLA Ops:
  0.6 13.0 %copy-start = (s32[4]{0:T(128)S(1)}, s32[4]{0:T(128)}, u32[]{:S(2)}) copy-start(s32[4]{0:T(128)} %constant.170.clone) | copy-start | bytes 52
  7.5 13.9 %collective-permute-start.2 = (bf16[96,1664]{1,0:T(8,128)(2,1)S(1)}, bf16[96,1664]{1,0:T(8,128)(2,1)S(1)}, u32[]{:S(2)}, u32[]{:S(2)}) collective-permute-start(bf16[96,1664]{1,0:T(8,128)(2,1)S(1)} %get-tuple-element.44), channel_id=1, source_target_pairs={{0,2},{1,3},{2,0},{3,1},{4,6},{5,7},{6,4},{7,5},{8,10},{9,11},{10,... | collective-permute-start | bytes 958472 | tf_op jit(solution)/shard_map/ppermute | solution.py:79
  11.6 9.9 %collective-permute-start.1 = (bf16[96,1664]{1,0:T(8,128)(2,1)S(1)}, bf16[96,1664]{1,0:T(8,128)(2,1)S(1)}, u32[]{:S(2)}, u32[]{:S(2)}) collective-permute-start(bf16[96,1664]{1,0:T(8,128)(2,1)S(1)} %get-tuple-element.44), channel_id=1, source_target_pairs={{0,3},{1,0},{2,1},{3,2},{4,7},{5,4},{6,5},{7,6},{8,11},{9,8},{10,9... | collective-permute-start | bytes 958472 | tf_op jit(solution)/shard_map/ppermute | solution.py:79
  12.3 9.2 %collective-permute-start = (bf16[96,1664]{1,0:T(8,128)(2,1)S(1)}, bf16[96,1664]{1,0:T(8,128)(2,1)S(1)}, u32[]{:S(2)}, u32[]{:S(2)}) collective-permute-start(bf16[96,1664]{1,0:T(8,128)(2,1)S(1)} %get-tuple-element.44), channel_id=1, source_target_pairs={{0,1},{1,2},{2,3},{3,0},{4,5},{5,6},{6,7},{7,4},{8,9},{9,10},{10,1... | collective-permute-start | bytes 958472 | tf_op jit(solution)/shard_map/ppermute | solution.py:79
  15.0 15.4 %slice-start = ((s8[9437184]{0:T(1024)(128)(4,1)}), s8[4194304]{0:T(1024)(128)(4,1)S(1)}, s32[]{:S(2)}) async-start(s8[9437184]{0:T(1024)(128)(4,1)} %bitcast.51), calls=%async_computation | async-start | bytes 8388608
  15.0 15.4 %slice-start.1 = ((s8[9437184]{0:T(1024)(128)(4,1)}), s8[4194304]{0:T(1024)(128)(4,1)S(1)}, s32[]{:S(2)}) async-start(s8[9437184]{0:T(1024)(128)(4,1)} %bitcast.51), calls=%async_computation.1 | async-start | bytes 8388608
  20.8 9.6 %slice-start.2 = ((s8[9437184]{0:T(1024)(128)(4,1)}), s8[1048576]{0:T(1024)(128)(4,1)S(1)}, s32[]{:S(2)}) async-start(s8[9437184]{0:T(1024)(128)(4,1)} %bitcast.51), calls=%async_computation.2 | async-start | bytes 2097152
  21.9 14.4 %collective-permute-start.7 = (bf16[4,48,1664]{2,1,0:T(8,128)(2,1)S(1)}, bf16[4,48,1664]{2,1,0:T(8,128)(2,1)S(1)}, u32[]{:S(2)}, u32[]{:S(2)}) collective-permute-start(bf16[4,48,1664]{2,1,0:T(8,128)(2,1)S(1)} %get-tuple-element.41), channel_id=1, source_target_pairs={{0,8},{1,9},{2,10},{3,11},{4,12},{5,13},{6,14},{7,15},{8,0},{9,1},... | collective-permute-start | bytes 1916936 | tf_op jit(solution)/shard_map/ppermute | solution.py:79
  25.0 28.6 %collective-permute-start.5 = (bf16[4,48,1664]{2,1,0:T(8,128)(2,1)S(1)}, bf16[4,48,1664]{2,1,0:T(8,128)(2,1)S(1)}, u32[]{:S(2)}, u32[]{:S(2)}) collective-permute-start(bf16[4,48,1664]{2,1,0:T(8,128)(2,1)S(1)} %get-tuple-element.41), channel_id=1, source_target_pairs={{0,12},{1,13},{2,14},{3,15},{4,0},{5,1},{6,2},{7,3},{8,4},{9,5},{1... | collective-permute-start | bytes 1916936 | tf_op jit(solution)/shard_map/ppermute | solution.py:79
  26.2 27.4 %collective-permute-start.3 = (bf16[4,48,1664]{2,1,0:T(8,128)(2,1)S(1)}, bf16[4,48,1664]{2,1,0:T(8,128)(2,1)S(1)}, u32[]{:S(2)}, u32[]{:S(2)}) collective-permute-start(bf16[4,48,1664]{2,1,0:T(8,128)(2,1)S(1)} %get-tuple-element.41), channel_id=1, source_target_pairs={{0,4},{1,5},{2,6},{3,7},{4,8},{5,9},{6,10},{7,11},{8,12},{9,13},{1... | collective-permute-start | bytes 1916936 | tf_op jit(solution)/shard_map/ppermute | solution.py:79
  27.1 20.7 %collective-permute-start.8 = (bf16[4,48,1664]{2,1,0:T(8,128)(2,1)S(1)}, bf16[4,48,1664]{2,1,0:T(8,128)(2,1)S(1)}, u32[]{:S(2)}, u32[]{:S(2)}) collective-permute-start(bf16[4,48,1664]{2,1,0:T(8,128)(2,1)S(1)} %get-tuple-element.42), channel_id=1, source_target_pairs={{0,8},{1,9},{2,10},{3,11},{4,12},{5,13},{6,14},{7,15},{8,0},{9,1},... | collective-permute-start | bytes 1916936 | tf_op jit(solution)/shard_map/ppermute | solution.py:79
  27.7 26.9 %collective-permute-start.6 = (bf16[4,48,1664]{2,1,0:T(8,128)(2,1)S(1)}, bf16[4,48,1664]{2,1,0:T(8,128)(2,1)S(1)}, u32[]{:S(2)}, u32[]{:S(2)}) collective-permute-start(bf16[4,48,1664]{2,1,0:T(8,128)(2,1)S(1)} %get-tuple-element.42), channel_id=1, source_target_pairs={{0,12},{1,13},{2,14},{3,15},{4,0},{5,1},{6,2},{7,3},{8,4},{9,5},{1... | collective-permute-start | bytes 1916936 | tf_op jit(solution)/shard_map/ppermute | solution.py:79
  36.3 18.3 %collective-permute-start.4 = (bf16[4,48,1664]{2,1,0:T(8,128)(2,1)S(1)}, bf16[4,48,1664]{2,1,0:T(8,128)(2,1)S(1)}, u32[]{:S(2)}, u32[]{:S(2)}) collective-permute-start(bf16[4,48,1664]{2,1,0:T(8,128)(2,1)S(1)} %get-tuple-element.42), channel_id=1, source_target_pairs={{0,4},{1,5},{2,6},{3,7},{4,8},{5,9},{6,10},{7,11},{8,12},{9,13},{1... | collective-permute-start | bytes 1916936 | tf_op jit(solution)/shard_map/ppermute | solution.py:79
  78.6 3.9 %collective-permute-start.9 = (f32[4,1536]{1,0:T(4,128)S(1)}, f32[4,1536]{1,0:T(4,128)S(1)}, u32[]{:S(2)}, u32[]{:S(2)}) collective-permute-start(f32[4,1536]{1,0:T(4,128)S(1)} %broadcast_select_fusion), channel_id=1, source_target_pairs={{0,1},{1,0},{2,3},{3,2},{4,5},{5,4},{6,7},{7,6},{8,9},{9,8},{10,11... | collective-permute-start | bytes 73736 | tf_op jit(solution)/shard_map/ppermute | solution.py:32
  82.6 5.1 %collective-permute-start.10 = (f32[4,1536]{1,0:T(4,128)S(1)}, f32[4,1536]{1,0:T(4,128)S(1)}, u32[]{:S(2)}, u32[]{:S(2)}) collective-permute-start(f32[4,1536]{1,0:T(4,128)S(1)} %pad_maximum_fusion.3), channel_id=1, source_target_pairs={{0,3},{1,2},{2,1},{3,0},{4,7},{5,6},{6,5},{7,4},{8,11},{9,10},{10,... | collective-permute-start | bytes 73736 | tf_op jit(solution)/shard_map/ppermute | solution.py:32
  87.9 3.9 %collective-permute-start.11 = (f32[4,1536]{1,0:T(4,128)S(1)}, f32[4,1536]{1,0:T(4,128)S(1)}, u32[]{:S(2)}, u32[]{:S(2)}) collective-permute-start(f32[4,1536]{1,0:T(4,128)S(1)} %pad_maximum_fusion.4), channel_id=1, source_target_pairs={{0,4},{1,5},{2,6},{3,7},{4,0},{5,1},{6,2},{7,3},{8,12},{9,13},{10,... | collective-permute-start | bytes 73736 | tf_op jit(solution)/shard_map/ppermute | solution.py:32
  92.0 5.1 %collective-permute-start.12 = (f32[4,1536]{1,0:T(4,128)S(1)}, f32[4,1536]{1,0:T(4,128)S(1)}, u32[]{:S(2)}, u32[]{:S(2)}) collective-permute-start(f32[4,1536]{1,0:T(4,128)S(1)} %pad_maximum_fusion.5), channel_id=1, source_target_pairs={{0,12},{1,13},{2,14},{3,15},{4,8},{5,9},{6,10},{7,11},{8,4},{9,5},... | collective-permute-start | bytes 73736 | tf_op jit(solution)/shard_map/ppermute | solution.py:32
  113.8 0.5 copy-start.2
  114.0 0.5 copy-start.3
  114.5 0.5 copy-start.1

commit v20 on v16

--- a/solution.py
+++ b/solution.py
@@ -125,9 +125,8 @@
     stats = lambda block: block_stats(block, head, position)
     left = shift(own, 0, 1, reqs, vocs)
     right = shift(own, 0, -1, reqs, vocs)
-    part_own = stats(own)
     far = shift(own, 0, 2, reqs, vocs)
-    part_near = stats(jnp.concatenate([left, right]))
+    part_near = stats(jnp.concatenate([own, left, right]))
     line = jnp.stack([own, left, right, far])
     halves = lambda step: jnp.concatenate(
         [shift(line[:, :HALF], 1, step, reqs, vocs), shift(line[:, HALF:], 1, step, reqs, vocs)], axis=1
@@ -138,7 +137,7 @@
     line_far = halves(2)
     part_lines = stats(jnp.concatenate([line_left, line_right]).reshape(-1, own.shape[1]))
     part_line_far = stats(line_far.reshape(-1, own.shape[1]))
-    processed = jnp.concatenate([part_own, part_near, part_far, part_lines, part_line_far], axis=1)
+    processed = jnp.concatenate([part_near, part_far, part_lines, part_line_far], axis=1)
     processed = processed.reshape(4, vocs, LIVE)
     count_of = lambda block: block[..., :1, width + 2].reshape(-1).astype(jnp.int32)
     processed_counts = jnp.concatenate(

time: 112 us -> 112 us (level)
  matrix products: 27.4 us -> 25.4 us
  local copies, waits for them, and re-layouts: 6.03 us -> 7.3 us
    dot_general x5 -> x4, matrix products: 25.2 us -> 23.2 us  [block_stats(): logits = jnp.dot(rows_in, head, preferred_element_type=jnp.float32)]
    reduce_sum x5 -> x4, other arithmetic: 12.3 us -> 12.1 us  [block_stats(): total = jnp.sum(expo, axis=-1)]
  transfers between devices with their start and end apart: 16 -> 16, of which waited for: 9 -> 11; matrix products, arithmetic and copies ran while one was open for 18% -> 17% of each run, Pallas kernels for 0% -> 0%
where the time goes in v20:
time: 112 us; the launch traced here: 111 us
  starting transfers between devices  27.3 us (24%)
  matrix products  25.4 us (23%)
  waiting for transfers between devices  24.3 us (22%)
  other arithmetic  19.4 us (17%)
  between operations  7.56 us (7%)
  local copies, waits for them, and re-layouts  7.3 us (7%)
    dot_general x4, matrix products, block_stats(): logits = jnp.dot(rows_in, head, preferred_element_type=jnp.float32)  23.2 us
    ppermute x9, starting transfers between devices, shift(): return lax.ppermute(value, AXES, pairs)  14.7 us
    ppermute x9, waiting for transfers between devices, shift(): return lax.ppermute(value, AXES, pairs)  12.6 us
    ppermute x7, starting transfers between devices, butterfly(): other = lax.ppermute(value, axis, [(i, i ^ flip) for i in range(size)])  12.6 us
    reduce_sum x4, other arithmetic, block_stats(): total = jnp.sum(expo, axis=-1)  12.1 us
    ppermute x7, waiting for transfers between devices, butterfly(): other = lax.ppermute(value, axis, [(i, i ^ flip) for i in range(size)])  11.7 us
  transfers between devices with their start and end apart: 16, of which 11 were waited for; matrix products, arithmetic and copies ran while one was open for 17% of the time, Pallas kernels for 0%

profile of v20, /device:TPU:0, one launch (start us, length us, event | category | flops | bytes accessed | tf_op | source)
XLA Modules:
  0.0 111.4 jit_solution(13441534147508610860)
XLA Ops:
  0.7 1.2 %fusion.11 = f32[128]{0:T(128)S(1)} fusion(bf16[128,1536]{1,0:T(8,128)(2,1)} %param.6), kind=kLoop, calls=%fused_computation.39 | loop fusion | flops 589696 | bytes 393728 | tf_op jit(solution)/shard_map/reduce_sum | solution.py:109
  1.8 1.3 %fusion.55 = (s32[1,1]{1,0:T(1,128)}, s32[1,1]{1,0:T(1,128)}) fusion(s32[1,2]{1,0:T(1,128)} %param.10), kind=kLoop, calls=%fused_computation.202 | loop fusion | bytes 16 | tf_op jit(solution)/shard_map/slice | solution.py:106
  3.1 0.6 iota_add_fusion
  5.1 0.9 and_select_fusion.1
  6.0 1.3 %convolution_convert_fusion = bf16[96,1536]{1,0:T(8,128)(2,1)S(1)} fusion(bf16[128,1536]{1,0:T(8,128)(2,1)} %param.6, f32[1536]{0:T(1024)} %param.7, f32[128]{0:T(128)S(1)} %add_rsqrt_fusion, s32[96]{0:T(128)S(1)} %iota_add_fusion), kind=kOutput, calls=%fused_computation.22 | convolution fusion | flops 38694912 | bytes 695168 | tf_op jit(solution)/shard_map/dot_general | solution.py:115
  7.3 0.1 select_convert_fusion
  7.5 4.1 %collective-permute-start.2 = (bf16[96,1664]{1,0:T(8,128)(2,1)S(1)}, bf16[96,1664]{1,0:T(8,128)(2,1)S(1)}, u32[]{:S(2)}, u32[]{:S(2)}) collective-permute-start(bf16[96,1664]{1,0:T(8,128)(2,1)S(1)} %get-tuple-element.41), channel_id=1, source_target_pairs={{0,2},{1,3},{2,0},{3,1},{4,6},{5,7},{6,4},{7,5},{8,10},{9,11},{10,... | collective-permute-start | bytes 958472 | tf_op jit(solution)/shard_map/ppermute | solution.py:79
  11.5 0.7 collective-permute-start.1
  12.3 1.3 %collective-permute-start = (bf16[96,1664]{1,0:T(8,128)(2,1)S(1)}, bf16[96,1664]{1,0:T(8,128)(2,1)S(1)}, u32[]{:S(2)}, u32[]{:S(2)}) collective-permute-start(bf16[96,1664]{1,0:T(8,128)(2,1)S(1)} %get-tuple-element.41), channel_id=1, source_target_pairs={{0,1},{1,2},{2,3},{3,0},{4,5},{5,6},{6,7},{7,4},{8,9},{9,10},{10,1... | collective-permute-start | bytes 958472 | tf_op jit(solution)/shard_map/ppermute | solution.py:79
  13.6 1.3 %gather_fusion = s32[16]{0:T(128)S(1)} fusion(s32[4]{0:T(128)} %constant.170.clone, s32[1024]{0:T(1024)S(1)} %pad_clamp_fusion.2), kind=kCustom, calls=%fused_computation | custom fusion | bytes 192 | tf_op jit(solution)/shard_map/gather | solution.py:153
  14.9 1.3 %gather_fusion.1 = s32[16]{0:T(128)S(1)} fusion(s32[4]{0:T(128)} %constant.170.clone, s32[1024]{0:T(1024)S(1)} %pad_clamp_fusion.1), kind=kCustom, calls=%fused_computation.1 | custom fusion | bytes 192 | tf_op jit(solution)/shard_map/gather | solution.py:153
  16.3 0.2 collective-permute-done.2
  16.5 4.5 %collective-permute-done.1 = bf16[96,1664]{1,0:T(8,128)(2,1)S(1)} collective-permute-done((bf16[96,1664]{1,0:T(8,128)(2,1)S(1)}, bf16[96,1664]{1,0:T(8,128)(2,1)S(1)}, u32[]{:S(2)}, u32[]{:S(2)}) %collective-permute-start.1) | collective-permute-done | bytes 319520 | tf_op jit(solution)/shard_map/ppermute | solution.py:79
  21.0 0.2 pad_maximum_fusion
  21.2 0.1 fusion.53
  21.3 3.1 %collective-permute-start.7 = (bf16[4,48,1664]{2,1,0:T(8,128)(2,1)S(1)}, bf16[4,48,1664]{2,1,0:T(8,128)(2,1)S(1)}, u32[]{:S(2)}, u32[]{:S(2)}) collective-permute-start(bf16[4,48,1664]{2,1,0:T(8,128)(2,1)S(1)} %get-tuple-element.38), channel_id=1, source_target_pairs={{0,8},{1,9},{2,10},{3,11},{4,12},{5,13},{6,14},{7,15},{8,0},{9,1},... | collective-permute-start | bytes 1916936 | tf_op jit(solution)/shard_map/ppermute | solution.py:79
  24.4 1.1 %collective-permute-start.5 = (bf16[4,48,1664]{2,1,0:T(8,128)(2,1)S(1)}, bf16[4,48,1664]{2,1,0:T(8,128)(2,1)S(1)}, u32[]{:S(2)}, u32[]{:S(2)}) collective-permute-start(bf16[4,48,1664]{2,1,0:T(8,128)(2,1)S(1)} %get-tuple-element.38), channel_id=1, source_target_pairs={{0,12},{1,13},{2,14},{3,15},{4,0},{5,1},{6,2},{7,3},{8,4},{9,5},{1... | collective-permute-start | bytes 1916936 | tf_op jit(solution)/shard_map/ppermute | solution.py:79
  25.5 0.9 collective-permute-start.3
  26.4 0.6 collective-permute-start.8
  27.1 2.6 %collective-permute-start.6 = (bf16[4,48,1664]{2,1,0:T(8,128)(2,1)S(1)}, bf16[4,48,1664]{2,1,0:T(8,128)(2,1)S(1)}, u32[]{:S(2)}, u32[]{:S(2)}) collective-permute-start(bf16[4,48,1664]{2,1,0:T(8,128)(2,1)S(1)} %get-tuple-element.39), channel_id=1, source_target_pairs={{0,12},{1,13},{2,14},{3,15},{4,0},{5,1},{6,2},{7,3},{8,4},{9,5},{1... | collective-permute-start | bytes 1916936 | tf_op jit(solution)/shard_map/ppermute | solution.py:79
  29.7 0.2 fusion.20
  30.0 5.8 %fusion.56 = (f32[288]{0:T(512)S(1)}, f32[288,3072]{1,0:T(8,128)S(1)}) fusion(bf16[1536,3072]{1,0:T(8,128)(2,1)} %param.8, bf16[288,1664]{1,0:T(8,128)(2,1)S(1)} %pad_maximum_fusion.2), kind=kOutput, calls=%fused_computation.203 | convolution fusion | flops 2718793472 | bytes 13862016 | tf_op jit(solution)/shard_map/dot_general | solution.py:89
  35.9 1.3 %fusion.2 = (f32[288]{0:T(512)S(1)}, f32[288]{0:T(512)S(1)}, f32[288]{0:T(512)S(1)}) fusion(f32[288,3072]{1,0:T(8,128)S(1)} %get-tuple-element.65, f32[288]{0:T(512)S(1)} %get-tuple-element.64, s32[288]{0:T(512)S(1)} %fusion.20), kind=kLoop, calls=%fused_computation.18 | loop fusion | flops 6192288 | bytes 3544704 | tf_op jit(solution)/shard_map/reduce_sum | solution.py:92
  37.2 1.8 %fusion.57 = (f32[96]{0:T(128)S(1)}, f32[96,3072]{1,0:T(8,128)S(1)}) fusion(bf16[1536,3072]{1,0:T(8,128)(2,1)S(1)} %bitcast.42, bf16[96,1664]{1,0:T(8,128)(2,1)S(1)} %collective-permute-done.2), kind=kOutput, calls=%fused_computation.204 | convolution fusion | flops 906264448 | bytes 10912128 | tf_op jit(solution)/shard_map/dot_general | solution.py:89
  39.1 0.2 maximum_reduce_fusion
  39.2 0.2 fusion.22
  39.4 0.5 fusion.7
  40.0 0.3 collective-permute-start.4
  40.3 6.9 %collective-permute-done.8 = bf16[4,48,1664]{2,1,0:T(8,128)(2,1)S(1)} collective-permute-done((bf16[4,48,1664]{2,1,0:T(8,128)(2,1)S(1)}, bf16[4,48,1664]{2,1,0:T(8,128)(2,1)S(1)}, u32[]{:S(2)}, u32[]{:S(2)}) %collective-permute-start.8) | collective-permute-done | bytes 639008 | tf_op jit(solution)/shard_map/ppermute | solution.py:79
  47.1 0.1 pad_maximum_fusion.1
  47.2 5.7 %fusion.59 = (f32[384]{0:T(512)S(1)}, f32[384,3072]{1,0:T(8,128)}) fusion(bf16[1536,3072]{1,0:T(8,128)(2,1)S(1)} %bitcast.42, bf16[384,1664]{1,0:T(8,128)(2,1)S(1)} %bitcast.52), kind=kOutput, calls=%fused_computation.206 | convolution fusion | flops 3625057792 | bytes 15336960 | tf_op jit(solution)/shard_map/dot_general | solution.py:89
  53.0 1.0 collective-permute-done.6
  54.0 0.2 maximum_maximum_fusion
  54.2 9.9 %fusion.58 = (f32[768]{0:T(1024)S(1)}, f32[768,3072]{1,0:T(8,128)}) fusion(bf16[1536,3072]{1,0:T(8,128)(2,1)S(1)} %bitcast.42, bf16[768,1664]{1,0:T(8,128)(2,1)S(1)} %bitcast.50), kind=kOutput, calls=%fused_computation.205 | convolution fusion | flops 7250115584 | bytes 21236736 | tf_op jit(solution)/shard_map/dot_general | solution.py:89
  64.2 0.2 slice_reduce_fusion.6
  64.3 0.2 slice_reduce_fusion.7
  64.5 0.2 slice_reduce_fusion.8
  64.8 0.7 gather_fusion.3
  65.5 0.6 fusion.51
  66.4 0.1 copy.16
  66.6 4.0 %fusion.1 = (f32[384]{0:T(512)S(1)}, f32[384]{0:T(512)S(1)}, f32[384]{0:T(512)S(1)}) fusion(f32[384,3072]{1,0:T(8,128)} %get-tuple-element.71, f32[384]{0:T(512)S(1)} %get-tuple-element.70, s32[384]{0:T(512)S(1)} %fusion.35), kind=kLoop, calls=%fused_computation.13 | loop fusion | flops 8256384 | bytes 4726272 | tf_op jit(solution)/shard_map/reduce_sum | solution.py:92
  70.6 6.3 %fusion = (f32[768]{0:T(1024)S(1)}, f32[768]{0:T(1024)S(1)}, f32[768]{0:T(1024)S(1)}) fusion(f32[768,3072]{1,0:T(8,128)} %get-tuple-element.69, f32[768]{0:T(1024)S(1)} %get-tuple-element.68, s32[768]{0:T(1024)S(1)} %fusion.33), kind=kLoop, calls=%fused_computation.8 | loop fusion | flops 16512768 | bytes 9452544 | tf_op jit(solution)/shard_map/reduce_sum | solution.py:92
  77.0 0.1 concatenate.33
  77.2 0.6 gather_fusion.2
  77.9 1.1 collective-permute-start.9
  79.0 2.8 %collective-permute-done.9 = f32[4,1536]{1,0:T(4,128)S(1)} collective-permute-done((f32[4,1536]{1,0:T(4,128)S(1)}, f32[4,1536]{1,0:T(4,128)S(1)}, u32[]{:S(2)}, u32[]{:S(2)}) %collective-permute-start.9) | collective-permute-done | bytes 24608 | tf_op jit(solution)/shard_map/ppermute | solution.py:32
  82.0 2.7 %collective-permute-start.10 = (f32[4,1536]{1,0:T(4,128)S(1)}, f32[4,1536]{1,0:T(4,128)S(1)}, u32[]{:S(2)}, u32[]{:S(2)}) collective-permute-start(f32[4,1536]{1,0:T(4,128)S(1)} %pad_maximum_fusion.4), channel_id=1, source_target_pairs={{0,3},{1,2},{2,1},{3,0},{4,7},{5,6},{6,5},{7,4},{8,11},{9,10},{10,... | collective-permute-start | bytes 73736 | tf_op jit(solution)/shard_map/ppermute | solution.py:32
  84.7 2.4 %collective-permute-done.10 = f32[4,1536]{1,0:T(4,128)S(1)} collective-permute-done((f32[4,1536]{1,0:T(4,128)S(1)}, f32[4,1536]{1,0:T(4,128)S(1)}, u32[]{:S(2)}, u32[]{:S(2)}) %collective-permute-start.10) | collective-permute-done | bytes 24608 | tf_op jit(solution)/shard_map/ppermute | solution.py:32
  87.3 1.5 %collective-permute-start.11 = (f32[4,1536]{1,0:T(4,128)S(1)}, f32[4,1536]{1,0:T(4,128)S(1)}, u32[]{:S(2)}, u32[]{:S(2)}) collective-permute-start(f32[4,1536]{1,0:T(4,128)S(1)} %pad_maximum_fusion.5), channel_id=1, source_target_pairs={{0,4},{1,5},{2,6},{3,7},{4,0},{5,1},{6,2},{7,3},{8,12},{9,13},{10,... | collective-permute-start | bytes 73736 | tf_op jit(solution)/shard_map/ppermute | solution.py:32
  90.7 0.4 collective-permute-done.11
  91.3 2.7 %collective-permute-start.12 = (f32[4,1536]{1,0:T(4,128)S(1)}, f32[4,1536]{1,0:T(4,128)S(1)}, u32[]{:S(2)}, u32[]{:S(2)}) collective-permute-start(f32[4,1536]{1,0:T(4,128)S(1)} %pad_maximum_fusion.6), channel_id=1, source_target_pairs={{0,12},{1,13},{2,14},{3,15},{4,8},{5,9},{6,10},{7,11},{8,4},{9,5},... | collective-permute-start | bytes 73736 | tf_op jit(solution)/shard_map/ppermute | solution.py:32
  94.8 1.6 %collective-permute-done.12 = f32[4,1536]{1,0:T(4,128)S(1)} collective-permute-done((f32[4,1536]{1,0:T(4,128)S(1)}, f32[4,1536]{1,0:T(4,128)S(1)}, u32[]{:S(2)}, u32[]{:S(2)}) %collective-permute-start.12) | collective-permute-done | bytes 24608 | tf_op jit(solution)/shard_map/ppermute | solution.py:32
  96.5 0.8 select_reduce_fusion.4
  97.2 0.7 pad_maximum_fusion.11
  98.0 0.2 fusion.49
  98.2 0.2 fusion.48
  98.4 0.2 select_dynamic-update-slice_fusion
  98.5 0.6 collective-permute-done.13
  99.1 0.7 fusion.40
  99.8 1.6 %collective-permute-start.14 = (f32[2]{0:T(128)S(1)}, f32[2]{0:T(128)S(1)}, u32[]{:S(2)}, u32[]{:S(2)}) collective-permute-start(f32[2]{0:T(128)S(1)} %fusion.40), channel_id=1, source_target_pairs={{0,32},{16,48},{32,0},{48,16},{64,96},{80,112},{96,64},{112,80},{1... | collective-permute-start | bytes 32 | tf_op jit(solution)/shard_map/ppermute | solution.py:32
  101.4 2.0 %collective-permute-done.14 = f32[2]{0:T(128)S(1)} collective-permute-done((f32[2]{0:T(128)S(1)}, f32[2]{0:T(128)S(1)}, u32[]{:S(2)}, u32[]{:S(2)}) %collective-permute-start.14) | collective-permute-done | bytes 40 | tf_op jit(solution)/shard_map/ppermute | solution.py:32
  103.4 3.0 %collective-permute-start.15 = (f32[2]{0:T(128)S(1)}, f32[2]{0:T(128)S(1)}, u32[]{:S(2)}, u32[]{:S(2)}) collective-permute-start(f32[2]{0:T(128)S(1)} %fusion.39), channel_id=1, source_target_pairs={{0,96},{16,112},{32,64},{48,80},{64,32},{80,48},{96,0},{112,16},{1... | collective-permute-start | bytes 32 | tf_op jit(solution)/shard_map/ppermute | solution.py:32
  106.4 1.8 %collective-permute-done.15 = f32[2]{0:T(128)S(1)} collective-permute-done((f32[2]{0:T(128)S(1)}, f32[2]{0:T(128)S(1)}, u32[]{:S(2)}, u32[]{:S(2)}) %collective-permute-start.15) | collective-permute-done | bytes 40 | tf_op jit(solution)/shard_map/ppermute | solution.py:32
  108.2 0.6 fusion.54
  (83 shorter events, 1.7 us)
Async XLA Ops:
  7.5 9.0 %collective-permute-start.2 = (bf16[96,1664]{1,0:T(8,128)(2,1)S(1)}, bf16[96,1664]{1,0:T(8,128)(2,1)S(1)}, u32[]{:S(2)}, u32[]{:S(2)}) collective-permute-start(bf16[96,1664]{1,0:T(8,128)(2,1)S(1)} %get-tuple-element.41), channel_id=1, source_target_pairs={{0,2},{1,3},{2,0},{3,1},{4,6},{5,7},{6,4},{7,5},{8,10},{9,11},{10,... | collective-permute-start | bytes 958472 | tf_op jit(solution)/shard_map/ppermute | solution.py:79
  11.5 9.4 %collective-permute-start.1 = (bf16[96,1664]{1,0:T(8,128)(2,1)S(1)}, bf16[96,1664]{1,0:T(8,128)(2,1)S(1)}, u32[]{:S(2)}, u32[]{:S(2)}) collective-permute-start(bf16[96,1664]{1,0:T(8,128)(2,1)S(1)} %get-tuple-element.41), channel_id=1, source_target_pairs={{0,3},{1,0},{2,1},{3,2},{4,7},{5,4},{6,5},{7,6},{8,11},{9,8},{10,9... | collective-permute-start | bytes 958472 | tf_op jit(solution)/shard_map/ppermute | solution.py:79
  12.3 8.7 %collective-permute-start = (bf16[96,1664]{1,0:T(8,128)(2,1)S(1)}, bf16[96,1664]{1,0:T(8,128)(2,1)S(1)}, u32[]{:S(2)}, u32[]{:S(2)}) collective-permute-start(bf16[96,1664]{1,0:T(8,128)(2,1)S(1)} %get-tuple-element.41), channel_id=1, source_target_pairs={{0,1},{1,2},{2,3},{3,0},{4,5},{5,6},{6,7},{7,4},{8,9},{9,10},{10,1... | collective-permute-start | bytes 958472 | tf_op jit(solution)/shard_map/ppermute | solution.py:79
  21.3 18.7 %collective-permute-start.7 = (bf16[4,48,1664]{2,1,0:T(8,128)(2,1)S(1)}, bf16[4,48,1664]{2,1,0:T(8,128)(2,1)S(1)}, u32[]{:S(2)}, u32[]{:S(2)}) collective-permute-start(bf16[4,48,1664]{2,1,0:T(8,128)(2,1)S(1)} %get-tuple-element.38), channel_id=1, source_target_pairs={{0,8},{1,9},{2,10},{3,11},{4,12},{5,13},{6,14},{7,15},{8,0},{9,1},... | collective-permute-start | bytes 1916936 | tf_op jit(solution)/shard_map/ppermute | solution.py:79
  24.4 28.6 %collective-permute-start.5 = (bf16[4,48,1664]{2,1,0:T(8,128)(2,1)S(1)}, bf16[4,48,1664]{2,1,0:T(8,128)(2,1)S(1)}, u32[]{:S(2)}, u32[]{:S(2)}) collective-permute-start(bf16[4,48,1664]{2,1,0:T(8,128)(2,1)S(1)} %get-tuple-element.38), channel_id=1, source_target_pairs={{0,12},{1,13},{2,14},{3,15},{4,0},{5,1},{6,2},{7,3},{8,4},{9,5},{1... | collective-permute-start | bytes 1916936 | tf_op jit(solution)/shard_map/ppermute | solution.py:79
  25.5 27.4 %collective-permute-start.3 = (bf16[4,48,1664]{2,1,0:T(8,128)(2,1)S(1)}, bf16[4,48,1664]{2,1,0:T(8,128)(2,1)S(1)}, u32[]{:S(2)}, u32[]{:S(2)}) collective-permute-start(bf16[4,48,1664]{2,1,0:T(8,128)(2,1)S(1)} %get-tuple-element.38), channel_id=1, source_target_pairs={{0,4},{1,5},{2,6},{3,7},{4,8},{5,9},{6,10},{7,11},{8,12},{9,13},{1... | collective-permute-start | bytes 1916936 | tf_op jit(solution)/shard_map/ppermute | solution.py:79
  26.4 20.7 %collective-permute-start.8 = (bf16[4,48,1664]{2,1,0:T(8,128)(2,1)S(1)}, bf16[4,48,1664]{2,1,0:T(8,128)(2,1)S(1)}, u32[]{:S(2)}, u32[]{:S(2)}) collective-permute-start(bf16[4,48,1664]{2,1,0:T(8,128)(2,1)S(1)} %get-tuple-element.39), channel_id=1, source_target_pairs={{0,8},{1,9},{2,10},{3,11},{4,12},{5,13},{6,14},{7,15},{8,0},{9,1},... | collective-permute-start | bytes 1916936 | tf_op jit(solution)/shard_map/ppermute | solution.py:79
  27.1 26.9 %collective-permute-start.6 = (bf16[4,48,1664]{2,1,0:T(8,128)(2,1)S(1)}, bf16[4,48,1664]{2,1,0:T(8,128)(2,1)S(1)}, u32[]{:S(2)}, u32[]{:S(2)}) collective-permute-start(bf16[4,48,1664]{2,1,0:T(8,128)(2,1)S(1)} %get-tuple-element.39), channel_id=1, source_target_pairs={{0,12},{1,13},{2,14},{3,15},{4,0},{5,1},{6,2},{7,3},{8,4},{9,5},{1... | collective-permute-start | bytes 1916936 | tf_op jit(solution)/shard_map/ppermute | solution.py:79
  29.9 7.3 %slice-start = ((s8[9437184]{0:T(1024)(128)(4,1)}), s8[4194304]{0:T(1024)(128)(4,1)S(1)}, s32[]{:S(2)}) async-start(s8[9437184]{0:T(1024)(128)(4,1)} %bitcast.41), calls=%async_computation | async-start | bytes 8388608
  30.0 7.2 %slice-start.1 = ((s8[9437184]{0:T(1024)(128)(4,1)}), s8[4194304]{0:T(1024)(128)(4,1)S(1)}, s32[]{:S(2)}) async-start(s8[9437184]{0:T(1024)(128)(4,1)} %bitcast.41), calls=%async_computation.1 | async-start | bytes 8388608
  30.0 7.2 %slice-start.2 = ((s8[9437184]{0:T(1024)(128)(4,1)}), s8[1048576]{0:T(1024)(128)(4,1)S(1)}, s32[]{:S(2)}) async-start(s8[9437184]{0:T(1024)(128)(4,1)} %bitcast.41), calls=%async_computation.2 | async-start | bytes 2097152
  40.0 14.0 %collective-permute-start.4 = (bf16[4,48,1664]{2,1,0:T(8,128)(2,1)S(1)}, bf16[4,48,1664]{2,1,0:T(8,128)(2,1)S(1)}, u32[]{:S(2)}, u32[]{:S(2)}) collective-permute-start(bf16[4,48,1664]{2,1,0:T(8,128)(2,1)S(1)} %get-tuple-element.39), channel_id=1, source_target_pairs={{0,4},{1,5},{2,6},{3,7},{4,8},{5,9},{6,10},{7,11},{8,12},{9,13},{1... | collective-permute-start | bytes 1916936 | tf_op jit(solution)/shard_map/ppermute | solution.py:79
  77.9 3.9 %collective-permute-start.9 = (f32[4,1536]{1,0:T(4,128)S(1)}, f32[4,1536]{1,0:T(4,128)S(1)}, u32[]{:S(2)}, u32[]{:S(2)}) collective-permute-start(f32[4,1536]{1,0:T(4,128)S(1)} %broadcast_select_fusion), channel_id=1, source_target_pairs={{0,1},{1,0},{2,3},{3,2},{4,5},{5,4},{6,7},{7,6},{8,9},{9,8},{10,11... | collective-permute-start | bytes 73736 | tf_op jit(solution)/shard_map/ppermute | solution.py:32
  82.0 5.1 %collective-permute-start.10 = (f32[4,1536]{1,0:T(4,128)S(1)}, f32[4,1536]{1,0:T(4,128)S(1)}, u32[]{:S(2)}, u32[]{:S(2)}) collective-permute-start(f32[4,1536]{1,0:T(4,128)S(1)} %pad_maximum_fusion.4), channel_id=1, source_target_pairs={{0,3},{1,2},{2,1},{3,0},{4,7},{5,6},{6,5},{7,4},{8,11},{9,10},{10,... | collective-permute-start | bytes 73736 | tf_op jit(solution)/shard_map/ppermute | solution.py:32
  87.3 3.9 %collective-permute-start.11 = (f32[4,1536]{1,0:T(4,128)S(1)}, f32[4,1536]{1,0:T(4,128)S(1)}, u32[]{:S(2)}, u32[]{:S(2)}) collective-permute-start(f32[4,1536]{1,0:T(4,128)S(1)} %pad_maximum_fusion.5), channel_id=1, source_target_pairs={{0,4},{1,5},{2,6},{3,7},{4,0},{5,1},{6,2},{7,3},{8,12},{9,13},{10,... | collective-permute-start | bytes 73736 | tf_op jit(solution)/shard_map/ppermute | solution.py:32
  91.3 5.1 %collective-permute-start.12 = (f32[4,1536]{1,0:T(4,128)S(1)}, f32[4,1536]{1,0:T(4,128)S(1)}, u32[]{:S(2)}, u32[]{:S(2)}) collective-permute-start(f32[4,1536]{1,0:T(4,128)S(1)} %pad_maximum_fusion.6), channel_id=1, source_target_pairs={{0,12},{1,13},{2,14},{3,15},{4,8},{5,9},{6,10},{7,11},{8,4},{9,5},... | collective-permute-start | bytes 73736 | tf_op jit(solution)/shard_map/ppermute | solution.py:32
  97.9 1.2 %collective-permute-start.13 = (f32[2]{0:T(128)S(1)}, f32[2]{0:T(128)S(1)}, u32[]{:S(2)}, u32[]{:S(2)}) collective-permute-start(f32[2]{0:T(128)S(1)} %pad_maximum_fusion.11), channel_id=1, source_target_pairs={{0,16},{16,0},{32,48},{48,32},{64,80},{80,64},{96,112},{112,96},{1... | collective-permute-start | bytes 32 | tf_op jit(solution)/shard_map/ppermute | solution.py:32
  98.2 12.0 %copy-start.1 = (f32[128]{0:T(128)}, f32[128]{0:T(128)S(1)}, u32[]{:S(2)}) copy-start(f32[128]{0:T(128)S(1)} %fusion.49) | copy-start | bytes 1540
  98.4 11.8 %copy-start.2 = (f32[128]{0:T(128)}, f32[128]{0:T(128)S(1)}, u32[]{:S(2)}) copy-start(f32[128]{0:T(128)S(1)} %fusion.48) | copy-start | bytes 1540
  98.5 11.7 %copy-start = (f32[128]{0:T(128)}, f32[128]{0:T(128)S(1)}, u32[]{:S(2)}) copy-start(f32[128]{0:T(128)S(1)} %select_dynamic-update-slice_fusion) | copy-start | bytes 1540
  99.8 3.6 %collective-permute-start.14 = (f32[2]{0:T(128)S(1)}, f32[2]{0:T(128)S(1)}, u32[]{:S(2)}, u32[]{:S(2)}) collective-permute-start(f32[2]{0:T(128)S(1)} %fusion.40), channel_id=1, source_target_pairs={{0,32},{16,48},{32,0},{48,16},{64,96},{80,112},{96,64},{112,80},{1... | collective-permute-start | bytes 32 | tf_op jit(solution)/shard_map/ppermute | solution.py:32
  103.4 4.8 %collective-permute-start.15 = (f32[2]{0:T(128)S(1)}, f32[2]{0:T(128)S(1)}, u32[]{:S(2)}, u32[]{:S(2)}) collective-permute-start(f32[2]{0:T(128)S(1)} %fusion.39), channel_id=1, source_target_pairs={{0,96},{16,112},{32,64},{48,80},{64,32},{80,48},{96,0},{112,16},{1... | collective-permute-start | bytes 32 | tf_op jit(solution)/shard_map/ppermute | solution.py:32

commit v21 on v20

--- a/solution.py
+++ b/solution.py
@@ -126,18 +126,17 @@
     left = shift(own, 0, 1, reqs, vocs)
     right = shift(own, 0, -1, reqs, vocs)
     far = shift(own, 0, 2, reqs, vocs)
-    part_near = stats(jnp.concatenate([own, left, right]))
     line = jnp.stack([own, left, right, far])
     halves = lambda step: jnp.concatenate(
         [shift(line[:, :HALF], 1, step, reqs, vocs), shift(line[:, HALF:], 1, step, reqs, vocs)], axis=1
     )
     line_left = halves(1)
     line_right = halves(-1)
-    part_far = stats(far)
+    part_near = stats(line.reshape(-1, own.shape[1]))
     line_far = halves(2)
     part_lines = stats(jnp.concatenate([line_left, line_right]).reshape(-1, own.shape[1]))
     part_line_far = stats(line_far.reshape(-1, own.shape[1]))
-    processed = jnp.concatenate([part_near, part_far, part_lines, part_line_far], axis=1)
+    processed = jnp.concatenate([part_near, part_lines, part_line_far], axis=1)
     processed = processed.reshape(4, vocs, LIVE)
     count_of = lambda block: block[..., :1, width + 2].reshape(-1).astype(jnp.int32)
     processed_counts = jnp.concatenate(

time: 112 us -> 116 us (1.036)
  waiting for transfers between devices: 24.3 us -> 30.5 us
  starting transfers between devices: 27.3 us -> 24 us
  other arithmetic: 19.4 us -> 21 us
  local copies, waits for them, and re-layouts: 7.3 us -> 8.52 us
    ppermute x7, starting transfers between devices: 12.6 us -> 9.32 us  [butterfly(): other = lax.ppermute(value, axis, [(i, i ^ flip) for i in range(size)])]
    ppermute x7, waiting for transfers between devices: 11.7 us -> 14.9 us  [butterfly(): other = lax.ppermute(value, axis, [(i, i ^ flip) for i in range(size)])]
    ppermute x9, waiting for transfers between devices: 12.6 us -> 15.6 us  [shift(): return lax.ppermute(value, AXES, pairs)]
    dot_general x4 -> x3, matrix products: 23.2 us -> 22.3 us  [block_stats(): logits = jnp.dot(rows_in, head, preferred_element_type=jnp.float32)]
    reduce_sum x4 -> x3, other arithmetic: 12.1 us -> 12.2 us  [block_stats(): total = jnp.sum(expo, axis=-1)]
  transfers between devices with their start and end apart: 16 -> 16, of which waited for: 11 -> 9; matrix products, arithmetic and copies ran while one was open for 17% -> 17% of each run, Pallas kernels for 0% -> 0%
where the time goes in v21:
time: 116 us
  waiting for transfers between devices  30.5 us (26%)
  matrix products  24.5 us (21%)
  starting transfers between devices  24 us (21%)
  other arithmetic  21 us (18%)
  local copies, waits for them, and re-layouts  8.52 us (7%)
  between operations  7.53 us (6%)
    dot_general x3, matrix products, block_stats(): logits = jnp.dot(rows_in, head, preferred_element_type=jnp.float32)  22.3 us
    ppermute x9, waiting for transfers between devices, shift(): return lax.ppermute(value, AXES, pairs)  15.6 us
    ppermute x7, waiting for transfers between devices, butterfly(): other = lax.ppermute(value, axis, [(i, i ^ flip) for i in range(size)])  14.9 us
    ppermute x9, starting transfers between devices, shift(): return lax.ppermute(value, AXES, pairs)  14.6 us
    reduce_sum x3, other arithmetic, block_stats(): total = jnp.sum(expo, axis=-1)  12.2 us
    ppermute x7, starting transfers between devices, butterfly(): other = lax.ppermute(value, axis, [(i, i ^ flip) for i in range(size)])  9.32 us
  transfers between devices with their start and end apart: 16, of which 9 were waited for; matrix products, arithmetic and copies ran while one was open for 17% of the time, Pallas kernels for 0%

profile of v21, /device:TPU:0, one launch (start us, length us, event | category | flops | bytes accessed | tf_op | source)
XLA Modules:
  0.0 116.0 jit_solution(4406432584088196328)
XLA Ops:
  0.7 1.2 fusion.10
  1.8 1.3 %fusion.50 = (s32[1,1]{1,0:T(1,128)}, s32[1,1]{1,0:T(1,128)}) fusion(s32[1,2]{1,0:T(1,128)} %param.10), kind=kLoop, calls=%fused_computation.185 | loop fusion | bytes 16 | tf_op jit(solution)/shard_map/slice | solution.py:106
  3.1 0.6 iota_add_fusion
  5.1 0.9 and_select_fusion.1
  6.0 1.3 %convolution_convert_fusion = bf16[96,1536]{1,0:T(8,128)(2,1)S(1)} fusion(bf16[128,1536]{1,0:T(8,128)(2,1)} %param.6, f32[1536]{0:T(1024)} %param.7, f32[128]{0:T(128)S(1)} %add_rsqrt_fusion, s32[96]{0:T(128)S(1)} %iota_add_fusion), kind=kOutput, calls=%fused_computation.22 | convolution fusion | flops 38694912 | bytes 695168 | tf_op jit(solution)/shard_map/dot_general | solution.py:115
  7.3 0.1 select_convert_fusion
  7.5 4.2 %collective-permute-start.1 = (bf16[96,1664]{1,0:T(8,128)(2,1)S(1)}, bf16[96,1664]{1,0:T(8,128)(2,1)S(1)}, u32[]{:S(2)}, u32[]{:S(2)}) collective-permute-start(bf16[96,1664]{1,0:T(8,128)(2,1)S(1)} %get-tuple-element.38), channel_id=1, source_target_pairs={{0,3},{1,0},{2,1},{3,2},{4,7},{5,4},{6,5},{7,6},{8,11},{9,8},{10,9... | collective-permute-start | bytes 958472 | tf_op jit(solution)/shard_map/ppermute | solution.py:79
  11.7 1.9 %collective-permute-start.2 = (bf16[96,1664]{1,0:T(8,128)(2,1)S(1)}, bf16[96,1664]{1,0:T(8,128)(2,1)S(1)}, u32[]{:S(2)}, u32[]{:S(2)}) collective-permute-start(bf16[96,1664]{1,0:T(8,128)(2,1)S(1)} %get-tuple-element.38), channel_id=1, source_target_pairs={{0,2},{1,3},{2,0},{3,1},{4,6},{5,7},{6,4},{7,5},{8,10},{9,11},{10,... | collective-permute-start | bytes 958472 | tf_op jit(solution)/shard_map/ppermute | solution.py:79
  13.6 1.3 %gather_fusion = s32[16]{0:T(128)S(1)} fusion(s32[4]{0:T(128)} %constant.168.clone, s32[1024]{0:T(1024)S(1)} %pad_clamp_fusion.2), kind=kCustom, calls=%fused_computation | custom fusion | bytes 192 | tf_op jit(solution)/shard_map/gather | solution.py:152
  14.9 1.3 %gather_fusion.1 = s32[16]{0:T(128)S(1)} fusion(s32[4]{0:T(128)} %constant.168.clone, s32[1024]{0:T(1024)S(1)} %pad_clamp_fusion.1), kind=kCustom, calls=%fused_computation.1 | custom fusion | bytes 192 | tf_op jit(solution)/shard_map/gather | solution.py:152
  16.3 7.0 %collective-permute-done = bf16[96,1664]{1,0:T(8,128)(2,1)S(1)} collective-permute-done((bf16[96,1664]{1,0:T(8,128)(2,1)S(1)}, bf16[96,1664]{1,0:T(8,128)(2,1)S(1)}, u32[]{:S(2)}, u32[]{:S(2)}) %collective-permute-start) | collective-permute-done | bytes 319520 | tf_op jit(solution)/shard_map/ppermute | solution.py:79
  23.3 0.2 pad_maximum_fusion
  23.5 1.1 fusion.48
  24.7 3.0 %collective-permute-start.7 = (bf16[4,48,1664]{2,1,0:T(8,128)(2,1)}, bf16[4,48,1664]{2,1,0:T(8,128)(2,1)S(1)}, u32[]{:S(2)}, u32[]{:S(2)}) collective-permute-start(bf16[4,48,1664]{2,1,0:T(8,128)(2,1)} %get-tuple-element.35), channel_id=1, source_target_pairs={{0,8},{1,9},{2,10},{3,11},{4,12},{5,13},{6,14},{7,15},{8,0},{9,1},... | collective-permute-start | bytes 1916936 | tf_op jit(solution)/shard_map/ppermute | solution.py:79
  27.7 1.1 collective-permute-start.5
  28.8 0.9 collective-permute-start.3
  29.7 0.6 collective-permute-start.8
  30.3 2.6 %collective-permute-start.6 = (bf16[4,48,1664]{2,1,0:T(8,128)(2,1)}, bf16[4,48,1664]{2,1,0:T(8,128)(2,1)}, u32[]{:S(2)}, u32[]{:S(2)}) collective-permute-start(bf16[4,48,1664]{2,1,0:T(8,128)(2,1)} %get-tuple-element.36), channel_id=1, source_target_pairs={{0,12},{1,13},{2,14},{3,15},{4,0},{5,1},{6,2},{7,3},{8,4},{9,5},{1... | collective-permute-start | bytes 1916936 | tf_op jit(solution)/shard_map/ppermute | solution.py:79
  33.0 0.1 copy.18
  33.1 6.7 %fusion.53 = (f32[384]{0:T(512)S(1)}, f32[384,3072]{1,0:T(8,128)S(1)}) fusion(bf16[1536,3072]{1,0:T(8,128)(2,1)} %param.8, bf16[384,1664]{1,0:T(8,128)(2,1)S(1)} %bitcast.38), kind=kOutput, calls=%fused_computation.188 | convolution fusion | flops 3625057792 | bytes 15336960 | tf_op jit(solution)/shard_map/dot_general | solution.py:89
  39.8 1.9 %fusion.2 = (f32[384]{0:T(512)S(1)}, f32[384]{0:T(512)S(1)}, f32[384]{0:T(512)S(1)}) fusion(f32[384,3072]{1,0:T(8,128)S(1)} %get-tuple-element.66, f32[384]{0:T(512)S(1)} %get-tuple-element.65, s32[384]{0:T(512)S(1)} %fusion.29), kind=kLoop, calls=%fused_computation.18 | loop fusion | flops 8256384 | bytes 4726272 | tf_op jit(solution)/shard_map/reduce_sum | solution.py:92
  41.7 0.2 slice_reduce_fusion.9
  41.9 0.2 collective-permute-start.4
  42.2 8.6 %collective-permute-done.8 = bf16[4,48,1664]{2,1,0:T(8,128)(2,1)} collective-permute-done((bf16[4,48,1664]{2,1,0:T(8,128)(2,1)}, bf16[4,48,1664]{2,1,0:T(8,128)(2,1)}, u32[]{:S(2)}, u32[]{:S(2)}) %collective-permute-start.8) | collective-permute-done | bytes 639008 | tf_op jit(solution)/shard_map/ppermute | solution.py:79
  50.7 1.2 %pad_maximum_fusion.1 = bf16[4,96,1664]{2,1,0:T(8,128)(2,1)S(1)} fusion(bf16[4,48,1664]{2,1,0:T(8,128)(2,1)} %collective-permute-done.8, bf16[4,48,1664]{2,1,0:T(8,128)(2,1)S(1)} %collective-permute-done.7), kind=kLoop, calls=%fused_computation.24 | loop fusion | flops 2555904 | bytes 2555904 | tf_op jit(solution)/shard_map/concatenate | solution.py:130
  52.0 5.7 %fusion.51 = (f32[384]{0:T(512)S(1)}, f32[384,3072]{1,0:T(8,128)}) fusion(bf16[1536,3072]{1,0:T(8,128)(2,1)S(1)} %bitcast.48, bf16[384,1664]{1,0:T(8,128)(2,1)S(1)} %bitcast.42), kind=kOutput, calls=%fused_computation.186 | convolution fusion | flops 3625057792 | bytes 15336960 | tf_op jit(solution)/shard_map/dot_general | solution.py:89
  57.7 1.3 %maximum_maximum_fusion = bf16[8,96,1664]{2,1,0:T(8,128)(2,1)S(1)} fusion(bf16[4,48,1664]{2,1,0:T(8,128)(2,1)} %collective-permute-done.6, bf16[4,48,1664]{2,1,0:T(8,128)(2,1)S(1)} %collective-permute-done.5, bf16[4,48,1664]{2,1,0:T(8,128)(2,1)S(1)} %collective-permute-done.4, bf16[4,48,1664]{2,1,0:T(8,128)(2,1)S(1)} %collective-permute-done.3), kind=kLoop, calls=%fused_computation.19 | loop fusion | flops 10223616 | bytes 5111808 | tf_op jit(solution)/shard_map/concatenate | solution.py:137
  59.0 9.9 %fusion.52 = (f32[768]{0:T(1024)S(1)}, f32[768,3072]{1,0:T(8,128)}) fusion(bf16[1536,3072]{1,0:T(8,128)(2,1)S(1)} %bitcast.48, bf16[768,1664]{1,0:T(8,128)(2,1)S(1)} %bitcast.40), kind=kOutput, calls=%fused_computation.187 | convolution fusion | flops 7250115584 | bytes 21236736 | tf_op jit(solution)/shard_map/dot_general | solution.py:89
  68.9 0.2 slice_reduce_fusion.6
  69.1 0.2 slice_reduce_fusion.7
  69.3 0.2 slice_reduce_fusion.8
  69.5 0.1 maximum_convert_fusion
  69.6 0.7 gather_fusion.3
  70.2 0.6 fusion.46
  70.9 0.1 broadcast_in_dim.71
  70.9 0.1 broadcast_in_dim.72
  71.0 0.1 copy.20
  71.2 0.1 copy.19
  71.4 4.0 %fusion.1 = (f32[384]{0:T(512)S(1)}, f32[384]{0:T(512)S(1)}, f32[384]{0:T(512)S(1)}) fusion(f32[384,3072]{1,0:T(8,128)} %get-tuple-element.62, f32[384]{0:T(512)S(1)} %get-tuple-element.61, s32[384]{0:T(512)S(1)} %fusion.30), kind=kLoop, calls=%fused_computation.13 | loop fusion | flops 8256384 | bytes 4726272 | tf_op jit(solution)/shard_map/reduce_sum | solution.py:92
  75.4 6.3 %fusion = (f32[768]{0:T(1024)S(1)}, f32[768]{0:T(1024)S(1)}, f32[768]{0:T(1024)S(1)}) fusion(f32[768,3072]{1,0:T(8,128)} %get-tuple-element.64, f32[768]{0:T(1024)S(1)} %get-tuple-element.63, s32[768]{0:T(1024)S(1)} %fusion.26), kind=kLoop, calls=%fused_computation.8 | loop fusion | flops 16512768 | bytes 9452544 | tf_op jit(solution)/shard_map/reduce_sum | solution.py:92
  81.8 0.1 reshape.294
  81.9 0.6 gather_fusion.2
  82.5 0.1 gather.19
  82.6 0.1 collective-permute-start.9
  82.7 3.8 %collective-permute-done.9 = f32[4,1536]{1,0:T(4,128)S(1)} collective-permute-done((f32[4,1536]{1,0:T(4,128)S(1)}, f32[4,1536]{1,0:T(4,128)S(1)}, u32[]{:S(2)}, u32[]{:S(2)}) %collective-permute-start.9) | collective-permute-done | bytes 24608 | tf_op jit(solution)/shard_map/ppermute | solution.py:32
  86.6 0.2 collective-permute-start.10
  86.8 4.9 %collective-permute-done.10 = f32[4,1536]{1,0:T(4,128)S(1)} collective-permute-done((f32[4,1536]{1,0:T(4,128)S(1)}, f32[4,1536]{1,0:T(4,128)S(1)}, u32[]{:S(2)}, u32[]{:S(2)}) %collective-permute-start.10) | collective-permute-done | bytes 24608 | tf_op jit(solution)/shard_map/ppermute | solution.py:32
  91.9 1.6 %collective-permute-start.11 = (f32[4,1536]{1,0:T(4,128)S(1)}, f32[4,1536]{1,0:T(4,128)S(1)}, u32[]{:S(2)}, u32[]{:S(2)}) collective-permute-start(f32[4,1536]{1,0:T(4,128)S(1)} %pad_maximum_fusion.4), channel_id=1, source_target_pairs={{0,4},{1,5},{2,6},{3,7},{4,0},{5,1},{6,2},{7,3},{8,12},{9,13},{10,... | collective-permute-start | bytes 73736 | tf_op jit(solution)/shard_map/ppermute | solution.py:32
  95.4 0.4 collective-permute-done.11
  96.0 2.8 %collective-permute-start.12 = (f32[4,1536]{1,0:T(4,128)S(1)}, f32[4,1536]{1,0:T(4,128)S(1)}, u32[]{:S(2)}, u32[]{:S(2)}) collective-permute-start(f32[4,1536]{1,0:T(4,128)S(1)} %pad_maximum_fusion.5), channel_id=1, source_target_pairs={{0,12},{1,13},{2,14},{3,15},{4,8},{5,9},{6,10},{7,11},{8,4},{9,5},... | collective-permute-start | bytes 73736 | tf_op jit(solution)/shard_map/ppermute | solution.py:32
  99.5 0.1 lt.137
  99.6 1.5 %collective-permute-done.12 = f32[4,1536]{1,0:T(4,128)S(1)} collective-permute-done((f32[4,1536]{1,0:T(4,128)S(1)}, f32[4,1536]{1,0:T(4,128)S(1)}, u32[]{:S(2)}, u32[]{:S(2)}) %collective-permute-start.12) | collective-permute-done | bytes 24608 | tf_op jit(solution)/shard_map/ppermute | solution.py:32
  101.1 0.8 select_reduce_fusion.3
  101.9 0.7 pad_maximum_fusion.6
  102.6 0.2 fusion.44
  102.8 0.2 fusion.43
  103.0 0.2 select_dynamic-update-slice_fusion
  103.2 0.6 collective-permute-done.13
  103.8 0.7 fusion.35
  104.5 1.6 %collective-permute-start.14 = (f32[2]{0:T(128)S(1)}, f32[2]{0:T(128)S(1)}, u32[]{:S(2)}, u32[]{:S(2)}) collective-permute-start(f32[2]{0:T(128)S(1)} %fusion.35), channel_id=1, source_target_pairs={{0,32},{16,48},{32,0},{48,16},{64,96},{80,112},{96,64},{112,80},{1... | collective-permute-start | bytes 32 | tf_op jit(solution)/shard_map/ppermute | solution.py:32
  106.1 2.0 %collective-permute-done.14 = f32[2]{0:T(128)S(1)} collective-permute-done((f32[2]{0:T(128)S(1)}, f32[2]{0:T(128)S(1)}, u32[]{:S(2)}, u32[]{:S(2)}) %collective-permute-start.14) | collective-permute-done | bytes 40 | tf_op jit(solution)/shard_map/ppermute | solution.py:32
  108.1 3.0 %collective-permute-start.15 = (f32[2]{0:T(128)S(1)}, f32[2]{0:T(128)S(1)}, u32[]{:S(2)}, u32[]{:S(2)}) collective-permute-start(f32[2]{0:T(128)S(1)} %fusion.34), channel_id=1, source_target_pairs={{0,96},{16,112},{32,64},{48,80},{64,32},{80,48},{96,0},{112,16},{1... | collective-permute-start | bytes 32 | tf_op jit(solution)/shard_map/ppermute | solution.py:32
  111.1 1.8 %collective-permute-done.15 = f32[2]{0:T(128)S(1)} collective-permute-done((f32[2]{0:T(128)S(1)}, f32[2]{0:T(128)S(1)}, u32[]{:S(2)}, u32[]{:S(2)}) %collective-permute-start.15) | collective-permute-done | bytes 40 | tf_op jit(solution)/shard_map/ppermute | solution.py:32
  112.9 0.6 fusion.49
  (76 shorter events, 1.0 us)
Async XLA Ops:
  7.5 8.8 %collective-permute-start.1 = (bf16[96,1664]{1,0:T(8,128)(2,1)S(1)}, bf16[96,1664]{1,0:T(8,128)(2,1)S(1)}, u32[]{:S(2)}, u32[]{:S(2)}) collective-permute-start(bf16[96,1664]{1,0:T(8,128)(2,1)S(1)} %get-tuple-element.38), channel_id=1, source_target_pairs={{0,3},{1,0},{2,1},{3,2},{4,7},{5,4},{6,5},{7,6},{8,11},{9,8},{10,9... | collective-permute-start | bytes 958472 | tf_op jit(solution)/shard_map/ppermute | solution.py:79
  11.7 11.6 %collective-permute-start = (bf16[96,1664]{1,0:T(8,128)(2,1)S(1)}, bf16[96,1664]{1,0:T(8,128)(2,1)S(1)}, u32[]{:S(2)}, u32[]{:S(2)}) collective-permute-start(bf16[96,1664]{1,0:T(8,128)(2,1)S(1)} %get-tuple-element.38), channel_id=1, source_target_pairs={{0,1},{1,2},{2,3},{3,0},{4,5},{5,6},{6,7},{7,4},{8,9},{9,10},{10,1... | collective-permute-start | bytes 958472 | tf_op jit(solution)/shard_map/ppermute | solution.py:79
  11.7 11.6 %collective-permute-start.2 = (bf16[96,1664]{1,0:T(8,128)(2,1)S(1)}, bf16[96,1664]{1,0:T(8,128)(2,1)S(1)}, u32[]{:S(2)}, u32[]{:S(2)}) collective-permute-start(bf16[96,1664]{1,0:T(8,128)(2,1)S(1)} %get-tuple-element.38), channel_id=1, source_target_pairs={{0,2},{1,3},{2,0},{3,1},{4,6},{5,7},{6,4},{7,5},{8,10},{9,11},{10,... | collective-permute-start | bytes 958472 | tf_op jit(solution)/shard_map/ppermute | solution.py:79
  24.7 17.3 %collective-permute-start.7 = (bf16[4,48,1664]{2,1,0:T(8,128)(2,1)}, bf16[4,48,1664]{2,1,0:T(8,128)(2,1)S(1)}, u32[]{:S(2)}, u32[]{:S(2)}) collective-permute-start(bf16[4,48,1664]{2,1,0:T(8,128)(2,1)} %get-tuple-element.35), channel_id=1, source_target_pairs={{0,8},{1,9},{2,10},{3,11},{4,12},{5,13},{6,14},{7,15},{8,0},{9,1},... | collective-permute-start | bytes 1916936 | tf_op jit(solution)/shard_map/ppermute | solution.py:79
  27.7 30.0 %collective-permute-start.5 = (bf16[4,48,1664]{2,1,0:T(8,128)(2,1)}, bf16[4,48,1664]{2,1,0:T(8,128)(2,1)S(1)}, u32[]{:S(2)}, u32[]{:S(2)}) collective-permute-start(bf16[4,48,1664]{2,1,0:T(8,128)(2,1)} %get-tuple-element.35), channel_id=1, source_target_pairs={{0,12},{1,13},{2,14},{3,15},{4,0},{5,1},{6,2},{7,3},{8,4},{9,5},{1... | collective-permute-start | bytes 1916936 | tf_op jit(solution)/shard_map/ppermute | solution.py:79
  28.8 28.8 %collective-permute-start.3 = (bf16[4,48,1664]{2,1,0:T(8,128)(2,1)}, bf16[4,48,1664]{2,1,0:T(8,128)(2,1)S(1)}, u32[]{:S(2)}, u32[]{:S(2)}) collective-permute-start(bf16[4,48,1664]{2,1,0:T(8,128)(2,1)} %get-tuple-element.35), channel_id=1, source_target_pairs={{0,4},{1,5},{2,6},{3,7},{4,8},{5,9},{6,10},{7,11},{8,12},{9,13},{1... | collective-permute-start | bytes 1916936 | tf_op jit(solution)/shard_map/ppermute | solution.py:79
  29.7 21.0 %collective-permute-start.8 = (bf16[4,48,1664]{2,1,0:T(8,128)(2,1)}, bf16[4,48,1664]{2,1,0:T(8,128)(2,1)}, u32[]{:S(2)}, u32[]{:S(2)}) collective-permute-start(bf16[4,48,1664]{2,1,0:T(8,128)(2,1)} %get-tuple-element.36), channel_id=1, source_target_pairs={{0,8},{1,9},{2,10},{3,11},{4,12},{5,13},{6,14},{7,15},{8,0},{9,1},... | collective-permute-start | bytes 1916936 | tf_op jit(solution)/shard_map/ppermute | solution.py:79
  30.3 27.3 %collective-permute-start.6 = (bf16[4,48,1664]{2,1,0:T(8,128)(2,1)}, bf16[4,48,1664]{2,1,0:T(8,128)(2,1)}, u32[]{:S(2)}, u32[]{:S(2)}) collective-permute-start(bf16[4,48,1664]{2,1,0:T(8,128)(2,1)} %get-tuple-element.36), channel_id=1, source_target_pairs={{0,12},{1,13},{2,14},{3,15},{4,0},{5,1},{6,2},{7,3},{8,4},{9,5},{1... | collective-permute-start | bytes 1916936 | tf_op jit(solution)/shard_map/ppermute | solution.py:79
  33.1 18.9 %slice-start = ((s8[9437184]{0:T(1024)(128)(4,1)}), s8[4194304]{0:T(1024)(128)(4,1)S(1)}, s32[]{:S(2)}) async-start(s8[9437184]{0:T(1024)(128)(4,1)} %bitcast.47), calls=%async_computation | async-start | bytes 8388608
  33.1 18.8 %slice-start.1 = ((s8[9437184]{0:T(1024)(128)(4,1)}), s8[4194304]{0:T(1024)(128)(4,1)S(1)}, s32[]{:S(2)}) async-start(s8[9437184]{0:T(1024)(128)(4,1)} %bitcast.47), calls=%async_computation.1 | async-start | bytes 8388608
  33.1 18.8 %slice-start.2 = ((s8[9437184]{0:T(1024)(128)(4,1)}), s8[1048576]{0:T(1024)(128)(4,1)S(1)}, s32[]{:S(2)}) async-start(s8[9437184]{0:T(1024)(128)(4,1)} %bitcast.47), calls=%async_computation.2 | async-start | bytes 2097152
  41.9 15.8 %collective-permute-start.4 = (bf16[4,48,1664]{2,1,0:T(8,128)(2,1)}, bf16[4,48,1664]{2,1,0:T(8,128)(2,1)S(1)}, u32[]{:S(2)}, u32[]{:S(2)}) collective-permute-start(bf16[4,48,1664]{2,1,0:T(8,128)(2,1)} %get-tuple-element.36), channel_id=1, source_target_pairs={{0,4},{1,5},{2,6},{3,7},{4,8},{5,9},{6,10},{7,11},{8,12},{9,13},{1... | collective-permute-start | bytes 1916936 | tf_op jit(solution)/shard_map/ppermute | solution.py:79
  82.6 3.9 %collective-permute-start.9 = (f32[4,1536]{1,0:T(4,128)S(1)}, f32[4,1536]{1,0:T(4,128)S(1)}, u32[]{:S(2)}, u32[]{:S(2)}) collective-permute-start(f32[4,1536]{1,0:T(4,128)S(1)} %broadcast_select_fusion), channel_id=1, source_target_pairs={{0,1},{1,0},{2,3},{3,2},{4,5},{5,4},{6,7},{7,6},{8,9},{9,8},{10,11... | collective-permute-start | bytes 73736 | tf_op jit(solution)/shard_map/ppermute | solution.py:32
  86.6 5.1 %collective-permute-start.10 = (f32[4,1536]{1,0:T(4,128)S(1)}, f32[4,1536]{1,0:T(4,128)S(1)}, u32[]{:S(2)}, u32[]{:S(2)}) collective-permute-start(f32[4,1536]{1,0:T(4,128)S(1)} %pad_maximum_fusion.3), channel_id=1, source_target_pairs={{0,3},{1,2},{2,1},{3,0},{4,7},{5,6},{6,5},{7,4},{8,11},{9,10},{10,... | collective-permute-start | bytes 73736 | tf_op jit(solution)/shard_map/ppermute | solution.py:32
  91.9 3.9 %collective-permute-start.11 = (f32[4,1536]{1,0:T(4,128)S(1)}, f32[4,1536]{1,0:T(4,128)S(1)}, u32[]{:S(2)}, u32[]{:S(2)}) collective-permute-start(f32[4,1536]{1,0:T(4,128)S(1)} %pad_maximum_fusion.4), channel_id=1, source_target_pairs={{0,4},{1,5},{2,6},{3,7},{4,0},{5,1},{6,2},{7,3},{8,12},{9,13},{10,... | collective-permute-start | bytes 73736 | tf_op jit(solution)/shard_map/ppermute | solution.py:32
  96.0 5.1 %collective-permute-start.12 = (f32[4,1536]{1,0:T(4,128)S(1)}, f32[4,1536]{1,0:T(4,128)S(1)}, u32[]{:S(2)}, u32[]{:S(2)}) collective-permute-start(f32[4,1536]{1,0:T(4,128)S(1)} %pad_maximum_fusion.5), channel_id=1, source_target_pairs={{0,12},{1,13},{2,14},{3,15},{4,8},{5,9},{6,10},{7,11},{8,4},{9,5},... | collective-permute-start | bytes 73736 | tf_op jit(solution)/shard_map/ppermute | solution.py:32
  102.6 1.2 %collective-permute-start.13 = (f32[2]{0:T(128)S(1)}, f32[2]{0:T(128)S(1)}, u32[]{:S(2)}, u32[]{:S(2)}) collective-permute-start(f32[2]{0:T(128)S(1)} %pad_maximum_fusion.6), channel_id=1, source_target_pairs={{0,16},{16,0},{32,48},{48,32},{64,80},{80,64},{96,112},{112,96},{1... | collective-permute-start | bytes 32 | tf_op jit(solution)/shard_map/ppermute | solution.py:32
  102.8 12.0 %copy-start.1 = (f32[128]{0:T(128)}, f32[128]{0:T(128)S(1)}, u32[]{:S(2)}) copy-start(f32[128]{0:T(128)S(1)} %fusion.44) | copy-start | bytes 1540
  103.0 11.8 %copy-start.2 = (f32[128]{0:T(128)}, f32[128]{0:T(128)S(1)}, u32[]{:S(2)}) copy-start(f32[128]{0:T(128)S(1)} %fusion.43) | copy-start | bytes 1540
  103.2 11.7 %copy-start = (f32[128]{0:T(128)}, f32[128]{0:T(128)S(1)}, u32[]{:S(2)}) copy-start(f32[128]{0:T(128)S(1)} %select_dynamic-update-slice_fusion) | copy-start | bytes 1540
  104.5 3.6 %collective-permute-start.14 = (f32[2]{0:T(128)S(1)}, f32[2]{0:T(128)S(1)}, u32[]{:S(2)}, u32[]{:S(2)}) collective-permute-start(f32[2]{0:T(128)S(1)} %fusion.35), channel_id=1, source_target_pairs={{0,32},{16,48},{32,0},{48,16},{64,96},{80,112},{96,64},{112,80},{1... | collective-permute-start | bytes 32 | tf_op jit(solution)/shard_map/ppermute | solution.py:32
  108.1 4.8 %collective-permute-start.15 = (f32[2]{0:T(128)S(1)}, f32[2]{0:T(128)S(1)}, u32[]{:S(2)}, u32[]{:S(2)}) collective-permute-start(f32[2]{0:T(128)S(1)} %fusion.34), channel_id=1, source_target_pairs={{0,96},{16,112},{32,64},{48,80},{64,32},{80,48},{96,0},{112,16},{1... | collective-permute-start | bytes 32 | tf_op jit(solution)/shard_map/ppermute | solution.py:32

commit v22 on v20

--- a/solution.py
+++ b/solution.py
@@ -168,7 +168,7 @@
     mine = lambda a: lax.dynamic_slice_in_dim(a, position * LIVE, LIVE, 0)
     live = slot < live_count
     zero = jnp.zeros((LIVE,), jnp.float32)
-    place = lambda a: lax.dynamic_update_slice_in_dim(jnp.zeros((slots,), jnp.float32), a, start, 0)
+    place = lambda a: jnp.dot(a, pick.astype(jnp.float32), precision=lax.Precision.HIGHEST)
     entropy = place(jnp.where(live, mine(row_entropy), zero))
     logprob = place(jnp.where(live, mine(row_logprob), zero))
     target_logit = place(jnp.where(live, mine(picked), zero))

time: 112 us -> 113 us (level)
  matrix products: 25.4 us -> 27.6 us
  between operations: 7.56 us -> 5.56 us
  waiting for transfers between devices: 24.3 us -> 25.7 us
    dot_general x0 -> x3, matrix products: none -> 2.19 us  [shards(): jnp.dot(a, pick.astype(jnp.float32), precision=lax.Precision.HIGHEST)]
    ppermute x7, waiting for transfers between devices: 11.7 us -> 13 us  [butterfly(): other = lax.ppermute(value, axis, [(i, i ^ flip) for i in range(size)])]
  transfers between devices with their start and end apart: 16 -> 16, of which waited for: 11 -> 10; matrix products, arithmetic and copies ran while one was open for 17% -> 19% of each run, Pallas kernels for 0% -> 0%
where the time goes in v22:
time: 113 us; the launch traced here: 112 us
  matrix products  27.6 us (24%)
  starting transfers between devices  27.3 us (24%)
  waiting for transfers between devices  25.7 us (23%)
  other arithmetic  18.9 us (17%)
  local copies, waits for them, and re-layouts  7.28 us (6%)
  between operations  5.56 us (5%)
    dot_general x4, matrix products, block_stats(): logits = jnp.dot(rows_in, head, preferred_element_type=jnp.float32)  23.2 us
    ppermute x9, starting transfers between devices, shift(): return lax.ppermute(value, AXES, pairs)  14.7 us
    ppermute x7, waiting for transfers between devices, butterfly(): other = lax.ppermute(value, axis, [(i, i ^ flip) for i in range(size)])  13 us
    ppermute x9, waiting for transfers between devices, shift(): return lax.ppermute(value, AXES, pairs)  12.7 us
    ppermute x7, starting transfers between devices, butterfly(): other = lax.ppermute(value, axis, [(i, i ^ flip) for i in range(size)])  12.6 us
    reduce_sum x4, other arithmetic, block_stats(): total = jnp.sum(expo, axis=-1)  12.1 us
  transfers between devices with their start and end apart: 16, of which 10 were waited for; matrix products, arithmetic and copies ran while one was open for 19% of the time, Pallas kernels for 0%

profile of v22, /device:TPU:0, one launch (start us, length us, event | category | flops | bytes accessed | tf_op | source)
XLA Modules:
  0.0 112.4 jit_solution(2573403167287758192)
XLA Ops:
  0.7 1.2 %fusion.11 = f32[128]{0:T(128)S(1)} fusion(bf16[128,1536]{1,0:T(8,128)(2,1)} %param.6), kind=kLoop, calls=%fused_computation.42 | loop fusion | flops 589696 | bytes 393728 | tf_op jit(solution)/shard_map/reduce_sum | solution.py:109
  1.8 1.3 %fusion.74 = (s32[1,1]{1,0:T(1,128)}, s32[1,1]{1,0:T(1,128)}) fusion(s32[1,2]{1,0:T(1,128)} %param.10), kind=kLoop, calls=%fused_computation.222 | loop fusion | bytes 16 | tf_op jit(solution)/shard_map/slice | solution.py:106
  3.1 0.6 iota_add_fusion
  5.1 0.9 and_select_fusion.1
  6.0 1.3 %convolution_convert_fusion = bf16[96,1536]{1,0:T(8,128)(2,1)S(1)} fusion(bf16[128,1536]{1,0:T(8,128)(2,1)} %param.6, f32[1536]{0:T(1024)} %param.7, f32[128]{0:T(128)S(1)} %add_rsqrt_fusion, s32[96]{0:T(128)S(1)} %iota_add_fusion), kind=kOutput, calls=%fused_computation.22 | convolution fusion | flops 38694912 | bytes 695168 | tf_op jit(solution)/shard_map/dot_general | solution.py:115
  7.3 0.1 select_convert_fusion
  7.5 4.1 %collective-permute-start.2 = (bf16[96,1664]{1,0:T(8,128)(2,1)S(1)}, bf16[96,1664]{1,0:T(8,128)(2,1)S(1)}, u32[]{:S(2)}, u32[]{:S(2)}) collective-permute-start(bf16[96,1664]{1,0:T(8,128)(2,1)S(1)} %get-tuple-element.41), channel_id=1, source_target_pairs={{0,2},{1,3},{2,0},{3,1},{4,6},{5,7},{6,4},{7,5},{8,10},{9,11},{10,... | collective-permute-start | bytes 958472 | tf_op jit(solution)/shard_map/ppermute | solution.py:79
  11.5 0.7 collective-permute-start.1
  12.3 1.3 %collective-permute-start = (bf16[96,1664]{1,0:T(8,128)(2,1)S(1)}, bf16[96,1664]{1,0:T(8,128)(2,1)S(1)}, u32[]{:S(2)}, u32[]{:S(2)}) collective-permute-start(bf16[96,1664]{1,0:T(8,128)(2,1)S(1)} %get-tuple-element.41), channel_id=1, source_target_pairs={{0,1},{1,2},{2,3},{3,0},{4,5},{5,6},{6,7},{7,4},{8,9},{9,10},{10,1... | collective-permute-start | bytes 958472 | tf_op jit(solution)/shard_map/ppermute | solution.py:79
  13.6 1.3 %gather_fusion = s32[16]{0:T(128)S(1)} fusion(s32[4]{0:T(128)} %constant.167.clone, s32[1024]{0:T(1024)S(1)} %pad_clamp_fusion.2), kind=kCustom, calls=%fused_computation | custom fusion | bytes 192 | tf_op jit(solution)/shard_map/gather | solution.py:153
  14.9 1.3 %gather_fusion.1 = s32[16]{0:T(128)S(1)} fusion(s32[4]{0:T(128)} %constant.167.clone, s32[1024]{0:T(1024)S(1)} %pad_clamp_fusion.1), kind=kCustom, calls=%fused_computation.1 | custom fusion | bytes 192 | tf_op jit(solution)/shard_map/gather | solution.py:153
  16.3 0.2 collective-permute-done.2
  16.5 4.5 %collective-permute-done.1 = bf16[96,1664]{1,0:T(8,128)(2,1)S(1)} collective-permute-done((bf16[96,1664]{1,0:T(8,128)(2,1)S(1)}, bf16[96,1664]{1,0:T(8,128)(2,1)S(1)}, u32[]{:S(2)}, u32[]{:S(2)}) %collective-permute-start.1) | collective-permute-done | bytes 319520 | tf_op jit(solution)/shard_map/ppermute | solution.py:79
  21.0 0.2 pad_maximum_fusion
  21.2 0.1 fusion.72
  21.3 3.1 %collective-permute-start.7 = (bf16[4,48,1664]{2,1,0:T(8,128)(2,1)S(1)}, bf16[4,48,1664]{2,1,0:T(8,128)(2,1)S(1)}, u32[]{:S(2)}, u32[]{:S(2)}) collective-permute-start(bf16[4,48,1664]{2,1,0:T(8,128)(2,1)S(1)} %get-tuple-element.38), channel_id=1, source_target_pairs={{0,8},{1,9},{2,10},{3,11},{4,12},{5,13},{6,14},{7,15},{8,0},{9,1},... | collective-permute-start | bytes 1916936 | tf_op jit(solution)/shard_map/ppermute | solution.py:79
  24.4 1.1 %collective-permute-start.5 = (bf16[4,48,1664]{2,1,0:T(8,128)(2,1)S(1)}, bf16[4,48,1664]{2,1,0:T(8,128)(2,1)S(1)}, u32[]{:S(2)}, u32[]{:S(2)}) collective-permute-start(bf16[4,48,1664]{2,1,0:T(8,128)(2,1)S(1)} %get-tuple-element.38), channel_id=1, source_target_pairs={{0,12},{1,13},{2,14},{3,15},{4,0},{5,1},{6,2},{7,3},{8,4},{9,5},{1... | collective-permute-start | bytes 1916936 | tf_op jit(solution)/shard_map/ppermute | solution.py:79
  25.5 0.9 collective-permute-start.3
  26.4 0.6 collective-permute-start.8
  27.1 2.6 %collective-permute-start.6 = (bf16[4,48,1664]{2,1,0:T(8,128)(2,1)S(1)}, bf16[4,48,1664]{2,1,0:T(8,128)(2,1)S(1)}, u32[]{:S(2)}, u32[]{:S(2)}) collective-permute-start(bf16[4,48,1664]{2,1,0:T(8,128)(2,1)S(1)} %get-tuple-element.39), channel_id=1, source_target_pairs={{0,12},{1,13},{2,14},{3,15},{4,0},{5,1},{6,2},{7,3},{8,4},{9,5},{1... | collective-permute-start | bytes 1916936 | tf_op jit(solution)/shard_map/ppermute | solution.py:79
  29.7 0.2 fusion.20
  30.0 5.8 %fusion.75 = (f32[288]{0:T(512)S(1)}, f32[288,3072]{1,0:T(8,128)S(1)}) fusion(bf16[1536,3072]{1,0:T(8,128)(2,1)} %param.8, bf16[288,1664]{1,0:T(8,128)(2,1)S(1)} %pad_maximum_fusion.2), kind=kOutput, calls=%fused_computation.223 | convolution fusion | flops 2718793472 | bytes 13862016 | tf_op jit(solution)/shard_map/dot_general | solution.py:89
  35.8 1.3 %fusion.2 = (f32[288]{0:T(512)S(1)}, f32[288]{0:T(512)S(1)}, f32[288]{0:T(512)S(1)}) fusion(f32[288,3072]{1,0:T(8,128)S(1)} %get-tuple-element.65, f32[288]{0:T(512)S(1)} %get-tuple-element.64, s32[288]{0:T(512)S(1)} %fusion.20), kind=kLoop, calls=%fused_computation.18 | loop fusion | flops 6192288 | bytes 3544704 | tf_op jit(solution)/shard_map/reduce_sum | solution.py:92
  37.2 1.8 %fusion.76 = (f32[96]{0:T(128)S(1)}, f32[96,3072]{1,0:T(8,128)S(1)}) fusion(bf16[1536,3072]{1,0:T(8,128)(2,1)S(1)} %bitcast.58, bf16[96,1664]{1,0:T(8,128)(2,1)S(1)} %collective-permute-done.2), kind=kOutput, calls=%fused_computation.224 | convolution fusion | flops 906264448 | bytes 10912128 | tf_op jit(solution)/shard_map/dot_general | solution.py:89
  39.0 0.2 maximum_reduce_fusion
  39.2 0.2 fusion.22
  39.4 0.5 fusion.7
  40.0 0.3 collective-permute-start.4
  40.2 6.9 %collective-permute-done.8 = bf16[4,48,1664]{2,1,0:T(8,128)(2,1)S(1)} collective-permute-done((bf16[4,48,1664]{2,1,0:T(8,128)(2,1)S(1)}, bf16[4,48,1664]{2,1,0:T(8,128)(2,1)S(1)}, u32[]{:S(2)}, u32[]{:S(2)}) %collective-permute-start.8) | collective-permute-done | bytes 639008 | tf_op jit(solution)/shard_map/ppermute | solution.py:79
  47.1 0.1 pad_maximum_fusion.1
  47.2 5.7 %fusion.78 = (f32[384]{0:T(512)S(1)}, f32[384,3072]{1,0:T(8,128)}) fusion(bf16[1536,3072]{1,0:T(8,128)(2,1)S(1)} %bitcast.58, bf16[384,1664]{1,0:T(8,128)(2,1)S(1)} %bitcast.68), kind=kOutput, calls=%fused_computation.226 | convolution fusion | flops 3625057792 | bytes 15336960 | tf_op jit(solution)/shard_map/dot_general | solution.py:89
  53.0 1.0 collective-permute-done.6
  54.0 0.2 maximum_maximum_fusion
  54.2 9.9 %fusion.77 = (f32[768]{0:T(1024)S(1)}, f32[768,3072]{1,0:T(8,128)}) fusion(bf16[1536,3072]{1,0:T(8,128)(2,1)S(1)} %bitcast.58, bf16[768,1664]{1,0:T(8,128)(2,1)S(1)} %bitcast.66), kind=kOutput, calls=%fused_computation.225 | convolution fusion | flops 7250115584 | bytes 21236736 | tf_op jit(solution)/shard_map/dot_general | solution.py:89
  64.2 0.2 slice_reduce_fusion.6
  64.3 0.2 slice_reduce_fusion.7
  64.5 0.2 slice_reduce_fusion.8
  64.8 0.7 gather_fusion.3
  65.5 0.6 fusion.70
  66.4 0.1 copy.16
  66.6 4.0 %fusion.1 = (f32[384]{0:T(512)S(1)}, f32[384]{0:T(512)S(1)}, f32[384]{0:T(512)S(1)}) fusion(f32[384,3072]{1,0:T(8,128)} %get-tuple-element.71, f32[384]{0:T(512)S(1)} %get-tuple-element.70, s32[384]{0:T(512)S(1)} %fusion.38), kind=kLoop, calls=%fused_computation.13 | loop fusion | flops 8256384 | bytes 4726272 | tf_op jit(solution)/shard_map/reduce_sum | solution.py:92
  70.6 6.3 %fusion = (f32[768]{0:T(1024)S(1)}, f32[768]{0:T(1024)S(1)}, f32[768]{0:T(1024)S(1)}) fusion(f32[768,3072]{1,0:T(8,128)} %get-tuple-element.69, f32[768]{0:T(1024)S(1)} %get-tuple-element.68, s32[768]{0:T(1024)S(1)} %fusion.36), kind=kLoop, calls=%fused_computation.8 | loop fusion | flops 16512768 | bytes 9452544 | tf_op jit(solution)/shard_map/reduce_sum | solution.py:92
  77.0 0.1 concatenate.33
  77.2 0.6 gather_fusion.2
  77.8 0.1 gather.19
  77.9 1.1 collective-permute-start.9
  79.0 2.8 %collective-permute-done.9 = f32[4,1536]{1,0:T(4,128)S(1)} collective-permute-done((f32[4,1536]{1,0:T(4,128)S(1)}, f32[4,1536]{1,0:T(4,128)S(1)}, u32[]{:S(2)}, u32[]{:S(2)}) %collective-permute-start.9) | collective-permute-done | bytes 24608 | tf_op jit(solution)/shard_map/ppermute | solution.py:32
  82.0 2.7 %collective-permute-start.10 = (f32[4,1536]{1,0:T(4,128)S(1)}, f32[4,1536]{1,0:T(4,128)S(1)}, u32[]{:S(2)}, u32[]{:S(2)}) collective-permute-start(f32[4,1536]{1,0:T(4,128)S(1)} %pad_maximum_fusion.4), channel_id=1, source_target_pairs={{0,3},{1,2},{2,1},{3,0},{4,7},{5,6},{6,5},{7,4},{8,11},{9,10},{10,... | collective-permute-start | bytes 73736 | tf_op jit(solution)/shard_map/ppermute | solution.py:32
  84.7 2.4 %collective-permute-done.10 = f32[4,1536]{1,0:T(4,128)S(1)} collective-permute-done((f32[4,1536]{1,0:T(4,128)S(1)}, f32[4,1536]{1,0:T(4,128)S(1)}, u32[]{:S(2)}, u32[]{:S(2)}) %collective-permute-start.10) | collective-permute-done | bytes 24608 | tf_op jit(solution)/shard_map/ppermute | solution.py:32
  87.3 1.5 %collective-permute-start.11 = (f32[4,1536]{1,0:T(4,128)S(1)}, f32[4,1536]{1,0:T(4,128)S(1)}, u32[]{:S(2)}, u32[]{:S(2)}) collective-permute-start(f32[4,1536]{1,0:T(4,128)S(1)} %pad_maximum_fusion.5), channel_id=1, source_target_pairs={{0,4},{1,5},{2,6},{3,7},{4,0},{5,1},{6,2},{7,3},{8,12},{9,13},{10,... | collective-permute-start | bytes 73736 | tf_op jit(solution)/shard_map/ppermute | solution.py:32
  88.8 2.4 %collective-permute-done.11 = f32[4,1536]{1,0:T(4,128)S(1)} collective-permute-done((f32[4,1536]{1,0:T(4,128)S(1)}, f32[4,1536]{1,0:T(4,128)S(1)}, u32[]{:S(2)}, u32[]{:S(2)}) %collective-permute-start.11) | collective-permute-done | bytes 24608 | tf_op jit(solution)/shard_map/ppermute | solution.py:32
  91.3 2.7 %collective-permute-start.12 = (f32[4,1536]{1,0:T(4,128)S(1)}, f32[4,1536]{1,0:T(4,128)S(1)}, u32[]{:S(2)}, u32[]{:S(2)}) collective-permute-start(f32[4,1536]{1,0:T(4,128)S(1)} %pad_maximum_fusion.6), channel_id=1, source_target_pairs={{0,12},{1,13},{2,14},{3,15},{4,8},{5,9},{6,10},{7,11},{8,4},{9,5},... | collective-permute-start | bytes 73736 | tf_op jit(solution)/shard_map/ppermute | solution.py:32
  94.8 1.6 %collective-permute-done.12 = f32[4,1536]{1,0:T(4,128)S(1)} collective-permute-done((f32[4,1536]{1,0:T(4,128)S(1)}, f32[4,1536]{1,0:T(4,128)S(1)}, u32[]{:S(2)}, u32[]{:S(2)}) %collective-permute-start.12) | collective-permute-done | bytes 24608 | tf_op jit(solution)/shard_map/ppermute | solution.py:32
  96.5 0.8 select_reduce_fusion.4
  97.2 0.7 pad_maximum_fusion.11
  98.0 0.7 convolution_bitcast_fusion
  98.7 0.7 convolution_bitcast_fusion.2
  99.5 0.7 convolution_bitcast_fusion.1
  100.2 0.7 fusion.43
  100.9 1.6 %collective-permute-start.14 = (f32[2]{0:T(128)S(1)}, f32[2]{0:T(128)S(1)}, u32[]{:S(2)}, u32[]{:S(2)}) collective-permute-start(f32[2]{0:T(128)S(1)} %fusion.43), channel_id=1, source_target_pairs={{0,32},{16,48},{32,0},{48,16},{64,96},{80,112},{96,64},{112,80},{1... | collective-permute-start | bytes 32 | tf_op jit(solution)/shard_map/ppermute | solution.py:32
  102.5 2.0 %collective-permute-done.14 = f32[2]{0:T(128)S(1)} collective-permute-done((f32[2]{0:T(128)S(1)}, f32[2]{0:T(128)S(1)}, u32[]{:S(2)}, u32[]{:S(2)}) %collective-permute-start.14) | collective-permute-done | bytes 40 | tf_op jit(solution)/shard_map/ppermute | solution.py:32
  104.5 3.0 %collective-permute-start.15 = (f32[2]{0:T(128)S(1)}, f32[2]{0:T(128)S(1)}, u32[]{:S(2)}, u32[]{:S(2)}) collective-permute-start(f32[2]{0:T(128)S(1)} %fusion.42), channel_id=1, source_target_pairs={{0,96},{16,112},{32,64},{48,80},{64,32},{80,48},{96,0},{112,16},{1... | collective-permute-start | bytes 32 | tf_op jit(solution)/shard_map/ppermute | solution.py:32
  107.5 1.8 %collective-permute-done.15 = f32[2]{0:T(128)S(1)} collective-permute-done((f32[2]{0:T(128)S(1)}, f32[2]{0:T(128)S(1)}, u32[]{:S(2)}, u32[]{:S(2)}) %collective-permute-start.15) | collective-permute-done | bytes 40 | tf_op jit(solution)/shard_map/ppermute | solution.py:32
  109.3 0.6 fusion.73
  (74 shorter events, 1.5 us)
Async XLA Ops:
  7.5 9.0 %collective-permute-start.2 = (bf16[96,1664]{1,0:T(8,128)(2,1)S(1)}, bf16[96,1664]{1,0:T(8,128)(2,1)S(1)}, u32[]{:S(2)}, u32[]{:S(2)}) collective-permute-start(bf16[96,1664]{1,0:T(8,128)(2,1)S(1)} %get-tuple-element.41), channel_id=1, source_target_pairs={{0,2},{1,3},{2,0},{3,1},{4,6},{5,7},{6,4},{7,5},{8,10},{9,11},{10,... | collective-permute-start | bytes 958472 | tf_op jit(solution)/shard_map/ppermute | solution.py:79
  11.5 9.4 %collective-permute-start.1 = (bf16[96,1664]{1,0:T(8,128)(2,1)S(1)}, bf16[96,1664]{1,0:T(8,128)(2,1)S(1)}, u32[]{:S(2)}, u32[]{:S(2)}) collective-permute-start(bf16[96,1664]{1,0:T(8,128)(2,1)S(1)} %get-tuple-element.41), channel_id=1, source_target_pairs={{0,3},{1,0},{2,1},{3,2},{4,7},{5,4},{6,5},{7,6},{8,11},{9,8},{10,9... | collective-permute-start | bytes 958472 | tf_op jit(solution)/shard_map/ppermute | solution.py:79
  12.3 8.7 %collective-permute-start = (bf16[96,1664]{1,0:T(8,128)(2,1)S(1)}, bf16[96,1664]{1,0:T(8,128)(2,1)S(1)}, u32[]{:S(2)}, u32[]{:S(2)}) collective-permute-start(bf16[96,1664]{1,0:T(8,128)(2,1)S(1)} %get-tuple-element.41), channel_id=1, source_target_pairs={{0,1},{1,2},{2,3},{3,0},{4,5},{5,6},{6,7},{7,4},{8,9},{9,10},{10,1... | collective-permute-start | bytes 958472 | tf_op jit(solution)/shard_map/ppermute | solution.py:79
  21.3 18.7 %collective-permute-start.7 = (bf16[4,48,1664]{2,1,0:T(8,128)(2,1)S(1)}, bf16[4,48,1664]{2,1,0:T(8,128)(2,1)S(1)}, u32[]{:S(2)}, u32[]{:S(2)}) collective-permute-start(bf16[4,48,1664]{2,1,0:T(8,128)(2,1)S(1)} %get-tuple-element.38), channel_id=1, source_target_pairs={{0,8},{1,9},{2,10},{3,11},{4,12},{5,13},{6,14},{7,15},{8,0},{9,1},... | collective-permute-start | bytes 1916936 | tf_op jit(solution)/shard_map/ppermute | solution.py:79
  24.4 28.6 %collective-permute-start.5 = (bf16[4,48,1664]{2,1,0:T(8,128)(2,1)S(1)}, bf16[4,48,1664]{2,1,0:T(8,128)(2,1)S(1)}, u32[]{:S(2)}, u32[]{:S(2)}) collective-permute-start(bf16[4,48,1664]{2,1,0:T(8,128)(2,1)S(1)} %get-tuple-element.38), channel_id=1, source_target_pairs={{0,12},{1,13},{2,14},{3,15},{4,0},{5,1},{6,2},{7,3},{8,4},{9,5},{1... | collective-permute-start | bytes 1916936 | tf_op jit(solution)/shard_map/ppermute | solution.py:79
  25.5 27.4 %collective-permute-start.3 = (bf16[4,48,1664]{2,1,0:T(8,128)(2,1)S(1)}, bf16[4,48,1664]{2,1,0:T(8,128)(2,1)S(1)}, u32[]{:S(2)}, u32[]{:S(2)}) collective-permute-start(bf16[4,48,1664]{2,1,0:T(8,128)(2,1)S(1)} %get-tuple-element.38), channel_id=1, source_target_pairs={{0,4},{1,5},{2,6},{3,7},{4,8},{5,9},{6,10},{7,11},{8,12},{9,13},{1... | collective-permute-start | bytes 1916936 | tf_op jit(solution)/shard_map/ppermute | solution.py:79
  26.4 20.7 %collective-permute-start.8 = (bf16[4,48,1664]{2,1,0:T(8,128)(2,1)S(1)}, bf16[4,48,1664]{2,1,0:T(8,128)(2,1)S(1)}, u32[]{:S(2)}, u32[]{:S(2)}) collective-permute-start(bf16[4,48,1664]{2,1,0:T(8,128)(2,1)S(1)} %get-tuple-element.39), channel_id=1, source_target_pairs={{0,8},{1,9},{2,10},{3,11},{4,12},{5,13},{6,14},{7,15},{8,0},{9,1},... | collective-permute-start | bytes 1916936 | tf_op jit(solution)/shard_map/ppermute | solution.py:79
  27.1 26.9 %collective-permute-start.6 = (bf16[4,48,1664]{2,1,0:T(8,128)(2,1)S(1)}, bf16[4,48,1664]{2,1,0:T(8,128)(2,1)S(1)}, u32[]{:S(2)}, u32[]{:S(2)}) collective-permute-start(bf16[4,48,1664]{2,1,0:T(8,128)(2,1)S(1)} %get-tuple-element.39), channel_id=1, source_target_pairs={{0,12},{1,13},{2,14},{3,15},{4,0},{5,1},{6,2},{7,3},{8,4},{9,5},{1... | collective-permute-start | bytes 1916936 | tf_op jit(solution)/shard_map/ppermute | solution.py:79
  29.9 7.3 %slice-start = ((s8[9437184]{0:T(1024)(128)(4,1)}), s8[4194304]{0:T(1024)(128)(4,1)S(1)}, s32[]{:S(2)}) async-start(s8[9437184]{0:T(1024)(128)(4,1)} %bitcast.57), calls=%async_computation | async-start | bytes 8388608
  30.0 7.2 %slice-start.1 = ((s8[9437184]{0:T(1024)(128)(4,1)}), s8[4194304]{0:T(1024)(128)(4,1)S(1)}, s32[]{:S(2)}) async-start(s8[9437184]{0:T(1024)(128)(4,1)} %bitcast.57), calls=%async_computation.1 | async-start | bytes 8388608
  30.0 7.2 %slice-start.2 = ((s8[9437184]{0:T(1024)(128)(4,1)}), s8[1048576]{0:T(1024)(128)(4,1)S(1)}, s32[]{:S(2)}) async-start(s8[9437184]{0:T(1024)(128)(4,1)} %bitcast.57), calls=%async_computation.2 | async-start | bytes 2097152
  40.0 14.0 %collective-permute-start.4 = (bf16[4,48,1664]{2,1,0:T(8,128)(2,1)S(1)}, bf16[4,48,1664]{2,1,0:T(8,128)(2,1)S(1)}, u32[]{:S(2)}, u32[]{:S(2)}) collective-permute-start(bf16[4,48,1664]{2,1,0:T(8,128)(2,1)S(1)} %get-tuple-element.39), channel_id=1, source_target_pairs={{0,4},{1,5},{2,6},{3,7},{4,8},{5,9},{6,10},{7,11},{8,12},{9,13},{1... | collective-permute-start | bytes 1916936 | tf_op jit(solution)/shard_map/ppermute | solution.py:79
  77.9 3.9 %collective-permute-start.9 = (f32[4,1536]{1,0:T(4,128)S(1)}, f32[4,1536]{1,0:T(4,128)S(1)}, u32[]{:S(2)}, u32[]{:S(2)}) collective-permute-start(f32[4,1536]{1,0:T(4,128)S(1)} %broadcast_select_fusion), channel_id=1, source_target_pairs={{0,1},{1,0},{2,3},{3,2},{4,5},{5,4},{6,7},{7,6},{8,9},{9,8},{10,11... | collective-permute-start | bytes 73736 | tf_op jit(solution)/shard_map/ppermute | solution.py:32
  82.0 5.1 %collective-permute-start.10 = (f32[4,1536]{1,0:T(4,128)S(1)}, f32[4,1536]{1,0:T(4,128)S(1)}, u32[]{:S(2)}, u32[]{:S(2)}) collective-permute-start(f32[4,1536]{1,0:T(4,128)S(1)} %pad_maximum_fusion.4), channel_id=1, source_target_pairs={{0,3},{1,2},{2,1},{3,0},{4,7},{5,6},{6,5},{7,4},{8,11},{9,10},{10,... | collective-permute-start | bytes 73736 | tf_op jit(solution)/shard_map/ppermute | solution.py:32
  87.3 3.9 %collective-permute-start.11 = (f32[4,1536]{1,0:T(4,128)S(1)}, f32[4,1536]{1,0:T(4,128)S(1)}, u32[]{:S(2)}, u32[]{:S(2)}) collective-permute-start(f32[4,1536]{1,0:T(4,128)S(1)} %pad_maximum_fusion.5), channel_id=1, source_target_pairs={{0,4},{1,5},{2,6},{3,7},{4,0},{5,1},{6,2},{7,3},{8,12},{9,13},{10,... | collective-permute-start | bytes 73736 | tf_op jit(solution)/shard_map/ppermute | solution.py:32
  91.3 5.1 %collective-permute-start.12 = (f32[4,1536]{1,0:T(4,128)S(1)}, f32[4,1536]{1,0:T(4,128)S(1)}, u32[]{:S(2)}, u32[]{:S(2)}) collective-permute-start(f32[4,1536]{1,0:T(4,128)S(1)} %pad_maximum_fusion.6), channel_id=1, source_target_pairs={{0,12},{1,13},{2,14},{3,15},{4,8},{5,9},{6,10},{7,11},{8,4},{9,5},... | collective-permute-start | bytes 73736 | tf_op jit(solution)/shard_map/ppermute | solution.py:32
  97.9 2.2 %collective-permute-start.13 = (f32[2]{0:T(128)S(1)}, f32[2]{0:T(128)S(1)}, u32[]{:S(2)}, u32[]{:S(2)}) collective-permute-start(f32[2]{0:T(128)S(1)} %pad_maximum_fusion.11), channel_id=1, source_target_pairs={{0,16},{16,0},{32,48},{48,32},{64,80},{80,64},{96,112},{112,96},{1... | collective-permute-start | bytes 32 | tf_op jit(solution)/shard_map/ppermute | solution.py:32
  100.9 3.6 %collective-permute-start.14 = (f32[2]{0:T(128)S(1)}, f32[2]{0:T(128)S(1)}, u32[]{:S(2)}, u32[]{:S(2)}) collective-permute-start(f32[2]{0:T(128)S(1)} %fusion.43), channel_id=1, source_target_pairs={{0,32},{16,48},{32,0},{48,16},{64,96},{80,112},{96,64},{112,80},{1... | collective-permute-start | bytes 32 | tf_op jit(solution)/shard_map/ppermute | solution.py:32
  104.5 4.8 %collective-permute-start.15 = (f32[2]{0:T(128)S(1)}, f32[2]{0:T(128)S(1)}, u32[]{:S(2)}, u32[]{:S(2)}) collective-permute-start(f32[2]{0:T(128)S(1)} %fusion.42), channel_id=1, source_target_pairs={{0,96},{16,112},{32,64},{48,80},{64,32},{80,48},{96,0},{112,16},{1... | collective-permute-start | bytes 32 | tf_op jit(solution)/shard_map/ppermute | solution.py:32
